TPU v7x, 768 devices: a whole 4x8x12 slice. The times are simulated.
768 devices in a mesh: blk: 24 (over x, z_hi, core), heads: 32 (over z_lo, y).
Axes of the slice: x: 4, y: 8, z: 12 (z_hi: 3, z_lo: 4; z = z_hi * 4 + z_lo), core: 2. Of those that a mesh axis runs over, the one named last changes fastest.
Arguments:
- q_nope: bfloat16 [3072, 8192], P('blk', 'heads'), may hold values from -6 to 6
- q_rope: bfloat16 [3072, 4096], P('blk', 'heads'), may hold values from -60 to 60
- d_out: bfloat16 [3072, 8192], P('blk', 'heads'), may hold values from -6 to 6
- latent: bfloat16 [3072, 576], P('blk'), may hold values from -6 to 6
- scale_exp: int32 [4, 3072], P(None, 'blk'), may hold values from -1 to 1
- positions: int32 [3072], P('blk'), may hold values from 0 to 3071, as said below
- spans: int32 [3072], P('blk'), may hold values from 0 to 3071
- w_uk: bfloat16 [512, 8192], P(None, 'heads'), may hold values from -0.25 to 0.25
- w_uv: bfloat16 [512, 8192], P(None, 'heads'), may hold values from -0.25 to 0.25
Outputs:
- grad_q_nope: bfloat16 [3072, 8192], P('blk', 'heads')
- grad_q_rope: bfloat16 [3072, 4096], P('blk', 'heads')
- grad_latent: bfloat16 [3072, 512], P('blk')
- grad_w_uk: float32 [512, 8192], P(None, 'heads')
- grad_w_uv: float32 [512, 8192], P(None, 'heads')
Inputs may be any that keep to these rules, and one draw needn't show every extreme that they name: A permutation of the positions that maps each aligned run of 64 rows onto 64 consecutive positions in order.
All inputs are finite; a program needn't handle non-finite values.
Results may differ from a plain program's by a relative error of at most 0.02.
Values may be sent and summed in bfloat16 or wider, within the bound.
No kernel may reach another device: no remote copies, remote signals or barrier semaphores. Data moves between devices by JAX's collectives and lax.ppermute only.
A program may use at most 32 MiB of HBM per device.

v0:
```python
import jax
import jax.numpy as jnp
from jax import lax
from jax.sharding import PartitionSpec as P

D_ROPE = 64
D_NOPE = 128
D_V = 128


lowest = -1e30


def shifted(x, axis, by):
    devices = lax.axis_size(axis)
    return lax.ppermute(x, axis, [(i, (i + by) % devices) for i in range(devices)])


def dequantize(latent_block, exponents):
    col_width = latent_block.shape[1] - D_ROPE
    col_group = col_width // exponents.shape[0]
    factor = jnp.exp2(jnp.repeat(jnp.transpose(exponents), col_group, axis=1).astype(jnp.float32))
    compressed = (latent_block[:, :col_width].astype(jnp.float32) * factor).astype(jnp.bfloat16)
    return (compressed, latent_block[:, col_width:], factor)


def visible(query_pos, query_span, key_pos):
    return (key_pos[None, :] <= query_pos[:, None]) & (
        key_pos[None, :] >= query_pos[:, None] - query_span[:, None]
    )


def logits(query_part, rope_part, key_part, key_rope):
    soft_scale = (query_part.shape[2] + rope_part.shape[2]) ** (-0.5)
    scores = jnp.einsum("qhd,khd->hqk", query_part, key_part, preferred_element_type=jnp.float32)
    scores = scores + jnp.einsum(
        "qhr,kr->hqk", rope_part, key_rope, preferred_element_type=jnp.float32
    )
    return scores * soft_scale


def forward_pair(running, queries, query_rope, grad_out, key_nope, key_rope, values, pairs):
    run_max, run_sum, run_dot = running
    scores = jnp.where(pairs[None], logits(queries, query_rope, key_nope, key_rope), lowest)
    new_max = jnp.maximum(run_max, jnp.max(scores, axis=2))
    powers = jnp.where(pairs[None], jnp.exp(scores - new_max[:, :, None]), 0.0)
    rescale = jnp.exp(run_max - new_max)
    grad_prob = jnp.einsum("qhd,khd->hqk", grad_out, values, preferred_element_type=jnp.float32)
    return (
        new_max,
        run_sum * rescale + jnp.sum(powers, axis=2),
        run_dot * rescale + jnp.sum(powers * grad_prob, axis=2),
    )


def backward_pair(
    queries, query_rope, grad_out, log_norm, delta_rows, key_nope, key_rope, values, pairs
):
    soft_scale = (queries.shape[2] + query_rope.shape[2]) ** (-0.5)
    scores = logits(queries, query_rope, key_nope, key_rope)
    prob_float = jnp.where(pairs[None], jnp.exp(scores - log_norm[:, :, None]), 0.0)
    grad_prob = jnp.einsum("qhd,khd->hqk", grad_out, values, preferred_element_type=jnp.float32)
    grad_score = (prob_float * (grad_prob - delta_rows[:, :, None]) * soft_scale).astype(
        jnp.bfloat16
    )
    prob_half = prob_float.astype(jnp.bfloat16)
    query_grad = jnp.einsum(
        "hqk,khd->qhd", grad_score, key_nope, preferred_element_type=jnp.float32
    )
    rope_grad = jnp.einsum("hqk,kr->qhr", grad_score, key_rope, preferred_element_type=jnp.float32)
    key_grad = jnp.einsum("hqk,qhd->khd", grad_score, queries, preferred_element_type=jnp.float32)
    value_grad = jnp.einsum("hqk,qhd->khd", prob_half, grad_out, preferred_element_type=jnp.float32)
    return (query_grad, rope_grad, key_grad, value_grad)


def body(q_nope, q_rope, d_out, latent, scale_exp, positions, spans, w_uk, w_uv):
    row_count = q_nope.shape[0]
    head_count = w_uk.shape[1] // D_NOPE
    cycle_size = lax.axis_size("blk")
    queries = q_nope.reshape(row_count, head_count, D_NOPE)
    query_rope = q_rope.reshape(row_count, head_count, D_ROPE)
    grad_out = d_out.reshape(row_count, head_count, D_V)
    compressed, rope_home, factor = dequantize(latent, scale_exp)

    def project(block_latent, weight):
        return jnp.dot(block_latent, weight, preferred_element_type=jnp.float32).astype(
            jnp.bfloat16
        )

    arrived = (latent, scale_exp, positions)

    def keys_of(incoming):
        block_latent, rope_part, unused = dequantize(incoming[0], incoming[1])
        return (project(block_latent, w_uk), project(block_latent, w_uv), rope_part, incoming[2])

    caches = (
        jnp.zeros((cycle_size, row_count, head_count * D_NOPE), jnp.bfloat16),
        jnp.zeros((cycle_size, row_count, head_count * D_V), jnp.bfloat16),
        jnp.zeros((cycle_size, row_count, D_ROPE), jnp.bfloat16),
        jnp.zeros((cycle_size, row_count), jnp.int32),
    )
    softmax_stats = (
        jnp.full((head_count, row_count), lowest, jnp.float32),
        jnp.zeros((head_count, row_count), jnp.float32),
        jnp.zeros((head_count, row_count), jnp.float32),
    )

    def forward_visit(turn_index, incoming, stats_now, caches_now):
        pieces = keys_of(incoming)
        pairs = visible(positions, spans, pieces[3])
        key_nope = pieces[0].reshape(row_count, head_count, D_NOPE)
        values = pieces[1].reshape(row_count, head_count, D_V)
        stats_now = forward_pair(
            stats_now, queries, query_rope, grad_out, key_nope, pieces[2], values, pairs
        )
        caches_now = tuple(
            (
                lax.dynamic_update_index_in_dim(stored, fresh_item, turn_index, 0)
                for stored, fresh_item in zip(caches_now, pieces)
            )
        )
        return (stats_now, caches_now)

    def forward_turn(turn_index, loop_state):
        incoming, stats_now, caches_now = loop_state
        stats_now, caches_now = forward_visit(turn_index, incoming, stats_now, caches_now)
        incoming = tuple(shifted((incoming[0], incoming[1], incoming[2]), "blk", 1))
        return (incoming, stats_now, caches_now)

    arrived, softmax_stats, caches = lax.fori_loop(
        0, cycle_size - 1, forward_turn, (arrived, softmax_stats, caches)
    )
    softmax_stats, caches = forward_visit(cycle_size - 1, arrived, softmax_stats, caches)
    log_norm = softmax_stats[0] + jnp.log(softmax_stats[1])
    delta_rows = softmax_stats[2] / softmax_stats[1]

    def grads_at(slot_index):
        fetched = tuple(
            (lax.dynamic_index_in_dim(stored, slot_index, 0, keepdims=False) for stored in caches)
        )
        pairs = visible(positions, spans, fetched[3])
        key_nope = fetched[0].reshape(row_count, head_count, D_NOPE)
        values = fetched[1].reshape(row_count, head_count, D_V)
        return backward_pair(
            queries, query_rope, grad_out, log_norm, delta_rows, key_nope, fetched[2], values, pairs
        )

    query_acc = (
        jnp.zeros((row_count, head_count, D_NOPE), jnp.float32),
        jnp.zeros((row_count, head_count, D_ROPE), jnp.float32),
    )

    def backward_visit(turn_index, query_now, block_grads):
        all_heads = grads_at((turn_index + 1) % cycle_size)
        query_now = (query_now[0] + all_heads[0], query_now[1] + all_heads[1])
        block_grads = (block_grads[0] + all_heads[2], block_grads[1] + all_heads[3])
        return (query_now, block_grads)

    def backward_turn(turn_index, loop_state):
        query_now, block_grads = backward_visit(turn_index, loop_state[0], loop_state[1])
        block_grads = tuple(shifted((block_grads[0], block_grads[1]), "blk", 1))
        return (query_now, block_grads)

    start_full = (
        jnp.zeros((row_count, head_count, D_NOPE), jnp.float32),
        jnp.zeros((row_count, head_count, D_V), jnp.float32),
    )
    loop_state = lax.fori_loop(0, cycle_size - 1, backward_turn, (query_acc, start_full))
    query_acc, block_grads = backward_visit(cycle_size - 1, loop_state[0], loop_state[1])
    key_grad, value_grad = block_grads
    key_flat = key_grad.reshape(row_count, head_count * D_NOPE).astype(jnp.bfloat16)
    value_flat = value_grad.reshape(row_count, head_count * D_V).astype(jnp.bfloat16)

    def back_project(grad_flat, weight):
        return lax.dot_general(
            grad_flat, weight, (((1,), (1,)), ((), ())), preferred_element_type=jnp.float32
        )

    latent_part = back_project(key_flat, w_uk) + back_project(value_flat, w_uv)
    latent_sum = lax.psum(latent_part, "heads")
    grad_latent = (latent_sum * factor).astype(jnp.bfloat16)

    def weight_part(grad_flat):
        product = lax.dot_general(
            compressed, grad_flat, (((0,), (0,)), ((), ())), preferred_element_type=jnp.float32
        )
        return lax.optimization_barrier(product.astype(jnp.bfloat16)).astype(jnp.float32)

    weight_key_grad, weight_value_grad = (
        lax.psum(weight_part(key_flat).astype(jnp.bfloat16), "blk").astype(jnp.float32),
        lax.psum(weight_part(value_flat).astype(jnp.bfloat16), "blk").astype(jnp.float32),
    )
    grad_q_nope = query_acc[0].reshape(row_count, head_count * D_NOPE).astype(jnp.bfloat16)
    grad_q_rope = query_acc[1].reshape(row_count, head_count * D_ROPE).astype(jnp.bfloat16)
    return (grad_q_nope, grad_q_rope, grad_latent, weight_key_grad, weight_value_grad)


def solution(mesh):
    in_specs = (
        P("blk", "heads"),
        P("blk", "heads"),
        P("blk", "heads"),
        P("blk", None),
        P(None, "blk"),
        P("blk"),
        P("blk"),
        P(None, "heads"),
        P(None, "heads"),
    )
    out_specs = (
        P("blk", "heads"),
        P("blk", "heads"),
        P("blk", None),
        P(None, "heads"),
        P(None, "heads"),
    )
    return jax.shard_map(body, mesh=mesh, in_specs=in_specs, out_specs=out_specs, check_vma=False)
```

profile of v0, /device:TPU:56, one launch (start us, length us, event | category | flops | bytes accessed | tf_op | source)
XLA Modules:
  0.0 1528.5 jit_solution(8305806227117300796)
XLA Ops:
  14.4 389.7 %while.56 = (s32[]{:T(128)}, bf16[128,576]{0,1:T(8,128)(2,1)S(1)}, s32[4,128]{1,0:T(4,128)S(1)}, s32[128]{0:T(128)S(1)}, f32[2,128]{1,0:T(2,128)S(1)}, /*index=5...) while((s32[]{:T(128)}, bf16[128,576]{0,1:T(8,128)(2,1)S(1)}, ...), condition=%wide.region_4.5_spmd.clone, body=%wide.region_0.4_spmd.clone.sunk | while | flops 88754944 | bytes 3696460 | solution.py:130
  16.3 11.0 collective-permute-start.2
  67.0 8.1 collective-permute-done.2
  249.2 8.2 collective-permute-done.2
  299.0 7.8 collective-permute-done.2
  348.3 7.6 collective-permute-done.2
  411.2 528.6 %while.57 = (s32[]{:T(128)}, f32[128,2,128]{0,2,1:T(8,128)S(1)}, f32[128,2,64]{0,2,1:T(8,128)S(1)}, f32[128,2,128]{2,0,1:T(8,128)S(1)}, f32[128,2,128]{2,0,1:T(8...) while((s32[]{:T(128)}, f32[128,2,128]{0,2,1:T(8,128)S(1)}, ...), condition=%wide.region_9.10_spmd.clone, body=%wide.region_8.9_spmd.clone.sunk | while | flops 50839564 | bytes 3707776 | solution.py:168
  446.6 10.5 collective-permute-done.4
  466.0 8.6 collective-permute-done.3
  484.9 7.3 collective-permute-done.3
  512.2 9.8 collective-permute-done.4
  530.9 7.4 collective-permute-done.3
  549.5 7.3 collective-permute-done.3
  556.8 10.5 collective-permute-done.4
  576.2 7.8 collective-permute-done.3
  594.6 7.3 collective-permute-done.3
  602.0 10.5 collective-permute-done.4
  621.4 9.3 collective-permute-done.3
  645.2 14.6 collective-permute-done.3
  670.1 7.5 collective-permute-done.3
  692.8 13.5 collective-permute-done.3
  716.6 8.6 collective-permute-done.3
  758.5 7.3 collective-permute-done.3
  765.8 10.5 collective-permute-done.4
  803.7 8.0 collective-permute-done.3
  811.7 9.3 collective-permute-done.4
  829.9 13.7 collective-permute-done.3
  876.6 9.5 collective-permute-done.3
  900.6 9.2 collective-permute-done.3
  924.3 14.2 collective-permute-done.3
  948.6 291.4 %all-reduce.4.cloned.1.call-done = f32[128,512]{1,0:T(8,128)} async-done(((f32[128,512]{1,0:T(8,128)}), f32[128,512]{1,0:T(8,128)}) %all-reduce.4.cloned.1.call-update) | async-done | bytes 262160 | tf_op jit(solution)/shard_map/psum | solution.py:180
  1241.6 276.5 %all-reduce.6.cloned.1.call-done = (bf16[512,256]{1,0:T(8,128)(2,1)}, bf16[512,256]{1,0:T(8,128)(2,1)}) async-done(((bf16[512,256]{1,0:T(8,128)(2,1)}, bf16[512,256]{1,0:T(8,128)(2,1)}), (bf16[512,256]{1,0:T(8,128)(2,1)}, bf16[512,256]{1,0:T(8,128)(2,1)})) %all-reduce.6.cloned.1.call-update) | async-done | bytes 524304 | tf_op jit(solution)/shard_map/psum | solution.py:190
  (1000 shorter events, 677.0 us)
Async XLA Ops:
  7.2 1232.8 %all-reduce.4.cloned.1.call-start = ((), (), s32[]{:S(2)}) async-start(), calls=%async_computation | async-start | bytes 524288 | tf_op jit(solution)/shard_map/psum | solution.py:180
  14.4 24.1 %collective-permute-start = (bf16[128,576]{0,1:T(8,128)(2,1)S(1)}, bf16[128,576]{0,1:T(8,128)(2,1)S(1)}, u32[]{:S(2)}, u32[]{:S(2)}) collective-permute-start(bf16[128,576]{0,1:T(8,128)(2,1)S(1)} %copy.142), channel_id=1, source_target_pairs={{0,32},{32,64},{64,96},{96,128},{128,160},{160,192},{192,224},{224... | collective-permute-start | bytes 442376 | tf_op jit(solution)/shard_map/while/body/eval_jaxpr/ppermute | solution.py:16
  16.3 17.6 %collective-permute-start.2 = (s32[128]{0:T(128)S(1)}, s32[128]{0:T(128)S(1)}, u32[]{:S(2)}, u32[]{:S(2)}) collective-permute-start(s32[128]{0:T(128)S(1)} %copy.144), channel_id=1, source_target_pairs={{0,32},{32,64},{64,96},{96,128},{128,160},{160,192},{192,224},{224... | collective-permute-start | bytes 1544 | tf_op jit(solution)/shard_map/while/body/eval_jaxpr/ppermute | solution.py:16
  38.5 19.2 %collective-permute-start = (bf16[128,576]{0,1:T(8,128)(2,1)S(1)}, bf16[128,576]{0,1:T(8,128)(2,1)S(1)}, u32[]{:S(2)}, u32[]{:S(2)}) collective-permute-start(bf16[128,576]{0,1:T(8,128)(2,1)S(1)} %copy.142), channel_id=1, source_target_pairs={{0,32},{32,64},{64,96},{96,128},{128,160},{160,192},{192,224},{224... | collective-permute-start | bytes 442376 | tf_op jit(solution)/shard_map/while/body/eval_jaxpr/ppermute | solution.py:16
  57.7 17.3 %collective-permute-start = (bf16[128,576]{0,1:T(8,128)(2,1)S(1)}, bf16[128,576]{0,1:T(8,128)(2,1)S(1)}, u32[]{:S(2)}, u32[]{:S(2)}) collective-permute-start(bf16[128,576]{0,1:T(8,128)(2,1)S(1)} %copy.142), channel_id=1, source_target_pairs={{0,32},{32,64},{64,96},{96,128},{128,160},{160,192},{192,224},{224... | collective-permute-start | bytes 442376 | tf_op jit(solution)/shard_map/while/body/eval_jaxpr/ppermute | solution.py:16
  75.1 17.5 %collective-permute-start = (bf16[128,576]{0,1:T(8,128)(2,1)S(1)}, bf16[128,576]{0,1:T(8,128)(2,1)S(1)}, u32[]{:S(2)}, u32[]{:S(2)}) collective-permute-start(bf16[128,576]{0,1:T(8,128)(2,1)S(1)} %copy.142), channel_id=1, source_target_pairs={{0,32},{32,64},{64,96},{96,128},{128,160},{160,192},{192,224},{224... | collective-permute-start | bytes 442376 | tf_op jit(solution)/shard_map/while/body/eval_jaxpr/ppermute | solution.py:16
  188.7 17.4 %collective-permute-start = (bf16[128,576]{0,1:T(8,128)(2,1)S(1)}, bf16[128,576]{0,1:T(8,128)(2,1)S(1)}, u32[]{:S(2)}, u32[]{:S(2)}) collective-permute-start(bf16[128,576]{0,1:T(8,128)(2,1)S(1)} %copy.142), channel_id=1, source_target_pairs={{0,32},{32,64},{64,96},{96,128},{128,160},{160,192},{192,224},{224... | collective-permute-start | bytes 442376 | tf_op jit(solution)/shard_map/while/body/eval_jaxpr/ppermute | solution.py:16
  206.1 18.2 %collective-permute-start = (bf16[128,576]{0,1:T(8,128)(2,1)S(1)}, bf16[128,576]{0,1:T(8,128)(2,1)S(1)}, u32[]{:S(2)}, u32[]{:S(2)}) collective-permute-start(bf16[128,576]{0,1:T(8,128)(2,1)S(1)} %copy.142), channel_id=1, source_target_pairs={{0,32},{32,64},{64,96},{96,128},{128,160},{160,192},{192,224},{224... | collective-permute-start | bytes 442376 | tf_op jit(solution)/shard_map/while/body/eval_jaxpr/ppermute | solution.py:16
  240.5 16.8 %collective-permute-start = (bf16[128,576]{0,1:T(8,128)(2,1)S(1)}, bf16[128,576]{0,1:T(8,128)(2,1)S(1)}, u32[]{:S(2)}, u32[]{:S(2)}) collective-permute-start(bf16[128,576]{0,1:T(8,128)(2,1)S(1)} %copy.142), channel_id=1, source_target_pairs={{0,32},{32,64},{64,96},{96,128},{128,160},{160,192},{192,224},{224... | collective-permute-start | bytes 442376 | tf_op jit(solution)/shard_map/while/body/eval_jaxpr/ppermute | solution.py:16
  272.5 17.0 %collective-permute-start = (bf16[128,576]{0,1:T(8,128)(2,1)S(1)}, bf16[128,576]{0,1:T(8,128)(2,1)S(1)}, u32[]{:S(2)}, u32[]{:S(2)}) collective-permute-start(bf16[128,576]{0,1:T(8,128)(2,1)S(1)} %copy.142), channel_id=1, source_target_pairs={{0,32},{32,64},{64,96},{96,128},{128,160},{160,192},{192,224},{224... | collective-permute-start | bytes 442376 | tf_op jit(solution)/shard_map/while/body/eval_jaxpr/ppermute | solution.py:16
  289.5 17.3 %collective-permute-start = (bf16[128,576]{0,1:T(8,128)(2,1)S(1)}, bf16[128,576]{0,1:T(8,128)(2,1)S(1)}, u32[]{:S(2)}, u32[]{:S(2)}) collective-permute-start(bf16[128,576]{0,1:T(8,128)(2,1)S(1)} %copy.142), channel_id=1, source_target_pairs={{0,32},{32,64},{64,96},{96,128},{128,160},{160,192},{192,224},{224... | collective-permute-start | bytes 442376 | tf_op jit(solution)/shard_map/while/body/eval_jaxpr/ppermute | solution.py:16
  338.6 17.3 %collective-permute-start = (bf16[128,576]{0,1:T(8,128)(2,1)S(1)}, bf16[128,576]{0,1:T(8,128)(2,1)S(1)}, u32[]{:S(2)}, u32[]{:S(2)}) collective-permute-start(bf16[128,576]{0,1:T(8,128)(2,1)S(1)} %copy.142), channel_id=1, source_target_pairs={{0,32},{32,64},{64,96},{96,128},{128,160},{160,192},{192,224},{224... | collective-permute-start | bytes 442376 | tf_op jit(solution)/shard_map/while/body/eval_jaxpr/ppermute | solution.py:16
  387.2 16.9 %collective-permute-start = (bf16[128,576]{0,1:T(8,128)(2,1)S(1)}, bf16[128,576]{0,1:T(8,128)(2,1)S(1)}, u32[]{:S(2)}, u32[]{:S(2)}) collective-permute-start(bf16[128,576]{0,1:T(8,128)(2,1)S(1)} %copy.142), channel_id=1, source_target_pairs={{0,32},{32,64},{64,96},{96,128},{128,160},{160,192},{192,224},{224... | collective-permute-start | bytes 442376 | tf_op jit(solution)/shard_map/while/body/eval_jaxpr/ppermute | solution.py:16
  436.4 20.7 %collective-permute-start.4 = (f32[128,2,128]{2,0,1:T(8,128)S(1)}, f32[128,2,128]{2,0,1:T(8,128)S(1)}, u32[]{:S(2)}, u32[]{:S(2)}) collective-permute-start(f32[128,2,128]{2,0,1:T(8,128)S(1)} %fusion.196), channel_id=1, source_target_pairs={{0,32},{32,64},{64,96},{96,128},{128,160},{160,192},{192,224},{224... | collective-permute-start | bytes 393224 | tf_op jit(solution)/shard_map/while/body/eval_jaxpr/ppermute | solution.py:16
  501.9 20.1 %collective-permute-start.4 = (f32[128,2,128]{2,0,1:T(8,128)S(1)}, f32[128,2,128]{2,0,1:T(8,128)S(1)}, u32[]{:S(2)}, u32[]{:S(2)}) collective-permute-start(f32[128,2,128]{2,0,1:T(8,128)S(1)} %fusion.196), channel_id=1, source_target_pairs={{0,32},{32,64},{64,96},{96,128},{128,160},{160,192},{192,224},{224... | collective-permute-start | bytes 393224 | tf_op jit(solution)/shard_map/while/body/eval_jaxpr/ppermute | solution.py:16
  546.5 20.9 %collective-permute-start.4 = (f32[128,2,128]{2,0,1:T(8,128)S(1)}, f32[128,2,128]{2,0,1:T(8,128)S(1)}, u32[]{:S(2)}, u32[]{:S(2)}) collective-permute-start(f32[128,2,128]{2,0,1:T(8,128)S(1)} %fusion.196), channel_id=1, source_target_pairs={{0,32},{32,64},{64,96},{96,128},{128,160},{160,192},{192,224},{224... | collective-permute-start | bytes 393224 | tf_op jit(solution)/shard_map/while/body/eval_jaxpr/ppermute | solution.py:16
  591.7 20.8 %collective-permute-start.4 = (f32[128,2,128]{2,0,1:T(8,128)S(1)}, f32[128,2,128]{2,0,1:T(8,128)S(1)}, u32[]{:S(2)}, u32[]{:S(2)}) collective-permute-start(f32[128,2,128]{2,0,1:T(8,128)S(1)} %fusion.196), channel_id=1, source_target_pairs={{0,32},{32,64},{64,96},{96,128},{128,160},{160,192},{192,224},{224... | collective-permute-start | bytes 393224 | tf_op jit(solution)/shard_map/while/body/eval_jaxpr/ppermute | solution.py:16
  618.4 17.9 %collective-permute-start.4 = (f32[128,2,128]{2,0,1:T(8,128)S(1)}, f32[128,2,128]{2,0,1:T(8,128)S(1)}, u32[]{:S(2)}, u32[]{:S(2)}) collective-permute-start(f32[128,2,128]{2,0,1:T(8,128)S(1)} %fusion.196), channel_id=1, source_target_pairs={{0,32},{32,64},{64,96},{96,128},{128,160},{160,192},{192,224},{224... | collective-permute-start | bytes 393224 | tf_op jit(solution)/shard_map/while/body/eval_jaxpr/ppermute | solution.py:16
  640.1 19.7 %collective-permute-start.3 = (f32[128,2,128]{2,0,1:T(8,128)S(1)}, f32[128,2,128]{2,0,1:T(8,128)S(1)}, u32[]{:S(2)}, u32[]{:S(2)}) collective-permute-start(f32[128,2,128]{2,0,1:T(8,128)S(1)} %fusion.195), channel_id=1, source_target_pairs={{0,32},{32,64},{64,96},{96,128},{128,160},{160,192},{192,224},{224... | collective-permute-start | bytes 393224 | tf_op jit(solution)/shard_map/while/body/eval_jaxpr/ppermute | solution.py:16
  642.2 19.0 %collective-permute-start.4 = (f32[128,2,128]{2,0,1:T(8,128)S(1)}, f32[128,2,128]{2,0,1:T(8,128)S(1)}, u32[]{:S(2)}, u32[]{:S(2)}) collective-permute-start(f32[128,2,128]{2,0,1:T(8,128)S(1)} %fusion.196), channel_id=1, source_target_pairs={{0,32},{32,64},{64,96},{96,128},{128,160},{160,192},{192,224},{224... | collective-permute-start | bytes 393224 | tf_op jit(solution)/shard_map/while/body/eval_jaxpr/ppermute | solution.py:16
  687.8 18.6 %collective-permute-start.3 = (f32[128,2,128]{2,0,1:T(8,128)S(1)}, f32[128,2,128]{2,0,1:T(8,128)S(1)}, u32[]{:S(2)}, u32[]{:S(2)}) collective-permute-start(f32[128,2,128]{2,0,1:T(8,128)S(1)} %fusion.195), channel_id=1, source_target_pairs={{0,32},{32,64},{64,96},{96,128},{128,160},{160,192},{192,224},{224... | collective-permute-start | bytes 393224 | tf_op jit(solution)/shard_map/while/body/eval_jaxpr/ppermute | solution.py:16
  689.8 17.9 %collective-permute-start.4 = (f32[128,2,128]{2,0,1:T(8,128)S(1)}, f32[128,2,128]{2,0,1:T(8,128)S(1)}, u32[]{:S(2)}, u32[]{:S(2)}) collective-permute-start(f32[128,2,128]{2,0,1:T(8,128)S(1)} %fusion.196), channel_id=1, source_target_pairs={{0,32},{32,64},{64,96},{96,128},{128,160},{160,192},{192,224},{224... | collective-permute-start | bytes 393224 | tf_op jit(solution)/shard_map/while/body/eval_jaxpr/ppermute | solution.py:16
  713.7 17.4 %collective-permute-start.4 = (f32[128,2,128]{2,0,1:T(8,128)S(1)}, f32[128,2,128]{2,0,1:T(8,128)S(1)}, u32[]{:S(2)}, u32[]{:S(2)}) collective-permute-start(f32[128,2,128]{2,0,1:T(8,128)S(1)} %fusion.196), channel_id=1, source_target_pairs={{0,32},{32,64},{64,96},{96,128},{128,160},{160,192},{192,224},{224... | collective-permute-start | bytes 393224 | tf_op jit(solution)/shard_map/while/body/eval_jaxpr/ppermute | solution.py:16
  755.5 20.9 %collective-permute-start.4 = (f32[128,2,128]{2,0,1:T(8,128)S(1)}, f32[128,2,128]{2,0,1:T(8,128)S(1)}, u32[]{:S(2)}, u32[]{:S(2)}) collective-permute-start(f32[128,2,128]{2,0,1:T(8,128)S(1)} %fusion.196), channel_id=1, source_target_pairs={{0,32},{32,64},{64,96},{96,128},{128,160},{160,192},{192,224},{224... | collective-permute-start | bytes 393224 | tf_op jit(solution)/shard_map/while/body/eval_jaxpr/ppermute | solution.py:16
  800.7 20.3 %collective-permute-start.4 = (f32[128,2,128]{2,0,1:T(8,128)S(1)}, f32[128,2,128]{2,0,1:T(8,128)S(1)}, u32[]{:S(2)}, u32[]{:S(2)}) collective-permute-start(f32[128,2,128]{2,0,1:T(8,128)S(1)} %fusion.196), channel_id=1, source_target_pairs={{0,32},{32,64},{64,96},{96,128},{128,160},{160,192},{192,224},{224... | collective-permute-start | bytes 393224 | tf_op jit(solution)/shard_map/while/body/eval_jaxpr/ppermute | solution.py:16
  824.9 18.8 %collective-permute-start.3 = (f32[128,2,128]{2,0,1:T(8,128)S(1)}, f32[128,2,128]{2,0,1:T(8,128)S(1)}, u32[]{:S(2)}, u32[]{:S(2)}) collective-permute-start(f32[128,2,128]{2,0,1:T(8,128)S(1)} %fusion.195), channel_id=1, source_target_pairs={{0,32},{32,64},{64,96},{96,128},{128,160},{160,192},{192,224},{224... | collective-permute-start | bytes 393224 | tf_op jit(solution)/shard_map/while/body/eval_jaxpr/ppermute | solution.py:16
  827.0 18.1 %collective-permute-start.4 = (f32[128,2,128]{2,0,1:T(8,128)S(1)}, f32[128,2,128]{2,0,1:T(8,128)S(1)}, u32[]{:S(2)}, u32[]{:S(2)}) collective-permute-start(f32[128,2,128]{2,0,1:T(8,128)S(1)} %fusion.196), channel_id=1, source_target_pairs={{0,32},{32,64},{64,96},{96,128},{128,160},{160,192},{192,224},{224... | collective-permute-start | bytes 393224 | tf_op jit(solution)/shard_map/while/body/eval_jaxpr/ppermute | solution.py:16
  873.6 18.0 %collective-permute-start.4 = (f32[128,2,128]{2,0,1:T(8,128)S(1)}, f32[128,2,128]{2,0,1:T(8,128)S(1)}, u32[]{:S(2)}, u32[]{:S(2)}) collective-permute-start(f32[128,2,128]{2,0,1:T(8,128)S(1)} %fusion.196), channel_id=1, source_target_pairs={{0,32},{32,64},{64,96},{96,128},{128,160},{160,192},{192,224},{224... | collective-permute-start | bytes 393224 | tf_op jit(solution)/shard_map/while/body/eval_jaxpr/ppermute | solution.py:16
  897.6 17.8 %collective-permute-start.4 = (f32[128,2,128]{2,0,1:T(8,128)S(1)}, f32[128,2,128]{2,0,1:T(8,128)S(1)}, u32[]{:S(2)}, u32[]{:S(2)}) collective-permute-start(f32[128,2,128]{2,0,1:T(8,128)S(1)} %fusion.196), channel_id=1, source_target_pairs={{0,32},{32,64},{64,96},{96,128},{128,160},{160,192},{192,224},{224... | collective-permute-start | bytes 393224 | tf_op jit(solution)/shard_map/while/body/eval_jaxpr/ppermute | solution.py:16
  919.2 19.2 %collective-permute-start.3 = (f32[128,2,128]{2,0,1:T(8,128)S(1)}, f32[128,2,128]{2,0,1:T(8,128)S(1)}, u32[]{:S(2)}, u32[]{:S(2)}) collective-permute-start(f32[128,2,128]{2,0,1:T(8,128)S(1)} %fusion.195), channel_id=1, source_target_pairs={{0,32},{32,64},{64,96},{96,128},{128,160},{160,192},{192,224},{224... | collective-permute-start | bytes 393224 | tf_op jit(solution)/shard_map/while/body/eval_jaxpr/ppermute | solution.py:16
  921.3 18.6 %collective-permute-start.4 = (f32[128,2,128]{2,0,1:T(8,128)S(1)}, f32[128,2,128]{2,0,1:T(8,128)S(1)}, u32[]{:S(2)}, u32[]{:S(2)}) collective-permute-start(f32[128,2,128]{2,0,1:T(8,128)S(1)} %fusion.196), channel_id=1, source_target_pairs={{0,32},{32,64},{64,96},{96,128},{128,160},{160,192},{192,224},{224... | collective-permute-start | bytes 393224 | tf_op jit(solution)/shard_map/while/body/eval_jaxpr/ppermute | solution.py:16
  943.6 574.4 %all-reduce.6.cloned.1.call-start = ((), (), s32[]{:S(2)}) async-start(), calls=%async_computation.1 | async-start | bytes 1048576 | tf_op jit(solution)/shard_map/psum | solution.py:190
  (96 other events, 1677.5 us)
Sparse Core Ops, SparseCore 0:
  943.8 296.1 all-reduce.3
  1243.6 274.3 all-reduce.5
where the time goes:
time: 1540 us; the launch traced here: 1530 us
  waiting for transfers between devices  1050 us (68%)
  starting transfers between devices  258 us (17%)
  matrix products  110 us (7%)
  local copies, waits for them, and re-layouts  82 us (5%)
    ppermute x115, waiting for transfers between devices, shifted(): lax.ppermute(x, axis, [(i, (i + by) % devices) for i in range(devices)])  477 us
    psum x1, waiting for transfers between devices, body(): latent_sum = lax.psum(latent_part, 'heads')  291 us
    psum x1, waiting for transfers between devices, body(): lax.psum(weight_part(key_flat).astype(jnp.bfloat16), 'blk')  276 us
    ppermute x115, starting transfers between devices, shifted(): lax.ppermute(x, axis, [(i, (i + by) % devices) for i in range(devices)])  258 us
    dynamic_slice x72, local copies, waits for them, and re-layouts, grads_at(): lax.dynamic_index_in_dim(stored, slot_index, 0, keepdims=False)  36.9 us
    dynamic_update_slice x118, local copies, waits for them, and re-layouts, forward_visit(): lax.dynamic_update_index_in_dim(stored, fresh_item, turn_index, 0)  35.9 us
  transfers between devices with their start and end apart: 117, of which 82 were waited for; matrix products, arithmetic and copies ran while one was open for 6% of the time, Pallas kernels for 0%

commit v1 on v0

v1 whole, which is shorter than its diff:
```python
import jax
import jax.numpy as jnp
from jax import lax
from jax.sharding import PartitionSpec as P

D_ROPE = 64
D_NOPE = 128
D_V = 128
POS_SPLIT = 64
W_CHUNK = 6


lowest = -1e30


def digits_of(size):
    found = []
    stride = 1
    rest = size
    for prime in (2, 3):
        if rest % prime == 0:
            found.append((prime, stride))
            stride *= prime
            rest //= prime
    prime = 2
    while rest > 1:
        while rest % prime == 0:
            found.append((prime, stride))
            stride *= prime
            rest //= prime
        prime += 1
    return found


def gather_order(size):
    found = digits_of(size)
    odd = [d for d in found if d[0] != 2]
    even = sorted([d for d in found if d[0] == 2], key=lambda d: -d[1])
    return odd + even


def digit_value(axis, radix, stride):
    return (lax.axis_index(axis) // stride) % radix


def shift_digit(x, axis, radix, stride, by):
    size = lax.axis_size(axis)
    pairs = []
    for i in range(size):
        r = (i // stride) % radix
        pairs.append((i, i + (((r + by) % radix) - r) * stride))
    return lax.ppermute(x, axis, pairs)


def ordered_pieces(own, axis, radix, stride):
    r = digit_value(axis, radix, stride)
    received = {by: shift_digit(own, axis, radix, stride, by) for by in range(1, radix)}
    pieces = []
    for k in range(radix):
        piece = own
        for by in range(1, radix):
            piece = jnp.where((r - k) % radix == by, received[by], piece)
        pieces.append(piece)
    return pieces


def gather_blocks(block, axis):
    size = lax.axis_size(axis)
    done = []
    buf = block
    for radix, stride in gather_order(size):
        pieces = ordered_pieces(buf, axis, radix, stride)
        at = sum(1 for unused, other in done if other > stride)
        buf = jnp.stack(pieces, axis=at)
        done.append((radix, stride))
    return buf.reshape((size,) + block.shape)


def scatter_sum(data, axis):
    size = lax.axis_size(axis)
    canon = sorted(digits_of(size), key=lambda d: -d[1])
    data = data.reshape(tuple(d[0] for d in canon) + data.shape[1:])
    remaining = list(canon)
    for radix, stride in reversed(gather_order(size)):
        at = remaining.index((radix, stride))
        r = digit_value(axis, radix, stride)
        total = lax.dynamic_index_in_dim(data, r, at, keepdims=False)
        for by in range(1, radix):
            part = lax.dynamic_index_in_dim(data, (r + by) % radix, at, keepdims=False)
            total = total + shift_digit(part, axis, radix, stride, by)
        data = total
        remaining.pop(at)
    return data


def total_over(x, axis):
    size = lax.axis_size(axis)
    for radix, stride in digits_of(size):
        if radix == 2:
            x = x + shift_digit(x, axis, radix, stride, 1)
        else:
            pieces = ordered_pieces(x, axis, radix, stride)
            x = pieces[0]
            for piece in pieces[1:]:
                x = x + piece
    return x


def body(q_nope, q_rope, d_out, latent, scale_exp, positions, spans, w_uk, w_uv):
    row_count = q_nope.shape[0]
    head_count = w_uk.shape[1] // D_NOPE
    col_width = latent.shape[1] - D_ROPE
    col_group = col_width // scale_exp.shape[0]
    block_count = lax.axis_size("blk")
    key_count = row_count * block_count
    soft_scale = (D_NOPE + D_ROPE) ** (-0.5)

    factor = jnp.exp2(jnp.repeat(jnp.transpose(scale_exp), col_group, axis=1).astype(jnp.float32))
    compressed = (latent[:, :col_width].astype(jnp.float32) * factor).astype(jnp.bfloat16)
    pos_hi = (positions // POS_SPLIT).astype(jnp.bfloat16)
    pos_lo = (positions % POS_SPLIT).astype(jnp.bfloat16)
    packed = jnp.concatenate(
        [compressed, latent[:, col_width:], pos_hi[:, None], pos_lo[:, None]], axis=1
    )
    everything = gather_blocks(packed, "blk").reshape(key_count, packed.shape[1])
    comp_all = everything[:, :col_width]
    rope_all = everything[:, col_width : col_width + D_ROPE]
    key_pos = everything[:, col_width + D_ROPE].astype(jnp.int32) * POS_SPLIT + everything[
        :, col_width + D_ROPE + 1
    ].astype(jnp.int32)

    keys = jnp.dot(comp_all, w_uk, preferred_element_type=jnp.float32).astype(jnp.bfloat16)
    values = jnp.dot(comp_all, w_uv, preferred_element_type=jnp.float32).astype(jnp.bfloat16)
    keys = keys.reshape(key_count, head_count, D_NOPE)
    values = values.reshape(key_count, head_count, D_V)
    queries = q_nope.reshape(row_count, head_count, D_NOPE)
    query_rope = q_rope.reshape(row_count, head_count, D_ROPE)
    grad_out = d_out.reshape(row_count, head_count, D_V)

    scores = jnp.einsum("qhd,khd->hqk", queries, keys, preferred_element_type=jnp.float32)
    scores = scores + jnp.einsum(
        "qhr,kr->hqk", query_rope, rope_all, preferred_element_type=jnp.float32
    )
    scores = scores * soft_scale
    pairs = (key_pos[None, :] <= positions[:, None]) & (
        key_pos[None, :] >= positions[:, None] - spans[:, None]
    )
    masked = jnp.where(pairs[None], scores, lowest)
    row_max = jnp.max(masked, axis=2, keepdims=True)
    row_sum = jnp.sum(
        jnp.where(pairs[None], jnp.exp(masked - row_max), 0.0), axis=2, keepdims=True
    )
    log_norm = row_max + jnp.log(row_sum)
    prob_float = jnp.where(pairs[None], jnp.exp(scores - log_norm), 0.0)
    grad_prob = jnp.einsum("qhd,khd->hqk", grad_out, values, preferred_element_type=jnp.float32)
    delta_rows = jnp.sum(prob_float * grad_prob, axis=2, keepdims=True)
    grad_score = (prob_float * (grad_prob - delta_rows) * soft_scale).astype(jnp.bfloat16)
    prob_half = prob_float.astype(jnp.bfloat16)

    query_grad = jnp.einsum("hqk,khd->qhd", grad_score, keys, preferred_element_type=jnp.float32)
    rope_grad = jnp.einsum("hqk,kr->qhr", grad_score, rope_all, preferred_element_type=jnp.float32)
    key_grad = jnp.einsum("hqk,qhd->khd", grad_score, queries, preferred_element_type=jnp.float32)
    value_grad = jnp.einsum("hqk,qhd->khd", prob_half, grad_out, preferred_element_type=jnp.float32)

    both = jnp.concatenate(
        [
            key_grad.reshape(block_count, row_count, head_count * D_NOPE),
            value_grad.reshape(block_count, row_count, head_count * D_V),
        ],
        axis=2,
    )
    flat = scatter_sum(both, "blk").astype(jnp.bfloat16)
    key_flat = flat[:, : head_count * D_NOPE]
    value_flat = flat[:, head_count * D_NOPE :]

    def back_project(grad_flat, weight):
        return lax.dot_general(
            grad_flat, weight, (((1,), (1,)), ((), ())), preferred_element_type=jnp.float32
        )

    latent_part = back_project(key_flat, w_uk) + back_project(value_flat, w_uv)
    latent_sum = total_over(latent_part, "heads")
    grad_latent = (latent_sum * factor).astype(jnp.bfloat16)

    flats = gather_blocks(flat, "blk")
    comp_blocks = comp_all.reshape(block_count, row_count, col_width)
    weight_sum = jnp.zeros((col_width, flat.shape[1]), jnp.float32)
    for start in range(0, block_count, W_CHUNK):
        stop = min(start + W_CHUNK, block_count)
        product = jnp.einsum(
            "btl,btk->blk",
            comp_blocks[start:stop],
            flats[start:stop],
            preferred_element_type=jnp.float32,
        )
        rounded = product.astype(jnp.bfloat16).astype(jnp.float32)
        for index in range(stop - start):
            weight_sum = weight_sum + rounded[index]
    weight_key_grad = weight_sum[:, : head_count * D_NOPE]
    weight_value_grad = weight_sum[:, head_count * D_NOPE :]

    grad_q_nope = query_grad.reshape(row_count, head_count * D_NOPE).astype(jnp.bfloat16)
    grad_q_rope = rope_grad.reshape(row_count, head_count * D_ROPE).astype(jnp.bfloat16)
    return (grad_q_nope, grad_q_rope, grad_latent, weight_key_grad, weight_value_grad)


def solution(mesh):
    in_specs = (
        P("blk", "heads"),
        P("blk", "heads"),
        P("blk", "heads"),
        P("blk", None),
        P(None, "blk"),
        P("blk"),
        P("blk"),
        P(None, "heads"),
        P(None, "heads"),
    )
    out_specs = (
        P("blk", "heads"),
        P("blk", "heads"),
        P("blk", None),
        P(None, "heads"),
        P(None, "heads"),
    )
    return jax.shard_map(body, mesh=mesh, in_specs=in_specs, out_specs=out_specs, check_vma=False)
```

time: 1540 us -> 417 us (0.27)
  waiting for transfers between devices: 1050 us -> 165 us
  starting transfers between devices: 258 us -> 95.7 us
  matrix products: 110 us -> 32.5 us
  other arithmetic: 14.5 us -> 30.5 us
    psum x2 -> x0, waiting for transfers between devices: 568 us -> none  [the longest x1 291 us: body(): latent_sum = lax.psum(latent_part, 'heads')]
    ppermute x115 -> x20, waiting for transfers between devices: 477 us -> 165 us  [shift_digit(): return lax.ppermute(x, axis, pairs)]
    ppermute x115 -> x20, starting transfers between devices: 258 us -> 95.7 us  [shift_digit(): return lax.ppermute(x, axis, pairs)]
    dot_general x290 -> x13, matrix products: 109 us -> 32.1 us  [the longest x1 6.63 us: body(): jnp.einsum('hqk,qhd->khd', grad_score, queries, preferred_element_type=jn...]
    dynamic_slice x72 -> x0, local copies, waits for them, and re-layouts: 36.9 us -> none  [grads_at(): lax.dynamic_index_in_dim(stored, slot_index, 0, keepdims=False)]
    dynamic_update_slice x118 -> x0, local copies, waits for them, and re-layouts: 35.9 us -> none  [forward_visit(): lax.dynamic_update_index_in_dim(stored, fresh_item, turn_index, 0)]
    another operation x4, local copies, waits for them, and re-layouts: 1.84 us -> 24 us  [the longest x3 15.1 us: gather_blocks(): buf = jnp.stack(pieces, axis=at)]
  transfers between devices with their start and end apart: 117 -> 20, of which waited for: 82 -> 17; matrix products, arithmetic and copies ran while one was open for 6% -> 6% of each run, Pallas kernels for 0% -> 0%
where the time goes in v1:
time: 417 us; the launch traced here: 412 us
  waiting for transfers between devices  165 us (40%)
  starting transfers between devices  95.7 us (23%)
  local copies, waits for them, and re-layouts  86.3 us (21%)
  matrix products  32.5 us (8%)
  other arithmetic  30.5 us (7%)
    ppermute x20, waiting for transfers between devices, shift_digit(): return lax.ppermute(x, axis, pairs)  165 us
    ppermute x20, starting transfers between devices, shift_digit(): return lax.ppermute(x, axis, pairs)  95.7 us
    another operation x3, local copies, waits for them, and re-layouts, gather_blocks(): buf = jnp.stack(pieces, axis=at)  15.1 us
    unnamed x56, local copies, waits for them, and re-layouts  11.8 us
    another operation x16, other arithmetic, gather_blocks(): buf = jnp.stack(pieces, axis=at)  11.7 us
    concatenate x3, local copies, waits for them, and re-layouts, body(): jnp.concatenate([key_grad.reshape(block_count, row_count, head_count * D_...  11.4 us
    slice x5, local copies, waits for them, and re-layouts, body(): comp_blocks[start:stop]  8.92 us
    another operation x1, local copies, waits for them, and re-layouts, body(): gather_blocks(packed, 'blk').reshape(key_count, packed.shape[1])  8.87 us
  transfers between devices with their start and end apart: 20, of which 17 were waited for; matrix products, arithmetic and copies ran while one was open for 6% of the time, Pallas kernels for 0%

profile of v1, /device:TPU:56, one launch (start us, length us, event | category | flops | bytes accessed | tf_op | source)
XLA Modules:
  0.0 412.4 jit_solution(14513949277033619176)
XLA Ops:
  5.4 10.9 %collective-permute-start.1 = (bf16[128,578]{1,0:T(8,128)(2,1)S(1)}, bf16[128,578]{1,0:T(8,128)(2,1)S(1)}, u32[]{:S(2)}, u32[]{:S(2)}) collective-permute-start(bf16[128,578]{1,0:T(8,128)(2,1)S(1)} %pad_maximum_fusion.8), channel_id=1, source_target_pairs={{0,64},{32,96},{64,128},{96,160},{128,0},{160,32},{192,256},{224,2... | collective-permute-start | bytes 443912 | tf_op jit(solution)/shard_map/ppermute | solution.py:52
  16.3 5.6 %collective-permute-start = (bf16[128,578]{1,0:T(8,128)(2,1)S(1)}, bf16[128,578]{1,0:T(8,128)(2,1)S(1)}, u32[]{:S(2)}, u32[]{:S(2)}) collective-permute-start(bf16[128,578]{1,0:T(8,128)(2,1)S(1)} %pad_maximum_fusion.8), channel_id=1, source_target_pairs={{0,128},{32,160},{64,0},{96,32},{128,64},{160,96},{192,320},{224,3... | collective-permute-start | bytes 443912 | tf_op jit(solution)/shard_map/ppermute | solution.py:52
  24.4 11.5 %collective-permute-done = bf16[128,578]{1,0:T(8,128)(2,1)S(1)} collective-permute-done((bf16[128,578]{1,0:T(8,128)(2,1)S(1)}, bf16[128,578]{1,0:T(8,128)(2,1)S(1)}, u32[]{:S(2)}, u32[]{:S(2)}) %collective-permute-start) | collective-permute-done | bytes 148000 | tf_op jit(solution)/shard_map/ppermute | solution.py:52
  36.2 4.9 %collective-permute-start.2 = (bf16[3,128,578]{2,1,0:T(8,128)(2,1)S(1)}, bf16[3,128,578]{2,1,0:T(8,128)(2,1)S(1)}, u32[]{:S(2)}, u32[]{:S(2)}) collective-permute-start(bf16[3,128,578]{2,1,0:T(8,128)(2,1)S(1)} %pad_maximum_fusion.6), channel_id=1, source_target_pairs={{0,384},{32,416},{64,448},{96,480},{128,512},{160,544},{192,576},{... | collective-permute-start | bytes 1331720 | tf_op jit(solution)/shard_map/ppermute | solution.py:52
  41.2 9.8 %collective-permute-done.2 = bf16[3,128,578]{2,1,0:T(8,128)(2,1)S(1)} collective-permute-done((bf16[3,128,578]{2,1,0:T(8,128)(2,1)S(1)}, bf16[3,128,578]{2,1,0:T(8,128)(2,1)S(1)}, u32[]{:S(2)}, u32[]{:S(2)}) %collective-permute-start.2) | collective-permute-done | bytes 443936 | tf_op jit(solution)/shard_map/ppermute | solution.py:52
  55.5 17.4 %collective-permute-done.3 = bf16[2,3,128,578]{2,0,3,1:T(2,128)(2,1)S(1)} collective-permute-done((bf16[2,3,128,578]{2,0,3,1:T(2,128)(2,1)S(1)}, bf16[2,3,128,578]{2,0,3,1:T(2,128)(2,1)S(1)}, u32[]{:S(2)}, u32[]{:S(2)}) %collective-permute-start.3) | collective-permute-done | bytes 887840 | tf_op jit(solution)/shard_map/ppermute | solution.py:52
  77.9 5.1 %copy.74 = bf16[2,2,3,128,578]{3,1,4,2,0:T(2,128)(2,1)} copy(bf16[2,2,3,128,578]{4,3,2,0,1:T(8,128)(2,1)} %pad_maximum_fusion.2) | data formatting | bytes 3551232 | tf_op jit(solution)/shard_map/stack | solution.py:74
  89.0 5.1 %copy.75 = bf16[2,2,3,128,578]{4,3,2,0,1:T(8,128)(2,1)} copy(bf16[2,2,3,128,578]{3,1,4,2,0:T(2,128)(2,1)} %collective-permute-done.4) | data formatting | bytes 3551232 | tf_op jit(solution)/shard_map/ppermute | solution.py:52
  98.6 9.2 %copy.77 = bf16[2,2,3,2,128,578]{4,3,2,1,0,5:T(2,128)(2,1)} copy(bf16[2,2,3,2,128,578]{5,4,2,0,1,3:T(8,128)(2,1)} %pad_maximum_fusion) | data formatting | bytes 7102464 | tf_op jit(solution)/shard_map/stack | solution.py:74
  107.9 8.9 %reshape_reshape.3 = bf16[3072,578]{0,1:T(8,128)(2,1)} reshape(bf16[2,2,3,2,128,578]{4,3,2,1,0,5:T(2,128)(2,1)} %copy.77) | data formatting | bytes 7102464 | tf_op jit(solution)/shard_map/reshape;reshape | solution.py:125
  130.5 6.6 %convolution_bitcast_fusion.1 = f32[3072,2,128]{2,0,1:T(8,128)} fusion(f32[2,128,3072]{1,2,0:T(8,128)} %convolution_bitcast_fusion.2, f32[2,128,3072]{1,2,0:T(8,128)S(1)} %get-tuple-element.50, f32[2,128]{1,0:T(2,128)S(1)} %log_add_fusion, pred[128,3072]{0,1:T(8,128)(4,1)} %copy-done.11, bf16[128,256]{1,0:T(8,128)(2,1)S(1)} %copy-done.22), kind=kOutput, calls=%fused_computation.2 | convolution fusion | flops 208407808 | bytes 9896960 | tf_op jit(solution)/shard_map/hqk,qhd->khd/dot_general | solution.py:162
  137.1 7.3 %copy.88 = f32[3072,2,128]{2,1,0:T(2,128)} copy(f32[3072,2,128]{2,0,1:T(8,128)} %convolution_bitcast_fusion) | data formatting | bytes 6291456 | tf_op jit(solution)/shard_map/hqk,qhd->khd/transpose | solution.py:163
  144.4 5.5 %concatenate.13 = f32[2,2,3,2,128,256]{5,4,3,2,1,0:T(8,128)} reshape(f32[3072,2,128]{2,1,0:T(2,128)} %copy.88) | data formatting | bytes 6291456 | tf_op jit(solution)/shard_map/concatenate | solution.py:165
  149.9 7.1 %copy.86 = f32[3072,2,128]{2,1,0:T(2,128)} copy(f32[3072,2,128]{2,0,1:T(8,128)} %convolution_bitcast_fusion.1) | data formatting | bytes 6291456 | tf_op jit(solution)/shard_map/hqk,qhd->khd/transpose | solution.py:162
  157.0 5.5 %concatenate.12 = f32[2,2,3,2,128,256]{5,4,3,2,1,0:T(8,128)} reshape(f32[3072,2,128]{2,1,0:T(2,128)} %copy.86) | data formatting | bytes 6291456 | tf_op jit(solution)/shard_map/concatenate | solution.py:165
  171.5 5.8 %collective-permute-done.5 = f32[2,2,3,128,512]{4,3,2,1,0:T(8,128)} collective-permute-done((f32[2,2,3,128,512]{4,3,2,1,0:T(8,128)}, f32[2,2,3,128,512]{4,3,2,1,0:T(8,128)}, u32[]{:S(2)}, u32[]{:S(2)}) %collective-permute-start.5) | collective-permute-done | bytes 3145760 | tf_op jit(solution)/shard_map/ppermute | solution.py:52
  187.4 35.2 %collective-permute-done.6 = f32[2,3,128,512]{3,2,1,0:T(8,128)} collective-permute-done((f32[2,3,128,512]{3,2,1,0:T(8,128)}, f32[2,3,128,512]{3,2,1,0:T(8,128)}, u32[]{:S(2)}, u32[]{:S(2)}) %collective-permute-start.6) | collective-permute-done | bytes 1572896 | tf_op jit(solution)/shard_map/ppermute | solution.py:52
  226.9 4.9 %collective-permute-start.7 = (f32[3,128,512]{2,1,0:T(8,128)}, f32[3,128,512]{2,1,0:T(8,128)}, u32[]{:S(2)}, u32[]{:S(2)}) collective-permute-start(f32[3,128,512]{2,1,0:T(8,128)} %dynamic-slice_bitcast_fusion.2), channel_id=1, source_target_pairs={{0,384},{32,416},{64,448},{96,480},{128,512},{160,544},{192,576},{... | collective-permute-start | bytes 2359304 | tf_op jit(solution)/shard_map/ppermute | solution.py:52
  231.9 17.5 %collective-permute-done.7 = f32[3,128,512]{2,1,0:T(8,128)} collective-permute-done((f32[3,128,512]{2,1,0:T(8,128)}, f32[3,128,512]{2,1,0:T(8,128)}, u32[]{:S(2)}, u32[]{:S(2)}) %collective-permute-start.7) | collective-permute-done | bytes 786464 | tf_op jit(solution)/shard_map/ppermute | solution.py:52
  252.6 5.7 %collective-permute-start.8 = (f32[128,512]{1,0:T(8,128)}, f32[128,512]{1,0:T(8,128)}, u32[]{:S(2)}, u32[]{:S(2)}) collective-permute-start(f32[128,512]{1,0:T(8,128)} %get-tuple-element.38), channel_id=1, source_target_pairs={{0,64},{32,96},{64,128},{96,160},{128,0},{160,32},{192,256},{224,2... | collective-permute-start | bytes 786440 | tf_op jit(solution)/shard_map/ppermute | solution.py:52
  262.4 15.2 %collective-permute-done.8 = f32[128,512]{1,0:T(8,128)} collective-permute-done((f32[128,512]{1,0:T(8,128)}, f32[128,512]{1,0:T(8,128)}, u32[]{:S(2)}, u32[]{:S(2)}) %collective-permute-start.8) | collective-permute-done | bytes 262176 | tf_op jit(solution)/shard_map/ppermute | solution.py:52
  278.8 6.8 %collective-permute-start.16 = (bf16[128,512]{1,0:T(8,128)(2,1)S(1)}, bf16[128,512]{1,0:T(8,128)(2,1)S(1)}, u32[]{:S(2)}, u32[]{:S(2)}) collective-permute-start(bf16[128,512]{1,0:T(8,128)(2,1)S(1)} %fusion.65), channel_id=1, source_target_pairs={{0,64},{32,96},{64,128},{96,160},{128,0},{160,32},{192,256},{224,2... | collective-permute-start | bytes 393224 | tf_op jit(solution)/shard_map/ppermute | solution.py:52
  292.0 5.0 %collective-permute-done.15 = bf16[128,512]{1,0:T(8,128)(2,1)S(1)} collective-permute-done((bf16[128,512]{1,0:T(8,128)(2,1)S(1)}, bf16[128,512]{1,0:T(8,128)(2,1)S(1)}, u32[]{:S(2)}, u32[]{:S(2)}) %collective-permute-start.15) | collective-permute-done | bytes 131104 | tf_op jit(solution)/shard_map/ppermute | solution.py:52
  297.1 5.1 %collective-permute-start.17 = (bf16[3,128,512]{2,1,0:T(8,128)(2,1)S(1)}, bf16[3,128,512]{2,1,0:T(8,128)(2,1)S(1)}, u32[]{:S(2)}, u32[]{:S(2)}) collective-permute-start(bf16[3,128,512]{2,1,0:T(8,128)(2,1)S(1)} %pad_maximum_fusion.7), channel_id=1, source_target_pairs={{0,384},{32,416},{64,448},{96,480},{128,512},{160,544},{192,576},{... | collective-permute-start | bytes 1179656 | tf_op jit(solution)/shard_map/ppermute | solution.py:52
  302.3 8.9 %collective-permute-done.17 = bf16[3,128,512]{2,1,0:T(8,128)(2,1)S(1)} collective-permute-done((bf16[3,128,512]{2,1,0:T(8,128)(2,1)S(1)}, bf16[3,128,512]{2,1,0:T(8,128)(2,1)S(1)}, u32[]{:S(2)}, u32[]{:S(2)}) %collective-permute-start.17) | collective-permute-done | bytes 393248 | tf_op jit(solution)/shard_map/ppermute | solution.py:52
  318.2 5.1 %collective-permute-done.10 = f32[128,512]{1,0:T(8,128)S(1)} collective-permute-done((f32[128,512]{1,0:T(8,128)S(1)}, f32[128,512]{1,0:T(8,128)S(1)}, u32[]{:S(2)}, u32[]{:S(2)}) %collective-permute-start.10) | collective-permute-done | bytes 262176 | tf_op jit(solution)/shard_map/ppermute | solution.py:52
  337.3 4.6 %collective-permute-start.12 = (f32[128,512]{1,0:T(8,128)S(1)}, f32[128,512]{1,0:T(8,128)S(1)}, u32[]{:S(2)}, u32[]{:S(2)}) collective-permute-start(f32[128,512]{1,0:T(8,128)S(1)} %add.313), channel_id=1, source_target_pairs={{0,4},{1,5},{2,6},{3,7},{4,0},{5,1},{6,2},{7,3},{8,12},{9,13},{10,... | collective-permute-start | bytes 786440 | tf_op jit(solution)/shard_map/ppermute | solution.py:52
  341.9 14.2 %collective-permute-done.12 = f32[128,512]{1,0:T(8,128)S(1)} collective-permute-done((f32[128,512]{1,0:T(8,128)S(1)}, f32[128,512]{1,0:T(8,128)S(1)}, u32[]{:S(2)}, u32[]{:S(2)}) %collective-permute-start.12) | collective-permute-done | bytes 262176 | tf_op jit(solution)/shard_map/ppermute | solution.py:52
  359.8 5.1 %collective-permute-done.13 = f32[128,512]{1,0:T(8,128)S(1)} collective-permute-done((f32[128,512]{1,0:T(8,128)S(1)}, f32[128,512]{1,0:T(8,128)S(1)}, u32[]{:S(2)}, u32[]{:S(2)}) %collective-permute-start.13) | collective-permute-done | bytes 262176 | tf_op jit(solution)/shard_map/ppermute | solution.py:52
  365.6 14.6 %collective-permute-start.14 = (f32[128,512]{1,0:T(8,128)}, f32[128,512]{1,0:T(8,128)}, u32[]{:S(2)}, u32[]{:S(2)}) collective-permute-start(f32[128,512]{1,0:T(8,128)} %add.315), channel_id=1, source_target_pairs={{0,16},{1,17},{2,18},{3,19},{4,20},{5,21},{6,22},{7,23},{8,24},{9,... | collective-permute-start | bytes 786440 | tf_op jit(solution)/shard_map/ppermute | solution.py:52
  380.2 5.8 %fusion.44 = bf16[2,128,128]{2,1,0:T(8,128)(2,1)S(1)} fusion(bf16[3072,2,128]{0,2,1:T(8,128)(2,1)} %bitcast.204, f32[2,128,3072]{1,2,0:T(8,128)} %convolution_bitcast_fusion.2, f32[2,128,3072]{1,2,0:T(8,128)S(1)} %get-tuple-element.50, f32[2,128]{1,0:T(2,128)S(1)} %log_add_fusion, pred[128,3072]{0,1:T(8,128)(4,1)} %copy-done.11), kind=kOutput, calls=%fused_computation.57 | convolution fusion | flops 208440576 | bytes 8324096 | tf_op jit(solution)/shard_map/hqk,khd->qhd/dot_general | solution.py:160
  389.1 5.1 %fusion.47 = bf16[64,2,128]{2,0,1:T(8,128)(2,1)S(1)} fusion(f32[2,128,3072]{1,2,0:T(8,128)} %convolution_bitcast_fusion.2, f32[2,128,3072]{1,2,0:T(8,128)S(1)} %get-tuple-element.50, f32[2,128]{1,0:T(2,128)S(1)} %log_add_fusion, pred[128,3072]{0,1:T(8,128)(4,1)} %copy-done.11, bf16[3072,578]{0,1:T(8,128)(2,1)} %reshape_reshape.3), kind=kOutput, calls=%fused_computation.58 | convolution fusion | flops 107760896 | bytes 13797376 | tf_op jit(solution)/shard_map/hqk,kr->qhr/dot_general | solution.py:161
  (140 shorter events, 125.3 us)
Async XLA Ops:
  0.6 117.0 %copy-start = (bf16[512,256]{1,0:T(8,128)(2,1)S(1)}, bf16[512,256]{1,0:T(8,128)(2,1)}, u32[]{:S(2)}) copy-start(bf16[512,256]{1,0:T(8,128)(2,1)} %param.17) | copy-start | bytes 786436
  5.4 19.0 %collective-permute-start.1 = (bf16[128,578]{1,0:T(8,128)(2,1)S(1)}, bf16[128,578]{1,0:T(8,128)(2,1)S(1)}, u32[]{:S(2)}, u32[]{:S(2)}) collective-permute-start(bf16[128,578]{1,0:T(8,128)(2,1)S(1)} %pad_maximum_fusion.8), channel_id=1, source_target_pairs={{0,64},{32,96},{64,128},{96,160},{128,0},{160,32},{192,256},{224,2... | collective-permute-start | bytes 443912 | tf_op jit(solution)/shard_map/ppermute | solution.py:52
  16.3 19.6 %collective-permute-start = (bf16[128,578]{1,0:T(8,128)(2,1)S(1)}, bf16[128,578]{1,0:T(8,128)(2,1)S(1)}, u32[]{:S(2)}, u32[]{:S(2)}) collective-permute-start(bf16[128,578]{1,0:T(8,128)(2,1)S(1)} %pad_maximum_fusion.8), channel_id=1, source_target_pairs={{0,128},{32,160},{64,0},{96,32},{128,64},{160,96},{192,320},{224,3... | collective-permute-start | bytes 443912 | tf_op jit(solution)/shard_map/ppermute | solution.py:52
  36.2 14.8 %collective-permute-start.2 = (bf16[3,128,578]{2,1,0:T(8,128)(2,1)S(1)}, bf16[3,128,578]{2,1,0:T(8,128)(2,1)S(1)}, u32[]{:S(2)}, u32[]{:S(2)}) collective-permute-start(bf16[3,128,578]{2,1,0:T(8,128)(2,1)S(1)} %pad_maximum_fusion.6), channel_id=1, source_target_pairs={{0,384},{32,416},{64,448},{96,480},{128,512},{160,544},{192,576},{... | collective-permute-start | bytes 1331720 | tf_op jit(solution)/shard_map/ppermute | solution.py:52
  52.1 20.9 %collective-permute-start.3 = (bf16[2,3,128,578]{2,0,3,1:T(2,128)(2,1)S(1)}, bf16[2,3,128,578]{2,0,3,1:T(2,128)(2,1)S(1)}, u32[]{:S(2)}, u32[]{:S(2)}) collective-permute-start(bf16[2,3,128,578]{2,0,3,1:T(2,128)(2,1)S(1)} %copy.71), channel_id=1, source_target_pairs={{0,192},{32,224},{64,256},{96,288},{128,320},{160,352},{192,0},{22... | collective-permute-start | bytes 2663432 | tf_op jit(solution)/shard_map/ppermute | solution.py:52
  76.3 9.2 %copy-start.23 = (bf16[128,128]{1,0:T(8,128)(2,1)S(1)}, bf16[128,128]{1,0:T(8,128)(2,1)}, u32[]{:S(2)}) copy-start(bf16[128,128]{1,0:T(8,128)(2,1)} %param.10) | copy-start | bytes 98308
  83.0 5.9 %collective-permute-start.4 = (bf16[2,2,3,128,578]{3,1,4,2,0:T(2,128)(2,1)}, bf16[2,2,3,128,578]{3,1,4,2,0:T(2,128)(2,1)}, u32[]{:S(2)}, u32[]{:S(2)}) collective-permute-start(bf16[2,2,3,128,578]{3,1,4,2,0:T(2,128)(2,1)} %copy.74), channel_id=1, source_target_pairs={{0,32},{32,0},{64,96},{96,64},{128,160},{160,128},{192,224},{224,1... | collective-permute-start | bytes 5326856 | tf_op jit(solution)/shard_map/ppermute | solution.py:52
  117.7 3.1 copy-start.1
  117.7 3.1 copy-start.20
  121.9 3.0 copy-start.18
  123.3 5.0 %copy-start.11 = (pred[128,3072]{0,1:T(8,128)(4,1)}, pred[128,3072]{0,1:T(8,128)(4,1)S(1)}, u32[]{:S(2)}) copy-start(pred[128,3072]{0,1:T(8,128)(4,1)S(1)} %compare_and_fusion) | copy-start | bytes 1179652
  165.8 3.6 copy-start.3
  169.4 7.9 %collective-permute-start.5 = (f32[2,2,3,128,512]{4,3,2,1,0:T(8,128)}, f32[2,2,3,128,512]{4,3,2,1,0:T(8,128)}, u32[]{:S(2)}, u32[]{:S(2)}) collective-permute-start(f32[2,2,3,128,512]{4,3,2,1,0:T(8,128)} %dynamic-slice_bitcast_fusion), channel_id=1, source_target_pairs={{0,32},{32,0},{64,96},{96,64},{128,160},{160,128},{192,224},{224,1... | collective-permute-start | bytes 9437192 | tf_op jit(solution)/shard_map/ppermute | solution.py:52
  183.9 38.6 %collective-permute-start.6 = (f32[2,3,128,512]{3,2,1,0:T(8,128)}, f32[2,3,128,512]{3,2,1,0:T(8,128)}, u32[]{:S(2)}, u32[]{:S(2)}) collective-permute-start(f32[2,3,128,512]{3,2,1,0:T(8,128)} %dynamic-slice_bitcast_fusion.1), channel_id=1, source_target_pairs={{0,192},{32,224},{64,256},{96,288},{128,320},{160,352},{192,0},{22... | collective-permute-start | bytes 4718600 | tf_op jit(solution)/shard_map/ppermute | solution.py:52
  226.9 22.5 %collective-permute-start.7 = (f32[3,128,512]{2,1,0:T(8,128)}, f32[3,128,512]{2,1,0:T(8,128)}, u32[]{:S(2)}, u32[]{:S(2)}) collective-permute-start(f32[3,128,512]{2,1,0:T(8,128)} %dynamic-slice_bitcast_fusion.2), channel_id=1, source_target_pairs={{0,384},{32,416},{64,448},{96,480},{128,512},{160,544},{192,576},{... | collective-permute-start | bytes 2359304 | tf_op jit(solution)/shard_map/ppermute | solution.py:52
  252.6 25.0 %collective-permute-start.8 = (f32[128,512]{1,0:T(8,128)}, f32[128,512]{1,0:T(8,128)}, u32[]{:S(2)}, u32[]{:S(2)}) collective-permute-start(f32[128,512]{1,0:T(8,128)} %get-tuple-element.38), channel_id=1, source_target_pairs={{0,64},{32,96},{64,128},{96,160},{128,0},{160,32},{192,256},{224,2... | collective-permute-start | bytes 786440 | tf_op jit(solution)/shard_map/ppermute | solution.py:52
  258.3 19.3 %collective-permute-start.9 = (f32[128,512]{1,0:T(8,128)}, f32[128,512]{1,0:T(8,128)}, u32[]{:S(2)}, u32[]{:S(2)}) collective-permute-start(f32[128,512]{1,0:T(8,128)} %get-tuple-element.39), channel_id=1, source_target_pairs={{0,128},{32,160},{64,0},{96,32},{128,64},{160,96},{192,320},{224,3... | collective-permute-start | bytes 786440 | tf_op jit(solution)/shard_map/ppermute | solution.py:52
  262.4 52.4 %copy-start.21 = (bf16[512,256]{1,0:T(8,128)(2,1)S(1)}, bf16[512,256]{1,0:T(8,128)(2,1)}, u32[]{:S(2)}) copy-start(bf16[512,256]{1,0:T(8,128)(2,1)} %param.16) | copy-start | bytes 786436
  278.8 13.2 %collective-permute-start.16 = (bf16[128,512]{1,0:T(8,128)(2,1)S(1)}, bf16[128,512]{1,0:T(8,128)(2,1)S(1)}, u32[]{:S(2)}, u32[]{:S(2)}) collective-permute-start(bf16[128,512]{1,0:T(8,128)(2,1)S(1)} %fusion.65), channel_id=1, source_target_pairs={{0,64},{32,96},{64,128},{96,160},{128,0},{160,32},{192,256},{224,2... | collective-permute-start | bytes 393224 | tf_op jit(solution)/shard_map/ppermute | solution.py:52
  285.6 11.4 %collective-permute-start.15 = (bf16[128,512]{1,0:T(8,128)(2,1)S(1)}, bf16[128,512]{1,0:T(8,128)(2,1)S(1)}, u32[]{:S(2)}, u32[]{:S(2)}) collective-permute-start(bf16[128,512]{1,0:T(8,128)(2,1)S(1)} %fusion.65), channel_id=1, source_target_pairs={{0,128},{32,160},{64,0},{96,32},{128,64},{160,96},{192,320},{224,3... | collective-permute-start | bytes 393224 | tf_op jit(solution)/shard_map/ppermute | solution.py:52
  297.1 14.1 %collective-permute-start.17 = (bf16[3,128,512]{2,1,0:T(8,128)(2,1)S(1)}, bf16[3,128,512]{2,1,0:T(8,128)(2,1)S(1)}, u32[]{:S(2)}, u32[]{:S(2)}) collective-permute-start(bf16[3,128,512]{2,1,0:T(8,128)(2,1)S(1)} %pad_maximum_fusion.7), channel_id=1, source_target_pairs={{0,384},{32,416},{64,448},{96,480},{128,512},{160,544},{192,576},{... | collective-permute-start | bytes 1179656 | tf_op jit(solution)/shard_map/ppermute | solution.py:52
  311.4 20.1 %collective-permute-start.18 = (bf16[2,3,128,512]{3,2,1,0:T(8,128)(2,1)S(1)}, bf16[2,3,128,512]{3,2,1,0:T(8,128)(2,1)S(1)}, u32[]{:S(2)}, u32[]{:S(2)}) collective-permute-start(bf16[2,3,128,512]{3,2,1,0:T(8,128)(2,1)S(1)} %pad_maximum_fusion.5), channel_id=1, source_target_pairs={{0,192},{32,224},{64,256},{96,288},{128,320},{160,352},{192,0},{22... | collective-permute-start | bytes 2359304 | tf_op jit(solution)/shard_map/ppermute | solution.py:52
  315.0 8.3 %collective-permute-start.10 = (f32[128,512]{1,0:T(8,128)S(1)}, f32[128,512]{1,0:T(8,128)S(1)}, u32[]{:S(2)}, u32[]{:S(2)}) collective-permute-start(f32[128,512]{1,0:T(8,128)S(1)} %convolution_add_fusion), channel_id=1, source_target_pairs={{0,1},{1,0},{2,3},{3,2},{4,5},{5,4},{6,7},{7,6},{8,9},{9,8},{10,11... | collective-permute-start | bytes 786440 | tf_op jit(solution)/shard_map/ppermute | solution.py:52
  323.3 13.9 %collective-permute-start.11 = (f32[128,512]{1,0:T(8,128)S(1)}, f32[128,512]{1,0:T(8,128)S(1)}, u32[]{:S(2)}, u32[]{:S(2)}) collective-permute-start(f32[128,512]{1,0:T(8,128)S(1)} %add.312), channel_id=1, source_target_pairs={{0,2},{1,3},{2,0},{3,1},{4,6},{5,7},{6,4},{7,5},{8,10},{9,11},{10,... | collective-permute-start | bytes 786440 | tf_op jit(solution)/shard_map/ppermute | solution.py:52
  331.6 26.5 %copy-start.2 = (bf16[3072,578]{0,1:T(8,128)(2,1)S(1)}, bf16[3072,578]{0,1:T(8,128)(2,1)}, u32[]{:S(2)}) copy-start(bf16[3072,578]{0,1:T(8,128)(2,1)} %reshape_reshape.3) | copy-start | bytes 10653700
  333.7 67.9 %collective-permute-start.19 = (bf16[2,2,3,128,512]{4,3,2,1,0:T(8,128)(2,1)}, bf16[2,2,3,128,512]{4,3,2,1,0:T(8,128)(2,1)}, u32[]{:S(2)}, u32[]{:S(2)}) collective-permute-start(bf16[2,2,3,128,512]{4,3,2,1,0:T(8,128)(2,1)} %pad_maximum_fusion.3), channel_id=1, source_target_pairs={{0,32},{32,0},{64,96},{96,64},{128,160},{160,128},{192,224},{224,1... | collective-permute-start | bytes 4718600 | tf_op jit(solution)/shard_map/ppermute | solution.py:52
  337.3 18.8 %collective-permute-start.12 = (f32[128,512]{1,0:T(8,128)S(1)}, f32[128,512]{1,0:T(8,128)S(1)}, u32[]{:S(2)}, u32[]{:S(2)}) collective-permute-start(f32[128,512]{1,0:T(8,128)S(1)} %add.313), channel_id=1, source_target_pairs={{0,4},{1,5},{2,6},{3,7},{4,0},{5,1},{6,2},{7,3},{8,12},{9,13},{10,... | collective-permute-start | bytes 786440 | tf_op jit(solution)/shard_map/ppermute | solution.py:52
  356.1 8.7 %collective-permute-start.13 = (f32[128,512]{1,0:T(8,128)S(1)}, f32[128,512]{1,0:T(8,128)S(1)}, u32[]{:S(2)}, u32[]{:S(2)}) collective-permute-start(f32[128,512]{1,0:T(8,128)S(1)} %add.314), channel_id=1, source_target_pairs={{0,8},{1,9},{2,10},{3,11},{4,12},{5,13},{6,14},{7,15},{8,0},{9,1},... | collective-permute-start | bytes 786440 | tf_op jit(solution)/shard_map/ppermute | solution.py:52
  365.6 34.3 %collective-permute-start.14 = (f32[128,512]{1,0:T(8,128)}, f32[128,512]{1,0:T(8,128)}, u32[]{:S(2)}, u32[]{:S(2)}) collective-permute-start(f32[128,512]{1,0:T(8,128)} %add.315), channel_id=1, source_target_pairs={{0,16},{1,17},{2,18},{3,19},{4,20},{5,21},{6,22},{7,23},{8,24},{9,... | collective-permute-start | bytes 786440 | tf_op jit(solution)/shard_map/ppermute | solution.py:52
  394.2 4.5 %copy-start.13 = (bf16[768,512]{0,1:T(8,128)(2,1)S(1)}, bf16[768,512]{0,1:T(8,128)(2,1)}, u32[]{:S(2)}) copy-start(bf16[768,512]{0,1:T(8,128)(2,1)} %get-tuple-element.25) | copy-start | bytes 2359300
  394.2 7.5 %copy-start.7 = (bf16[2,1,3,128,512]{4,3,2,1,0:T(8,128)(2,1)S(1)}, bf16[2,1,3,128,512]{4,3,2,1,0:T(8,128)(2,1)}, u32[]{:S(2)}) copy-start(bf16[2,1,3,128,512]{4,3,2,1,0:T(8,128)(2,1)} %copy-done.6) | copy-start | bytes 2359300
  394.2 7.4 %copy-start.9 = (bf16[2,1,3,128,512]{4,3,2,1,0:T(8,128)(2,1)S(1)}, bf16[2,1,3,128,512]{4,3,2,1,0:T(8,128)(2,1)}, u32[]{:S(2)}) copy-start(bf16[2,1,3,128,512]{4,3,2,1,0:T(8,128)(2,1)} %copy-done.8) | copy-start | bytes 2359300
  (13 other events, 18.2 us)

commit v2 on v1

--- a/solution.py
+++ b/solution.py
@@ -7,7 +7,6 @@
 D_NOPE = 128
 D_V = 128
 POS_SPLIT = 64
-W_CHUNK = 6
 
 
 lowest = -1e30
@@ -55,6 +54,10 @@
 def ordered_pieces(own, axis, radix, stride):
     r = digit_value(axis, radix, stride)
     received = {by: shift_digit(own, axis, radix, stride, by) for by in range(1, radix)}
+    return canonical(own, received, r, radix)
+
+
+def canonical(own, received, r, radix):
     pieces = []
     for k in range(radix):
         piece = own
@@ -64,32 +67,27 @@
     return pieces
 
 
-def gather_blocks(block, axis):
-    size = lax.axis_size(axis)
-    done = []
+def gather_relative(block, axis):
     buf = block
-    for radix, stride in gather_order(size):
-        pieces = ordered_pieces(buf, axis, radix, stride)
-        at = sum(1 for unused, other in done if other > stride)
-        buf = jnp.stack(pieces, axis=at)
-        done.append((radix, stride))
-    return buf.reshape((size,) + block.shape)
-
-
-def scatter_sum(data, axis):
-    size = lax.axis_size(axis)
-    canon = sorted(digits_of(size), key=lambda d: -d[1])
-    data = data.reshape(tuple(d[0] for d in canon) + data.shape[1:])
-    remaining = list(canon)
-    for radix, stride in reversed(gather_order(size)):
-        at = remaining.index((radix, stride))
-        r = digit_value(axis, radix, stride)
-        total = lax.dynamic_index_in_dim(data, r, at, keepdims=False)
+    for radix, stride in gather_order(lax.axis_size(axis)):
+        received = [shift_digit(buf, axis, radix, stride, by) for by in range(1, radix)]
+        pieces = [buf] + [received[radix - k - 1] for k in range(1, radix)]
+        buf = jnp.stack(pieces, axis=0)
+    return buf
+
+
+def scatter_relative(data, axis, lead, wire):
+    level = 0
+    for radix, stride in reversed(gather_order(lax.axis_size(axis))):
+        head = (slice(None),) * lead
+        total = data[head + (0,)]
         for by in range(1, radix):
-            part = lax.dynamic_index_in_dim(data, (r + by) % radix, at, keepdims=False)
-            total = total + shift_digit(part, axis, radix, stride, by)
+            part = data[head + (by,)]
+            if level > 0:
+                part = part.astype(wire)
+            total = total + shift_digit(part, axis, radix, stride, by).astype(jnp.float32)
         data = total
-        remaining.pop(at)
+        level += 1
     return data
 
 
@@ -122,7 +120,7 @@
     packed = jnp.concatenate(
         [compressed, latent[:, col_width:], pos_hi[:, None], pos_lo[:, None]], axis=1
     )
-    everything = gather_blocks(packed, "blk").reshape(key_count, packed.shape[1])
+    everything = gather_relative(packed, "blk").reshape(key_count, packed.shape[1])
     comp_all = everything[:, :col_width]
     rope_all = everything[:, col_width : col_width + D_ROPE]
     key_pos = everything[:, col_width + D_ROPE].astype(jnp.int32) * POS_SPLIT + everything[
@@ -159,17 +157,18 @@
 
     query_grad = jnp.einsum("hqk,khd->qhd", grad_score, keys, preferred_element_type=jnp.float32)
     rope_grad = jnp.einsum("hqk,kr->qhr", grad_score, rope_all, preferred_element_type=jnp.float32)
-    key_grad = jnp.einsum("hqk,qhd->khd", grad_score, queries, preferred_element_type=jnp.float32)
-    value_grad = jnp.einsum("hqk,qhd->khd", prob_half, grad_out, preferred_element_type=jnp.float32)
-
-    both = jnp.concatenate(
-        [
-            key_grad.reshape(block_count, row_count, head_count * D_NOPE),
-            value_grad.reshape(block_count, row_count, head_count * D_V),
-        ],
-        axis=2,
-    )
-    flat = scatter_sum(both, "blk").astype(jnp.bfloat16)
+    stacked_left = jnp.stack([grad_score, prob_half], axis=0)
+    stacked_right = jnp.stack(
+        [jnp.transpose(queries, (1, 0, 2)), jnp.transpose(grad_out, (1, 0, 2))], axis=0
+    )
+    both = jnp.einsum(
+        "ghqk,ghqd->ghkd", stacked_left, stacked_right, preferred_element_type=jnp.float32
+    )
+    radices = tuple(d[0] for d in reversed(gather_order(block_count)))
+    both = both.reshape(both.shape[:2] + radices + (row_count, both.shape[3]))
+    mine = scatter_relative(both, "blk", 2, jnp.bfloat16)
+    mine = jnp.transpose(mine, (2, 0, 1, 3)).reshape(row_count, -1)
+    flat = mine.astype(jnp.bfloat16)
     key_flat = flat[:, : head_count * D_NOPE]
     value_flat = flat[:, head_count * D_NOPE :]
 
@@ -182,20 +181,27 @@
     latent_sum = total_over(latent_part, "heads")
     grad_latent = (latent_sum * factor).astype(jnp.bfloat16)
 
-    flats = gather_blocks(flat, "blk")
-    comp_blocks = comp_all.reshape(block_count, row_count, col_width)
-    weight_sum = jnp.zeros((col_width, flat.shape[1]), jnp.float32)
-    for start in range(0, block_count, W_CHUNK):
-        stop = min(start + W_CHUNK, block_count)
-        product = jnp.einsum(
-            "btl,btk->blk",
-            comp_blocks[start:stop],
-            flats[start:stop],
-            preferred_element_type=jnp.float32,
-        )
-        rounded = product.astype(jnp.bfloat16).astype(jnp.float32)
-        for index in range(stop - start):
-            weight_sum = weight_sum + rounded[index]
+    flats = gather_relative(flat, "blk")
+    order = gather_order(block_count)
+    first_radix, first_stride = order[0]
+    lead = radices[:-1]
+    comp_rel = comp_all.reshape(radices + (row_count, col_width))
+    slot_sums = []
+    for slot in range(first_radix):
+        left = comp_rel[..., slot, :, :].reshape((-1, row_count, col_width))
+        right = flats[..., slot, :, :].reshape((-1, row_count, flat.shape[1]))
+        product = jnp.einsum("btl,btk->blk", left, right, preferred_element_type=jnp.float32)
+        partial = product.astype(jnp.bfloat16).astype(jnp.float32)
+        partial = partial.reshape(lead + partial.shape[1:])
+        for unused in lead:
+            partial = partial[0] + partial[1]
+        slot_sums.append(partial)
+    first_digit = digit_value("blk", first_radix, first_stride)
+    received = {by: slot_sums[first_radix - by] for by in range(1, first_radix)}
+    ordered = canonical(slot_sums[0], received, first_digit, first_radix)
+    weight_sum = ordered[0]
+    for piece in ordered[1:]:
+        weight_sum = weight_sum + piece
     weight_key_grad = weight_sum[:, : head_count * D_NOPE]
     weight_value_grad = weight_sum[:, head_count * D_NOPE :]
 

time: 417 us -> 319 us (0.76)
  local copies, waits for them, and re-layouts: 86.3 us -> 39 us
  waiting for transfers between devices: 165 us -> 139 us
  matrix products: 32.5 us -> 12 us
    ppermute x20, waiting for transfers between devices: 165 us -> 139 us  [shift_digit(): return lax.ppermute(x, axis, pairs)]
    another operation x4 -> x2, local copies, waits for them, and re-layouts: 24 us -> 7.17 us  [gather_relative(): buf = jnp.stack(pieces, axis=0)]
    transpose x2 -> x0, local copies, waits for them, and re-layouts: 14.4 us -> none  [the longest x1 7.26 us: body(): jnp.einsum('hqk,qhd->khd', prob_half, grad_out, preferred_element_type=jn...]
    concatenate x3 -> x0, local copies, waits for them, and re-layouts: 11.4 us -> none  [body(): jnp.concatenate([key_grad.reshape(block_count, row_count, head_count * D_...]
    dot_general x6 -> x4, matrix products: 13 us -> 4.85 us  [the longest x3 3.89 us: body(): jnp.einsum('btl,btk->blk', left, right, preferred_element_type=jnp.float32)]
    squeeze x4 -> x0, local copies, waits for them, and re-layouts: 5.43 us -> none  [scatter_sum(): part = lax.dynamic_index_in_dim(data, (r + by) % radix, at, keepdims=False)]
    dot_general x1, matrix products: 5.8 us -> 0.56 us  [body(): jnp.einsum('hqk,khd->qhd', grad_score, keys, preferred_element_type=jnp.f...]
    another operation x16 -> x11, other arithmetic: 11.7 us -> 9.85 us  [the longest x9 9.1 us: gather_relative(): buf = jnp.stack(pieces, axis=0)]
  transfers between devices with their start and end apart: 20 -> 20, of which waited for: 17 -> 18; matrix products, arithmetic and copies ran while one was open for 6% -> 7% of each run, Pallas kernels for 0% -> 0%
where the time goes in v2:
time: 319 us; the launch traced here: 318 us
  waiting for transfers between devices  139 us (44%)
  starting transfers between devices  96.9 us (30%)
  local copies, waits for them, and re-layouts  39 us (12%)
  other arithmetic  29.3 us (9%)
  matrix products  12 us (4%)
    ppermute x20, waiting for transfers between devices, shift_digit(): return lax.ppermute(x, axis, pairs)  139 us
    ppermute x20, starting transfers between devices, shift_digit(): return lax.ppermute(x, axis, pairs)  96.9 us
    unnamed x39, local copies, waits for them, and re-layouts  10.1 us
    another operation x9, other arithmetic, gather_relative(): buf = jnp.stack(pieces, axis=0)  9.1 us
    ppermute x2, local copies, waits for them, and re-layouts, shift_digit(): return lax.ppermute(x, axis, pairs)  7.54 us
    another operation x2, local copies, waits for them, and re-layouts, gather_relative(): buf = jnp.stack(pieces, axis=0)  7.17 us
  transfers between devices with their start and end apart: 20, of which 18 were waited for; matrix products, arithmetic and copies ran while one was open for 7% of the time, Pallas kernels for 0%

profile of v2, /device:TPU:56, one launch (start us, length us, event | category | flops | bytes accessed | tf_op | source)
XLA Modules:
  0.0 317.5 jit_solution(13148330410593570432)
XLA Ops:
  4.7 10.9 %collective-permute-start.1 = (bf16[128,578]{1,0:T(8,128)(2,1)S(1)}, bf16[128,578]{1,0:T(8,128)(2,1)S(1)}, u32[]{:S(2)}, u32[]{:S(2)}) collective-permute-start(bf16[128,578]{1,0:T(8,128)(2,1)S(1)} %pad_maximum_fusion.8), channel_id=1, source_target_pairs={{0,64},{32,96},{64,128},{96,160},{128,0},{160,32},{192,256},{224,2... | collective-permute-start | bytes 443912 | tf_op jit(solution)/shard_map/ppermute | solution.py:51
  15.6 5.6 %collective-permute-start = (bf16[128,578]{1,0:T(8,128)(2,1)S(1)}, bf16[128,578]{1,0:T(8,128)(2,1)S(1)}, u32[]{:S(2)}, u32[]{:S(2)}) collective-permute-start(bf16[128,578]{1,0:T(8,128)(2,1)S(1)} %pad_maximum_fusion.8), channel_id=1, source_target_pairs={{0,128},{32,160},{64,0},{96,32},{128,64},{160,96},{192,320},{224,3... | collective-permute-start | bytes 443912 | tf_op jit(solution)/shard_map/ppermute | solution.py:51
  23.7 11.5 %collective-permute-done = bf16[128,578]{1,0:T(8,128)(2,1)S(1)} collective-permute-done((bf16[128,578]{1,0:T(8,128)(2,1)S(1)}, bf16[128,578]{1,0:T(8,128)(2,1)S(1)}, u32[]{:S(2)}, u32[]{:S(2)}) %collective-permute-start) | collective-permute-done | bytes 148000 | tf_op jit(solution)/shard_map/ppermute | solution.py:51
  35.3 4.9 %collective-permute-start.2 = (bf16[3,128,578]{2,1,0:T(8,128)(2,1)S(1)}, bf16[3,128,578]{2,1,0:T(8,128)(2,1)S(1)}, u32[]{:S(2)}, u32[]{:S(2)}) collective-permute-start(bf16[3,128,578]{2,1,0:T(8,128)(2,1)S(1)} %get-tuple-element.46), channel_id=1, source_target_pairs={{0,384},{32,416},{64,448},{96,480},{128,512},{160,544},{192,576},{... | collective-permute-start | bytes 1331720 | tf_op jit(solution)/shard_map/ppermute | solution.py:51
  40.3 9.8 %collective-permute-done.2 = bf16[3,128,578]{2,1,0:T(8,128)(2,1)S(1)} collective-permute-done((bf16[3,128,578]{2,1,0:T(8,128)(2,1)S(1)}, bf16[3,128,578]{2,1,0:T(8,128)(2,1)S(1)}, u32[]{:S(2)}, u32[]{:S(2)}) %collective-permute-start.2) | collective-permute-done | bytes 443936 | tf_op jit(solution)/shard_map/ppermute | solution.py:51
  55.7 17.8 %collective-permute-done.3 = bf16[2,3,128,578]{2,0,3,1:T(2,128)(2,1)} collective-permute-done((bf16[2,3,128,578]{2,0,3,1:T(2,128)(2,1)}, bf16[2,3,128,578]{2,0,3,1:T(2,128)(2,1)}, u32[]{:S(2)}, u32[]{:S(2)}) %collective-permute-start.3) | collective-permute-done | bytes 887840 | tf_op jit(solution)/shard_map/ppermute | solution.py:51
  78.1 5.2 %copy.99 = bf16[2,2,3,128,578]{3,1,4,2,0:T(2,128)(2,1)} copy(bf16[2,2,3,128,578]{4,3,2,1,0:T(8,128)(2,1)} %get-tuple-element.36) | data formatting | bytes 3551232 | tf_op jit(solution)/shard_map/stack | solution.py:75
  89.3 5.1 %copy.100 = bf16[2,2,3,128,578]{4,3,2,1,0:T(8,128)(2,1)} copy(bf16[2,2,3,128,578]{3,1,4,2,0:T(2,128)(2,1)} %collective-permute-done.4) | data formatting | bytes 3551232 | tf_op jit(solution)/shard_map/ppermute | solution.py:51
  112.1 3.6 %copy.133 = f32[2,2,1,2,2,3,128,128]{6,7,1,0,5,4,3,2:T(8,128)} copy(f32[2,2,1,2,2,3,128,128]{7,6,5,4,3,2,1,0:T(8,128)} %get-tuple-element.28) | data formatting | bytes 6291456
  117.9 3.5 %copy.132 = f32[2,2,1,2,2,3,128,128]{6,7,1,0,5,4,3,2:T(8,128)} copy(f32[2,2,1,2,2,3,128,128]{7,6,5,4,3,2,1,0:T(8,128)} %get-tuple-element.27) | data formatting | bytes 6291456
  123.8 3.5 %bitcast_add_fusion = f32[2,2,2,2,3,128,128]{5,6,1,0,4,3,2:T(8,128)S(1)} fusion(f32[2,2,2,2,3,128,128]{5,6,1,0,4,3,2:T(8,128)} %collective-permute-done.5, f32[2,2,1,2,2,3,128,128]{6,7,1,0,5,4,3,2:T(8,128)} %copy.132), kind=kLoop, calls=%fused_computation.27 | loop fusion | flops 786432 | bytes 9437184 | tf_op jit(solution)/shard_map/add | solution.py:88
  130.9 18.1 %collective-permute-done.6 = bf16[2,2,2,3,128,128]{4,5,1,0,3,2:T(8,128)(2,1)S(1)} collective-permute-done((bf16[2,2,2,3,128,128]{4,5,1,0,3,2:T(8,128)(2,1)S(1)}, bf16[2,2,2,3,128,128]{4,5,1,0,3,2:T(8,128)(2,1)S(1)}, u32[]{:S(2)}, u32[]{:S(2)}) %collective-permute-start.6) | collective-permute-done | bytes 786464 | tf_op jit(solution)/shard_map/ppermute | solution.py:51
  149.2 4.9 %collective-permute-start.7 = (bf16[2,2,3,128,128]{3,4,1,0,2:T(8,128)(2,1)S(1)}, bf16[2,2,3,128,128]{3,4,1,0,2:T(8,128)(2,1)S(1)}, u32[]{:S(2)}, u32[]{:S(2)}) collective-permute-start(bf16[2,2,3,128,128]{3,4,1,0,2:T(8,128)(2,1)S(1)} %fusion.25), channel_id=1, source_target_pairs={{0,384},{32,416},{64,448},{96,480},{128,512},{160,544},{192,576},{... | collective-permute-start | bytes 1179656 | tf_op jit(solution)/shard_map/ppermute | solution.py:51
  154.1 8.8 %collective-permute-done.7 = bf16[2,2,3,128,128]{3,4,1,0,2:T(8,128)(2,1)S(1)} collective-permute-done((bf16[2,2,3,128,128]{3,4,1,0,2:T(8,128)(2,1)S(1)}, bf16[2,2,3,128,128]{3,4,1,0,2:T(8,128)(2,1)S(1)}, u32[]{:S(2)}, u32[]{:S(2)}) %collective-permute-start.7) | collective-permute-done | bytes 393248 | tf_op jit(solution)/shard_map/ppermute | solution.py:51
  163.1 6.6 %collective-permute-start.9 = (bf16[2,2,128,128]{2,3,1,0:T(8,128)(2,1)S(1)}, bf16[2,2,128,128]{2,3,1,0:T(8,128)(2,1)S(1)}, u32[]{:S(2)}, u32[]{:S(2)}) collective-permute-start(bf16[2,2,128,128]{2,3,1,0:T(8,128)(2,1)S(1)} %get-tuple-element.50), channel_id=1, source_target_pairs={{0,128},{32,160},{64,0},{96,32},{128,64},{160,96},{192,320},{224,3... | collective-permute-start | bytes 393224 | tf_op jit(solution)/shard_map/ppermute | solution.py:51
  173.0 3.7 %collective-permute-done.9 = bf16[2,2,128,128]{2,3,1,0:T(8,128)(2,1)S(1)} collective-permute-done((bf16[2,2,128,128]{2,3,1,0:T(8,128)(2,1)S(1)}, bf16[2,2,128,128]{2,3,1,0:T(8,128)(2,1)S(1)}, u32[]{:S(2)}, u32[]{:S(2)}) %collective-permute-start.9) | collective-permute-done | bytes 131104 | tf_op jit(solution)/shard_map/ppermute | solution.py:51
  176.7 5.8 %collective-permute-done.8 = bf16[2,2,128,128]{2,3,1,0:T(8,128)(2,1)S(1)} collective-permute-done((bf16[2,2,128,128]{2,3,1,0:T(8,128)(2,1)S(1)}, bf16[2,2,128,128]{2,3,1,0:T(8,128)(2,1)S(1)}, u32[]{:S(2)}, u32[]{:S(2)}) %collective-permute-start.8) | collective-permute-done | bytes 131104 | tf_op jit(solution)/shard_map/ppermute | solution.py:51
  184.8 7.4 %collective-permute-start.15 = (bf16[128,512]{0,1:T(8,128)(2,1)S(1)}, bf16[128,512]{0,1:T(8,128)(2,1)S(1)}, u32[]{:S(2)}, u32[]{:S(2)}) collective-permute-start(bf16[128,512]{0,1:T(8,128)(2,1)S(1)} %bitcast.172), channel_id=1, source_target_pairs={{0,128},{32,160},{64,0},{96,32},{128,64},{160,96},{192,320},{224,3... | collective-permute-start | bytes 393224 | tf_op jit(solution)/shard_map/ppermute | solution.py:51
  193.6 4.0 %collective-permute-done.15 = bf16[128,512]{0,1:T(8,128)(2,1)S(1)} collective-permute-done((bf16[128,512]{0,1:T(8,128)(2,1)S(1)}, bf16[128,512]{0,1:T(8,128)(2,1)S(1)}, u32[]{:S(2)}, u32[]{:S(2)}) %collective-permute-start.15) | collective-permute-done | bytes 131104 | tf_op jit(solution)/shard_map/ppermute | solution.py:51
  197.6 4.9 %collective-permute-start.17 = (bf16[3,128,512]{1,2,0:T(8,128)(2,1)S(1)}, bf16[3,128,512]{1,2,0:T(8,128)(2,1)S(1)}, u32[]{:S(2)}, u32[]{:S(2)}) collective-permute-start(bf16[3,128,512]{1,2,0:T(8,128)(2,1)S(1)} %get-tuple-element.48), channel_id=1, source_target_pairs={{0,384},{32,416},{64,448},{96,480},{128,512},{160,544},{192,576},{... | collective-permute-start | bytes 1179656 | tf_op jit(solution)/shard_map/ppermute | solution.py:51
  202.6 6.2 %collective-permute-done.17 = bf16[3,128,512]{1,2,0:T(8,128)(2,1)S(1)} collective-permute-done((bf16[3,128,512]{1,2,0:T(8,128)(2,1)S(1)}, bf16[3,128,512]{1,2,0:T(8,128)(2,1)S(1)}, u32[]{:S(2)}, u32[]{:S(2)}) %collective-permute-start.17) | collective-permute-done | bytes 393248 | tf_op jit(solution)/shard_map/ppermute | solution.py:51
  208.9 3.4 %collective-permute-start.18 = (bf16[2,3,128,512]{2,3,1,0:T(8,128)(2,1)S(1)}, bf16[2,3,128,512]{2,3,1,0:T(8,128)(2,1)S(1)}, u32[]{:S(2)}, u32[]{:S(2)}) collective-permute-start(bf16[2,3,128,512]{2,3,1,0:T(8,128)(2,1)S(1)} %get-tuple-element.44), channel_id=1, source_target_pairs={{0,192},{32,224},{64,256},{96,288},{128,320},{160,352},{192,0},{22... | collective-permute-start | bytes 2359304 | tf_op jit(solution)/shard_map/ppermute | solution.py:51
  216.1 9.7 %collective-permute-done.18 = bf16[2,3,128,512]{2,3,1,0:T(8,128)(2,1)S(1)} collective-permute-done((bf16[2,3,128,512]{2,3,1,0:T(8,128)(2,1)S(1)}, bf16[2,3,128,512]{2,3,1,0:T(8,128)(2,1)S(1)}, u32[]{:S(2)}, u32[]{:S(2)}) %collective-permute-start.18) | collective-permute-done | bytes 786464 | tf_op jit(solution)/shard_map/ppermute | solution.py:51
  229.7 4.0 %collective-permute-start.11 = (f32[128,512]{1,0:T(8,128)S(1)}, f32[128,512]{1,0:T(8,128)}, u32[]{:S(2)}, u32[]{:S(2)}) collective-permute-start(f32[128,512]{1,0:T(8,128)S(1)} %add.145), channel_id=1, source_target_pairs={{0,2},{1,3},{2,0},{3,1},{4,6},{5,7},{6,4},{7,5},{8,10},{9,11},{10,... | collective-permute-start | bytes 786440 | tf_op jit(solution)/shard_map/ppermute | solution.py:51
  233.8 3.8 %slice.194 = bf16[3072,512]{1,0:T(8,128)(2,1)} slice(bf16[3072,578]{1,0:T(8,128)(2,1)} %bitcast.152), slice={[0:3072], [0:512]} | slice | bytes 6291456 | tf_op jit(solution)/shard_map/slice | solution.py:124
  237.6 9.3 %collective-permute-done.11 = f32[128,512]{1,0:T(8,128)} collective-permute-done((f32[128,512]{1,0:T(8,128)S(1)}, f32[128,512]{1,0:T(8,128)}, u32[]{:S(2)}, u32[]{:S(2)}) %collective-permute-start.11) | collective-permute-done | bytes 262176 | tf_op jit(solution)/shard_map/ppermute | solution.py:51
  248.6 4.6 %collective-permute-start.12 = (f32[128,512]{1,0:T(8,128)}, f32[128,512]{1,0:T(8,128)}, u32[]{:S(2)}, u32[]{:S(2)}) collective-permute-start(f32[128,512]{1,0:T(8,128)} %add.146), channel_id=1, source_target_pairs={{0,4},{1,5},{2,6},{3,7},{4,0},{5,1},{6,2},{7,3},{8,12},{9,13},{10,... | collective-permute-start | bytes 786440 | tf_op jit(solution)/shard_map/ppermute | solution.py:51
  254.5 13.3 %collective-permute-done.12 = f32[128,512]{1,0:T(8,128)} collective-permute-done((f32[128,512]{1,0:T(8,128)}, f32[128,512]{1,0:T(8,128)}, u32[]{:S(2)}, u32[]{:S(2)}) %collective-permute-start.12) | collective-permute-done | bytes 262176 | tf_op jit(solution)/shard_map/ppermute | solution.py:51
  268.9 7.2 %collective-permute-start.13 = (f32[128,512]{1,0:T(8,128)S(1)}, f32[128,512]{1,0:T(8,128)S(1)}, u32[]{:S(2)}, u32[]{:S(2)}) collective-permute-start(f32[128,512]{1,0:T(8,128)S(1)} %add.147), channel_id=1, source_target_pairs={{0,8},{1,9},{2,10},{3,11},{4,12},{5,13},{6,14},{7,15},{8,0},{9,1},... | collective-permute-start | bytes 786440 | tf_op jit(solution)/shard_map/ppermute | solution.py:51
  278.4 4.2 %collective-permute-done.13 = f32[128,512]{1,0:T(8,128)S(1)} collective-permute-done((f32[128,512]{1,0:T(8,128)S(1)}, f32[128,512]{1,0:T(8,128)S(1)}, u32[]{:S(2)}, u32[]{:S(2)}) %collective-permute-start.13) | collective-permute-done | bytes 262176 | tf_op jit(solution)/shard_map/ppermute | solution.py:51
  282.6 10.7 %collective-permute-start.14 = (f32[128,512]{1,0:T(8,128)S(1)}, f32[128,512]{1,0:T(8,128)S(1)}, u32[]{:S(2)}, u32[]{:S(2)}) collective-permute-start(f32[128,512]{1,0:T(8,128)S(1)} %add.148), channel_id=1, source_target_pairs={{0,16},{1,17},{2,18},{3,19},{4,20},{5,21},{6,22},{7,23},{8,24},{9,... | collective-permute-start | bytes 786440 | tf_op jit(solution)/shard_map/ppermute | solution.py:51
  295.6 9.2 %collective-permute-done.14 = f32[128,512]{1,0:T(8,128)S(1)} collective-permute-done((f32[128,512]{1,0:T(8,128)S(1)}, f32[128,512]{1,0:T(8,128)S(1)}, u32[]{:S(2)}, u32[]{:S(2)}) %collective-permute-start.14) | collective-permute-done | bytes 262176 | tf_op jit(solution)/shard_map/ppermute | solution.py:51
  (113 shorter events, 84.8 us)
Async XLA Ops:
  0.6 97.6 %copy-start = (bf16[512,256]{1,0:T(8,128)(2,1)S(1)}, bf16[512,256]{1,0:T(8,128)(2,1)}, u32[]{:S(2)}) copy-start(bf16[512,256]{1,0:T(8,128)(2,1)} %param.16) | copy-start | bytes 786436
  4.5 45.6 %copy-start.4 = (f32[128,4,128]{2,1,0:T(4,128)}, f32[128,4,128]{2,1,0:T(4,128)S(1)}, u32[]{:S(2)}) copy-start(f32[128,4,128]{2,1,0:T(4,128)S(1)} %broadcast_in_dim.42) | copy-start | bytes 786436
  4.7 19.0 %collective-permute-start.1 = (bf16[128,578]{1,0:T(8,128)(2,1)S(1)}, bf16[128,578]{1,0:T(8,128)(2,1)S(1)}, u32[]{:S(2)}, u32[]{:S(2)}) collective-permute-start(bf16[128,578]{1,0:T(8,128)(2,1)S(1)} %pad_maximum_fusion.8), channel_id=1, source_target_pairs={{0,64},{32,96},{64,128},{96,160},{128,0},{160,32},{192,256},{224,2... | collective-permute-start | bytes 443912 | tf_op jit(solution)/shard_map/ppermute | solution.py:51
  15.6 19.6 %collective-permute-start = (bf16[128,578]{1,0:T(8,128)(2,1)S(1)}, bf16[128,578]{1,0:T(8,128)(2,1)S(1)}, u32[]{:S(2)}, u32[]{:S(2)}) collective-permute-start(bf16[128,578]{1,0:T(8,128)(2,1)S(1)} %pad_maximum_fusion.8), channel_id=1, source_target_pairs={{0,128},{32,160},{64,0},{96,32},{128,64},{160,96},{192,320},{224,3... | collective-permute-start | bytes 443912 | tf_op jit(solution)/shard_map/ppermute | solution.py:51
  35.3 14.8 %collective-permute-start.2 = (bf16[3,128,578]{2,1,0:T(8,128)(2,1)S(1)}, bf16[3,128,578]{2,1,0:T(8,128)(2,1)S(1)}, u32[]{:S(2)}, u32[]{:S(2)}) collective-permute-start(bf16[3,128,578]{2,1,0:T(8,128)(2,1)S(1)} %get-tuple-element.46), channel_id=1, source_target_pairs={{0,384},{32,416},{64,448},{96,480},{128,512},{160,544},{192,576},{... | collective-permute-start | bytes 1331720 | tf_op jit(solution)/shard_map/ppermute | solution.py:51
  52.3 21.2 %collective-permute-start.3 = (bf16[2,3,128,578]{2,0,3,1:T(2,128)(2,1)}, bf16[2,3,128,578]{2,0,3,1:T(2,128)(2,1)}, u32[]{:S(2)}, u32[]{:S(2)}) collective-permute-start(bf16[2,3,128,578]{2,0,3,1:T(2,128)(2,1)} %copy.97), channel_id=1, source_target_pairs={{0,192},{32,224},{64,256},{96,288},{128,320},{160,352},{192,0},{22... | collective-permute-start | bytes 2663432 | tf_op jit(solution)/shard_map/ppermute | solution.py:51
  78.1 7.1 %copy-start.11 = (bf16[128,256]{1,0:T(8,128)(2,1)S(1)}, bf16[128,256]{1,0:T(8,128)(2,1)}, u32[]{:S(2)}) copy-start(bf16[128,256]{1,0:T(8,128)(2,1)} %param.11) | copy-start | bytes 196612
  78.1 7.3 %copy-start.13 = (bf16[128,128]{1,0:T(8,128)(2,1)S(1)}, bf16[128,128]{1,0:T(8,128)(2,1)}, u32[]{:S(2)}) copy-start(bf16[128,128]{1,0:T(8,128)(2,1)} %param.10) | copy-start | bytes 98308
  78.1 8.0 %copy-start.12 = (bf16[128,256]{1,0:T(8,128)(2,1)S(1)}, bf16[128,256]{1,0:T(8,128)(2,1)}, u32[]{:S(2)}) copy-start(bf16[128,256]{1,0:T(8,128)(2,1)} %param.9) | copy-start | bytes 196612
  83.3 5.9 %collective-permute-start.4 = (bf16[2,2,3,128,578]{3,1,4,2,0:T(2,128)(2,1)}, bf16[2,2,3,128,578]{3,1,4,2,0:T(2,128)(2,1)}, u32[]{:S(2)}, u32[]{:S(2)}) collective-permute-start(bf16[2,2,3,128,578]{3,1,4,2,0:T(2,128)(2,1)} %copy.99), channel_id=1, source_target_pairs={{0,32},{32,0},{64,96},{96,64},{128,160},{160,128},{192,224},{224,1... | collective-permute-start | bytes 5326856 | tf_op jit(solution)/shard_map/ppermute | solution.py:51
  97.1 4.1 %copy-start.2 = (bf16[2,2,2,3,128,578]{5,4,3,2,1,0:T(8,128)(2,1)}, bf16[2,2,2,3,128,578]{5,4,3,2,1,0:T(8,128)(2,1)S(1)}, u32[]{:S(2)}) copy-start(bf16[2,2,2,3,128,578]{5,4,3,2,1,0:T(8,128)(2,1)S(1)} %pad_maximum_fusion) | copy-start | bytes 10653700
  105.8 2.1 copy-start.6
  105.8 2.1 copy-start.7
  115.7 8.1 %collective-permute-start.5 = (f32[2,2,2,2,3,128,128]{5,6,1,0,4,3,2:T(8,128)}, f32[2,2,2,2,3,128,128]{5,6,1,0,4,3,2:T(8,128)}, u32[]{:S(2)}, u32[]{:S(2)}) collective-permute-start(f32[2,2,2,2,3,128,128]{5,6,1,0,4,3,2:T(8,128)} %bitcast.167), channel_id=1, source_target_pairs={{0,32},{32,0},{64,96},{96,64},{128,160},{160,128},{192,224},{224,1... | collective-permute-start | bytes 9437192 | tf_op jit(solution)/shard_map/ppermute | solution.py:51
  127.5 21.5 %collective-permute-start.6 = (bf16[2,2,2,3,128,128]{4,5,1,0,3,2:T(8,128)(2,1)S(1)}, bf16[2,2,2,3,128,128]{4,5,1,0,3,2:T(8,128)(2,1)S(1)}, u32[]{:S(2)}, u32[]{:S(2)}) collective-permute-start(bf16[2,2,2,3,128,128]{4,5,1,0,3,2:T(8,128)(2,1)S(1)} %fusion.23), channel_id=1, source_target_pairs={{0,192},{32,224},{64,256},{96,288},{128,320},{160,352},{192,0},{22... | collective-permute-start | bytes 2359304 | tf_op jit(solution)/shard_map/ppermute | solution.py:51
  149.2 13.7 %collective-permute-start.7 = (bf16[2,2,3,128,128]{3,4,1,0,2:T(8,128)(2,1)S(1)}, bf16[2,2,3,128,128]{3,4,1,0,2:T(8,128)(2,1)S(1)}, u32[]{:S(2)}, u32[]{:S(2)}) collective-permute-start(bf16[2,2,3,128,128]{3,4,1,0,2:T(8,128)(2,1)S(1)} %fusion.25), channel_id=1, source_target_pairs={{0,384},{32,416},{64,448},{96,480},{128,512},{160,544},{192,576},{... | collective-permute-start | bytes 1179656 | tf_op jit(solution)/shard_map/ppermute | solution.py:51
  163.1 49.5 %copy-start.9 = (bf16[512,256]{1,0:T(8,128)(2,1)S(1)}, bf16[512,256]{1,0:T(8,128)(2,1)}, u32[]{:S(2)}) copy-start(bf16[512,256]{1,0:T(8,128)(2,1)} %param.17) | copy-start | bytes 786436
  163.1 13.6 %collective-permute-start.9 = (bf16[2,2,128,128]{2,3,1,0:T(8,128)(2,1)S(1)}, bf16[2,2,128,128]{2,3,1,0:T(8,128)(2,1)S(1)}, u32[]{:S(2)}, u32[]{:S(2)}) collective-permute-start(bf16[2,2,128,128]{2,3,1,0:T(8,128)(2,1)S(1)} %get-tuple-element.50), channel_id=1, source_target_pairs={{0,128},{32,160},{64,0},{96,32},{128,64},{160,96},{192,320},{224,3... | collective-permute-start | bytes 393224 | tf_op jit(solution)/shard_map/ppermute | solution.py:51
  169.7 12.7 %collective-permute-start.8 = (bf16[2,2,128,128]{2,3,1,0:T(8,128)(2,1)S(1)}, bf16[2,2,128,128]{2,3,1,0:T(8,128)(2,1)S(1)}, u32[]{:S(2)}, u32[]{:S(2)}) collective-permute-start(bf16[2,2,128,128]{2,3,1,0:T(8,128)(2,1)S(1)} %get-tuple-element.49), channel_id=1, source_target_pairs={{0,64},{32,96},{64,128},{96,160},{128,0},{160,32},{192,256},{224,2... | collective-permute-start | bytes 393224 | tf_op jit(solution)/shard_map/ppermute | solution.py:51
  182.5 11.1 %collective-permute-start.16 = (bf16[128,512]{0,1:T(8,128)(2,1)S(1)}, bf16[128,512]{0,1:T(8,128)(2,1)S(1)}, u32[]{:S(2)}, u32[]{:S(2)}) collective-permute-start(bf16[128,512]{0,1:T(8,128)(2,1)S(1)} %bitcast.171), channel_id=1, source_target_pairs={{0,64},{32,96},{64,128},{96,160},{128,0},{160,32},{192,256},{224,2... | collective-permute-start | bytes 393224 | tf_op jit(solution)/shard_map/ppermute | solution.py:51
  184.8 12.7 %collective-permute-start.15 = (bf16[128,512]{0,1:T(8,128)(2,1)S(1)}, bf16[128,512]{0,1:T(8,128)(2,1)S(1)}, u32[]{:S(2)}, u32[]{:S(2)}) collective-permute-start(bf16[128,512]{0,1:T(8,128)(2,1)S(1)} %bitcast.172), channel_id=1, source_target_pairs={{0,128},{32,160},{64,0},{96,32},{128,64},{160,96},{192,320},{224,3... | collective-permute-start | bytes 393224 | tf_op jit(solution)/shard_map/ppermute | solution.py:51
  197.6 11.2 %collective-permute-start.17 = (bf16[3,128,512]{1,2,0:T(8,128)(2,1)S(1)}, bf16[3,128,512]{1,2,0:T(8,128)(2,1)S(1)}, u32[]{:S(2)}, u32[]{:S(2)}) collective-permute-start(bf16[3,128,512]{1,2,0:T(8,128)(2,1)S(1)} %get-tuple-element.48), channel_id=1, source_target_pairs={{0,384},{32,416},{64,448},{96,480},{128,512},{160,544},{192,576},{... | collective-permute-start | bytes 1179656 | tf_op jit(solution)/shard_map/ppermute | solution.py:51
  208.9 16.8 %collective-permute-start.18 = (bf16[2,3,128,512]{2,3,1,0:T(8,128)(2,1)S(1)}, bf16[2,3,128,512]{2,3,1,0:T(8,128)(2,1)S(1)}, u32[]{:S(2)}, u32[]{:S(2)}) collective-permute-start(bf16[2,3,128,512]{2,3,1,0:T(8,128)(2,1)S(1)} %get-tuple-element.44), channel_id=1, source_target_pairs={{0,192},{32,224},{64,256},{96,288},{128,320},{160,352},{192,0},{22... | collective-permute-start | bytes 2359304 | tf_op jit(solution)/shard_map/ppermute | solution.py:51
  212.8 16.8 %collective-permute-start.10 = (f32[128,512]{1,0:T(8,128)S(1)}, f32[128,512]{1,0:T(8,128)S(1)}, u32[]{:S(2)}, u32[]{:S(2)}) collective-permute-start(f32[128,512]{1,0:T(8,128)S(1)} %convolution_add_fusion), channel_id=1, source_target_pairs={{0,1},{1,0},{2,3},{3,2},{4,5},{5,4},{6,7},{7,6},{8,9},{9,8},{10,11... | collective-permute-start | bytes 786440 | tf_op jit(solution)/shard_map/ppermute | solution.py:51
  227.7 77.8 %collective-permute-start.19 = (bf16[2,2,3,128,512]{3,4,2,1,0:T(8,128)(2,1)}, bf16[2,2,3,128,512]{3,4,2,1,0:T(8,128)(2,1)}, u32[]{:S(2)}, u32[]{:S(2)}) collective-permute-start(bf16[2,2,3,128,512]{3,4,2,1,0:T(8,128)(2,1)} %get-tuple-element.37), channel_id=1, source_target_pairs={{0,32},{32,0},{64,96},{96,64},{128,160},{160,128},{192,224},{224,1... | collective-permute-start | bytes 4718600 | tf_op jit(solution)/shard_map/ppermute | solution.py:51
  229.7 17.2 %collective-permute-start.11 = (f32[128,512]{1,0:T(8,128)S(1)}, f32[128,512]{1,0:T(8,128)}, u32[]{:S(2)}, u32[]{:S(2)}) collective-permute-start(f32[128,512]{1,0:T(8,128)S(1)} %add.145), channel_id=1, source_target_pairs={{0,2},{1,3},{2,0},{3,1},{4,6},{5,7},{6,4},{7,5},{8,10},{9,11},{10,... | collective-permute-start | bytes 786440 | tf_op jit(solution)/shard_map/ppermute | solution.py:51
  248.6 19.2 %collective-permute-start.12 = (f32[128,512]{1,0:T(8,128)}, f32[128,512]{1,0:T(8,128)}, u32[]{:S(2)}, u32[]{:S(2)}) collective-permute-start(f32[128,512]{1,0:T(8,128)} %add.146), channel_id=1, source_target_pairs={{0,4},{1,5},{2,6},{3,7},{4,0},{5,1},{6,2},{7,3},{8,12},{9,13},{10,... | collective-permute-start | bytes 786440 | tf_op jit(solution)/shard_map/ppermute | solution.py:51
  268.9 13.7 %collective-permute-start.13 = (f32[128,512]{1,0:T(8,128)S(1)}, f32[128,512]{1,0:T(8,128)S(1)}, u32[]{:S(2)}, u32[]{:S(2)}) collective-permute-start(f32[128,512]{1,0:T(8,128)S(1)} %add.147), channel_id=1, source_target_pairs={{0,8},{1,9},{2,10},{3,11},{4,12},{5,13},{6,14},{7,15},{8,0},{9,1},... | collective-permute-start | bytes 786440 | tf_op jit(solution)/shard_map/ppermute | solution.py:51
  282.6 22.2 %collective-permute-start.14 = (f32[128,512]{1,0:T(8,128)S(1)}, f32[128,512]{1,0:T(8,128)S(1)}, u32[]{:S(2)}, u32[]{:S(2)}) collective-permute-start(f32[128,512]{1,0:T(8,128)S(1)} %add.148), channel_id=1, source_target_pairs={{0,16},{1,17},{2,18},{3,19},{4,20},{5,21},{6,22},{7,23},{8,24},{9,... | collective-permute-start | bytes 786440 | tf_op jit(solution)/shard_map/ppermute | solution.py:51
  293.2 11.6 %copy-start.5 = (f32[128,4,128]{2,1,0:T(4,128)S(1)}, f32[128,4,128]{2,1,0:T(4,128)}, u32[]{:S(2)}) copy-start(f32[128,4,128]{2,1,0:T(4,128)} %copy-done.4) | copy-start | bytes 786436
  293.3 12.3 %copy-start.3 = (bf16[1,2,2,3,128,512]{4,5,3,2,1,0:T(8,128)(2,1)S(1)}, bf16[1,2,2,3,128,512]{4,5,3,2,1,0:T(8,128)(2,1)}, u32[]{:S(2)}) copy-start(bf16[1,2,2,3,128,512]{4,5,3,2,1,0:T(8,128)(2,1)} %get-tuple-element.38) | copy-start | bytes 4718596
  315.6 1.9 copy-start.1
  (3 other events, 2.6 us)

commit v3 on v2

--- a/solution.py
+++ b/solution.py
@@ -21,6 +21,10 @@
             found.append((prime, stride))
             stride *= prime
             rest //= prime
+    while rest % 4 == 0:
+        found.append((4, stride))
+        stride *= 4
+        rest //= 4
     prime = 2
     while rest > 1:
         while rest % prime == 0:
@@ -32,10 +36,7 @@
 
 
 def gather_order(size):
-    found = digits_of(size)
-    odd = [d for d in found if d[0] != 2]
-    even = sorted([d for d in found if d[0] == 2], key=lambda d: -d[1])
-    return odd + even
+    return sorted(digits_of(size), key=lambda d: (d[0] != 3, -d[1]))
 
 
 def digit_value(axis, radix, stride):
@@ -91,6 +92,16 @@
     return data
 
 
+def ordered_sum(slots, axis, radix, stride):
+    r = digit_value(axis, radix, stride)
+    received = {by: slots[radix - by] for by in range(1, radix)}
+    ordered = canonical(slots[0], received, r, radix)
+    total = ordered[0]
+    for piece in ordered[1:]:
+        total = total + piece
+    return total
+
+
 def total_over(x, axis):
     size = lax.axis_size(axis)
     for radix, stride in digits_of(size):
@@ -185,6 +196,7 @@
     order = gather_order(block_count)
     first_radix, first_stride = order[0]
     lead = radices[:-1]
+    lead_digits = list(reversed(order))[:-1]
     comp_rel = comp_all.reshape(radices + (row_count, col_width))
     slot_sums = []
     for slot in range(first_radix):
@@ -193,15 +205,10 @@
         product = jnp.einsum("btl,btk->blk", left, right, preferred_element_type=jnp.float32)
         partial = product.astype(jnp.bfloat16).astype(jnp.float32)
         partial = partial.reshape(lead + partial.shape[1:])
-        for unused in lead:
-            partial = partial[0] + partial[1]
+        for radix, stride in lead_digits:
+            partial = ordered_sum([partial[k] for k in range(radix)], "blk", radix, stride)
         slot_sums.append(partial)
-    first_digit = digit_value("blk", first_radix, first_stride)
-    received = {by: slot_sums[first_radix - by] for by in range(1, first_radix)}
-    ordered = canonical(slot_sums[0], received, first_digit, first_radix)
-    weight_sum = ordered[0]
-    for piece in ordered[1:]:
-        weight_sum = weight_sum + piece
+    weight_sum = ordered_sum(slot_sums, "blk", first_radix, first_stride)
     weight_key_grad = weight_sum[:, : head_count * D_NOPE]
     weight_value_grad = weight_sum[:, head_count * D_NOPE :]
 

time: 319 us -> 301 us (0.944)
  waiting for transfers between devices: 139 us -> 116 us
  starting transfers between devices: 96.9 us -> 108 us
  local copies, waits for them, and re-layouts: 39 us -> 33.7 us
    ppermute x20 -> x25, waiting for transfers between devices: 139 us -> 116 us  [shift_digit(): return lax.ppermute(x, axis, pairs)]
    ppermute x20 -> x25, starting transfers between devices: 96.9 us -> 108 us  [shift_digit(): return lax.ppermute(x, axis, pairs)]
    add x8 -> x4, other arithmetic: 9.05 us -> 5.26 us  [the longest x3 5.12 us: ordered_sum(): total = total + piece]
    another operation x1 -> x2, other arithmetic: 0.14 us -> 3.72 us
    ppermute x2 -> x1, local copies, waits for them, and re-layouts: 7.54 us -> 4.79 us  [shift_digit(): return lax.ppermute(x, axis, pairs)]
    another operation x2 -> x1, local copies, waits for them, and re-layouts: 7.17 us -> 4.75 us  [gather_relative(): buf = jnp.stack(pieces, axis=0)]
    another operation x9 -> x7, other arithmetic: 9.1 us -> 11 us  [gather_relative(): buf = jnp.stack(pieces, axis=0)]
    unnamed x39 -> x43, local copies, waits for them, and re-layouts: 10.1 us -> 10.1 us
  transfers between devices with their start and end apart: 20 -> 25, of which waited for: 18 -> 19; matrix products, arithmetic and copies ran while one was open for 7% -> 6% of each run, Pallas kernels for 0% -> 0%
where the time goes in v3:
time: 301 us; the launch traced here: 300 us
  waiting for transfers between devices  116 us (39%)
  starting transfers between devices  108 us (36%)
  local copies, waits for them, and re-layouts  33.7 us (11%)
  other arithmetic  29.3 us (10%)
  matrix products  12 us (4%)
    ppermute x25, waiting for transfers between devices, shift_digit(): return lax.ppermute(x, axis, pairs)  116 us
    ppermute x25, starting transfers between devices, shift_digit(): return lax.ppermute(x, axis, pairs)  108 us
    another operation x7, other arithmetic, gather_relative(): buf = jnp.stack(pieces, axis=0)  11 us
    unnamed x43, local copies, waits for them, and re-layouts  10.1 us
  transfers between devices with their start and end apart: 25, of which 19 were waited for; matrix products, arithmetic and copies ran while one was open for 6% of the time, Pallas kernels for 0%

profile of v3, /device:TPU:56, one launch (start us, length us, event | category | flops | bytes accessed | tf_op | source)
XLA Modules:
  0.0 300.1 jit_solution(14561308965347467039)
XLA Ops:
  4.7 10.9 %collective-permute-start.1 = (bf16[128,578]{1,0:T(8,128)(2,1)S(1)}, bf16[128,578]{1,0:T(8,128)(2,1)S(1)}, u32[]{:S(2)}, u32[]{:S(2)}) collective-permute-start(bf16[128,578]{1,0:T(8,128)(2,1)S(1)} %pad_maximum_fusion.6), channel_id=1, source_target_pairs={{0,64},{32,96},{64,128},{96,160},{128,0},{160,32},{192,256},{224,2... | collective-permute-start | bytes 443912 | tf_op jit(solution)/shard_map/ppermute | solution.py:52
  15.6 5.6 %collective-permute-start = (bf16[128,578]{1,0:T(8,128)(2,1)S(1)}, bf16[128,578]{1,0:T(8,128)(2,1)S(1)}, u32[]{:S(2)}, u32[]{:S(2)}) collective-permute-start(bf16[128,578]{1,0:T(8,128)(2,1)S(1)} %pad_maximum_fusion.6), channel_id=1, source_target_pairs={{0,128},{32,160},{64,0},{96,32},{128,64},{160,96},{192,320},{224,3... | collective-permute-start | bytes 443912 | tf_op jit(solution)/shard_map/ppermute | solution.py:52
  23.7 11.5 %collective-permute-done = bf16[128,578]{1,0:T(8,128)(2,1)S(1)} collective-permute-done((bf16[128,578]{1,0:T(8,128)(2,1)S(1)}, bf16[128,578]{1,0:T(8,128)(2,1)S(1)}, u32[]{:S(2)}, u32[]{:S(2)}) %collective-permute-start) | collective-permute-done | bytes 148000 | tf_op jit(solution)/shard_map/ppermute | solution.py:52
  35.3 3.4 %collective-permute-start.4 = (bf16[3,128,578]{2,1,0:T(8,128)(2,1)S(1)}, bf16[3,128,578]{2,1,0:T(8,128)(2,1)S(1)}, u32[]{:S(2)}, u32[]{:S(2)}) collective-permute-start(bf16[3,128,578]{2,1,0:T(8,128)(2,1)S(1)} %get-tuple-element.47), channel_id=1, source_target_pairs={{0,192},{32,224},{64,256},{96,288},{128,320},{160,352},{192,384},{... | collective-permute-start | bytes 1331720 | tf_op jit(solution)/shard_map/ppermute | solution.py:52
  38.8 4.6 %collective-permute-start.3 = (bf16[3,128,578]{2,1,0:T(8,128)(2,1)S(1)}, bf16[3,128,578]{2,1,0:T(8,128)(2,1)S(1)}, u32[]{:S(2)}, u32[]{:S(2)}) collective-permute-start(bf16[3,128,578]{2,1,0:T(8,128)(2,1)S(1)} %get-tuple-element.47), channel_id=1, source_target_pairs={{0,384},{32,416},{64,448},{96,480},{128,512},{160,544},{192,576},{... | collective-permute-start | bytes 1331720 | tf_op jit(solution)/shard_map/ppermute | solution.py:52
  46.7 4.9 %collective-permute-done.4 = bf16[3,128,578]{2,1,0:T(8,128)(2,1)S(1)} collective-permute-done((bf16[3,128,578]{2,1,0:T(8,128)(2,1)S(1)}, bf16[3,128,578]{2,1,0:T(8,128)(2,1)S(1)}, u32[]{:S(2)}, u32[]{:S(2)}) %collective-permute-start.4) | collective-permute-done | bytes 443936 | tf_op jit(solution)/shard_map/ppermute | solution.py:52
  51.6 9.7 %collective-permute-done.3 = bf16[3,128,578]{2,1,0:T(8,128)(2,1)S(1)} collective-permute-done((bf16[3,128,578]{2,1,0:T(8,128)(2,1)S(1)}, bf16[3,128,578]{2,1,0:T(8,128)(2,1)S(1)}, u32[]{:S(2)}, u32[]{:S(2)}) %collective-permute-start.3) | collective-permute-done | bytes 443936 | tf_op jit(solution)/shard_map/ppermute | solution.py:52
  65.3 4.7 %copy.99 = bf16[4,3,128,578]{2,0,3,1:T(4,128)(2,1)} copy(bf16[4,3,128,578]{3,2,1,0:T(8,128)(2,1)} %get-tuple-element.38) | data formatting | bytes 3551232 | tf_op jit(solution)/shard_map/stack | solution.py:76
  75.9 4.8 %copy.100 = bf16[4,3,128,578]{3,2,1,0:T(8,128)(2,1)} copy(bf16[4,3,128,578]{2,0,3,1:T(4,128)(2,1)} %collective-permute-done.5) | data formatting | bytes 3551232 | tf_op jit(solution)/shard_map/ppermute | solution.py:52
  98.4 3.6 %copy.133 = f32[2,2,1,4,3,128,128]{5,6,1,0,4,3,2:T(8,128)} copy(f32[2,2,1,4,3,128,128]{6,5,4,3,2,1,0:T(8,128)} %get-tuple-element.30) | data formatting | bytes 6291456
  104.0 3.5 %copy.132 = f32[2,2,1,4,3,128,128]{5,6,1,0,4,3,2:T(8,128)} copy(f32[2,2,1,4,3,128,128]{6,5,4,3,2,1,0:T(8,128)} %get-tuple-element.29) | data formatting | bytes 6291456
  109.9 3.5 %fusion.45 = (bf16[2,2,4,3,128,128]{4,5,1,0,3,2:T(8,128)(2,1)S(1)}, f32[2,2,4,3,128,128]{4,5,1,0,3,2:T(8,128)S(1)}) fusion(f32[2,2,4,3,128,128]{4,5,1,0,3,2:T(8,128)} %collective-permute-done.6, f32[2,2,1,4,3,128,128]{5,6,1,0,4,3,2:T(8,128)} %copy.132), kind=kLoop, calls=%fused_computation.96 | loop fusion | flops 1572864 | bytes 11010048 | tf_op jit(solution)/shard_map/convert.4
  113.5 4.5 %collective-permute-start.9 = (bf16[2,2,3,128,128]{3,4,1,0,2:T(8,128)(2,1)S(1)}, bf16[2,2,3,128,128]{3,4,1,0,2:T(8,128)(2,1)S(1)}, u32[]{:S(2)}, u32[]{:S(2)}) collective-permute-start(bf16[2,2,3,128,128]{3,4,1,0,2:T(8,128)(2,1)S(1)} %get-tuple-element.42), channel_id=1, source_target_pairs={{0,576},{32,608},{64,640},{96,672},{128,704},{160,736},{192,0},{22... | collective-permute-start | bytes 1179656 | tf_op jit(solution)/shard_map/ppermute | solution.py:52
  118.0 3.7 %collective-permute-start.8 = (bf16[2,2,3,128,128]{3,4,1,0,2:T(8,128)(2,1)S(1)}, bf16[2,2,3,128,128]{3,4,1,0,2:T(8,128)(2,1)S(1)}, u32[]{:S(2)}, u32[]{:S(2)}) collective-permute-start(bf16[2,2,3,128,128]{3,4,1,0,2:T(8,128)(2,1)S(1)} %get-tuple-element.43), channel_id=1, source_target_pairs={{0,384},{32,416},{64,448},{96,480},{128,512},{160,544},{192,576},{... | collective-permute-start | bytes 1179656 | tf_op jit(solution)/shard_map/ppermute | solution.py:52
  123.7 11.5 %collective-permute-done.9 = bf16[2,2,3,128,128]{3,4,1,0,2:T(8,128)(2,1)S(1)} collective-permute-done((bf16[2,2,3,128,128]{3,4,1,0,2:T(8,128)(2,1)S(1)}, bf16[2,2,3,128,128]{3,4,1,0,2:T(8,128)(2,1)S(1)}, u32[]{:S(2)}, u32[]{:S(2)}) %collective-permute-start.9) | collective-permute-done | bytes 393248 | tf_op jit(solution)/shard_map/ppermute | solution.py:52
  135.1 5.6 %collective-permute-done.7 = bf16[2,2,3,128,128]{3,4,1,0,2:T(8,128)(2,1)S(1)} collective-permute-done((bf16[2,2,3,128,128]{3,4,1,0,2:T(8,128)(2,1)S(1)}, bf16[2,2,3,128,128]{3,4,1,0,2:T(8,128)(2,1)S(1)}, u32[]{:S(2)}, u32[]{:S(2)}) %collective-permute-start.7) | collective-permute-done | bytes 393248 | tf_op jit(solution)/shard_map/ppermute | solution.py:52
  141.0 7.1 %collective-permute-start.11 = (bf16[2,2,128,128]{2,3,1,0:T(8,128)(2,1)S(1)}, bf16[2,2,128,128]{2,3,1,0:T(8,128)(2,1)S(1)}, u32[]{:S(2)}, u32[]{:S(2)}) collective-permute-start(bf16[2,2,128,128]{2,3,1,0:T(8,128)(2,1)S(1)} %get-tuple-element.51), channel_id=1, source_target_pairs={{0,128},{32,160},{64,0},{96,32},{128,64},{160,96},{192,320},{224,3... | collective-permute-start | bytes 393224 | tf_op jit(solution)/shard_map/ppermute | solution.py:52
  153.2 7.9 %collective-permute-done.10 = bf16[2,2,128,128]{2,3,1,0:T(8,128)(2,1)S(1)} collective-permute-done((bf16[2,2,128,128]{2,3,1,0:T(8,128)(2,1)S(1)}, bf16[2,2,128,128]{2,3,1,0:T(8,128)(2,1)S(1)}, u32[]{:S(2)}, u32[]{:S(2)}) %collective-permute-start.10) | collective-permute-done | bytes 131104 | tf_op jit(solution)/shard_map/ppermute | solution.py:52
  161.2 4.1 %collective-permute-start.20 = (bf16[128,512]{0,1:T(8,128)(2,1)S(1)}, bf16[128,512]{0,1:T(8,128)(2,1)S(1)}, u32[]{:S(2)}, u32[]{:S(2)}) collective-permute-start(bf16[128,512]{0,1:T(8,128)(2,1)S(1)} %bitcast.165), channel_id=1, source_target_pairs={{0,64},{32,96},{64,128},{96,160},{128,0},{160,32},{192,256},{224,2... | collective-permute-start | bytes 393224 | tf_op jit(solution)/shard_map/ppermute | solution.py:52
  165.3 5.6 %collective-permute-start.19 = (bf16[128,512]{0,1:T(8,128)(2,1)S(1)}, bf16[128,512]{0,1:T(8,128)(2,1)S(1)}, u32[]{:S(2)}, u32[]{:S(2)}) collective-permute-start(bf16[128,512]{0,1:T(8,128)(2,1)S(1)} %bitcast.166), channel_id=1, source_target_pairs={{0,128},{32,160},{64,0},{96,32},{128,64},{160,96},{192,320},{224,3... | collective-permute-start | bytes 393224 | tf_op jit(solution)/shard_map/ppermute | solution.py:52
  170.9 4.7 %collective-permute-done.20 = bf16[128,512]{0,1:T(8,128)(2,1)S(1)} collective-permute-done((bf16[128,512]{0,1:T(8,128)(2,1)S(1)}, bf16[128,512]{0,1:T(8,128)(2,1)S(1)}, u32[]{:S(2)}, u32[]{:S(2)}) %collective-permute-start.20) | collective-permute-done | bytes 131104 | tf_op jit(solution)/shard_map/ppermute | solution.py:52
  179.7 3.8 %collective-permute-start.23 = (bf16[3,128,512]{1,2,0:T(8,128)(2,1)}, bf16[3,128,512]{1,2,0:T(8,128)(2,1)}, u32[]{:S(2)}, u32[]{:S(2)}) collective-permute-start(bf16[3,128,512]{1,2,0:T(8,128)(2,1)} %get-tuple-element.49), channel_id=1, source_target_pairs={{0,192},{32,224},{64,256},{96,288},{128,320},{160,352},{192,384},{... | collective-permute-start | bytes 1179656 | tf_op jit(solution)/shard_map/ppermute | solution.py:52
  183.5 3.6 %collective-permute-start.22 = (bf16[3,128,512]{1,2,0:T(8,128)(2,1)}, bf16[3,128,512]{1,2,0:T(8,128)(2,1)}, u32[]{:S(2)}, u32[]{:S(2)}) collective-permute-start(bf16[3,128,512]{1,2,0:T(8,128)(2,1)} %get-tuple-element.49), channel_id=1, source_target_pairs={{0,384},{32,416},{64,448},{96,480},{128,512},{160,544},{192,576},{... | collective-permute-start | bytes 1179656 | tf_op jit(solution)/shard_map/ppermute | solution.py:52
  190.5 3.8 %slice.183 = bf16[3072,512]{1,0:T(8,128)(2,1)} slice(bf16[3072,578]{1,0:T(8,128)(2,1)} %bitcast.147), slice={[0:3072], [0:512]} | slice | bytes 6291456 | tf_op jit(solution)/shard_map/slice | solution.py:135
  194.6 3.6 %collective-permute-done.23 = bf16[3,128,512]{1,2,0:T(8,128)(2,1)} collective-permute-done((bf16[3,128,512]{1,2,0:T(8,128)(2,1)}, bf16[3,128,512]{1,2,0:T(8,128)(2,1)}, u32[]{:S(2)}, u32[]{:S(2)}) %collective-permute-start.23) | collective-permute-done | bytes 393248 | tf_op jit(solution)/shard_map/ppermute | solution.py:52
  210.7 6.1 %collective-permute-done.12 = f32[128,512]{1,0:T(8,128)} collective-permute-done((f32[128,512]{1,0:T(8,128)S(1)}, f32[128,512]{1,0:T(8,128)}, u32[]{:S(2)}, u32[]{:S(2)}) %collective-permute-start.12) | collective-permute-done | bytes 262176 | tf_op jit(solution)/shard_map/ppermute | solution.py:52
  217.9 4.0 %collective-permute-start.13 = (f32[128,512]{1,0:T(8,128)S(1)}, f32[128,512]{1,0:T(8,128)S(1)}, u32[]{:S(2)}, u32[]{:S(2)}) collective-permute-start(f32[128,512]{1,0:T(8,128)S(1)} %add.280), channel_id=1, source_target_pairs={{0,6},{1,7},{2,0},{3,1},{4,2},{5,3},{6,4},{7,5},{8,14},{9,15},{10,... | collective-permute-start | bytes 786440 | tf_op jit(solution)/shard_map/ppermute | solution.py:52
  224.8 5.7 %collective-permute-start.15 = (f32[128,512]{1,0:T(8,128)S(1)}, f32[128,512]{1,0:T(8,128)S(1)}, u32[]{:S(2)}, u32[]{:S(2)}) collective-permute-start(f32[128,512]{1,0:T(8,128)S(1)} %add.280), channel_id=1, source_target_pairs={{0,2},{1,3},{2,4},{3,5},{4,6},{5,7},{6,0},{7,1},{8,10},{9,11},{10,... | collective-permute-start | bytes 786440 | tf_op jit(solution)/shard_map/ppermute | solution.py:52
  232.8 8.4 %collective-permute-done.13 = f32[128,512]{1,0:T(8,128)S(1)} collective-permute-done((f32[128,512]{1,0:T(8,128)S(1)}, f32[128,512]{1,0:T(8,128)S(1)}, u32[]{:S(2)}, u32[]{:S(2)}) %collective-permute-start.13) | collective-permute-done | bytes 262176 | tf_op jit(solution)/shard_map/ppermute | solution.py:52
  241.3 10.2 %collective-permute-done.15 = f32[128,512]{1,0:T(8,128)S(1)} collective-permute-done((f32[128,512]{1,0:T(8,128)S(1)}, f32[128,512]{1,0:T(8,128)S(1)}, u32[]{:S(2)}, u32[]{:S(2)}) %collective-permute-start.15) | collective-permute-done | bytes 262176 | tf_op jit(solution)/shard_map/ppermute | solution.py:52
  251.7 13.9 %collective-permute-start.16 = (f32[128,512]{1,0:T(8,128)S(1)}, f32[128,512]{1,0:T(8,128)S(1)}, u32[]{:S(2)}, u32[]{:S(2)}) collective-permute-start(f32[128,512]{1,0:T(8,128)S(1)} %select_add_fusion.3), channel_id=1, source_target_pairs={{0,24},{1,25},{2,26},{3,27},{4,28},{5,29},{6,30},{7,31},{8,0},{9,1... | collective-permute-start | bytes 786440 | tf_op jit(solution)/shard_map/ppermute | solution.py:52
  272.3 15.3 %collective-permute-done.17 = f32[128,512]{1,0:T(8,128)S(1)} collective-permute-done((f32[128,512]{1,0:T(8,128)S(1)}, f32[128,512]{1,0:T(8,128)S(1)}, u32[]{:S(2)}, u32[]{:S(2)}) %collective-permute-start.17) | collective-permute-done | bytes 262176 | tf_op jit(solution)/shard_map/ppermute | solution.py:52
  (116 shorter events, 94.3 us)
Async XLA Ops:
  0.6 83.9 %copy-start = (bf16[512,256]{1,0:T(8,128)(2,1)S(1)}, bf16[512,256]{1,0:T(8,128)(2,1)}, u32[]{:S(2)}) copy-start(bf16[512,256]{1,0:T(8,128)(2,1)} %param.16) | copy-start | bytes 786436
  4.5 60.7 %copy-start.4 = (f32[128,4,128]{2,1,0:T(4,128)}, f32[128,4,128]{2,1,0:T(4,128)S(1)}, u32[]{:S(2)}) copy-start(f32[128,4,128]{2,1,0:T(4,128)S(1)} %broadcast_in_dim.42) | copy-start | bytes 786436
  4.7 19.0 %collective-permute-start.1 = (bf16[128,578]{1,0:T(8,128)(2,1)S(1)}, bf16[128,578]{1,0:T(8,128)(2,1)S(1)}, u32[]{:S(2)}, u32[]{:S(2)}) collective-permute-start(bf16[128,578]{1,0:T(8,128)(2,1)S(1)} %pad_maximum_fusion.6), channel_id=1, source_target_pairs={{0,64},{32,96},{64,128},{96,160},{128,0},{160,32},{192,256},{224,2... | collective-permute-start | bytes 443912 | tf_op jit(solution)/shard_map/ppermute | solution.py:52
  15.6 19.6 %collective-permute-start = (bf16[128,578]{1,0:T(8,128)(2,1)S(1)}, bf16[128,578]{1,0:T(8,128)(2,1)S(1)}, u32[]{:S(2)}, u32[]{:S(2)}) collective-permute-start(bf16[128,578]{1,0:T(8,128)(2,1)S(1)} %pad_maximum_fusion.6), channel_id=1, source_target_pairs={{0,128},{32,160},{64,0},{96,32},{128,64},{160,96},{192,320},{224,3... | collective-permute-start | bytes 443912 | tf_op jit(solution)/shard_map/ppermute | solution.py:52
  35.3 16.3 %collective-permute-start.4 = (bf16[3,128,578]{2,1,0:T(8,128)(2,1)S(1)}, bf16[3,128,578]{2,1,0:T(8,128)(2,1)S(1)}, u32[]{:S(2)}, u32[]{:S(2)}) collective-permute-start(bf16[3,128,578]{2,1,0:T(8,128)(2,1)S(1)} %get-tuple-element.47), channel_id=1, source_target_pairs={{0,192},{32,224},{64,256},{96,288},{128,320},{160,352},{192,384},{... | collective-permute-start | bytes 1331720 | tf_op jit(solution)/shard_map/ppermute | solution.py:52
  38.8 22.6 %collective-permute-start.3 = (bf16[3,128,578]{2,1,0:T(8,128)(2,1)S(1)}, bf16[3,128,578]{2,1,0:T(8,128)(2,1)S(1)}, u32[]{:S(2)}, u32[]{:S(2)}) collective-permute-start(bf16[3,128,578]{2,1,0:T(8,128)(2,1)S(1)} %get-tuple-element.47), channel_id=1, source_target_pairs={{0,384},{32,416},{64,448},{96,480},{128,512},{160,544},{192,576},{... | collective-permute-start | bytes 1331720 | tf_op jit(solution)/shard_map/ppermute | solution.py:52
  43.4 19.5 %collective-permute-start.2 = (bf16[3,128,578]{2,1,0:T(8,128)(2,1)S(1)}, bf16[3,128,578]{2,1,0:T(8,128)(2,1)S(1)}, u32[]{:S(2)}, u32[]{:S(2)}) collective-permute-start(bf16[3,128,578]{2,1,0:T(8,128)(2,1)S(1)} %get-tuple-element.47), channel_id=1, source_target_pairs={{0,576},{32,608},{64,640},{96,672},{128,704},{160,736},{192,0},{22... | collective-permute-start | bytes 1331720 | tf_op jit(solution)/shard_map/ppermute | solution.py:52
  65.3 7.5 %copy-start.14 = (bf16[128,256]{1,0:T(8,128)(2,1)S(1)}, bf16[128,256]{1,0:T(8,128)(2,1)}, u32[]{:S(2)}) copy-start(bf16[128,256]{1,0:T(8,128)(2,1)} %param.9) | copy-start | bytes 196612
  70.0 5.9 %collective-permute-start.5 = (bf16[4,3,128,578]{2,0,3,1:T(4,128)(2,1)}, bf16[4,3,128,578]{2,0,3,1:T(4,128)(2,1)}, u32[]{:S(2)}, u32[]{:S(2)}) collective-permute-start(bf16[4,3,128,578]{2,0,3,1:T(4,128)(2,1)} %copy.99), channel_id=1, source_target_pairs={{0,32},{32,0},{64,96},{96,64},{128,160},{160,128},{192,224},{224,1... | collective-permute-start | bytes 5326856 | tf_op jit(solution)/shard_map/ppermute | solution.py:52
  102.0 7.9 %collective-permute-start.6 = (f32[2,2,4,3,128,128]{4,5,1,0,3,2:T(8,128)}, f32[2,2,4,3,128,128]{4,5,1,0,3,2:T(8,128)}, u32[]{:S(2)}, u32[]{:S(2)}) collective-permute-start(f32[2,2,4,3,128,128]{4,5,1,0,3,2:T(8,128)} %bitcast.161), channel_id=1, source_target_pairs={{0,32},{32,0},{64,96},{96,64},{128,160},{160,128},{192,224},{224,1... | collective-permute-start | bytes 9437192 | tf_op jit(solution)/shard_map/ppermute | solution.py:52
  113.5 21.7 %collective-permute-start.9 = (bf16[2,2,3,128,128]{3,4,1,0,2:T(8,128)(2,1)S(1)}, bf16[2,2,3,128,128]{3,4,1,0,2:T(8,128)(2,1)S(1)}, u32[]{:S(2)}, u32[]{:S(2)}) collective-permute-start(bf16[2,2,3,128,128]{3,4,1,0,2:T(8,128)(2,1)S(1)} %get-tuple-element.42), channel_id=1, source_target_pairs={{0,576},{32,608},{64,640},{96,672},{128,704},{160,736},{192,0},{22... | collective-permute-start | bytes 1179656 | tf_op jit(solution)/shard_map/ppermute | solution.py:52
  118.0 17.1 %collective-permute-start.8 = (bf16[2,2,3,128,128]{3,4,1,0,2:T(8,128)(2,1)S(1)}, bf16[2,2,3,128,128]{3,4,1,0,2:T(8,128)(2,1)S(1)}, u32[]{:S(2)}, u32[]{:S(2)}) collective-permute-start(bf16[2,2,3,128,128]{3,4,1,0,2:T(8,128)(2,1)S(1)} %get-tuple-element.43), channel_id=1, source_target_pairs={{0,384},{32,416},{64,448},{96,480},{128,512},{160,544},{192,576},{... | collective-permute-start | bytes 1179656 | tf_op jit(solution)/shard_map/ppermute | solution.py:52
  121.7 19.0 %collective-permute-start.7 = (bf16[2,2,3,128,128]{3,4,1,0,2:T(8,128)(2,1)S(1)}, bf16[2,2,3,128,128]{3,4,1,0,2:T(8,128)(2,1)S(1)}, u32[]{:S(2)}, u32[]{:S(2)}) collective-permute-start(bf16[2,2,3,128,128]{3,4,1,0,2:T(8,128)(2,1)S(1)} %get-tuple-element.41), channel_id=1, source_target_pairs={{0,192},{32,224},{64,256},{96,288},{128,320},{160,352},{192,384},{... | collective-permute-start | bytes 1179656 | tf_op jit(solution)/shard_map/ppermute | solution.py:52
  141.0 12.2 %collective-permute-start.11 = (bf16[2,2,128,128]{2,3,1,0:T(8,128)(2,1)S(1)}, bf16[2,2,128,128]{2,3,1,0:T(8,128)(2,1)S(1)}, u32[]{:S(2)}, u32[]{:S(2)}) collective-permute-start(bf16[2,2,128,128]{2,3,1,0:T(8,128)(2,1)S(1)} %get-tuple-element.51), channel_id=1, source_target_pairs={{0,128},{32,160},{64,0},{96,32},{128,64},{160,96},{192,320},{224,3... | collective-permute-start | bytes 393224 | tf_op jit(solution)/shard_map/ppermute | solution.py:52
  148.0 13.1 %collective-permute-start.10 = (bf16[2,2,128,128]{2,3,1,0:T(8,128)(2,1)S(1)}, bf16[2,2,128,128]{2,3,1,0:T(8,128)(2,1)S(1)}, u32[]{:S(2)}, u32[]{:S(2)}) collective-permute-start(bf16[2,2,128,128]{2,3,1,0:T(8,128)(2,1)S(1)} %get-tuple-element.50), channel_id=1, source_target_pairs={{0,64},{32,96},{64,128},{96,160},{128,0},{160,32},{192,256},{224,2... | collective-permute-start | bytes 393224 | tf_op jit(solution)/shard_map/ppermute | solution.py:52
  161.2 14.5 %collective-permute-start.20 = (bf16[128,512]{0,1:T(8,128)(2,1)S(1)}, bf16[128,512]{0,1:T(8,128)(2,1)S(1)}, u32[]{:S(2)}, u32[]{:S(2)}) collective-permute-start(bf16[128,512]{0,1:T(8,128)(2,1)S(1)} %bitcast.165), channel_id=1, source_target_pairs={{0,64},{32,96},{64,128},{96,160},{128,0},{160,32},{192,256},{224,2... | collective-permute-start | bytes 393224 | tf_op jit(solution)/shard_map/ppermute | solution.py:52
  165.3 13.5 %collective-permute-start.19 = (bf16[128,512]{0,1:T(8,128)(2,1)S(1)}, bf16[128,512]{0,1:T(8,128)(2,1)S(1)}, u32[]{:S(2)}, u32[]{:S(2)}) collective-permute-start(bf16[128,512]{0,1:T(8,128)(2,1)S(1)} %bitcast.166), channel_id=1, source_target_pairs={{0,128},{32,160},{64,0},{96,32},{128,64},{160,96},{192,320},{224,3... | collective-permute-start | bytes 393224 | tf_op jit(solution)/shard_map/ppermute | solution.py:52
  179.7 18.4 %collective-permute-start.23 = (bf16[3,128,512]{1,2,0:T(8,128)(2,1)}, bf16[3,128,512]{1,2,0:T(8,128)(2,1)}, u32[]{:S(2)}, u32[]{:S(2)}) collective-permute-start(bf16[3,128,512]{1,2,0:T(8,128)(2,1)} %get-tuple-element.49), channel_id=1, source_target_pairs={{0,192},{32,224},{64,256},{96,288},{128,320},{160,352},{192,384},{... | collective-permute-start | bytes 1179656 | tf_op jit(solution)/shard_map/ppermute | solution.py:52
  183.5 14.6 %collective-permute-start.22 = (bf16[3,128,512]{1,2,0:T(8,128)(2,1)}, bf16[3,128,512]{1,2,0:T(8,128)(2,1)}, u32[]{:S(2)}, u32[]{:S(2)}) collective-permute-start(bf16[3,128,512]{1,2,0:T(8,128)(2,1)} %get-tuple-element.49), channel_id=1, source_target_pairs={{0,384},{32,416},{64,448},{96,480},{128,512},{160,544},{192,576},{... | collective-permute-start | bytes 1179656 | tf_op jit(solution)/shard_map/ppermute | solution.py:52
  187.1 13.6 %collective-permute-start.21 = (bf16[3,128,512]{1,2,0:T(8,128)(2,1)}, bf16[3,128,512]{1,2,0:T(8,128)(2,1)}, u32[]{:S(2)}, u32[]{:S(2)}) collective-permute-start(bf16[3,128,512]{1,2,0:T(8,128)(2,1)} %get-tuple-element.49), channel_id=1, source_target_pairs={{0,576},{32,608},{64,640},{96,672},{128,704},{160,736},{192,0},{22... | collective-permute-start | bytes 1179656 | tf_op jit(solution)/shard_map/ppermute | solution.py:52
  190.5 10.2 %copy-start.6 = (bf16[1,3,128,512]{2,3,1,0:T(8,128)(2,1)S(1)}, bf16[1,3,128,512]{2,3,1,0:T(8,128)(2,1)}, u32[]{:S(2)}) copy-start(bf16[1,3,128,512]{2,3,1,0:T(8,128)(2,1)} %get-tuple-element.48) | copy-start | bytes 1179652
  194.3 11.5 %copy-start.11 = (bf16[512,256]{1,0:T(8,128)(2,1)S(1)}, bf16[512,256]{1,0:T(8,128)(2,1)}, u32[]{:S(2)}) copy-start(bf16[512,256]{1,0:T(8,128)(2,1)} %param.17) | copy-start | bytes 786436
  203.9 84.5 %collective-permute-start.24 = (bf16[4,3,128,512]{2,3,1,0:T(8,128)(2,1)}, bf16[4,3,128,512]{2,3,1,0:T(8,128)(2,1)}, u32[]{:S(2)}, u32[]{:S(2)}) collective-permute-start(bf16[4,3,128,512]{2,3,1,0:T(8,128)(2,1)} %get-tuple-element.40), channel_id=1, source_target_pairs={{0,32},{32,0},{64,96},{96,64},{128,160},{160,128},{192,224},{224,1... | collective-permute-start | bytes 4718600 | tf_op jit(solution)/shard_map/ppermute | solution.py:52
  206.1 10.7 %collective-permute-start.12 = (f32[128,512]{1,0:T(8,128)S(1)}, f32[128,512]{1,0:T(8,128)}, u32[]{:S(2)}, u32[]{:S(2)}) collective-permute-start(f32[128,512]{1,0:T(8,128)S(1)} %convolution_add_fusion), channel_id=1, source_target_pairs={{0,1},{1,0},{2,3},{3,2},{4,5},{5,4},{6,7},{7,6},{8,9},{9,8},{10,11... | collective-permute-start | bytes 786440 | tf_op jit(solution)/shard_map/ppermute | solution.py:52
  217.9 23.4 %collective-permute-start.13 = (f32[128,512]{1,0:T(8,128)S(1)}, f32[128,512]{1,0:T(8,128)S(1)}, u32[]{:S(2)}, u32[]{:S(2)}) collective-permute-start(f32[128,512]{1,0:T(8,128)S(1)} %add.280), channel_id=1, source_target_pairs={{0,6},{1,7},{2,0},{3,1},{4,2},{5,3},{6,4},{7,5},{8,14},{9,15},{10,... | collective-permute-start | bytes 786440 | tf_op jit(solution)/shard_map/ppermute | solution.py:52
  221.9 19.4 %collective-permute-start.14 = (f32[128,512]{1,0:T(8,128)S(1)}, f32[128,512]{1,0:T(8,128)S(1)}, u32[]{:S(2)}, u32[]{:S(2)}) collective-permute-start(f32[128,512]{1,0:T(8,128)S(1)} %add.280), channel_id=1, source_target_pairs={{0,4},{1,5},{2,6},{3,7},{4,0},{5,1},{6,2},{7,3},{8,12},{9,13},{10,... | collective-permute-start | bytes 786440 | tf_op jit(solution)/shard_map/ppermute | solution.py:52
  224.8 26.7 %collective-permute-start.15 = (f32[128,512]{1,0:T(8,128)S(1)}, f32[128,512]{1,0:T(8,128)S(1)}, u32[]{:S(2)}, u32[]{:S(2)}) collective-permute-start(f32[128,512]{1,0:T(8,128)S(1)} %add.280), channel_id=1, source_target_pairs={{0,2},{1,3},{2,4},{3,5},{4,6},{5,7},{6,0},{7,1},{8,10},{9,11},{10,... | collective-permute-start | bytes 786440 | tf_op jit(solution)/shard_map/ppermute | solution.py:52
  251.7 20.6 %collective-permute-start.16 = (f32[128,512]{1,0:T(8,128)S(1)}, f32[128,512]{1,0:T(8,128)S(1)}, u32[]{:S(2)}, u32[]{:S(2)}) collective-permute-start(f32[128,512]{1,0:T(8,128)S(1)} %select_add_fusion.3), channel_id=1, source_target_pairs={{0,24},{1,25},{2,26},{3,27},{4,28},{5,29},{6,30},{7,31},{8,0},{9,1... | collective-permute-start | bytes 786440 | tf_op jit(solution)/shard_map/ppermute | solution.py:52
  265.6 22.0 %collective-permute-start.17 = (f32[128,512]{1,0:T(8,128)S(1)}, f32[128,512]{1,0:T(8,128)S(1)}, u32[]{:S(2)}, u32[]{:S(2)}) collective-permute-start(f32[128,512]{1,0:T(8,128)S(1)} %select_add_fusion.3), channel_id=1, source_target_pairs={{0,16},{1,17},{2,18},{3,19},{4,20},{5,21},{6,22},{7,23},{8,24},{9,... | collective-permute-start | bytes 786440 | tf_op jit(solution)/shard_map/ppermute | solution.py:52
  267.5 20.1 %collective-permute-start.18 = (f32[128,512]{1,0:T(8,128)S(1)}, f32[128,512]{1,0:T(8,128)S(1)}, u32[]{:S(2)}, u32[]{:S(2)}) collective-permute-start(f32[128,512]{1,0:T(8,128)S(1)} %select_add_fusion.3), channel_id=1, source_target_pairs={{0,8},{1,9},{2,10},{3,11},{4,12},{5,13},{6,14},{7,15},{8,16},{9,17... | collective-permute-start | bytes 786440 | tf_op jit(solution)/shard_map/ppermute | solution.py:52
  270.0 17.6 %copy-start.5 = (f32[128,4,128]{2,1,0:T(4,128)S(1)}, f32[128,4,128]{2,1,0:T(4,128)}, u32[]{:S(2)}) copy-start(f32[128,4,128]{2,1,0:T(4,128)} %copy-done.4) | copy-start | bytes 786436
  270.0 18.4 %copy-start.3 = (bf16[1,4,3,128,512]{3,4,2,1,0:T(8,128)(2,1)S(1)}, bf16[1,4,3,128,512]{3,4,2,1,0:T(8,128)(2,1)}, u32[]{:S(2)}) copy-start(bf16[1,4,3,128,512]{3,4,2,1,0:T(8,128)(2,1)} %get-tuple-element.39) | copy-start | bytes 4718596
  (10 other events, 32.0 us)

commit v4 on v3

--- a/solution.py
+++ b/solution.py
@@ -68,12 +68,16 @@
     return pieces
 
 
+def gather_step(buf, axis, radix, stride):
+    received = [shift_digit(buf, axis, radix, stride, by) for by in range(1, radix)]
+    pieces = [buf] + [received[radix - k - 1] for k in range(1, radix)]
+    return jnp.stack(pieces, axis=0)
+
+
 def gather_relative(block, axis):
     buf = block
     for radix, stride in gather_order(lax.axis_size(axis)):
-        received = [shift_digit(buf, axis, radix, stride, by) for by in range(1, radix)]
-        pieces = [buf] + [received[radix - k - 1] for k in range(1, radix)]
-        buf = jnp.stack(pieces, axis=0)
+        buf = gather_step(buf, axis, radix, stride)
     return buf
 
 
@@ -102,17 +106,14 @@
     return total
 
 
-def total_over(x, axis):
-    size = lax.axis_size(axis)
-    for radix, stride in digits_of(size):
-        if radix == 2:
-            x = x + shift_digit(x, axis, radix, stride, 1)
-        else:
-            pieces = ordered_pieces(x, axis, radix, stride)
-            x = pieces[0]
-            for piece in pieces[1:]:
-                x = x + piece
-    return x
+def reduce_step(x, axis, radix, stride):
+    if radix == 2:
+        return x + shift_digit(x, axis, radix, stride, 1)
+    pieces = ordered_pieces(x, axis, radix, stride)
+    total = pieces[0]
+    for piece in pieces[1:]:
+        total = total + piece
+    return total
 
 
 def body(q_nope, q_rope, d_out, latent, scale_exp, positions, spans, w_uk, w_uv):
@@ -189,10 +190,18 @@
         )
 
     latent_part = back_project(key_flat, w_uk) + back_project(value_flat, w_uv)
-    latent_sum = total_over(latent_part, "heads")
+    sum_levels = digits_of(lax.axis_size("heads"))
+    gather_levels = gather_order(block_count)
+    latent_sum = latent_part
+    flats = flat
+    for level in range(max(len(sum_levels), len(gather_levels))):
+        if level < len(gather_levels):
+            flats = gather_step(flats, "blk", *gather_levels[level])
+        if level < len(sum_levels):
+            latent_sum = reduce_step(latent_sum, "heads", *sum_levels[level])
+        flats, latent_sum = lax.optimization_barrier((flats, latent_sum))
     grad_latent = (latent_sum * factor).astype(jnp.bfloat16)
 
-    flats = gather_relative(flat, "blk")
     order = gather_order(block_count)
     first_radix, first_stride = order[0]
     lead = radices[:-1]

time: 301 us -> 282 us (0.937)
  waiting for transfers between devices: 116 us -> 91.9 us
    ppermute x25, waiting for transfers between devices: 116 us -> 91.9 us  [shift_digit(): return lax.ppermute(x, axis, pairs)]
    unnamed x43 -> x39, local copies, waits for them, and re-layouts: 10.1 us -> 10.8 us
  transfers between devices with their start and end apart: 25 -> 25, of which waited for: 19 -> 17; matrix products, arithmetic and copies ran while one was open for 6% -> 7% of each run, Pallas kernels for 0% -> 0%
where the time goes in v4:
time: 282 us; the launch traced here: 279 us
  starting transfers between devices  107 us (38%)
  waiting for transfers between devices  91.9 us (33%)
  local copies, waits for them, and re-layouts  34.6 us (12%)
  other arithmetic  31.1 us (11%)
  matrix products  12 us (4%)
    ppermute x25, starting transfers between devices, shift_digit(): return lax.ppermute(x, axis, pairs)  107 us
    ppermute x25, waiting for transfers between devices, shift_digit(): return lax.ppermute(x, axis, pairs)  91.9 us
    another operation x7, other arithmetic, gather_step(): return jnp.stack(pieces, axis=0)  11 us
    unnamed x39, local copies, waits for them, and re-layouts  10.8 us
  transfers between devices with their start and end apart: 25, of which 17 were waited for; matrix products, arithmetic and copies ran while one was open for 7% of the time, Pallas kernels for 0%

profile of v4, /device:TPU:56, one launch (start us, length us, event | category | flops | bytes accessed | tf_op | source)
XLA Modules:
  0.0 278.5 jit_solution(2712659042314094689)
XLA Ops:
  4.7 10.9 %collective-permute-start.1 = (bf16[128,578]{1,0:T(8,128)(2,1)S(1)}, bf16[128,578]{1,0:T(8,128)(2,1)S(1)}, u32[]{:S(2)}, u32[]{:S(2)}) collective-permute-start(bf16[128,578]{1,0:T(8,128)(2,1)S(1)} %pad_maximum_fusion.6), channel_id=1, source_target_pairs={{0,64},{32,96},{64,128},{96,160},{128,0},{160,32},{192,256},{224,2... | collective-permute-start | bytes 443912 | tf_op jit(solution)/shard_map/ppermute | solution.py:52
  15.6 5.6 %collective-permute-start = (bf16[128,578]{1,0:T(8,128)(2,1)S(1)}, bf16[128,578]{1,0:T(8,128)(2,1)S(1)}, u32[]{:S(2)}, u32[]{:S(2)}) collective-permute-start(bf16[128,578]{1,0:T(8,128)(2,1)S(1)} %pad_maximum_fusion.6), channel_id=1, source_target_pairs={{0,128},{32,160},{64,0},{96,32},{128,64},{160,96},{192,320},{224,3... | collective-permute-start | bytes 443912 | tf_op jit(solution)/shard_map/ppermute | solution.py:52
  23.7 11.5 %collective-permute-done = bf16[128,578]{1,0:T(8,128)(2,1)S(1)} collective-permute-done((bf16[128,578]{1,0:T(8,128)(2,1)S(1)}, bf16[128,578]{1,0:T(8,128)(2,1)S(1)}, u32[]{:S(2)}, u32[]{:S(2)}) %collective-permute-start) | collective-permute-done | bytes 148000 | tf_op jit(solution)/shard_map/ppermute | solution.py:52
  35.3 3.4 %collective-permute-start.4 = (bf16[3,128,578]{2,1,0:T(8,128)(2,1)S(1)}, bf16[3,128,578]{2,1,0:T(8,128)(2,1)S(1)}, u32[]{:S(2)}, u32[]{:S(2)}) collective-permute-start(bf16[3,128,578]{2,1,0:T(8,128)(2,1)S(1)} %get-tuple-element.57), channel_id=1, source_target_pairs={{0,192},{32,224},{64,256},{96,288},{128,320},{160,352},{192,384},{... | collective-permute-start | bytes 1331720 | tf_op jit(solution)/shard_map/ppermute | solution.py:52
  38.8 4.6 %collective-permute-start.3 = (bf16[3,128,578]{2,1,0:T(8,128)(2,1)S(1)}, bf16[3,128,578]{2,1,0:T(8,128)(2,1)S(1)}, u32[]{:S(2)}, u32[]{:S(2)}) collective-permute-start(bf16[3,128,578]{2,1,0:T(8,128)(2,1)S(1)} %get-tuple-element.57), channel_id=1, source_target_pairs={{0,384},{32,416},{64,448},{96,480},{128,512},{160,544},{192,576},{... | collective-permute-start | bytes 1331720 | tf_op jit(solution)/shard_map/ppermute | solution.py:52
  43.4 3.3 %collective-permute-start.2 = (bf16[3,128,578]{2,1,0:T(8,128)(2,1)S(1)}, bf16[3,128,578]{2,1,0:T(8,128)(2,1)S(1)}, u32[]{:S(2)}, u32[]{:S(2)}) collective-permute-start(bf16[3,128,578]{2,1,0:T(8,128)(2,1)S(1)} %get-tuple-element.57), channel_id=1, source_target_pairs={{0,576},{32,608},{64,640},{96,672},{128,704},{160,736},{192,0},{22... | collective-permute-start | bytes 1331720 | tf_op jit(solution)/shard_map/ppermute | solution.py:52
  46.7 4.9 %collective-permute-done.4 = bf16[3,128,578]{2,1,0:T(8,128)(2,1)S(1)} collective-permute-done((bf16[3,128,578]{2,1,0:T(8,128)(2,1)S(1)}, bf16[3,128,578]{2,1,0:T(8,128)(2,1)S(1)}, u32[]{:S(2)}, u32[]{:S(2)}) %collective-permute-start.4) | collective-permute-done | bytes 443936 | tf_op jit(solution)/shard_map/ppermute | solution.py:52
  51.6 9.7 %collective-permute-done.3 = bf16[3,128,578]{2,1,0:T(8,128)(2,1)S(1)} collective-permute-done((bf16[3,128,578]{2,1,0:T(8,128)(2,1)S(1)}, bf16[3,128,578]{2,1,0:T(8,128)(2,1)S(1)}, u32[]{:S(2)}, u32[]{:S(2)}) %collective-permute-start.3) | collective-permute-done | bytes 443936 | tf_op jit(solution)/shard_map/ppermute | solution.py:52
  65.3 4.8 %copy.99 = bf16[4,3,128,578]{2,0,3,1:T(4,128)(2,1)} copy(bf16[4,3,128,578]{3,2,1,0:T(8,128)(2,1)} %get-tuple-element.50) | data formatting | bytes 3551232 | tf_op jit(solution)/shard_map/stack | solution.py:74
  76.0 4.7 %copy.100 = bf16[4,3,128,578]{3,2,1,0:T(8,128)(2,1)} copy(bf16[4,3,128,578]{2,0,3,1:T(4,128)(2,1)} %collective-permute-done.5) | data formatting | bytes 3551232 | tf_op jit(solution)/shard_map/ppermute | solution.py:52
  95.2 3.2 %fusion.42 = (f32[2,2,1,4,3,128,128]{6,5,4,3,2,1,0:T(8,128)}, f32[2,2,1,4,3,128,128]{6,5,4,3,2,1,0:T(8,128)}) fusion(f32[2,2,2,4,3,128,128]{6,5,4,3,2,1,0:T(8,128)S(1)} %bitcast.147), kind=kLoop, calls=%fused_computation.90 | loop fusion | bytes 12582912 | tf_op jit(solution)/shard_map/slice | solution.py:88
  98.4 3.6 %copy.133 = f32[2,2,1,4,3,128,128]{5,6,1,0,4,3,2:T(8,128)} copy(f32[2,2,1,4,3,128,128]{6,5,4,3,2,1,0:T(8,128)} %get-tuple-element.42) | data formatting | bytes 6291456
  104.1 3.5 %copy.132 = f32[2,2,1,4,3,128,128]{5,6,1,0,4,3,2:T(8,128)} copy(f32[2,2,1,4,3,128,128]{6,5,4,3,2,1,0:T(8,128)} %get-tuple-element.41) | data formatting | bytes 6291456
  109.9 3.5 %fusion.41 = (bf16[2,2,4,3,128,128]{4,5,1,0,3,2:T(8,128)(2,1)S(1)}, f32[2,2,4,3,128,128]{4,5,1,0,3,2:T(8,128)S(1)}) fusion(f32[2,2,4,3,128,128]{4,5,1,0,3,2:T(8,128)} %collective-permute-done.6, f32[2,2,1,4,3,128,128]{5,6,1,0,4,3,2:T(8,128)} %copy.132), kind=kLoop, calls=%fused_computation.89 | loop fusion | flops 1572864 | bytes 11010048 | tf_op jit(solution)/shard_map/convert.4
  113.5 4.5 %collective-permute-start.9 = (bf16[2,2,3,128,128]{3,4,1,0,2:T(8,128)(2,1)S(1)}, bf16[2,2,3,128,128]{3,4,1,0,2:T(8,128)(2,1)S(1)}, u32[]{:S(2)}, u32[]{:S(2)}) collective-permute-start(bf16[2,2,3,128,128]{3,4,1,0,2:T(8,128)(2,1)S(1)} %get-tuple-element.52), channel_id=1, source_target_pairs={{0,576},{32,608},{64,640},{96,672},{128,704},{160,736},{192,0},{22... | collective-permute-start | bytes 1179656 | tf_op jit(solution)/shard_map/ppermute | solution.py:52
  118.1 3.7 %collective-permute-start.8 = (bf16[2,2,3,128,128]{3,4,1,0,2:T(8,128)(2,1)S(1)}, bf16[2,2,3,128,128]{3,4,1,0,2:T(8,128)(2,1)S(1)}, u32[]{:S(2)}, u32[]{:S(2)}) collective-permute-start(bf16[2,2,3,128,128]{3,4,1,0,2:T(8,128)(2,1)S(1)} %get-tuple-element.53), channel_id=1, source_target_pairs={{0,384},{32,416},{64,448},{96,480},{128,512},{160,544},{192,576},{... | collective-permute-start | bytes 1179656 | tf_op jit(solution)/shard_map/ppermute | solution.py:52
  123.7 11.5 %collective-permute-done.9 = bf16[2,2,3,128,128]{3,4,1,0,2:T(8,128)(2,1)S(1)} collective-permute-done((bf16[2,2,3,128,128]{3,4,1,0,2:T(8,128)(2,1)S(1)}, bf16[2,2,3,128,128]{3,4,1,0,2:T(8,128)(2,1)S(1)}, u32[]{:S(2)}, u32[]{:S(2)}) %collective-permute-start.9) | collective-permute-done | bytes 393248 | tf_op jit(solution)/shard_map/ppermute | solution.py:52
  135.2 5.6 %collective-permute-done.7 = bf16[2,2,3,128,128]{3,4,1,0,2:T(8,128)(2,1)S(1)} collective-permute-done((bf16[2,2,3,128,128]{3,4,1,0,2:T(8,128)(2,1)S(1)}, bf16[2,2,3,128,128]{3,4,1,0,2:T(8,128)(2,1)S(1)}, u32[]{:S(2)}, u32[]{:S(2)}) %collective-permute-start.7) | collective-permute-done | bytes 393248 | tf_op jit(solution)/shard_map/ppermute | solution.py:52
  141.0 7.1 %collective-permute-start.11 = (bf16[2,2,128,128]{2,3,1,0:T(8,128)(2,1)S(1)}, bf16[2,2,128,128]{2,3,1,0:T(8,128)(2,1)S(1)}, u32[]{:S(2)}, u32[]{:S(2)}) collective-permute-start(bf16[2,2,128,128]{2,3,1,0:T(8,128)(2,1)S(1)} %get-tuple-element.59), channel_id=1, source_target_pairs={{0,128},{32,160},{64,0},{96,32},{128,64},{160,96},{192,320},{224,3... | collective-permute-start | bytes 393224 | tf_op jit(solution)/shard_map/ppermute | solution.py:52
  153.3 7.8 %collective-permute-done.10 = bf16[2,2,128,128]{2,3,1,0:T(8,128)(2,1)S(1)} collective-permute-done((bf16[2,2,128,128]{2,3,1,0:T(8,128)(2,1)S(1)}, bf16[2,2,128,128]{2,3,1,0:T(8,128)(2,1)S(1)}, u32[]{:S(2)}, u32[]{:S(2)}) %collective-permute-start.10) | collective-permute-done | bytes 131104 | tf_op jit(solution)/shard_map/ppermute | solution.py:52
  161.6 3.3 %collective-permute-start.14 = (f32[128,512]{1,0:T(8,128)S(1)}, f32[128,512]{1,0:T(8,128)S(1)}, u32[]{:S(2)}, u32[]{:S(2)}) collective-permute-start(f32[128,512]{1,0:T(8,128)S(1)} %convolution_add_fusion), channel_id=1, source_target_pairs={{0,1},{1,0},{2,3},{3,2},{4,5},{5,4},{6,7},{7,6},{8,9},{9,8},{10,11... | collective-permute-start | bytes 786440 | tf_op jit(solution)/shard_map/ppermute | solution.py:52
  164.8 4.2 %collective-permute-start.13 = (bf16[128,512]{0,1:T(8,128)(2,1)S(1)}, bf16[128,512]{0,1:T(8,128)(2,1)S(1)}, u32[]{:S(2)}, u32[]{:S(2)}) collective-permute-start(bf16[128,512]{0,1:T(8,128)(2,1)S(1)} %bitcast.165), channel_id=1, source_target_pairs={{0,64},{32,96},{64,128},{96,160},{128,0},{160,32},{192,256},{224,2... | collective-permute-start | bytes 393224 | tf_op jit(solution)/shard_map/ppermute | solution.py:52
  169.1 5.5 %collective-permute-start.12 = (bf16[128,512]{0,1:T(8,128)(2,1)S(1)}, bf16[128,512]{0,1:T(8,128)(2,1)S(1)}, u32[]{:S(2)}, u32[]{:S(2)}) collective-permute-start(bf16[128,512]{0,1:T(8,128)(2,1)S(1)} %bitcast.166), channel_id=1, source_target_pairs={{0,128},{32,160},{64,0},{96,32},{128,64},{160,96},{192,320},{224,3... | collective-permute-start | bytes 393224 | tf_op jit(solution)/shard_map/ppermute | solution.py:52
  177.3 5.0 %collective-permute-done.12 = bf16[128,512]{0,1:T(8,128)(2,1)S(1)} collective-permute-done((bf16[128,512]{0,1:T(8,128)(2,1)S(1)}, bf16[128,512]{0,1:T(8,128)(2,1)S(1)}, u32[]{:S(2)}, u32[]{:S(2)}) %collective-permute-start.12) | collective-permute-done | bytes 131104 | tf_op jit(solution)/shard_map/ppermute | solution.py:52
  183.1 4.0 %collective-permute-start.18 = (f32[128,512]{1,0:T(8,128)S(1)}, f32[128,512]{1,0:T(8,128)S(1)}, u32[]{:S(2)}, u32[]{:S(2)}) collective-permute-start(f32[128,512]{1,0:T(8,128)S(1)} %add.276), channel_id=1, source_target_pairs={{0,6},{1,7},{2,0},{3,1},{4,2},{5,3},{6,4},{7,5},{8,14},{9,15},{10,... | collective-permute-start | bytes 786440 | tf_op jit(solution)/shard_map/ppermute | solution.py:52
  189.2 5.7 %collective-permute-start.20 = (f32[128,512]{1,0:T(8,128)S(1)}, f32[128,512]{1,0:T(8,128)}, u32[]{:S(2)}, u32[]{:S(2)}) collective-permute-start(f32[128,512]{1,0:T(8,128)S(1)} %add.276), channel_id=1, source_target_pairs={{0,2},{1,3},{2,4},{3,5},{4,6},{5,7},{6,0},{7,1},{8,10},{9,11},{10,... | collective-permute-start | bytes 786440 | tf_op jit(solution)/shard_map/ppermute | solution.py:52
  194.9 4.0 %collective-permute-start.17 = (bf16[3,128,512]{1,2,0:T(8,128)(2,1)}, bf16[3,128,512]{1,2,0:T(8,128)(2,1)}, u32[]{:S(2)}, u32[]{:S(2)}) collective-permute-start(bf16[3,128,512]{1,2,0:T(8,128)(2,1)} %pad_maximum_fusion.5), channel_id=1, source_target_pairs={{0,192},{32,224},{64,256},{96,288},{128,320},{160,352},{192,384},{... | collective-permute-start | bytes 1179656 | tf_op jit(solution)/shard_map/ppermute | solution.py:52
  198.9 3.6 %collective-permute-start.16 = (bf16[3,128,512]{1,2,0:T(8,128)(2,1)}, bf16[3,128,512]{1,2,0:T(8,128)(2,1)}, u32[]{:S(2)}, u32[]{:S(2)}) collective-permute-start(bf16[3,128,512]{1,2,0:T(8,128)(2,1)} %pad_maximum_fusion.5), channel_id=1, source_target_pairs={{0,384},{32,416},{64,448},{96,480},{128,512},{160,544},{192,576},{... | collective-permute-start | bytes 1179656 | tf_op jit(solution)/shard_map/ppermute | solution.py:52
  206.3 5.6 %collective-permute-done.20 = f32[128,512]{1,0:T(8,128)} collective-permute-done((f32[128,512]{1,0:T(8,128)S(1)}, f32[128,512]{1,0:T(8,128)}, u32[]{:S(2)}, u32[]{:S(2)}) %collective-permute-start.20) | collective-permute-done | bytes 262176 | tf_op jit(solution)/shard_map/ppermute | solution.py:52
  220.1 3.8 %slice.183 = bf16[3072,512]{1,0:T(8,128)(2,1)} slice(bf16[3072,578]{1,0:T(8,128)(2,1)} %bitcast.145), slice={[0:3072], [0:512]} | slice | bytes 6291456 | tf_op jit(solution)/shard_map/slice | solution.py:136
  227.5 13.9 %collective-permute-start.22 = (f32[128,512]{1,0:T(8,128)}, f32[128,512]{1,0:T(8,128)S(1)}, u32[]{:S(2)}, u32[]{:S(2)}) collective-permute-start(f32[128,512]{1,0:T(8,128)} %select_add_fusion.4), channel_id=1, source_target_pairs={{0,24},{1,25},{2,26},{3,27},{4,28},{5,29},{6,30},{7,31},{8,0},{9,1... | collective-permute-start | bytes 786440 | tf_op jit(solution)/shard_map/ppermute | solution.py:52
  248.3 15.7 %collective-permute-done.23 = f32[128,512]{1,0:T(8,128)S(1)} collective-permute-done((f32[128,512]{1,0:T(8,128)}, f32[128,512]{1,0:T(8,128)S(1)}, u32[]{:S(2)}, u32[]{:S(2)}) %collective-permute-start.23) | collective-permute-done | bytes 262176 | tf_op jit(solution)/shard_map/ppermute | solution.py:52
  (114 shorter events, 84.9 us)
Async XLA Ops:
  0.6 83.9 %copy-start = (bf16[512,256]{1,0:T(8,128)(2,1)S(1)}, bf16[512,256]{1,0:T(8,128)(2,1)}, u32[]{:S(2)}) copy-start(bf16[512,256]{1,0:T(8,128)(2,1)} %param.16) | copy-start | bytes 786436
  4.5 60.7 %copy-start.3 = (f32[128,4,128]{2,1,0:T(4,128)}, f32[128,4,128]{2,1,0:T(4,128)S(1)}, u32[]{:S(2)}) copy-start(f32[128,4,128]{2,1,0:T(4,128)S(1)} %broadcast_in_dim.42) | copy-start | bytes 786436
  4.7 19.0 %collective-permute-start.1 = (bf16[128,578]{1,0:T(8,128)(2,1)S(1)}, bf16[128,578]{1,0:T(8,128)(2,1)S(1)}, u32[]{:S(2)}, u32[]{:S(2)}) collective-permute-start(bf16[128,578]{1,0:T(8,128)(2,1)S(1)} %pad_maximum_fusion.6), channel_id=1, source_target_pairs={{0,64},{32,96},{64,128},{96,160},{128,0},{160,32},{192,256},{224,2... | collective-permute-start | bytes 443912 | tf_op jit(solution)/shard_map/ppermute | solution.py:52
  15.6 19.6 %collective-permute-start = (bf16[128,578]{1,0:T(8,128)(2,1)S(1)}, bf16[128,578]{1,0:T(8,128)(2,1)S(1)}, u32[]{:S(2)}, u32[]{:S(2)}) collective-permute-start(bf16[128,578]{1,0:T(8,128)(2,1)S(1)} %pad_maximum_fusion.6), channel_id=1, source_target_pairs={{0,128},{32,160},{64,0},{96,32},{128,64},{160,96},{192,320},{224,3... | collective-permute-start | bytes 443912 | tf_op jit(solution)/shard_map/ppermute | solution.py:52
  35.3 16.3 %collective-permute-start.4 = (bf16[3,128,578]{2,1,0:T(8,128)(2,1)S(1)}, bf16[3,128,578]{2,1,0:T(8,128)(2,1)S(1)}, u32[]{:S(2)}, u32[]{:S(2)}) collective-permute-start(bf16[3,128,578]{2,1,0:T(8,128)(2,1)S(1)} %get-tuple-element.57), channel_id=1, source_target_pairs={{0,192},{32,224},{64,256},{96,288},{128,320},{160,352},{192,384},{... | collective-permute-start | bytes 1331720 | tf_op jit(solution)/shard_map/ppermute | solution.py:52
  38.8 22.6 %collective-permute-start.3 = (bf16[3,128,578]{2,1,0:T(8,128)(2,1)S(1)}, bf16[3,128,578]{2,1,0:T(8,128)(2,1)S(1)}, u32[]{:S(2)}, u32[]{:S(2)}) collective-permute-start(bf16[3,128,578]{2,1,0:T(8,128)(2,1)S(1)} %get-tuple-element.57), channel_id=1, source_target_pairs={{0,384},{32,416},{64,448},{96,480},{128,512},{160,544},{192,576},{... | collective-permute-start | bytes 1331720 | tf_op jit(solution)/shard_map/ppermute | solution.py:52
  43.4 19.5 %collective-permute-start.2 = (bf16[3,128,578]{2,1,0:T(8,128)(2,1)S(1)}, bf16[3,128,578]{2,1,0:T(8,128)(2,1)S(1)}, u32[]{:S(2)}, u32[]{:S(2)}) collective-permute-start(bf16[3,128,578]{2,1,0:T(8,128)(2,1)S(1)} %get-tuple-element.57), channel_id=1, source_target_pairs={{0,576},{32,608},{64,640},{96,672},{128,704},{160,736},{192,0},{22... | collective-permute-start | bytes 1331720 | tf_op jit(solution)/shard_map/ppermute | solution.py:52
  65.3 6.7 %copy-start.11 = (bf16[128,256]{1,0:T(8,128)(2,1)S(1)}, bf16[128,256]{1,0:T(8,128)(2,1)}, u32[]{:S(2)}) copy-start(bf16[128,256]{1,0:T(8,128)(2,1)} %param.11) | copy-start | bytes 196612
  65.3 6.8 %copy-start.13 = (bf16[128,128]{1,0:T(8,128)(2,1)S(1)}, bf16[128,128]{1,0:T(8,128)(2,1)}, u32[]{:S(2)}) copy-start(bf16[128,128]{1,0:T(8,128)(2,1)} %param.10) | copy-start | bytes 98308
  65.3 7.5 %copy-start.12 = (bf16[128,256]{1,0:T(8,128)(2,1)S(1)}, bf16[128,256]{1,0:T(8,128)(2,1)}, u32[]{:S(2)}) copy-start(bf16[128,256]{1,0:T(8,128)(2,1)} %param.9) | copy-start | bytes 196612
  70.0 5.9 %collective-permute-start.5 = (bf16[4,3,128,578]{2,0,3,1:T(4,128)(2,1)}, bf16[4,3,128,578]{2,0,3,1:T(4,128)(2,1)}, u32[]{:S(2)}, u32[]{:S(2)}) collective-permute-start(bf16[4,3,128,578]{2,0,3,1:T(4,128)(2,1)} %copy.99), channel_id=1, source_target_pairs={{0,32},{32,0},{64,96},{96,64},{128,160},{160,128},{192,224},{224,1... | collective-permute-start | bytes 5326856 | tf_op jit(solution)/shard_map/ppermute | solution.py:52
  83.4 4.1 %copy-start.2 = (bf16[2,4,3,128,578]{4,3,2,1,0:T(8,128)(2,1)}, bf16[2,4,3,128,578]{4,3,2,1,0:T(8,128)(2,1)S(1)}, u32[]{:S(2)}) copy-start(bf16[2,4,3,128,578]{4,3,2,1,0:T(8,128)(2,1)S(1)} %pad_maximum_fusion) | copy-start | bytes 10653700
  102.0 7.9 %collective-permute-start.6 = (f32[2,2,4,3,128,128]{4,5,1,0,3,2:T(8,128)}, f32[2,2,4,3,128,128]{4,5,1,0,3,2:T(8,128)}, u32[]{:S(2)}, u32[]{:S(2)}) collective-permute-start(f32[2,2,4,3,128,128]{4,5,1,0,3,2:T(8,128)} %bitcast.159), channel_id=1, source_target_pairs={{0,32},{32,0},{64,96},{96,64},{128,160},{160,128},{192,224},{224,1... | collective-permute-start | bytes 9437192 | tf_op jit(solution)/shard_map/ppermute | solution.py:52
  113.4 47.9 %copy-start.9 = (bf16[512,256]{1,0:T(8,128)(2,1)S(1)}, bf16[512,256]{1,0:T(8,128)(2,1)}, u32[]{:S(2)}) copy-start(bf16[512,256]{1,0:T(8,128)(2,1)} %param.17) | copy-start | bytes 786436
  113.5 21.7 %collective-permute-start.9 = (bf16[2,2,3,128,128]{3,4,1,0,2:T(8,128)(2,1)S(1)}, bf16[2,2,3,128,128]{3,4,1,0,2:T(8,128)(2,1)S(1)}, u32[]{:S(2)}, u32[]{:S(2)}) collective-permute-start(bf16[2,2,3,128,128]{3,4,1,0,2:T(8,128)(2,1)S(1)} %get-tuple-element.52), channel_id=1, source_target_pairs={{0,576},{32,608},{64,640},{96,672},{128,704},{160,736},{192,0},{22... | collective-permute-start | bytes 1179656 | tf_op jit(solution)/shard_map/ppermute | solution.py:52
  118.1 17.1 %collective-permute-start.8 = (bf16[2,2,3,128,128]{3,4,1,0,2:T(8,128)(2,1)S(1)}, bf16[2,2,3,128,128]{3,4,1,0,2:T(8,128)(2,1)S(1)}, u32[]{:S(2)}, u32[]{:S(2)}) collective-permute-start(bf16[2,2,3,128,128]{3,4,1,0,2:T(8,128)(2,1)S(1)} %get-tuple-element.53), channel_id=1, source_target_pairs={{0,384},{32,416},{64,448},{96,480},{128,512},{160,544},{192,576},{... | collective-permute-start | bytes 1179656 | tf_op jit(solution)/shard_map/ppermute | solution.py:52
  121.8 19.0 %collective-permute-start.7 = (bf16[2,2,3,128,128]{3,4,1,0,2:T(8,128)(2,1)S(1)}, bf16[2,2,3,128,128]{3,4,1,0,2:T(8,128)(2,1)S(1)}, u32[]{:S(2)}, u32[]{:S(2)}) collective-permute-start(bf16[2,2,3,128,128]{3,4,1,0,2:T(8,128)(2,1)S(1)} %get-tuple-element.51), channel_id=1, source_target_pairs={{0,192},{32,224},{64,256},{96,288},{128,320},{160,352},{192,384},{... | collective-permute-start | bytes 1179656 | tf_op jit(solution)/shard_map/ppermute | solution.py:52
  141.0 12.3 %collective-permute-start.11 = (bf16[2,2,128,128]{2,3,1,0:T(8,128)(2,1)S(1)}, bf16[2,2,128,128]{2,3,1,0:T(8,128)(2,1)S(1)}, u32[]{:S(2)}, u32[]{:S(2)}) collective-permute-start(bf16[2,2,128,128]{2,3,1,0:T(8,128)(2,1)S(1)} %get-tuple-element.59), channel_id=1, source_target_pairs={{0,128},{32,160},{64,0},{96,32},{128,64},{160,96},{192,320},{224,3... | collective-permute-start | bytes 393224 | tf_op jit(solution)/shard_map/ppermute | solution.py:52
  148.1 13.0 %collective-permute-start.10 = (bf16[2,2,128,128]{2,3,1,0:T(8,128)(2,1)S(1)}, bf16[2,2,128,128]{2,3,1,0:T(8,128)(2,1)S(1)}, u32[]{:S(2)}, u32[]{:S(2)}) collective-permute-start(bf16[2,2,128,128]{2,3,1,0:T(8,128)(2,1)S(1)} %get-tuple-element.58), channel_id=1, source_target_pairs={{0,64},{32,96},{64,128},{96,160},{128,0},{160,32},{192,256},{224,2... | collective-permute-start | bytes 393224 | tf_op jit(solution)/shard_map/ppermute | solution.py:52
  161.6 21.5 %collective-permute-start.14 = (f32[128,512]{1,0:T(8,128)S(1)}, f32[128,512]{1,0:T(8,128)S(1)}, u32[]{:S(2)}, u32[]{:S(2)}) collective-permute-start(f32[128,512]{1,0:T(8,128)S(1)} %convolution_add_fusion), channel_id=1, source_target_pairs={{0,1},{1,0},{2,3},{3,2},{4,5},{5,4},{6,7},{7,6},{8,9},{9,8},{10,11... | collective-permute-start | bytes 786440 | tf_op jit(solution)/shard_map/ppermute | solution.py:52
  164.8 12.4 %collective-permute-start.13 = (bf16[128,512]{0,1:T(8,128)(2,1)S(1)}, bf16[128,512]{0,1:T(8,128)(2,1)S(1)}, u32[]{:S(2)}, u32[]{:S(2)}) collective-permute-start(bf16[128,512]{0,1:T(8,128)(2,1)S(1)} %bitcast.165), channel_id=1, source_target_pairs={{0,64},{32,96},{64,128},{96,160},{128,0},{160,32},{192,256},{224,2... | collective-permute-start | bytes 393224 | tf_op jit(solution)/shard_map/ppermute | solution.py:52
  169.1 13.2 %collective-permute-start.12 = (bf16[128,512]{0,1:T(8,128)(2,1)S(1)}, bf16[128,512]{0,1:T(8,128)(2,1)S(1)}, u32[]{:S(2)}, u32[]{:S(2)}) collective-permute-start(bf16[128,512]{0,1:T(8,128)(2,1)S(1)} %bitcast.166), channel_id=1, source_target_pairs={{0,128},{32,160},{64,0},{96,32},{128,64},{160,96},{192,320},{224,3... | collective-permute-start | bytes 393224 | tf_op jit(solution)/shard_map/ppermute | solution.py:52
  183.1 19.5 %collective-permute-start.18 = (f32[128,512]{1,0:T(8,128)S(1)}, f32[128,512]{1,0:T(8,128)S(1)}, u32[]{:S(2)}, u32[]{:S(2)}) collective-permute-start(f32[128,512]{1,0:T(8,128)S(1)} %add.276), channel_id=1, source_target_pairs={{0,6},{1,7},{2,0},{3,1},{4,2},{5,3},{6,4},{7,5},{8,14},{9,15},{10,... | collective-permute-start | bytes 786440 | tf_op jit(solution)/shard_map/ppermute | solution.py:52
  187.2 19.1 %collective-permute-start.19 = (f32[128,512]{1,0:T(8,128)S(1)}, f32[128,512]{1,0:T(8,128)}, u32[]{:S(2)}, u32[]{:S(2)}) collective-permute-start(f32[128,512]{1,0:T(8,128)S(1)} %add.276), channel_id=1, source_target_pairs={{0,4},{1,5},{2,6},{3,7},{4,0},{5,1},{6,2},{7,3},{8,12},{9,13},{10,... | collective-permute-start | bytes 786440 | tf_op jit(solution)/shard_map/ppermute | solution.py:52
  189.2 22.7 %collective-permute-start.20 = (f32[128,512]{1,0:T(8,128)S(1)}, f32[128,512]{1,0:T(8,128)}, u32[]{:S(2)}, u32[]{:S(2)}) collective-permute-start(f32[128,512]{1,0:T(8,128)S(1)} %add.276), channel_id=1, source_target_pairs={{0,2},{1,3},{2,4},{3,5},{4,6},{5,7},{6,0},{7,1},{8,10},{9,11},{10,... | collective-permute-start | bytes 786440 | tf_op jit(solution)/shard_map/ppermute | solution.py:52
  194.9 18.9 %collective-permute-start.17 = (bf16[3,128,512]{1,2,0:T(8,128)(2,1)}, bf16[3,128,512]{1,2,0:T(8,128)(2,1)}, u32[]{:S(2)}, u32[]{:S(2)}) collective-permute-start(bf16[3,128,512]{1,2,0:T(8,128)(2,1)} %pad_maximum_fusion.5), channel_id=1, source_target_pairs={{0,192},{32,224},{64,256},{96,288},{128,320},{160,352},{192,384},{... | collective-permute-start | bytes 1179656 | tf_op jit(solution)/shard_map/ppermute | solution.py:52
  198.9 14.9 %collective-permute-start.16 = (bf16[3,128,512]{1,2,0:T(8,128)(2,1)}, bf16[3,128,512]{1,2,0:T(8,128)(2,1)}, u32[]{:S(2)}, u32[]{:S(2)}) collective-permute-start(bf16[3,128,512]{1,2,0:T(8,128)(2,1)} %pad_maximum_fusion.5), channel_id=1, source_target_pairs={{0,384},{32,416},{64,448},{96,480},{128,512},{160,544},{192,576},{... | collective-permute-start | bytes 1179656 | tf_op jit(solution)/shard_map/ppermute | solution.py:52
  203.3 11.8 %collective-permute-start.15 = (bf16[3,128,512]{1,2,0:T(8,128)(2,1)}, bf16[3,128,512]{1,2,0:T(8,128)(2,1)}, u32[]{:S(2)}, u32[]{:S(2)}) collective-permute-start(bf16[3,128,512]{1,2,0:T(8,128)(2,1)} %pad_maximum_fusion.5), channel_id=1, source_target_pairs={{0,576},{32,608},{64,640},{96,672},{128,704},{160,736},{192,0},{22... | collective-permute-start | bytes 1179656 | tf_op jit(solution)/shard_map/ppermute | solution.py:52
  217.8 47.3 %collective-permute-start.21 = (bf16[4,3,128,512]{2,3,1,0:T(8,128)(2,1)}, bf16[4,3,128,512]{2,3,1,0:T(8,128)(2,1)}, u32[]{:S(2)}, u32[]{:S(2)}) collective-permute-start(bf16[4,3,128,512]{2,3,1,0:T(8,128)(2,1)} %pad_maximum_fusion.3), channel_id=1, source_target_pairs={{0,32},{32,0},{64,96},{96,64},{128,160},{160,128},{192,224},{224,1... | collective-permute-start | bytes 4718600 | tf_op jit(solution)/shard_map/ppermute | solution.py:52
  227.5 20.9 %collective-permute-start.22 = (f32[128,512]{1,0:T(8,128)}, f32[128,512]{1,0:T(8,128)S(1)}, u32[]{:S(2)}, u32[]{:S(2)}) collective-permute-start(f32[128,512]{1,0:T(8,128)} %select_add_fusion.4), channel_id=1, source_target_pairs={{0,24},{1,25},{2,26},{3,27},{4,28},{5,29},{6,30},{7,31},{8,0},{9,1... | collective-permute-start | bytes 786440 | tf_op jit(solution)/shard_map/ppermute | solution.py:52
  241.4 22.7 %collective-permute-start.23 = (f32[128,512]{1,0:T(8,128)}, f32[128,512]{1,0:T(8,128)S(1)}, u32[]{:S(2)}, u32[]{:S(2)}) collective-permute-start(f32[128,512]{1,0:T(8,128)} %select_add_fusion.4), channel_id=1, source_target_pairs={{0,16},{1,17},{2,18},{3,19},{4,20},{5,21},{6,22},{7,23},{8,24},{9,... | collective-permute-start | bytes 786440 | tf_op jit(solution)/shard_map/ppermute | solution.py:52
  243.3 20.7 %collective-permute-start.24 = (f32[128,512]{1,0:T(8,128)}, f32[128,512]{1,0:T(8,128)S(1)}, u32[]{:S(2)}, u32[]{:S(2)}) collective-permute-start(f32[128,512]{1,0:T(8,128)} %select_add_fusion.4), channel_id=1, source_target_pairs={{0,8},{1,9},{2,10},{3,11},{4,12},{5,13},{6,14},{7,15},{8,16},{9,17... | collective-permute-start | bytes 786440 | tf_op jit(solution)/shard_map/ppermute | solution.py:52
  (8 other events, 12.8 us)

commit v5 on v4

--- a/solution.py
+++ b/solution.py
@@ -106,13 +106,14 @@
     return total
 
 
-def reduce_step(x, axis, radix, stride):
+def reduce_step(x, axis, radix, stride, wire):
+    own = x.astype(wire)
     if radix == 2:
-        return x + shift_digit(x, axis, radix, stride, 1)
-    pieces = ordered_pieces(x, axis, radix, stride)
-    total = pieces[0]
+        return own.astype(jnp.float32) + shift_digit(own, axis, radix, stride, 1).astype(jnp.float32)
+    pieces = ordered_pieces(own, axis, radix, stride)
+    total = pieces[0].astype(jnp.float32)
     for piece in pieces[1:]:
-        total = total + piece
+        total = total + piece.astype(jnp.float32)
     return total
 
 
@@ -198,7 +199,7 @@
         if level < len(gather_levels):
             flats = gather_step(flats, "blk", *gather_levels[level])
         if level < len(sum_levels):
-            latent_sum = reduce_step(latent_sum, "heads", *sum_levels[level])
+            latent_sum = reduce_step(latent_sum, "heads", *sum_levels[level], jnp.bfloat16)
         flats, latent_sum = lax.optimization_barrier((flats, latent_sum))
     grad_latent = (latent_sum * factor).astype(jnp.bfloat16)
 

time: 282 us -> 261 us (0.926)
  waiting for transfers between devices: 91.9 us -> 76.1 us
    ppermute x25, waiting for transfers between devices: 91.9 us -> 76.1 us  [shift_digit(): return lax.ppermute(x, axis, pairs)]
    unnamed x39 -> x43, local copies, waits for them, and re-layouts: 10.8 us -> 11.6 us
  transfers between devices with their start and end apart: 25 -> 25, of which waited for: 17 -> 16; matrix products, arithmetic and copies ran while one was open for 7% -> 6% of each run, Pallas kernels for 0% -> 0%
where the time goes in v5:
time: 261 us; the launch traced here: 259 us
  starting transfers between devices  106 us (41%)
  waiting for transfers between devices  76.1 us (29%)
  local copies, waits for them, and re-layouts  33.3 us (13%)
  other arithmetic  29.2 us (11%)
  matrix products  12 us (5%)
    ppermute x25, starting transfers between devices, shift_digit(): return lax.ppermute(x, axis, pairs)  106 us
    ppermute x25, waiting for transfers between devices, shift_digit(): return lax.ppermute(x, axis, pairs)  76.1 us
    unnamed x43, local copies, waits for them, and re-layouts  11.6 us
    another operation x7, other arithmetic, gather_step(): return jnp.stack(pieces, axis=0)  11 us
  transfers between devices with their start and end apart: 25, of which 16 were waited for; matrix products, arithmetic and copies ran while one was open for 6% of the time, Pallas kernels for 0%

profile of v5, /device:TPU:56, one launch (start us, length us, event | category | flops | bytes accessed | tf_op | source)
XLA Modules:
  0.0 258.8 jit_solution(5460334758719846063)
XLA Ops:
  4.7 10.9 %collective-permute-start.1 = (bf16[128,578]{1,0:T(8,128)(2,1)S(1)}, bf16[128,578]{1,0:T(8,128)(2,1)S(1)}, u32[]{:S(2)}, u32[]{:S(2)}) collective-permute-start(bf16[128,578]{1,0:T(8,128)(2,1)S(1)} %pad_maximum_fusion.6), channel_id=1, source_target_pairs={{0,64},{32,96},{64,128},{96,160},{128,0},{160,32},{192,256},{224,2... | collective-permute-start | bytes 443912 | tf_op jit(solution)/shard_map/ppermute | solution.py:52
  15.6 5.6 %collective-permute-start = (bf16[128,578]{1,0:T(8,128)(2,1)S(1)}, bf16[128,578]{1,0:T(8,128)(2,1)S(1)}, u32[]{:S(2)}, u32[]{:S(2)}) collective-permute-start(bf16[128,578]{1,0:T(8,128)(2,1)S(1)} %pad_maximum_fusion.6), channel_id=1, source_target_pairs={{0,128},{32,160},{64,0},{96,32},{128,64},{160,96},{192,320},{224,3... | collective-permute-start | bytes 443912 | tf_op jit(solution)/shard_map/ppermute | solution.py:52
  23.7 11.5 %collective-permute-done = bf16[128,578]{1,0:T(8,128)(2,1)S(1)} collective-permute-done((bf16[128,578]{1,0:T(8,128)(2,1)S(1)}, bf16[128,578]{1,0:T(8,128)(2,1)S(1)}, u32[]{:S(2)}, u32[]{:S(2)}) %collective-permute-start) | collective-permute-done | bytes 148000 | tf_op jit(solution)/shard_map/ppermute | solution.py:52
  35.3 3.4 %collective-permute-start.4 = (bf16[3,128,578]{2,1,0:T(8,128)(2,1)S(1)}, bf16[3,128,578]{2,1,0:T(8,128)(2,1)S(1)}, u32[]{:S(2)}, u32[]{:S(2)}) collective-permute-start(bf16[3,128,578]{2,1,0:T(8,128)(2,1)S(1)} %get-tuple-element.57), channel_id=1, source_target_pairs={{0,192},{32,224},{64,256},{96,288},{128,320},{160,352},{192,384},{... | collective-permute-start | bytes 1331720 | tf_op jit(solution)/shard_map/ppermute | solution.py:52
  38.8 4.6 %collective-permute-start.3 = (bf16[3,128,578]{2,1,0:T(8,128)(2,1)S(1)}, bf16[3,128,578]{2,1,0:T(8,128)(2,1)S(1)}, u32[]{:S(2)}, u32[]{:S(2)}) collective-permute-start(bf16[3,128,578]{2,1,0:T(8,128)(2,1)S(1)} %get-tuple-element.57), channel_id=1, source_target_pairs={{0,384},{32,416},{64,448},{96,480},{128,512},{160,544},{192,576},{... | collective-permute-start | bytes 1331720 | tf_op jit(solution)/shard_map/ppermute | solution.py:52
  43.4 3.3 %collective-permute-start.2 = (bf16[3,128,578]{2,1,0:T(8,128)(2,1)S(1)}, bf16[3,128,578]{2,1,0:T(8,128)(2,1)S(1)}, u32[]{:S(2)}, u32[]{:S(2)}) collective-permute-start(bf16[3,128,578]{2,1,0:T(8,128)(2,1)S(1)} %get-tuple-element.57), channel_id=1, source_target_pairs={{0,576},{32,608},{64,640},{96,672},{128,704},{160,736},{192,0},{22... | collective-permute-start | bytes 1331720 | tf_op jit(solution)/shard_map/ppermute | solution.py:52
  46.8 4.9 %collective-permute-done.4 = bf16[3,128,578]{2,1,0:T(8,128)(2,1)S(1)} collective-permute-done((bf16[3,128,578]{2,1,0:T(8,128)(2,1)S(1)}, bf16[3,128,578]{2,1,0:T(8,128)(2,1)S(1)}, u32[]{:S(2)}, u32[]{:S(2)}) %collective-permute-start.4) | collective-permute-done | bytes 443936 | tf_op jit(solution)/shard_map/ppermute | solution.py:52
  51.6 9.7 %collective-permute-done.3 = bf16[3,128,578]{2,1,0:T(8,128)(2,1)S(1)} collective-permute-done((bf16[3,128,578]{2,1,0:T(8,128)(2,1)S(1)}, bf16[3,128,578]{2,1,0:T(8,128)(2,1)S(1)}, u32[]{:S(2)}, u32[]{:S(2)}) %collective-permute-start.3) | collective-permute-done | bytes 443936 | tf_op jit(solution)/shard_map/ppermute | solution.py:52
  65.3 4.8 %copy.99 = bf16[4,3,128,578]{2,0,3,1:T(4,128)(2,1)} copy(bf16[4,3,128,578]{3,2,1,0:T(8,128)(2,1)} %get-tuple-element.50) | data formatting | bytes 3551232 | tf_op jit(solution)/shard_map/stack | solution.py:74
  76.0 4.8 %copy.100 = bf16[4,3,128,578]{3,2,1,0:T(8,128)(2,1)} copy(bf16[4,3,128,578]{2,0,3,1:T(4,128)(2,1)} %collective-permute-done.5) | data formatting | bytes 3551232 | tf_op jit(solution)/shard_map/ppermute | solution.py:52
  95.2 3.1 %fusion.43 = (f32[2,2,1,4,3,128,128]{6,5,4,3,2,1,0:T(8,128)}, f32[2,2,1,4,3,128,128]{6,5,4,3,2,1,0:T(8,128)}) fusion(f32[2,2,2,4,3,128,128]{6,5,4,3,2,1,0:T(8,128)S(1)} %bitcast.147), kind=kLoop, calls=%fused_computation.92 | loop fusion | bytes 12582912 | tf_op jit(solution)/shard_map/slice | solution.py:88
  98.4 3.6 %copy.133 = f32[2,2,1,4,3,128,128]{5,6,1,0,4,3,2:T(8,128)} copy(f32[2,2,1,4,3,128,128]{6,5,4,3,2,1,0:T(8,128)} %get-tuple-element.42) | data formatting | bytes 6291456
  104.0 3.5 %copy.132 = f32[2,2,1,4,3,128,128]{5,6,1,0,4,3,2:T(8,128)} copy(f32[2,2,1,4,3,128,128]{6,5,4,3,2,1,0:T(8,128)} %get-tuple-element.41) | data formatting | bytes 6291456
  109.9 3.5 %fusion.42 = (bf16[2,2,4,3,128,128]{4,5,1,0,3,2:T(8,128)(2,1)S(1)}, f32[2,2,4,3,128,128]{4,5,1,0,3,2:T(8,128)S(1)}) fusion(f32[2,2,4,3,128,128]{4,5,1,0,3,2:T(8,128)} %collective-permute-done.6, f32[2,2,1,4,3,128,128]{5,6,1,0,4,3,2:T(8,128)} %copy.132), kind=kLoop, calls=%fused_computation.91 | loop fusion | flops 1572864 | bytes 11010048 | tf_op jit(solution)/shard_map/convert.4
  113.5 4.5 %collective-permute-start.9 = (bf16[2,2,3,128,128]{3,4,1,0,2:T(8,128)(2,1)S(1)}, bf16[2,2,3,128,128]{3,4,1,0,2:T(8,128)(2,1)S(1)}, u32[]{:S(2)}, u32[]{:S(2)}) collective-permute-start(bf16[2,2,3,128,128]{3,4,1,0,2:T(8,128)(2,1)S(1)} %get-tuple-element.52), channel_id=1, source_target_pairs={{0,576},{32,608},{64,640},{96,672},{128,704},{160,736},{192,0},{22... | collective-permute-start | bytes 1179656 | tf_op jit(solution)/shard_map/ppermute | solution.py:52
  118.0 3.7 %collective-permute-start.8 = (bf16[2,2,3,128,128]{3,4,1,0,2:T(8,128)(2,1)S(1)}, bf16[2,2,3,128,128]{3,4,1,0,2:T(8,128)(2,1)S(1)}, u32[]{:S(2)}, u32[]{:S(2)}) collective-permute-start(bf16[2,2,3,128,128]{3,4,1,0,2:T(8,128)(2,1)S(1)} %get-tuple-element.53), channel_id=1, source_target_pairs={{0,384},{32,416},{64,448},{96,480},{128,512},{160,544},{192,576},{... | collective-permute-start | bytes 1179656 | tf_op jit(solution)/shard_map/ppermute | solution.py:52
  123.7 11.5 %collective-permute-done.9 = bf16[2,2,3,128,128]{3,4,1,0,2:T(8,128)(2,1)S(1)} collective-permute-done((bf16[2,2,3,128,128]{3,4,1,0,2:T(8,128)(2,1)S(1)}, bf16[2,2,3,128,128]{3,4,1,0,2:T(8,128)(2,1)S(1)}, u32[]{:S(2)}, u32[]{:S(2)}) %collective-permute-start.9) | collective-permute-done | bytes 393248 | tf_op jit(solution)/shard_map/ppermute | solution.py:52
  135.2 5.6 %collective-permute-done.7 = bf16[2,2,3,128,128]{3,4,1,0,2:T(8,128)(2,1)S(1)} collective-permute-done((bf16[2,2,3,128,128]{3,4,1,0,2:T(8,128)(2,1)S(1)}, bf16[2,2,3,128,128]{3,4,1,0,2:T(8,128)(2,1)S(1)}, u32[]{:S(2)}, u32[]{:S(2)}) %collective-permute-start.7) | collective-permute-done | bytes 393248 | tf_op jit(solution)/shard_map/ppermute | solution.py:52
  141.0 7.1 %collective-permute-start.11 = (bf16[2,2,128,128]{2,3,1,0:T(8,128)(2,1)S(1)}, bf16[2,2,128,128]{2,3,1,0:T(8,128)(2,1)S(1)}, u32[]{:S(2)}, u32[]{:S(2)}) collective-permute-start(bf16[2,2,128,128]{2,3,1,0:T(8,128)(2,1)S(1)} %get-tuple-element.59), channel_id=1, source_target_pairs={{0,128},{32,160},{64,0},{96,32},{128,64},{160,96},{192,320},{224,3... | collective-permute-start | bytes 393224 | tf_op jit(solution)/shard_map/ppermute | solution.py:52
  153.2 7.9 %collective-permute-done.10 = bf16[2,2,128,128]{2,3,1,0:T(8,128)(2,1)S(1)} collective-permute-done((bf16[2,2,128,128]{2,3,1,0:T(8,128)(2,1)S(1)}, bf16[2,2,128,128]{2,3,1,0:T(8,128)(2,1)S(1)}, u32[]{:S(2)}, u32[]{:S(2)}) %collective-permute-start.10) | collective-permute-done | bytes 131104 | tf_op jit(solution)/shard_map/ppermute | solution.py:52
  161.2 4.1 %collective-permute-start.13 = (bf16[128,512]{0,1:T(8,128)(2,1)S(1)}, bf16[128,512]{0,1:T(8,128)(2,1)S(1)}, u32[]{:S(2)}, u32[]{:S(2)}) collective-permute-start(bf16[128,512]{0,1:T(8,128)(2,1)S(1)} %bitcast.163), channel_id=1, source_target_pairs={{0,64},{32,96},{64,128},{96,160},{128,0},{160,32},{192,256},{224,2... | collective-permute-start | bytes 393224 | tf_op jit(solution)/shard_map/ppermute | solution.py:52
  165.3 5.6 %collective-permute-start.12 = (bf16[128,512]{0,1:T(8,128)(2,1)S(1)}, bf16[128,512]{0,1:T(8,128)(2,1)S(1)}, u32[]{:S(2)}, u32[]{:S(2)}) collective-permute-start(bf16[128,512]{0,1:T(8,128)(2,1)S(1)} %bitcast.164), channel_id=1, source_target_pairs={{0,128},{32,160},{64,0},{96,32},{128,64},{160,96},{192,320},{224,3... | collective-permute-start | bytes 393224 | tf_op jit(solution)/shard_map/ppermute | solution.py:52
  171.4 3.3 %collective-permute-start.14 = (bf16[128,512]{1,0:T(8,128)(2,1)S(1)}, bf16[128,512]{1,0:T(8,128)(2,1)S(1)}, u32[]{:S(2)}, u32[]{:S(2)}) collective-permute-start(bf16[128,512]{1,0:T(8,128)(2,1)S(1)} %fusion.17), channel_id=1, source_target_pairs={{0,1},{1,0},{2,3},{3,2},{4,5},{5,4},{6,7},{7,6},{8,9},{9,8},{10,11... | collective-permute-start | bytes 393224 | tf_op jit(solution)/shard_map/ppermute | solution.py:52
  175.7 3.1 %collective-permute-done.12 = bf16[128,512]{0,1:T(8,128)(2,1)S(1)} collective-permute-done((bf16[128,512]{0,1:T(8,128)(2,1)S(1)}, bf16[128,512]{0,1:T(8,128)(2,1)S(1)}, u32[]{:S(2)}, u32[]{:S(2)}) %collective-permute-start.12) | collective-permute-done | bytes 131104 | tf_op jit(solution)/shard_map/ppermute | solution.py:52
  179.6 4.0 %collective-permute-start.18 = (bf16[128,512]{1,0:T(8,128)(2,1)S(1)}, bf16[128,512]{1,0:T(8,128)(2,1)S(1)}, u32[]{:S(2)}, u32[]{:S(2)}) collective-permute-start(bf16[128,512]{1,0:T(8,128)(2,1)S(1)} %convert_add_fusion.2), channel_id=1, source_target_pairs={{0,6},{1,7},{2,0},{3,1},{4,2},{5,3},{6,4},{7,5},{8,14},{9,15},{10,... | collective-permute-start | bytes 393224 | tf_op jit(solution)/shard_map/ppermute | solution.py:52
  183.7 3.7 %collective-permute-start.17 = (bf16[3,128,512]{1,2,0:T(8,128)(2,1)}, bf16[3,128,512]{1,2,0:T(8,128)(2,1)}, u32[]{:S(2)}, u32[]{:S(2)}) collective-permute-start(bf16[3,128,512]{1,2,0:T(8,128)(2,1)} %pad_maximum_fusion.5), channel_id=1, source_target_pairs={{0,192},{32,224},{64,256},{96,288},{128,320},{160,352},{192,384},{... | collective-permute-start | bytes 1179656 | tf_op jit(solution)/shard_map/ppermute | solution.py:52
  187.4 3.7 %collective-permute-start.16 = (bf16[3,128,512]{1,2,0:T(8,128)(2,1)}, bf16[3,128,512]{1,2,0:T(8,128)(2,1)}, u32[]{:S(2)}, u32[]{:S(2)}) collective-permute-start(bf16[3,128,512]{1,2,0:T(8,128)(2,1)} %pad_maximum_fusion.5), channel_id=1, source_target_pairs={{0,384},{32,416},{64,448},{96,480},{128,512},{160,544},{192,576},{... | collective-permute-start | bytes 1179656 | tf_op jit(solution)/shard_map/ppermute | solution.py:52
  193.9 3.0 %collective-permute-start.19 = (bf16[128,512]{1,0:T(8,128)(2,1)S(1)}, bf16[128,512]{1,0:T(8,128)(2,1)S(1)}, u32[]{:S(2)}, u32[]{:S(2)}) collective-permute-start(bf16[128,512]{1,0:T(8,128)(2,1)S(1)} %convert_add_fusion.2), channel_id=1, source_target_pairs={{0,4},{1,5},{2,6},{3,7},{4,0},{5,1},{6,2},{7,3},{8,12},{9,13},{10,... | collective-permute-start | bytes 393224 | tf_op jit(solution)/shard_map/ppermute | solution.py:52
  197.0 5.7 %collective-permute-start.20 = (bf16[128,512]{1,0:T(8,128)(2,1)S(1)}, bf16[128,512]{1,0:T(8,128)(2,1)}, u32[]{:S(2)}, u32[]{:S(2)}) collective-permute-start(bf16[128,512]{1,0:T(8,128)(2,1)S(1)} %convert_add_fusion.2), channel_id=1, source_target_pairs={{0,2},{1,3},{2,4},{3,5},{4,6},{5,7},{6,0},{7,1},{8,10},{9,11},{10,... | collective-permute-start | bytes 393224 | tf_op jit(solution)/shard_map/ppermute | solution.py:52
  205.5 3.5 %collective-permute-done.20 = bf16[128,512]{1,0:T(8,128)(2,1)} collective-permute-done((bf16[128,512]{1,0:T(8,128)(2,1)S(1)}, bf16[128,512]{1,0:T(8,128)(2,1)}, u32[]{:S(2)}, u32[]{:S(2)}) %collective-permute-start.20) | collective-permute-done | bytes 131104 | tf_op jit(solution)/shard_map/ppermute | solution.py:52
  219.5 12.3 %collective-permute-start.22 = (bf16[128,512]{1,0:T(8,128)(2,1)S(1)}, bf16[128,512]{1,0:T(8,128)(2,1)S(1)}, u32[]{:S(2)}, u32[]{:S(2)}) collective-permute-start(bf16[128,512]{1,0:T(8,128)(2,1)S(1)} %convert_add_fusion.1), channel_id=1, source_target_pairs={{0,24},{1,25},{2,26},{3,27},{4,28},{5,29},{6,30},{7,31},{8,0},{9,1... | collective-permute-start | bytes 393224 | tf_op jit(solution)/shard_map/ppermute | solution.py:52
  239.2 5.1 %collective-permute-done.23 = bf16[128,512]{1,0:T(8,128)(2,1)S(1)} collective-permute-done((bf16[128,512]{1,0:T(8,128)(2,1)S(1)}, bf16[128,512]{1,0:T(8,128)(2,1)S(1)}, u32[]{:S(2)}, u32[]{:S(2)}) %collective-permute-start.23) | collective-permute-done | bytes 131104 | tf_op jit(solution)/shard_map/ppermute | solution.py:52
  (118 shorter events, 82.2 us)
Async XLA Ops:
  0.6 83.9 %copy-start = (bf16[512,256]{1,0:T(8,128)(2,1)S(1)}, bf16[512,256]{1,0:T(8,128)(2,1)}, u32[]{:S(2)}) copy-start(bf16[512,256]{1,0:T(8,128)(2,1)} %param.16) | copy-start | bytes 786436
  4.5 60.7 %copy-start.5 = (f32[128,4,128]{2,1,0:T(4,128)}, f32[128,4,128]{2,1,0:T(4,128)S(1)}, u32[]{:S(2)}) copy-start(f32[128,4,128]{2,1,0:T(4,128)S(1)} %broadcast_in_dim.42) | copy-start | bytes 786436
  4.7 19.0 %collective-permute-start.1 = (bf16[128,578]{1,0:T(8,128)(2,1)S(1)}, bf16[128,578]{1,0:T(8,128)(2,1)S(1)}, u32[]{:S(2)}, u32[]{:S(2)}) collective-permute-start(bf16[128,578]{1,0:T(8,128)(2,1)S(1)} %pad_maximum_fusion.6), channel_id=1, source_target_pairs={{0,64},{32,96},{64,128},{96,160},{128,0},{160,32},{192,256},{224,2... | collective-permute-start | bytes 443912 | tf_op jit(solution)/shard_map/ppermute | solution.py:52
  15.6 19.6 %collective-permute-start = (bf16[128,578]{1,0:T(8,128)(2,1)S(1)}, bf16[128,578]{1,0:T(8,128)(2,1)S(1)}, u32[]{:S(2)}, u32[]{:S(2)}) collective-permute-start(bf16[128,578]{1,0:T(8,128)(2,1)S(1)} %pad_maximum_fusion.6), channel_id=1, source_target_pairs={{0,128},{32,160},{64,0},{96,32},{128,64},{160,96},{192,320},{224,3... | collective-permute-start | bytes 443912 | tf_op jit(solution)/shard_map/ppermute | solution.py:52
  35.3 16.3 %collective-permute-start.4 = (bf16[3,128,578]{2,1,0:T(8,128)(2,1)S(1)}, bf16[3,128,578]{2,1,0:T(8,128)(2,1)S(1)}, u32[]{:S(2)}, u32[]{:S(2)}) collective-permute-start(bf16[3,128,578]{2,1,0:T(8,128)(2,1)S(1)} %get-tuple-element.57), channel_id=1, source_target_pairs={{0,192},{32,224},{64,256},{96,288},{128,320},{160,352},{192,384},{... | collective-permute-start | bytes 1331720 | tf_op jit(solution)/shard_map/ppermute | solution.py:52
  38.8 22.6 %collective-permute-start.3 = (bf16[3,128,578]{2,1,0:T(8,128)(2,1)S(1)}, bf16[3,128,578]{2,1,0:T(8,128)(2,1)S(1)}, u32[]{:S(2)}, u32[]{:S(2)}) collective-permute-start(bf16[3,128,578]{2,1,0:T(8,128)(2,1)S(1)} %get-tuple-element.57), channel_id=1, source_target_pairs={{0,384},{32,416},{64,448},{96,480},{128,512},{160,544},{192,576},{... | collective-permute-start | bytes 1331720 | tf_op jit(solution)/shard_map/ppermute | solution.py:52
  43.4 19.5 %collective-permute-start.2 = (bf16[3,128,578]{2,1,0:T(8,128)(2,1)S(1)}, bf16[3,128,578]{2,1,0:T(8,128)(2,1)S(1)}, u32[]{:S(2)}, u32[]{:S(2)}) collective-permute-start(bf16[3,128,578]{2,1,0:T(8,128)(2,1)S(1)} %get-tuple-element.57), channel_id=1, source_target_pairs={{0,576},{32,608},{64,640},{96,672},{128,704},{160,736},{192,0},{22... | collective-permute-start | bytes 1331720 | tf_op jit(solution)/shard_map/ppermute | solution.py:52
  65.3 6.7 %copy-start.13 = (bf16[128,256]{1,0:T(8,128)(2,1)S(1)}, bf16[128,256]{1,0:T(8,128)(2,1)}, u32[]{:S(2)}) copy-start(bf16[128,256]{1,0:T(8,128)(2,1)} %param.11) | copy-start | bytes 196612
  65.3 6.8 %copy-start.15 = (bf16[128,128]{1,0:T(8,128)(2,1)S(1)}, bf16[128,128]{1,0:T(8,128)(2,1)}, u32[]{:S(2)}) copy-start(bf16[128,128]{1,0:T(8,128)(2,1)} %param.10) | copy-start | bytes 98308
  65.3 7.6 %copy-start.14 = (bf16[128,256]{1,0:T(8,128)(2,1)S(1)}, bf16[128,256]{1,0:T(8,128)(2,1)}, u32[]{:S(2)}) copy-start(bf16[128,256]{1,0:T(8,128)(2,1)} %param.9) | copy-start | bytes 196612
  70.0 5.9 %collective-permute-start.5 = (bf16[4,3,128,578]{2,0,3,1:T(4,128)(2,1)}, bf16[4,3,128,578]{2,0,3,1:T(4,128)(2,1)}, u32[]{:S(2)}, u32[]{:S(2)}) collective-permute-start(bf16[4,3,128,578]{2,0,3,1:T(4,128)(2,1)} %copy.99), channel_id=1, source_target_pairs={{0,32},{32,0},{64,96},{96,64},{128,160},{160,128},{192,224},{224,1... | collective-permute-start | bytes 5326856 | tf_op jit(solution)/shard_map/ppermute | solution.py:52
  83.5 4.1 %copy-start.2 = (bf16[2,4,3,128,578]{4,3,2,1,0:T(8,128)(2,1)}, bf16[2,4,3,128,578]{4,3,2,1,0:T(8,128)(2,1)S(1)}, u32[]{:S(2)}) copy-start(bf16[2,4,3,128,578]{4,3,2,1,0:T(8,128)(2,1)S(1)} %pad_maximum_fusion) | copy-start | bytes 10653700
  102.0 7.9 %collective-permute-start.6 = (f32[2,2,4,3,128,128]{4,5,1,0,3,2:T(8,128)}, f32[2,2,4,3,128,128]{4,5,1,0,3,2:T(8,128)}, u32[]{:S(2)}, u32[]{:S(2)}) collective-permute-start(f32[2,2,4,3,128,128]{4,5,1,0,3,2:T(8,128)} %bitcast.159), channel_id=1, source_target_pairs={{0,32},{32,0},{64,96},{96,64},{128,160},{160,128},{192,224},{224,1... | collective-permute-start | bytes 9437192 | tf_op jit(solution)/shard_map/ppermute | solution.py:52
  113.4 57.8 %copy-start.10 = (bf16[512,256]{1,0:T(8,128)(2,1)S(1)}, bf16[512,256]{1,0:T(8,128)(2,1)}, u32[]{:S(2)}) copy-start(bf16[512,256]{1,0:T(8,128)(2,1)} %param.17) | copy-start | bytes 786436
  113.5 21.7 %collective-permute-start.9 = (bf16[2,2,3,128,128]{3,4,1,0,2:T(8,128)(2,1)S(1)}, bf16[2,2,3,128,128]{3,4,1,0,2:T(8,128)(2,1)S(1)}, u32[]{:S(2)}, u32[]{:S(2)}) collective-permute-start(bf16[2,2,3,128,128]{3,4,1,0,2:T(8,128)(2,1)S(1)} %get-tuple-element.52), channel_id=1, source_target_pairs={{0,576},{32,608},{64,640},{96,672},{128,704},{160,736},{192,0},{22... | collective-permute-start | bytes 1179656 | tf_op jit(solution)/shard_map/ppermute | solution.py:52
  118.0 17.1 %collective-permute-start.8 = (bf16[2,2,3,128,128]{3,4,1,0,2:T(8,128)(2,1)S(1)}, bf16[2,2,3,128,128]{3,4,1,0,2:T(8,128)(2,1)S(1)}, u32[]{:S(2)}, u32[]{:S(2)}) collective-permute-start(bf16[2,2,3,128,128]{3,4,1,0,2:T(8,128)(2,1)S(1)} %get-tuple-element.53), channel_id=1, source_target_pairs={{0,384},{32,416},{64,448},{96,480},{128,512},{160,544},{192,576},{... | collective-permute-start | bytes 1179656 | tf_op jit(solution)/shard_map/ppermute | solution.py:52
  121.8 19.0 %collective-permute-start.7 = (bf16[2,2,3,128,128]{3,4,1,0,2:T(8,128)(2,1)S(1)}, bf16[2,2,3,128,128]{3,4,1,0,2:T(8,128)(2,1)S(1)}, u32[]{:S(2)}, u32[]{:S(2)}) collective-permute-start(bf16[2,2,3,128,128]{3,4,1,0,2:T(8,128)(2,1)S(1)} %get-tuple-element.51), channel_id=1, source_target_pairs={{0,192},{32,224},{64,256},{96,288},{128,320},{160,352},{192,384},{... | collective-permute-start | bytes 1179656 | tf_op jit(solution)/shard_map/ppermute | solution.py:52
  141.0 12.2 %collective-permute-start.11 = (bf16[2,2,128,128]{2,3,1,0:T(8,128)(2,1)S(1)}, bf16[2,2,128,128]{2,3,1,0:T(8,128)(2,1)S(1)}, u32[]{:S(2)}, u32[]{:S(2)}) collective-permute-start(bf16[2,2,128,128]{2,3,1,0:T(8,128)(2,1)S(1)} %get-tuple-element.59), channel_id=1, source_target_pairs={{0,128},{32,160},{64,0},{96,32},{128,64},{160,96},{192,320},{224,3... | collective-permute-start | bytes 393224 | tf_op jit(solution)/shard_map/ppermute | solution.py:52
  148.1 13.1 %collective-permute-start.10 = (bf16[2,2,128,128]{2,3,1,0:T(8,128)(2,1)S(1)}, bf16[2,2,128,128]{2,3,1,0:T(8,128)(2,1)S(1)}, u32[]{:S(2)}, u32[]{:S(2)}) collective-permute-start(bf16[2,2,128,128]{2,3,1,0:T(8,128)(2,1)S(1)} %get-tuple-element.58), channel_id=1, source_target_pairs={{0,64},{32,96},{64,128},{96,160},{128,0},{160,32},{192,256},{224,2... | collective-permute-start | bytes 393224 | tf_op jit(solution)/shard_map/ppermute | solution.py:52
  161.2 14.5 %collective-permute-start.13 = (bf16[128,512]{0,1:T(8,128)(2,1)S(1)}, bf16[128,512]{0,1:T(8,128)(2,1)S(1)}, u32[]{:S(2)}, u32[]{:S(2)}) collective-permute-start(bf16[128,512]{0,1:T(8,128)(2,1)S(1)} %bitcast.163), channel_id=1, source_target_pairs={{0,64},{32,96},{64,128},{96,160},{128,0},{160,32},{192,256},{224,2... | collective-permute-start | bytes 393224 | tf_op jit(solution)/shard_map/ppermute | solution.py:52
  165.3 13.5 %collective-permute-start.12 = (bf16[128,512]{0,1:T(8,128)(2,1)S(1)}, bf16[128,512]{0,1:T(8,128)(2,1)S(1)}, u32[]{:S(2)}, u32[]{:S(2)}) collective-permute-start(bf16[128,512]{0,1:T(8,128)(2,1)S(1)} %bitcast.164), channel_id=1, source_target_pairs={{0,128},{32,160},{64,0},{96,32},{128,64},{160,96},{192,320},{224,3... | collective-permute-start | bytes 393224 | tf_op jit(solution)/shard_map/ppermute | solution.py:52
  171.4 8.2 %collective-permute-start.14 = (bf16[128,512]{1,0:T(8,128)(2,1)S(1)}, bf16[128,512]{1,0:T(8,128)(2,1)S(1)}, u32[]{:S(2)}, u32[]{:S(2)}) collective-permute-start(bf16[128,512]{1,0:T(8,128)(2,1)S(1)} %fusion.17), channel_id=1, source_target_pairs={{0,1},{1,0},{2,3},{3,2},{4,5},{5,4},{6,7},{7,6},{8,9},{9,8},{10,11... | collective-permute-start | bytes 393224 | tf_op jit(solution)/shard_map/ppermute | solution.py:52
  179.6 17.3 %collective-permute-start.18 = (bf16[128,512]{1,0:T(8,128)(2,1)S(1)}, bf16[128,512]{1,0:T(8,128)(2,1)S(1)}, u32[]{:S(2)}, u32[]{:S(2)}) collective-permute-start(bf16[128,512]{1,0:T(8,128)(2,1)S(1)} %convert_add_fusion.2), channel_id=1, source_target_pairs={{0,6},{1,7},{2,0},{3,1},{4,2},{5,3},{6,4},{7,5},{8,14},{9,15},{10,... | collective-permute-start | bytes 393224 | tf_op jit(solution)/shard_map/ppermute | solution.py:52
  183.7 26.3 %collective-permute-start.17 = (bf16[3,128,512]{1,2,0:T(8,128)(2,1)}, bf16[3,128,512]{1,2,0:T(8,128)(2,1)}, u32[]{:S(2)}, u32[]{:S(2)}) collective-permute-start(bf16[3,128,512]{1,2,0:T(8,128)(2,1)} %pad_maximum_fusion.5), channel_id=1, source_target_pairs={{0,192},{32,224},{64,256},{96,288},{128,320},{160,352},{192,384},{... | collective-permute-start | bytes 1179656 | tf_op jit(solution)/shard_map/ppermute | solution.py:52
  187.4 22.6 %collective-permute-start.16 = (bf16[3,128,512]{1,2,0:T(8,128)(2,1)}, bf16[3,128,512]{1,2,0:T(8,128)(2,1)}, u32[]{:S(2)}, u32[]{:S(2)}) collective-permute-start(bf16[3,128,512]{1,2,0:T(8,128)(2,1)} %pad_maximum_fusion.5), channel_id=1, source_target_pairs={{0,384},{32,416},{64,448},{96,480},{128,512},{160,544},{192,576},{... | collective-permute-start | bytes 1179656 | tf_op jit(solution)/shard_map/ppermute | solution.py:52
  191.2 18.9 %collective-permute-start.15 = (bf16[3,128,512]{1,2,0:T(8,128)(2,1)}, bf16[3,128,512]{1,2,0:T(8,128)(2,1)}, u32[]{:S(2)}, u32[]{:S(2)}) collective-permute-start(bf16[3,128,512]{1,2,0:T(8,128)(2,1)} %pad_maximum_fusion.5), channel_id=1, source_target_pairs={{0,576},{32,608},{64,640},{96,672},{128,704},{160,736},{192,0},{22... | collective-permute-start | bytes 1179656 | tf_op jit(solution)/shard_map/ppermute | solution.py:52
  193.9 10.9 %collective-permute-start.19 = (bf16[128,512]{1,0:T(8,128)(2,1)S(1)}, bf16[128,512]{1,0:T(8,128)(2,1)S(1)}, u32[]{:S(2)}, u32[]{:S(2)}) collective-permute-start(bf16[128,512]{1,0:T(8,128)(2,1)S(1)} %convert_add_fusion.2), channel_id=1, source_target_pairs={{0,4},{1,5},{2,6},{3,7},{4,0},{5,1},{6,2},{7,3},{8,12},{9,13},{10,... | collective-permute-start | bytes 393224 | tf_op jit(solution)/shard_map/ppermute | solution.py:52
  197.0 12.0 %collective-permute-start.20 = (bf16[128,512]{1,0:T(8,128)(2,1)S(1)}, bf16[128,512]{1,0:T(8,128)(2,1)}, u32[]{:S(2)}, u32[]{:S(2)}) collective-permute-start(bf16[128,512]{1,0:T(8,128)(2,1)S(1)} %convert_add_fusion.2), channel_id=1, source_target_pairs={{0,2},{1,3},{2,4},{3,5},{4,6},{5,7},{6,0},{7,1},{8,10},{9,11},{10,... | collective-permute-start | bytes 393224 | tf_op jit(solution)/shard_map/ppermute | solution.py:52
  212.8 31.6 %collective-permute-start.21 = (bf16[4,3,128,512]{2,3,1,0:T(8,128)(2,1)}, bf16[4,3,128,512]{2,3,1,0:T(8,128)(2,1)}, u32[]{:S(2)}, u32[]{:S(2)}) collective-permute-start(bf16[4,3,128,512]{2,3,1,0:T(8,128)(2,1)} %pad_maximum_fusion.3), channel_id=1, source_target_pairs={{0,32},{32,0},{64,96},{96,64},{128,160},{160,128},{192,224},{224,1... | collective-permute-start | bytes 4718600 | tf_op jit(solution)/shard_map/ppermute | solution.py:52
  219.5 19.7 %collective-permute-start.22 = (bf16[128,512]{1,0:T(8,128)(2,1)S(1)}, bf16[128,512]{1,0:T(8,128)(2,1)S(1)}, u32[]{:S(2)}, u32[]{:S(2)}) collective-permute-start(bf16[128,512]{1,0:T(8,128)(2,1)S(1)} %convert_add_fusion.1), channel_id=1, source_target_pairs={{0,24},{1,25},{2,26},{3,27},{4,28},{5,29},{6,30},{7,31},{8,0},{9,1... | collective-permute-start | bytes 393224 | tf_op jit(solution)/shard_map/ppermute | solution.py:52
  231.7 12.6 %collective-permute-start.23 = (bf16[128,512]{1,0:T(8,128)(2,1)S(1)}, bf16[128,512]{1,0:T(8,128)(2,1)S(1)}, u32[]{:S(2)}, u32[]{:S(2)}) collective-permute-start(bf16[128,512]{1,0:T(8,128)(2,1)S(1)} %convert_add_fusion.1), channel_id=1, source_target_pairs={{0,16},{1,17},{2,18},{3,19},{4,20},{5,21},{6,22},{7,23},{8,24},{9,... | collective-permute-start | bytes 393224 | tf_op jit(solution)/shard_map/ppermute | solution.py:52
  233.7 10.6 %collective-permute-start.24 = (bf16[128,512]{1,0:T(8,128)(2,1)S(1)}, bf16[128,512]{1,0:T(8,128)(2,1)S(1)}, u32[]{:S(2)}, u32[]{:S(2)}) collective-permute-start(bf16[128,512]{1,0:T(8,128)(2,1)S(1)} %convert_add_fusion.1), channel_id=1, source_target_pairs={{0,8},{1,9},{2,10},{3,11},{4,12},{5,13},{6,14},{7,15},{8,16},{9,17... | collective-permute-start | bytes 393224 | tf_op jit(solution)/shard_map/ppermute | solution.py:52
  (10 other events, 15.3 us)

commit v6 on v5

--- a/solution.py
+++ b/solution.py
@@ -193,32 +193,35 @@
     latent_part = back_project(key_flat, w_uk) + back_project(value_flat, w_uv)
     sum_levels = digits_of(lax.axis_size("heads"))
     gather_levels = gather_order(block_count)
+    comp_own = comp_all.reshape(radices + (row_count, col_width))[0]
+
+    def own_products(flats):
+        first_radix, first_stride = gather_levels[0]
+        inner = list(reversed(gather_levels[1:-1]))
+        slot_sums = []
+        for slot in range(first_radix):
+            left = comp_own[..., slot, :, :].reshape((-1, row_count, col_width))
+            right = flats[..., slot, :, :].reshape((-1, row_count, flat.shape[1]))
+            product = jnp.einsum("btl,btk->blk", left, right, preferred_element_type=jnp.float32)
+            partial = product.astype(jnp.bfloat16).astype(jnp.float32)
+            partial = partial.reshape(tuple(d[0] for d in inner) + partial.shape[1:])
+            for radix, stride in inner:
+                partial = ordered_sum([partial[k] for k in range(radix)], "blk", radix, stride)
+            slot_sums.append(partial)
+        return ordered_sum(slot_sums, "blk", first_radix, first_stride)
+
     latent_sum = latent_part
     flats = flat
     for level in range(max(len(sum_levels), len(gather_levels))):
-        if level < len(gather_levels):
+        if level < len(gather_levels) - 1:
             flats = gather_step(flats, "blk", *gather_levels[level])
+        elif level == len(gather_levels) - 1:
+            flats = reduce_step(own_products(flats), "blk", *gather_levels[level], jnp.float32)
         if level < len(sum_levels):
             latent_sum = reduce_step(latent_sum, "heads", *sum_levels[level], jnp.bfloat16)
         flats, latent_sum = lax.optimization_barrier((flats, latent_sum))
     grad_latent = (latent_sum * factor).astype(jnp.bfloat16)
-
-    order = gather_order(block_count)
-    first_radix, first_stride = order[0]
-    lead = radices[:-1]
-    lead_digits = list(reversed(order))[:-1]
-    comp_rel = comp_all.reshape(radices + (row_count, col_width))
-    slot_sums = []
-    for slot in range(first_radix):
-        left = comp_rel[..., slot, :, :].reshape((-1, row_count, col_width))
-        right = flats[..., slot, :, :].reshape((-1, row_count, flat.shape[1]))
-        product = jnp.einsum("btl,btk->blk", left, right, preferred_element_type=jnp.float32)
-        partial = product.astype(jnp.bfloat16).astype(jnp.float32)
-        partial = partial.reshape(lead + partial.shape[1:])
-        for radix, stride in lead_digits:
-            partial = ordered_sum([partial[k] for k in range(radix)], "blk", radix, stride)
-        slot_sums.append(partial)
-    weight_sum = ordered_sum(slot_sums, "blk", first_radix, first_stride)
+    weight_sum = flats
     weight_key_grad = weight_sum[:, : head_count * D_NOPE]
     weight_value_grad = weight_sum[:, head_count * D_NOPE :]
 

time: 261 us -> 243 us (0.931)
  local copies, waits for them, and re-layouts: 33.3 us -> 21.2 us
  other arithmetic: 29.2 us -> 24 us
    unnamed x43 -> x39, local copies, waits for them, and re-layouts: 11.6 us -> 5.07 us
    slice x4 -> x1, local copies, waits for them, and re-layouts: 7.26 us -> 1.55 us  [body(): comp_own = comp_all.reshape(radices + (row_count, col_width))[0]]
    another operation x7 -> x6, other arithmetic: 11 us -> 7.43 us  [gather_step(): return jnp.stack(pieces, axis=0)]
    add x1 -> x2, other arithmetic: 0.03 us -> 2.75 us  [reduce_step(): own.astype(jnp.float32)]
    another operation x2, other arithmetic: 3.72 us -> 1.09 us
  transfers between devices with their start and end apart: 25 -> 25, of which waited for: 16 -> 15; matrix products, arithmetic and copies ran while one was open for 6% -> 7% of each run, Pallas kernels for 0% -> 0%
where the time goes in v6:
time: 243 us; the launch traced here: 241 us
  starting transfers between devices  107 us (44%)
  waiting for transfers between devices  73.6 us (30%)
  other arithmetic  24 us (10%)
  local copies, waits for them, and re-layouts  21.2 us (9%)
  matrix products  13.5 us (6%)
    ppermute x25, starting transfers between devices, shift_digit(): return lax.ppermute(x, axis, pairs)  107 us
    ppermute x25, waiting for transfers between devices, shift_digit(): return lax.ppermute(x, axis, pairs)  73.6 us
    another operation x6, other arithmetic, gather_step(): return jnp.stack(pieces, axis=0)  7.43 us
    unnamed x39, local copies, waits for them, and re-layouts  5.07 us
  transfers between devices with their start and end apart: 25, of which 15 were waited for; matrix products, arithmetic and copies ran while one was open for 7% of the time, Pallas kernels for 0%

profile of v6, /device:TPU:56, one launch (start us, length us, event | category | flops | bytes accessed | tf_op | source)
XLA Modules:
  0.0 241.0 jit_solution(6805345749971296551)
XLA Ops:
  5.4 10.9 %collective-permute-start.1 = (bf16[128,578]{1,0:T(8,128)(2,1)S(1)}, bf16[128,578]{1,0:T(8,128)(2,1)S(1)}, u32[]{:S(2)}, u32[]{:S(2)}) collective-permute-start(bf16[128,578]{1,0:T(8,128)(2,1)S(1)} %pad_maximum_fusion.5), channel_id=1, source_target_pairs={{0,64},{32,96},{64,128},{96,160},{128,0},{160,32},{192,256},{224,2... | collective-permute-start | bytes 443912 | tf_op jit(solution)/shard_map/ppermute | solution.py:52
  16.3 5.6 %collective-permute-start = (bf16[128,578]{1,0:T(8,128)(2,1)S(1)}, bf16[128,578]{1,0:T(8,128)(2,1)S(1)}, u32[]{:S(2)}, u32[]{:S(2)}) collective-permute-start(bf16[128,578]{1,0:T(8,128)(2,1)S(1)} %pad_maximum_fusion.5), channel_id=1, source_target_pairs={{0,128},{32,160},{64,0},{96,32},{128,64},{160,96},{192,320},{224,3... | collective-permute-start | bytes 443912 | tf_op jit(solution)/shard_map/ppermute | solution.py:52
  24.4 11.5 %collective-permute-done = bf16[128,578]{1,0:T(8,128)(2,1)S(1)} collective-permute-done((bf16[128,578]{1,0:T(8,128)(2,1)S(1)}, bf16[128,578]{1,0:T(8,128)(2,1)S(1)}, u32[]{:S(2)}, u32[]{:S(2)}) %collective-permute-start) | collective-permute-done | bytes 148000 | tf_op jit(solution)/shard_map/ppermute | solution.py:52
  36.0 3.4 %collective-permute-start.4 = (bf16[3,128,578]{2,1,0:T(8,128)(2,1)S(1)}, bf16[3,128,578]{2,1,0:T(8,128)(2,1)S(1)}, u32[]{:S(2)}, u32[]{:S(2)}) collective-permute-start(bf16[3,128,578]{2,1,0:T(8,128)(2,1)S(1)} %get-tuple-element.49), channel_id=1, source_target_pairs={{0,192},{32,224},{64,256},{96,288},{128,320},{160,352},{192,384},{... | collective-permute-start | bytes 1331720 | tf_op jit(solution)/shard_map/ppermute | solution.py:52
  39.4 4.6 %collective-permute-start.3 = (bf16[3,128,578]{2,1,0:T(8,128)(2,1)S(1)}, bf16[3,128,578]{2,1,0:T(8,128)(2,1)S(1)}, u32[]{:S(2)}, u32[]{:S(2)}) collective-permute-start(bf16[3,128,578]{2,1,0:T(8,128)(2,1)S(1)} %get-tuple-element.49), channel_id=1, source_target_pairs={{0,384},{32,416},{64,448},{96,480},{128,512},{160,544},{192,576},{... | collective-permute-start | bytes 1331720 | tf_op jit(solution)/shard_map/ppermute | solution.py:52
  44.1 3.3 %collective-permute-start.2 = (bf16[3,128,578]{2,1,0:T(8,128)(2,1)S(1)}, bf16[3,128,578]{2,1,0:T(8,128)(2,1)S(1)}, u32[]{:S(2)}, u32[]{:S(2)}) collective-permute-start(bf16[3,128,578]{2,1,0:T(8,128)(2,1)S(1)} %get-tuple-element.49), channel_id=1, source_target_pairs={{0,576},{32,608},{64,640},{96,672},{128,704},{160,736},{192,0},{22... | collective-permute-start | bytes 1331720 | tf_op jit(solution)/shard_map/ppermute | solution.py:52
  47.4 4.9 %collective-permute-done.4 = bf16[3,128,578]{2,1,0:T(8,128)(2,1)S(1)} collective-permute-done((bf16[3,128,578]{2,1,0:T(8,128)(2,1)S(1)}, bf16[3,128,578]{2,1,0:T(8,128)(2,1)S(1)}, u32[]{:S(2)}, u32[]{:S(2)}) %collective-permute-start.4) | collective-permute-done | bytes 443936 | tf_op jit(solution)/shard_map/ppermute | solution.py:52
  52.3 9.7 %collective-permute-done.3 = bf16[3,128,578]{2,1,0:T(8,128)(2,1)S(1)} collective-permute-done((bf16[3,128,578]{2,1,0:T(8,128)(2,1)S(1)}, bf16[3,128,578]{2,1,0:T(8,128)(2,1)S(1)}, u32[]{:S(2)}, u32[]{:S(2)}) %collective-permute-start.3) | collective-permute-done | bytes 443936 | tf_op jit(solution)/shard_map/ppermute | solution.py:52
  65.3 3.1 %copy.112 = bf16[4,3,128,578]{2,0,3,1:T(4,128)(2,1)} copy(bf16[4,3,128,578]{3,2,1,0:T(8,128)(2,1)S(1)} %get-tuple-element.42) | data formatting | bytes 3551232 | tf_op jit(solution)/shard_map/stack | solution.py:74
  74.5 4.8 %copy.113 = bf16[4,3,128,578]{3,2,1,0:T(8,128)(2,1)} copy(bf16[4,3,128,578]{2,0,3,1:T(4,128)(2,1)} %collective-permute-done.5) | data formatting | bytes 3551232 | tf_op jit(solution)/shard_map/ppermute | solution.py:52
  95.6 5.3 %collective-permute-done.6 = f32[2,2,4,3,128,128]{5,4,3,2,1,0:T(8,128)S(1)} collective-permute-done((f32[2,2,4,3,128,128]{5,4,3,2,1,0:T(8,128)S(1)}, f32[2,2,4,3,128,128]{5,4,3,2,1,0:T(8,128)S(1)}, u32[]{:S(2)}, u32[]{:S(2)}) %collective-permute-start.6) | collective-permute-done | bytes 3145760 | tf_op jit(solution)/shard_map/ppermute | solution.py:52
  101.9 4.5 %collective-permute-start.9 = (bf16[2,2,3,128,128]{4,3,2,1,0:T(8,128)(2,1)S(1)}, bf16[2,2,3,128,128]{4,3,2,1,0:T(8,128)(2,1)S(1)}, u32[]{:S(2)}, u32[]{:S(2)}) collective-permute-start(bf16[2,2,3,128,128]{4,3,2,1,0:T(8,128)(2,1)S(1)} %get-tuple-element.44), channel_id=1, source_target_pairs={{0,576},{32,608},{64,640},{96,672},{128,704},{160,736},{192,0},{22... | collective-permute-start | bytes 1179656 | tf_op jit(solution)/shard_map/ppermute | solution.py:52
  106.5 3.7 %collective-permute-start.8 = (bf16[2,2,3,128,128]{4,3,2,1,0:T(8,128)(2,1)S(1)}, bf16[2,2,3,128,128]{4,3,2,1,0:T(8,128)(2,1)S(1)}, u32[]{:S(2)}, u32[]{:S(2)}) collective-permute-start(bf16[2,2,3,128,128]{4,3,2,1,0:T(8,128)(2,1)S(1)} %get-tuple-element.45), channel_id=1, source_target_pairs={{0,384},{32,416},{64,448},{96,480},{128,512},{160,544},{192,576},{... | collective-permute-start | bytes 1179656 | tf_op jit(solution)/shard_map/ppermute | solution.py:52
  112.1 11.5 %collective-permute-done.9 = bf16[2,2,3,128,128]{4,3,2,1,0:T(8,128)(2,1)S(1)} collective-permute-done((bf16[2,2,3,128,128]{4,3,2,1,0:T(8,128)(2,1)S(1)}, bf16[2,2,3,128,128]{4,3,2,1,0:T(8,128)(2,1)S(1)}, u32[]{:S(2)}, u32[]{:S(2)}) %collective-permute-start.9) | collective-permute-done | bytes 393248 | tf_op jit(solution)/shard_map/ppermute | solution.py:52
  123.6 5.6 %collective-permute-done.7 = bf16[2,2,3,128,128]{4,3,2,1,0:T(8,128)(2,1)S(1)} collective-permute-done((bf16[2,2,3,128,128]{4,3,2,1,0:T(8,128)(2,1)S(1)}, bf16[2,2,3,128,128]{4,3,2,1,0:T(8,128)(2,1)S(1)}, u32[]{:S(2)}, u32[]{:S(2)}) %collective-permute-start.7) | collective-permute-done | bytes 393248 | tf_op jit(solution)/shard_map/ppermute | solution.py:52
  129.4 7.1 %collective-permute-start.11 = (bf16[2,2,128,128]{3,2,1,0:T(8,128)(2,1)S(1)}, bf16[2,2,128,128]{3,2,1,0:T(8,128)(2,1)S(1)}, u32[]{:S(2)}, u32[]{:S(2)}) collective-permute-start(bf16[2,2,128,128]{3,2,1,0:T(8,128)(2,1)S(1)} %get-tuple-element.51), channel_id=1, source_target_pairs={{0,128},{32,160},{64,0},{96,32},{128,64},{160,96},{192,320},{224,3... | collective-permute-start | bytes 393224 | tf_op jit(solution)/shard_map/ppermute | solution.py:52
  136.5 2.7 %collective-permute-start.10 = (bf16[2,2,128,128]{3,2,1,0:T(8,128)(2,1)S(1)}, bf16[2,2,128,128]{3,2,1,0:T(8,128)(2,1)S(1)}, u32[]{:S(2)}, u32[]{:S(2)}) collective-permute-start(bf16[2,2,128,128]{3,2,1,0:T(8,128)(2,1)S(1)} %get-tuple-element.50), channel_id=1, source_target_pairs={{0,64},{32,96},{64,128},{96,160},{128,0},{160,32},{192,256},{224,2... | collective-permute-start | bytes 393224 | tf_op jit(solution)/shard_map/ppermute | solution.py:52
  139.2 2.5 %collective-permute-done.11 = bf16[2,2,128,128]{3,2,1,0:T(8,128)(2,1)S(1)} collective-permute-done((bf16[2,2,128,128]{3,2,1,0:T(8,128)(2,1)S(1)}, bf16[2,2,128,128]{3,2,1,0:T(8,128)(2,1)S(1)}, u32[]{:S(2)}, u32[]{:S(2)}) %collective-permute-start.11) | collective-permute-done | bytes 131104 | tf_op jit(solution)/shard_map/ppermute | solution.py:52
  141.7 7.8 %collective-permute-done.10 = bf16[2,2,128,128]{3,2,1,0:T(8,128)(2,1)S(1)} collective-permute-done((bf16[2,2,128,128]{3,2,1,0:T(8,128)(2,1)S(1)}, bf16[2,2,128,128]{3,2,1,0:T(8,128)(2,1)S(1)}, u32[]{:S(2)}, u32[]{:S(2)}) %collective-permute-start.10) | collective-permute-done | bytes 131104 | tf_op jit(solution)/shard_map/ppermute | solution.py:52
  150.4 4.2 %collective-permute-start.13 = (bf16[128,512]{1,0:T(8,128)(2,1)}, bf16[128,512]{1,0:T(8,128)(2,1)}, u32[]{:S(2)}, u32[]{:S(2)}) collective-permute-start(bf16[128,512]{1,0:T(8,128)(2,1)} %convert_element_type.209), channel_id=1, source_target_pairs={{0,64},{32,96},{64,128},{96,160},{128,0},{160,32},{192,256},{224,2... | collective-permute-start | bytes 393224 | tf_op jit(solution)/shard_map/ppermute | solution.py:52
  154.6 5.5 %collective-permute-start.12 = (bf16[128,512]{1,0:T(8,128)(2,1)}, bf16[128,512]{1,0:T(8,128)(2,1)}, u32[]{:S(2)}, u32[]{:S(2)}) collective-permute-start(bf16[128,512]{1,0:T(8,128)(2,1)} %convert_element_type.209), channel_id=1, source_target_pairs={{0,128},{32,160},{64,0},{96,32},{128,64},{160,96},{192,320},{224,3... | collective-permute-start | bytes 393224 | tf_op jit(solution)/shard_map/ppermute | solution.py:52
  163.1 3.2 %collective-permute-start.14 = (bf16[128,512]{1,0:T(8,128)(2,1)}, bf16[128,512]{1,0:T(8,128)(2,1)}, u32[]{:S(2)}, u32[]{:S(2)}) collective-permute-start(bf16[128,512]{1,0:T(8,128)(2,1)} %fusion.20), channel_id=1, source_target_pairs={{0,1},{1,0},{2,3},{3,2},{4,5},{5,4},{6,7},{7,6},{8,9},{9,8},{10,11... | collective-permute-start | bytes 393224 | tf_op jit(solution)/shard_map/ppermute | solution.py:52
  171.3 4.0 %collective-permute-start.18 = (bf16[128,512]{1,0:T(8,128)(2,1)S(1)}, bf16[128,512]{1,0:T(8,128)(2,1)S(1)}, u32[]{:S(2)}, u32[]{:S(2)}) collective-permute-start(bf16[128,512]{1,0:T(8,128)(2,1)S(1)} %convert_add_fusion.2), channel_id=1, source_target_pairs={{0,6},{1,7},{2,0},{3,1},{4,2},{5,3},{6,4},{7,5},{8,14},{9,15},{10,... | collective-permute-start | bytes 393224 | tf_op jit(solution)/shard_map/ppermute | solution.py:52
  175.3 5.9 %collective-permute-start.17 = (bf16[3,128,512]{2,1,0:T(8,128)(2,1)}, bf16[3,128,512]{2,1,0:T(8,128)(2,1)}, u32[]{:S(2)}, u32[]{:S(2)}) collective-permute-start(bf16[3,128,512]{2,1,0:T(8,128)(2,1)} %pad_maximum_fusion.4), channel_id=1, source_target_pairs={{0,192},{32,224},{64,256},{96,288},{128,320},{160,352},{192,384},{... | collective-permute-start | bytes 1179656 | tf_op jit(solution)/shard_map/ppermute | solution.py:52
  181.2 3.6 %collective-permute-start.16 = (bf16[3,128,512]{2,1,0:T(8,128)(2,1)}, bf16[3,128,512]{2,1,0:T(8,128)(2,1)}, u32[]{:S(2)}, u32[]{:S(2)}) collective-permute-start(bf16[3,128,512]{2,1,0:T(8,128)(2,1)} %pad_maximum_fusion.4), channel_id=1, source_target_pairs={{0,384},{32,416},{64,448},{96,480},{128,512},{160,544},{192,576},{... | collective-permute-start | bytes 1179656 | tf_op jit(solution)/shard_map/ppermute | solution.py:52
  184.9 2.9 %collective-permute-start.15 = (bf16[3,128,512]{2,1,0:T(8,128)(2,1)}, bf16[3,128,512]{2,1,0:T(8,128)(2,1)}, u32[]{:S(2)}, u32[]{:S(2)}) collective-permute-start(bf16[3,128,512]{2,1,0:T(8,128)(2,1)} %pad_maximum_fusion.4), channel_id=1, source_target_pairs={{0,576},{32,608},{64,640},{96,672},{128,704},{160,736},{192,0},{22... | collective-permute-start | bytes 1179656 | tf_op jit(solution)/shard_map/ppermute | solution.py:52
  187.7 2.9 %collective-permute-start.19 = (bf16[128,512]{1,0:T(8,128)(2,1)S(1)}, bf16[128,512]{1,0:T(8,128)(2,1)}, u32[]{:S(2)}, u32[]{:S(2)}) collective-permute-start(bf16[128,512]{1,0:T(8,128)(2,1)S(1)} %convert_add_fusion.2), channel_id=1, source_target_pairs={{0,4},{1,5},{2,6},{3,7},{4,0},{5,1},{6,2},{7,3},{8,12},{9,13},{10,... | collective-permute-start | bytes 393224 | tf_op jit(solution)/shard_map/ppermute | solution.py:52
  191.3 5.6 %collective-permute-start.20 = (bf16[128,512]{1,0:T(8,128)(2,1)S(1)}, bf16[128,512]{1,0:T(8,128)(2,1)}, u32[]{:S(2)}, u32[]{:S(2)}) collective-permute-start(bf16[128,512]{1,0:T(8,128)(2,1)S(1)} %convert_add_fusion.2), channel_id=1, source_target_pairs={{0,2},{1,3},{2,4},{3,5},{4,6},{5,7},{6,0},{7,1},{8,10},{9,11},{10,... | collective-permute-start | bytes 393224 | tf_op jit(solution)/shard_map/ppermute | solution.py:52
  198.8 3.6 %collective-permute-done.20 = bf16[128,512]{1,0:T(8,128)(2,1)} collective-permute-done((bf16[128,512]{1,0:T(8,128)(2,1)S(1)}, bf16[128,512]{1,0:T(8,128)(2,1)}, u32[]{:S(2)}, u32[]{:S(2)}) %collective-permute-start.20) | collective-permute-done | bytes 131104 | tf_op jit(solution)/shard_map/ppermute | solution.py:52
  208.0 2.7 %add_bitcast_fusion = f32[512,512]{1,0:T(8,128)} fusion(f32[4,512,512]{2,1,0:T(8,128)S(1)} %convert_convert_fusion, f32[4,512,512]{2,1,0:T(8,128)S(1)} %convert_convert_fusion.1, f32[4,512,512]{2,1,0:T(8,128)S(1)} %convert_convert_fusion.2, pred[]{:T(512)S(6)} %eq.253, pred[]{:T(512)S(6)} %eq.251, pred[]{:T(512)S(6)} %eq.225, pred[]{:T(512)S(6)} %eq.254, ...), kind=kLoop, calls=%fused_computation.43 | loop fusion | flops 13893632 | bytes 13631506 | tf_op jit(solution)/shard_map/add | solution.py:105
  214.1 10.7 %collective-permute-start.22 = (bf16[128,512]{1,0:T(8,128)(2,1)S(1)}, bf16[128,512]{1,0:T(8,128)(2,1)S(1)}, u32[]{:S(2)}, u32[]{:S(2)}) collective-permute-start(bf16[128,512]{1,0:T(8,128)(2,1)S(1)} %copy-done.5), channel_id=1, source_target_pairs={{0,24},{1,25},{2,26},{3,27},{4,28},{5,29},{6,30},{7,31},{8,0},{9,1... | collective-permute-start | bytes 393224 | tf_op jit(solution)/shard_map/ppermute | solution.py:52
  233.1 4.3 %collective-permute-done.23 = bf16[128,512]{1,0:T(8,128)(2,1)S(1)} collective-permute-done((bf16[128,512]{1,0:T(8,128)(2,1)S(1)}, bf16[128,512]{1,0:T(8,128)(2,1)S(1)}, u32[]{:S(2)}, u32[]{:S(2)}) %collective-permute-start.23) | collective-permute-done | bytes 131104 | tf_op jit(solution)/shard_map/ppermute | solution.py:52
  (113 shorter events, 67.6 us)
Async XLA Ops:
  0.6 81.9 %copy-start = (bf16[512,256]{1,0:T(8,128)(2,1)S(1)}, bf16[512,256]{1,0:T(8,128)(2,1)}, u32[]{:S(2)}) copy-start(bf16[512,256]{1,0:T(8,128)(2,1)} %param.16) | copy-start | bytes 786436
  5.4 19.0 %collective-permute-start.1 = (bf16[128,578]{1,0:T(8,128)(2,1)S(1)}, bf16[128,578]{1,0:T(8,128)(2,1)S(1)}, u32[]{:S(2)}, u32[]{:S(2)}) collective-permute-start(bf16[128,578]{1,0:T(8,128)(2,1)S(1)} %pad_maximum_fusion.5), channel_id=1, source_target_pairs={{0,64},{32,96},{64,128},{96,160},{128,0},{160,32},{192,256},{224,2... | collective-permute-start | bytes 443912 | tf_op jit(solution)/shard_map/ppermute | solution.py:52
  16.3 19.6 %collective-permute-start = (bf16[128,578]{1,0:T(8,128)(2,1)S(1)}, bf16[128,578]{1,0:T(8,128)(2,1)S(1)}, u32[]{:S(2)}, u32[]{:S(2)}) collective-permute-start(bf16[128,578]{1,0:T(8,128)(2,1)S(1)} %pad_maximum_fusion.5), channel_id=1, source_target_pairs={{0,128},{32,160},{64,0},{96,32},{128,64},{160,96},{192,320},{224,3... | collective-permute-start | bytes 443912 | tf_op jit(solution)/shard_map/ppermute | solution.py:52
  36.0 16.3 %collective-permute-start.4 = (bf16[3,128,578]{2,1,0:T(8,128)(2,1)S(1)}, bf16[3,128,578]{2,1,0:T(8,128)(2,1)S(1)}, u32[]{:S(2)}, u32[]{:S(2)}) collective-permute-start(bf16[3,128,578]{2,1,0:T(8,128)(2,1)S(1)} %get-tuple-element.49), channel_id=1, source_target_pairs={{0,192},{32,224},{64,256},{96,288},{128,320},{160,352},{192,384},{... | collective-permute-start | bytes 1331720 | tf_op jit(solution)/shard_map/ppermute | solution.py:52
  39.4 22.6 %collective-permute-start.3 = (bf16[3,128,578]{2,1,0:T(8,128)(2,1)S(1)}, bf16[3,128,578]{2,1,0:T(8,128)(2,1)S(1)}, u32[]{:S(2)}, u32[]{:S(2)}) collective-permute-start(bf16[3,128,578]{2,1,0:T(8,128)(2,1)S(1)} %get-tuple-element.49), channel_id=1, source_target_pairs={{0,384},{32,416},{64,448},{96,480},{128,512},{160,544},{192,576},{... | collective-permute-start | bytes 1331720 | tf_op jit(solution)/shard_map/ppermute | solution.py:52
  44.1 19.5 %collective-permute-start.2 = (bf16[3,128,578]{2,1,0:T(8,128)(2,1)S(1)}, bf16[3,128,578]{2,1,0:T(8,128)(2,1)S(1)}, u32[]{:S(2)}, u32[]{:S(2)}) collective-permute-start(bf16[3,128,578]{2,1,0:T(8,128)(2,1)S(1)} %get-tuple-element.49), channel_id=1, source_target_pairs={{0,576},{32,608},{64,640},{96,672},{128,704},{160,736},{192,0},{22... | collective-permute-start | bytes 1331720 | tf_op jit(solution)/shard_map/ppermute | solution.py:52
  65.3 5.2 %copy-start.12 = (bf16[128,256]{1,0:T(8,128)(2,1)S(1)}, bf16[128,256]{1,0:T(8,128)(2,1)}, u32[]{:S(2)}) copy-start(bf16[128,256]{1,0:T(8,128)(2,1)} %param.11) | copy-start | bytes 196612
  65.3 5.3 %copy-start.14 = (bf16[128,128]{1,0:T(8,128)(2,1)S(1)}, bf16[128,128]{1,0:T(8,128)(2,1)}, u32[]{:S(2)}) copy-start(bf16[128,128]{1,0:T(8,128)(2,1)} %param.10) | copy-start | bytes 98308
  65.3 6.0 %copy-start.13 = (bf16[128,256]{1,0:T(8,128)(2,1)S(1)}, bf16[128,256]{1,0:T(8,128)(2,1)}, u32[]{:S(2)}) copy-start(bf16[128,256]{1,0:T(8,128)(2,1)} %param.9) | copy-start | bytes 196612
  68.4 10.8 %copy-start.2 = (bf16[1,4,3,128,578]{4,3,2,1,0:T(8,128)(2,1)S(1)}, bf16[1,4,3,128,578]{4,3,2,1,0:T(8,128)(2,1)}, u32[]{:S(2)}) copy-start(bf16[1,4,3,128,578]{4,3,2,1,0:T(8,128)(2,1)} %get-tuple-element.41) | copy-start | bytes 5326852
  68.4 6.1 %collective-permute-start.5 = (bf16[4,3,128,578]{2,0,3,1:T(4,128)(2,1)}, bf16[4,3,128,578]{2,0,3,1:T(4,128)(2,1)}, u32[]{:S(2)}, u32[]{:S(2)}) collective-permute-start(bf16[4,3,128,578]{2,0,3,1:T(4,128)(2,1)} %copy.112), channel_id=1, source_target_pairs={{0,32},{32,0},{64,96},{96,64},{128,160},{160,128},{192,224},{224,1... | collective-permute-start | bytes 5326856 | tf_op jit(solution)/shard_map/ppermute | solution.py:52
  93.4 7.6 %collective-permute-start.6 = (f32[2,2,4,3,128,128]{5,4,3,2,1,0:T(8,128)S(1)}, f32[2,2,4,3,128,128]{5,4,3,2,1,0:T(8,128)S(1)}, u32[]{:S(2)}, u32[]{:S(2)}) collective-permute-start(f32[2,2,4,3,128,128]{5,4,3,2,1,0:T(8,128)S(1)} %slice_bitcast_fusion), channel_id=1, source_target_pairs={{0,32},{32,0},{64,96},{96,64},{128,160},{160,128},{192,224},{224,1... | collective-permute-start | bytes 9437192 | tf_op jit(solution)/shard_map/ppermute | solution.py:52
  101.9 21.7 %collective-permute-start.9 = (bf16[2,2,3,128,128]{4,3,2,1,0:T(8,128)(2,1)S(1)}, bf16[2,2,3,128,128]{4,3,2,1,0:T(8,128)(2,1)S(1)}, u32[]{:S(2)}, u32[]{:S(2)}) collective-permute-start(bf16[2,2,3,128,128]{4,3,2,1,0:T(8,128)(2,1)S(1)} %get-tuple-element.44), channel_id=1, source_target_pairs={{0,576},{32,608},{64,640},{96,672},{128,704},{160,736},{192,0},{22... | collective-permute-start | bytes 1179656 | tf_op jit(solution)/shard_map/ppermute | solution.py:52
  106.5 17.1 %collective-permute-start.8 = (bf16[2,2,3,128,128]{4,3,2,1,0:T(8,128)(2,1)S(1)}, bf16[2,2,3,128,128]{4,3,2,1,0:T(8,128)(2,1)S(1)}, u32[]{:S(2)}, u32[]{:S(2)}) collective-permute-start(bf16[2,2,3,128,128]{4,3,2,1,0:T(8,128)(2,1)S(1)} %get-tuple-element.45), channel_id=1, source_target_pairs={{0,384},{32,416},{64,448},{96,480},{128,512},{160,544},{192,576},{... | collective-permute-start | bytes 1179656 | tf_op jit(solution)/shard_map/ppermute | solution.py:52
  110.2 19.0 %collective-permute-start.7 = (bf16[2,2,3,128,128]{4,3,2,1,0:T(8,128)(2,1)S(1)}, bf16[2,2,3,128,128]{4,3,2,1,0:T(8,128)(2,1)S(1)}, u32[]{:S(2)}, u32[]{:S(2)}) collective-permute-start(bf16[2,2,3,128,128]{4,3,2,1,0:T(8,128)(2,1)S(1)} %get-tuple-element.43), channel_id=1, source_target_pairs={{0,192},{32,224},{64,256},{96,288},{128,320},{160,352},{192,384},{... | collective-permute-start | bytes 1179656 | tf_op jit(solution)/shard_map/ppermute | solution.py:52
  129.4 12.2 %collective-permute-start.11 = (bf16[2,2,128,128]{3,2,1,0:T(8,128)(2,1)S(1)}, bf16[2,2,128,128]{3,2,1,0:T(8,128)(2,1)S(1)}, u32[]{:S(2)}, u32[]{:S(2)}) collective-permute-start(bf16[2,2,128,128]{3,2,1,0:T(8,128)(2,1)S(1)} %get-tuple-element.51), channel_id=1, source_target_pairs={{0,128},{32,160},{64,0},{96,32},{128,64},{160,96},{192,320},{224,3... | collective-permute-start | bytes 393224 | tf_op jit(solution)/shard_map/ppermute | solution.py:52
  136.5 13.0 %collective-permute-start.10 = (bf16[2,2,128,128]{3,2,1,0:T(8,128)(2,1)S(1)}, bf16[2,2,128,128]{3,2,1,0:T(8,128)(2,1)S(1)}, u32[]{:S(2)}, u32[]{:S(2)}) collective-permute-start(bf16[2,2,128,128]{3,2,1,0:T(8,128)(2,1)S(1)} %get-tuple-element.50), channel_id=1, source_target_pairs={{0,64},{32,96},{64,128},{96,160},{128,0},{160,32},{192,256},{224,2... | collective-permute-start | bytes 393224 | tf_op jit(solution)/shard_map/ppermute | solution.py:52
  150.4 16.7 %collective-permute-start.13 = (bf16[128,512]{1,0:T(8,128)(2,1)}, bf16[128,512]{1,0:T(8,128)(2,1)}, u32[]{:S(2)}, u32[]{:S(2)}) collective-permute-start(bf16[128,512]{1,0:T(8,128)(2,1)} %convert_element_type.209), channel_id=1, source_target_pairs={{0,64},{32,96},{64,128},{96,160},{128,0},{160,32},{192,256},{224,2... | collective-permute-start | bytes 393224 | tf_op jit(solution)/shard_map/ppermute | solution.py:52
  154.6 13.8 %collective-permute-start.12 = (bf16[128,512]{1,0:T(8,128)(2,1)}, bf16[128,512]{1,0:T(8,128)(2,1)}, u32[]{:S(2)}, u32[]{:S(2)}) collective-permute-start(bf16[128,512]{1,0:T(8,128)(2,1)} %convert_element_type.209), channel_id=1, source_target_pairs={{0,128},{32,160},{64,0},{96,32},{128,64},{160,96},{192,320},{224,3... | collective-permute-start | bytes 393224 | tf_op jit(solution)/shard_map/ppermute | solution.py:52
  163.1 7.2 %collective-permute-start.14 = (bf16[128,512]{1,0:T(8,128)(2,1)}, bf16[128,512]{1,0:T(8,128)(2,1)}, u32[]{:S(2)}, u32[]{:S(2)}) collective-permute-start(bf16[128,512]{1,0:T(8,128)(2,1)} %fusion.20), channel_id=1, source_target_pairs={{0,1},{1,0},{2,3},{3,2},{4,5},{5,4},{6,7},{7,6},{8,9},{9,8},{10,11... | collective-permute-start | bytes 393224 | tf_op jit(solution)/shard_map/ppermute | solution.py:52
  171.3 19.4 %collective-permute-start.18 = (bf16[128,512]{1,0:T(8,128)(2,1)S(1)}, bf16[128,512]{1,0:T(8,128)(2,1)S(1)}, u32[]{:S(2)}, u32[]{:S(2)}) collective-permute-start(bf16[128,512]{1,0:T(8,128)(2,1)S(1)} %convert_add_fusion.2), channel_id=1, source_target_pairs={{0,6},{1,7},{2,0},{3,1},{4,2},{5,3},{6,4},{7,5},{8,14},{9,15},{10,... | collective-permute-start | bytes 393224 | tf_op jit(solution)/shard_map/ppermute | solution.py:52
  175.3 28.8 %collective-permute-start.17 = (bf16[3,128,512]{2,1,0:T(8,128)(2,1)}, bf16[3,128,512]{2,1,0:T(8,128)(2,1)}, u32[]{:S(2)}, u32[]{:S(2)}) collective-permute-start(bf16[3,128,512]{2,1,0:T(8,128)(2,1)} %pad_maximum_fusion.4), channel_id=1, source_target_pairs={{0,192},{32,224},{64,256},{96,288},{128,320},{160,352},{192,384},{... | collective-permute-start | bytes 1179656 | tf_op jit(solution)/shard_map/ppermute | solution.py:52
  181.2 22.9 %collective-permute-start.16 = (bf16[3,128,512]{2,1,0:T(8,128)(2,1)}, bf16[3,128,512]{2,1,0:T(8,128)(2,1)}, u32[]{:S(2)}, u32[]{:S(2)}) collective-permute-start(bf16[3,128,512]{2,1,0:T(8,128)(2,1)} %pad_maximum_fusion.4), channel_id=1, source_target_pairs={{0,384},{32,416},{64,448},{96,480},{128,512},{160,544},{192,576},{... | collective-permute-start | bytes 1179656 | tf_op jit(solution)/shard_map/ppermute | solution.py:52
  184.9 19.3 %collective-permute-start.15 = (bf16[3,128,512]{2,1,0:T(8,128)(2,1)}, bf16[3,128,512]{2,1,0:T(8,128)(2,1)}, u32[]{:S(2)}, u32[]{:S(2)}) collective-permute-start(bf16[3,128,512]{2,1,0:T(8,128)(2,1)} %pad_maximum_fusion.4), channel_id=1, source_target_pairs={{0,576},{32,608},{64,640},{96,672},{128,704},{160,736},{192,0},{22... | collective-permute-start | bytes 1179656 | tf_op jit(solution)/shard_map/ppermute | solution.py:52
  187.7 11.1 %collective-permute-start.19 = (bf16[128,512]{1,0:T(8,128)(2,1)S(1)}, bf16[128,512]{1,0:T(8,128)(2,1)}, u32[]{:S(2)}, u32[]{:S(2)}) collective-permute-start(bf16[128,512]{1,0:T(8,128)(2,1)S(1)} %convert_add_fusion.2), channel_id=1, source_target_pairs={{0,4},{1,5},{2,6},{3,7},{4,0},{5,1},{6,2},{7,3},{8,12},{9,13},{10,... | collective-permute-start | bytes 393224 | tf_op jit(solution)/shard_map/ppermute | solution.py:52
  191.3 11.1 %collective-permute-start.20 = (bf16[128,512]{1,0:T(8,128)(2,1)S(1)}, bf16[128,512]{1,0:T(8,128)(2,1)}, u32[]{:S(2)}, u32[]{:S(2)}) collective-permute-start(bf16[128,512]{1,0:T(8,128)(2,1)S(1)} %convert_add_fusion.2), channel_id=1, source_target_pairs={{0,2},{1,3},{2,4},{3,5},{4,6},{5,7},{6,0},{7,1},{8,10},{9,11},{10,... | collective-permute-start | bytes 393224 | tf_op jit(solution)/shard_map/ppermute | solution.py:52
  197.3 5.1 %copy-start.11 = (bf16[128,512]{1,0:T(8,128)(2,1)S(1)}, bf16[128,512]{1,0:T(8,128)(2,1)}, u32[]{:S(2)}) copy-start(bf16[128,512]{1,0:T(8,128)(2,1)} %copy-done.10) | copy-start | bytes 393220
  210.7 26.8 %collective-permute-start.21 = (f32[512,512]{1,0:T(8,128)}, f32[512,512]{1,0:T(8,128)}, u32[]{:S(2)}, u32[]{:S(2)}) collective-permute-start(f32[512,512]{1,0:T(8,128)} %add_bitcast_fusion), channel_id=1, source_target_pairs={{0,32},{32,0},{64,96},{96,64},{128,160},{160,128},{192,224},{224,1... | collective-permute-start | bytes 3145736 | tf_op jit(solution)/shard_map/ppermute | solution.py:52
  214.1 25.2 %copy-start.4 = (f32[128,4,128]{2,1,0:T(4,128)S(1)}, f32[128,4,128]{2,1,0:T(4,128)}, u32[]{:S(2)}) copy-start(f32[128,4,128]{2,1,0:T(4,128)} %copy-done.3) | copy-start | bytes 786436
  214.1 19.0 %collective-permute-start.22 = (bf16[128,512]{1,0:T(8,128)(2,1)S(1)}, bf16[128,512]{1,0:T(8,128)(2,1)S(1)}, u32[]{:S(2)}, u32[]{:S(2)}) collective-permute-start(bf16[128,512]{1,0:T(8,128)(2,1)S(1)} %copy-done.5), channel_id=1, source_target_pairs={{0,24},{1,25},{2,26},{3,27},{4,28},{5,29},{6,30},{7,31},{8,0},{9,1... | collective-permute-start | bytes 393224 | tf_op jit(solution)/shard_map/ppermute | solution.py:52
  224.8 12.6 %collective-permute-start.23 = (bf16[128,512]{1,0:T(8,128)(2,1)S(1)}, bf16[128,512]{1,0:T(8,128)(2,1)S(1)}, u32[]{:S(2)}, u32[]{:S(2)}) collective-permute-start(bf16[128,512]{1,0:T(8,128)(2,1)S(1)} %copy-done.5), channel_id=1, source_target_pairs={{0,16},{1,17},{2,18},{3,19},{4,20},{5,21},{6,22},{7,23},{8,24},{9,... | collective-permute-start | bytes 393224 | tf_op jit(solution)/shard_map/ppermute | solution.py:52
  226.7 10.6 %collective-permute-start.24 = (bf16[128,512]{1,0:T(8,128)(2,1)S(1)}, bf16[128,512]{1,0:T(8,128)(2,1)S(1)}, u32[]{:S(2)}, u32[]{:S(2)}) collective-permute-start(bf16[128,512]{1,0:T(8,128)(2,1)S(1)} %copy-done.5), channel_id=1, source_target_pairs={{0,8},{1,9},{2,10},{3,11},{4,12},{5,13},{6,14},{7,15},{8,16},{9,17... | collective-permute-start | bytes 393224 | tf_op jit(solution)/shard_map/ppermute | solution.py:52
  (9 other events, 15.7 us)

commit v7 on v6

--- a/solution.py
+++ b/solution.py
@@ -82,17 +82,13 @@
 
 
 def scatter_relative(data, axis, lead, wire):
-    level = 0
     for radix, stride in reversed(gather_order(lax.axis_size(axis))):
         head = (slice(None),) * lead
         total = data[head + (0,)]
         for by in range(1, radix):
-            part = data[head + (by,)]
-            if level > 0:
-                part = part.astype(wire)
+            part = data[head + (by,)].astype(wire)
             total = total + shift_digit(part, axis, radix, stride, by).astype(jnp.float32)
         data = total
-        level += 1
     return data
 
 

time: 243 us -> 241 us (level)
  no operation moved by 1% of the time
where the time goes in v7:
time: 241 us; the launch traced here: 239 us
  starting transfers between devices  107 us (44%)
  waiting for transfers between devices  71.3 us (30%)
  other arithmetic  23.9 us (10%)
  local copies, waits for them, and re-layouts  21.2 us (9%)
  matrix products  13.5 us (6%)
    ppermute x25, starting transfers between devices, shift_digit(): return lax.ppermute(x, axis, pairs)  107 us
    ppermute x25, waiting for transfers between devices, shift_digit(): return lax.ppermute(x, axis, pairs)  71.3 us
    another operation x6, other arithmetic, gather_step(): return jnp.stack(pieces, axis=0)  7.43 us
    unnamed x39, local copies, waits for them, and re-layouts  5.07 us
  transfers between devices with their start and end apart: 25, of which 15 were waited for; matrix products, arithmetic and copies ran while one was open for 7% of the time, Pallas kernels for 0%

profile of v7, /device:TPU:56, one launch (start us, length us, event | category | flops | bytes accessed | tf_op | source)
XLA Modules:
  0.0 238.7 jit_solution(482837573866517609)
XLA Ops:
  5.4 10.9 %collective-permute-start.1 = (bf16[128,578]{1,0:T(8,128)(2,1)S(1)}, bf16[128,578]{1,0:T(8,128)(2,1)S(1)}, u32[]{:S(2)}, u32[]{:S(2)}) collective-permute-start(bf16[128,578]{1,0:T(8,128)(2,1)S(1)} %pad_maximum_fusion.5), channel_id=1, source_target_pairs={{0,64},{32,96},{64,128},{96,160},{128,0},{160,32},{192,256},{224,2... | collective-permute-start | bytes 443912 | tf_op jit(solution)/shard_map/ppermute | solution.py:52
  16.3 5.6 %collective-permute-start = (bf16[128,578]{1,0:T(8,128)(2,1)S(1)}, bf16[128,578]{1,0:T(8,128)(2,1)S(1)}, u32[]{:S(2)}, u32[]{:S(2)}) collective-permute-start(bf16[128,578]{1,0:T(8,128)(2,1)S(1)} %pad_maximum_fusion.5), channel_id=1, source_target_pairs={{0,128},{32,160},{64,0},{96,32},{128,64},{160,96},{192,320},{224,3... | collective-permute-start | bytes 443912 | tf_op jit(solution)/shard_map/ppermute | solution.py:52
  24.4 11.5 %collective-permute-done = bf16[128,578]{1,0:T(8,128)(2,1)S(1)} collective-permute-done((bf16[128,578]{1,0:T(8,128)(2,1)S(1)}, bf16[128,578]{1,0:T(8,128)(2,1)S(1)}, u32[]{:S(2)}, u32[]{:S(2)}) %collective-permute-start) | collective-permute-done | bytes 148000 | tf_op jit(solution)/shard_map/ppermute | solution.py:52
  36.0 3.4 %collective-permute-start.4 = (bf16[3,128,578]{2,1,0:T(8,128)(2,1)S(1)}, bf16[3,128,578]{2,1,0:T(8,128)(2,1)S(1)}, u32[]{:S(2)}, u32[]{:S(2)}) collective-permute-start(bf16[3,128,578]{2,1,0:T(8,128)(2,1)S(1)} %get-tuple-element.49), channel_id=1, source_target_pairs={{0,192},{32,224},{64,256},{96,288},{128,320},{160,352},{192,384},{... | collective-permute-start | bytes 1331720 | tf_op jit(solution)/shard_map/ppermute | solution.py:52
  39.4 4.6 %collective-permute-start.3 = (bf16[3,128,578]{2,1,0:T(8,128)(2,1)S(1)}, bf16[3,128,578]{2,1,0:T(8,128)(2,1)S(1)}, u32[]{:S(2)}, u32[]{:S(2)}) collective-permute-start(bf16[3,128,578]{2,1,0:T(8,128)(2,1)S(1)} %get-tuple-element.49), channel_id=1, source_target_pairs={{0,384},{32,416},{64,448},{96,480},{128,512},{160,544},{192,576},{... | collective-permute-start | bytes 1331720 | tf_op jit(solution)/shard_map/ppermute | solution.py:52
  44.1 3.3 %collective-permute-start.2 = (bf16[3,128,578]{2,1,0:T(8,128)(2,1)S(1)}, bf16[3,128,578]{2,1,0:T(8,128)(2,1)S(1)}, u32[]{:S(2)}, u32[]{:S(2)}) collective-permute-start(bf16[3,128,578]{2,1,0:T(8,128)(2,1)S(1)} %get-tuple-element.49), channel_id=1, source_target_pairs={{0,576},{32,608},{64,640},{96,672},{128,704},{160,736},{192,0},{22... | collective-permute-start | bytes 1331720 | tf_op jit(solution)/shard_map/ppermute | solution.py:52
  47.4 4.9 %collective-permute-done.4 = bf16[3,128,578]{2,1,0:T(8,128)(2,1)S(1)} collective-permute-done((bf16[3,128,578]{2,1,0:T(8,128)(2,1)S(1)}, bf16[3,128,578]{2,1,0:T(8,128)(2,1)S(1)}, u32[]{:S(2)}, u32[]{:S(2)}) %collective-permute-start.4) | collective-permute-done | bytes 443936 | tf_op jit(solution)/shard_map/ppermute | solution.py:52
  52.3 9.7 %collective-permute-done.3 = bf16[3,128,578]{2,1,0:T(8,128)(2,1)S(1)} collective-permute-done((bf16[3,128,578]{2,1,0:T(8,128)(2,1)S(1)}, bf16[3,128,578]{2,1,0:T(8,128)(2,1)S(1)}, u32[]{:S(2)}, u32[]{:S(2)}) %collective-permute-start.3) | collective-permute-done | bytes 443936 | tf_op jit(solution)/shard_map/ppermute | solution.py:52
  65.3 3.1 %copy.112 = bf16[4,3,128,578]{2,0,3,1:T(4,128)(2,1)} copy(bf16[4,3,128,578]{3,2,1,0:T(8,128)(2,1)S(1)} %get-tuple-element.42) | data formatting | bytes 3551232 | tf_op jit(solution)/shard_map/stack | solution.py:74
  74.5 4.8 %copy.113 = bf16[4,3,128,578]{3,2,1,0:T(8,128)(2,1)} copy(bf16[4,3,128,578]{2,0,3,1:T(4,128)(2,1)} %collective-permute-done.5) | data formatting | bytes 3551232 | tf_op jit(solution)/shard_map/ppermute | solution.py:52
  95.7 3.1 %collective-permute-done.6 = bf16[2,2,4,3,128,128]{5,4,3,2,1,0:T(8,128)(2,1)S(1)} collective-permute-done((bf16[2,2,4,3,128,128]{5,4,3,2,1,0:T(8,128)(2,1)S(1)}, bf16[2,2,4,3,128,128]{5,4,3,2,1,0:T(8,128)(2,1)S(1)}, u32[]{:S(2)}, u32[]{:S(2)}) %collective-permute-start.6) | collective-permute-done | bytes 1572896 | tf_op jit(solution)/shard_map/ppermute | solution.py:52
  99.6 4.5 %collective-permute-start.9 = (bf16[2,2,3,128,128]{4,3,2,1,0:T(8,128)(2,1)S(1)}, bf16[2,2,3,128,128]{4,3,2,1,0:T(8,128)(2,1)S(1)}, u32[]{:S(2)}, u32[]{:S(2)}) collective-permute-start(bf16[2,2,3,128,128]{4,3,2,1,0:T(8,128)(2,1)S(1)} %get-tuple-element.44), channel_id=1, source_target_pairs={{0,576},{32,608},{64,640},{96,672},{128,704},{160,736},{192,0},{22... | collective-permute-start | bytes 1179656 | tf_op jit(solution)/shard_map/ppermute | solution.py:52
  104.1 3.7 %collective-permute-start.8 = (bf16[2,2,3,128,128]{4,3,2,1,0:T(8,128)(2,1)S(1)}, bf16[2,2,3,128,128]{4,3,2,1,0:T(8,128)(2,1)S(1)}, u32[]{:S(2)}, u32[]{:S(2)}) collective-permute-start(bf16[2,2,3,128,128]{4,3,2,1,0:T(8,128)(2,1)S(1)} %get-tuple-element.45), channel_id=1, source_target_pairs={{0,384},{32,416},{64,448},{96,480},{128,512},{160,544},{192,576},{... | collective-permute-start | bytes 1179656 | tf_op jit(solution)/shard_map/ppermute | solution.py:52
  109.8 11.5 %collective-permute-done.9 = bf16[2,2,3,128,128]{4,3,2,1,0:T(8,128)(2,1)S(1)} collective-permute-done((bf16[2,2,3,128,128]{4,3,2,1,0:T(8,128)(2,1)S(1)}, bf16[2,2,3,128,128]{4,3,2,1,0:T(8,128)(2,1)S(1)}, u32[]{:S(2)}, u32[]{:S(2)}) %collective-permute-start.9) | collective-permute-done | bytes 393248 | tf_op jit(solution)/shard_map/ppermute | solution.py:52
  121.3 5.6 %collective-permute-done.7 = bf16[2,2,3,128,128]{4,3,2,1,0:T(8,128)(2,1)S(1)} collective-permute-done((bf16[2,2,3,128,128]{4,3,2,1,0:T(8,128)(2,1)S(1)}, bf16[2,2,3,128,128]{4,3,2,1,0:T(8,128)(2,1)S(1)}, u32[]{:S(2)}, u32[]{:S(2)}) %collective-permute-start.7) | collective-permute-done | bytes 393248 | tf_op jit(solution)/shard_map/ppermute | solution.py:52
  127.1 7.1 %collective-permute-start.11 = (bf16[2,2,128,128]{3,2,1,0:T(8,128)(2,1)S(1)}, bf16[2,2,128,128]{3,2,1,0:T(8,128)(2,1)S(1)}, u32[]{:S(2)}, u32[]{:S(2)}) collective-permute-start(bf16[2,2,128,128]{3,2,1,0:T(8,128)(2,1)S(1)} %get-tuple-element.51), channel_id=1, source_target_pairs={{0,128},{32,160},{64,0},{96,32},{128,64},{160,96},{192,320},{224,3... | collective-permute-start | bytes 393224 | tf_op jit(solution)/shard_map/ppermute | solution.py:52
  134.2 2.7 %collective-permute-start.10 = (bf16[2,2,128,128]{3,2,1,0:T(8,128)(2,1)S(1)}, bf16[2,2,128,128]{3,2,1,0:T(8,128)(2,1)S(1)}, u32[]{:S(2)}, u32[]{:S(2)}) collective-permute-start(bf16[2,2,128,128]{3,2,1,0:T(8,128)(2,1)S(1)} %get-tuple-element.50), channel_id=1, source_target_pairs={{0,64},{32,96},{64,128},{96,160},{128,0},{160,32},{192,256},{224,2... | collective-permute-start | bytes 393224 | tf_op jit(solution)/shard_map/ppermute | solution.py:52
  136.9 2.5 %collective-permute-done.11 = bf16[2,2,128,128]{3,2,1,0:T(8,128)(2,1)S(1)} collective-permute-done((bf16[2,2,128,128]{3,2,1,0:T(8,128)(2,1)S(1)}, bf16[2,2,128,128]{3,2,1,0:T(8,128)(2,1)S(1)}, u32[]{:S(2)}, u32[]{:S(2)}) %collective-permute-start.11) | collective-permute-done | bytes 131104 | tf_op jit(solution)/shard_map/ppermute | solution.py:52
  139.3 7.8 %collective-permute-done.10 = bf16[2,2,128,128]{3,2,1,0:T(8,128)(2,1)S(1)} collective-permute-done((bf16[2,2,128,128]{3,2,1,0:T(8,128)(2,1)S(1)}, bf16[2,2,128,128]{3,2,1,0:T(8,128)(2,1)S(1)}, u32[]{:S(2)}, u32[]{:S(2)}) %collective-permute-start.10) | collective-permute-done | bytes 131104 | tf_op jit(solution)/shard_map/ppermute | solution.py:52
  148.1 4.2 %collective-permute-start.13 = (bf16[128,512]{1,0:T(8,128)(2,1)}, bf16[128,512]{1,0:T(8,128)(2,1)}, u32[]{:S(2)}, u32[]{:S(2)}) collective-permute-start(bf16[128,512]{1,0:T(8,128)(2,1)} %convert_element_type.218), channel_id=1, source_target_pairs={{0,64},{32,96},{64,128},{96,160},{128,0},{160,32},{192,256},{224,2... | collective-permute-start | bytes 393224 | tf_op jit(solution)/shard_map/ppermute | solution.py:52
  152.3 5.5 %collective-permute-start.12 = (bf16[128,512]{1,0:T(8,128)(2,1)}, bf16[128,512]{1,0:T(8,128)(2,1)}, u32[]{:S(2)}, u32[]{:S(2)}) collective-permute-start(bf16[128,512]{1,0:T(8,128)(2,1)} %convert_element_type.218), channel_id=1, source_target_pairs={{0,128},{32,160},{64,0},{96,32},{128,64},{160,96},{192,320},{224,3... | collective-permute-start | bytes 393224 | tf_op jit(solution)/shard_map/ppermute | solution.py:52
  160.8 3.2 %collective-permute-start.14 = (bf16[128,512]{1,0:T(8,128)(2,1)}, bf16[128,512]{1,0:T(8,128)(2,1)}, u32[]{:S(2)}, u32[]{:S(2)}) collective-permute-start(bf16[128,512]{1,0:T(8,128)(2,1)} %fusion.21), channel_id=1, source_target_pairs={{0,1},{1,0},{2,3},{3,2},{4,5},{5,4},{6,7},{7,6},{8,9},{9,8},{10,11... | collective-permute-start | bytes 393224 | tf_op jit(solution)/shard_map/ppermute | solution.py:52
  169.0 4.0 %collective-permute-start.18 = (bf16[128,512]{1,0:T(8,128)(2,1)S(1)}, bf16[128,512]{1,0:T(8,128)(2,1)S(1)}, u32[]{:S(2)}, u32[]{:S(2)}) collective-permute-start(bf16[128,512]{1,0:T(8,128)(2,1)S(1)} %convert_add_fusion.2), channel_id=1, source_target_pairs={{0,6},{1,7},{2,0},{3,1},{4,2},{5,3},{6,4},{7,5},{8,14},{9,15},{10,... | collective-permute-start | bytes 393224 | tf_op jit(solution)/shard_map/ppermute | solution.py:52
  173.0 5.9 %collective-permute-start.17 = (bf16[3,128,512]{2,1,0:T(8,128)(2,1)}, bf16[3,128,512]{2,1,0:T(8,128)(2,1)}, u32[]{:S(2)}, u32[]{:S(2)}) collective-permute-start(bf16[3,128,512]{2,1,0:T(8,128)(2,1)} %pad_maximum_fusion.4), channel_id=1, source_target_pairs={{0,192},{32,224},{64,256},{96,288},{128,320},{160,352},{192,384},{... | collective-permute-start | bytes 1179656 | tf_op jit(solution)/shard_map/ppermute | solution.py:52
  178.9 3.6 %collective-permute-start.16 = (bf16[3,128,512]{2,1,0:T(8,128)(2,1)}, bf16[3,128,512]{2,1,0:T(8,128)(2,1)}, u32[]{:S(2)}, u32[]{:S(2)}) collective-permute-start(bf16[3,128,512]{2,1,0:T(8,128)(2,1)} %pad_maximum_fusion.4), channel_id=1, source_target_pairs={{0,384},{32,416},{64,448},{96,480},{128,512},{160,544},{192,576},{... | collective-permute-start | bytes 1179656 | tf_op jit(solution)/shard_map/ppermute | solution.py:52
  182.5 2.9 %collective-permute-start.15 = (bf16[3,128,512]{2,1,0:T(8,128)(2,1)}, bf16[3,128,512]{2,1,0:T(8,128)(2,1)}, u32[]{:S(2)}, u32[]{:S(2)}) collective-permute-start(bf16[3,128,512]{2,1,0:T(8,128)(2,1)} %pad_maximum_fusion.4), channel_id=1, source_target_pairs={{0,576},{32,608},{64,640},{96,672},{128,704},{160,736},{192,0},{22... | collective-permute-start | bytes 1179656 | tf_op jit(solution)/shard_map/ppermute | solution.py:52
  185.4 2.9 %collective-permute-start.19 = (bf16[128,512]{1,0:T(8,128)(2,1)S(1)}, bf16[128,512]{1,0:T(8,128)(2,1)}, u32[]{:S(2)}, u32[]{:S(2)}) collective-permute-start(bf16[128,512]{1,0:T(8,128)(2,1)S(1)} %convert_add_fusion.2), channel_id=1, source_target_pairs={{0,4},{1,5},{2,6},{3,7},{4,0},{5,1},{6,2},{7,3},{8,12},{9,13},{10,... | collective-permute-start | bytes 393224 | tf_op jit(solution)/shard_map/ppermute | solution.py:52
  189.0 5.6 %collective-permute-start.20 = (bf16[128,512]{1,0:T(8,128)(2,1)S(1)}, bf16[128,512]{1,0:T(8,128)(2,1)}, u32[]{:S(2)}, u32[]{:S(2)}) collective-permute-start(bf16[128,512]{1,0:T(8,128)(2,1)S(1)} %convert_add_fusion.2), channel_id=1, source_target_pairs={{0,2},{1,3},{2,4},{3,5},{4,6},{5,7},{6,0},{7,1},{8,10},{9,11},{10,... | collective-permute-start | bytes 393224 | tf_op jit(solution)/shard_map/ppermute | solution.py:52
  196.5 3.6 %collective-permute-done.20 = bf16[128,512]{1,0:T(8,128)(2,1)} collective-permute-done((bf16[128,512]{1,0:T(8,128)(2,1)S(1)}, bf16[128,512]{1,0:T(8,128)(2,1)}, u32[]{:S(2)}, u32[]{:S(2)}) %collective-permute-start.20) | collective-permute-done | bytes 131104 | tf_op jit(solution)/shard_map/ppermute | solution.py:52
  205.7 2.7 %add_bitcast_fusion = f32[512,512]{1,0:T(8,128)} fusion(f32[4,512,512]{2,1,0:T(8,128)S(1)} %convert_convert_fusion, f32[4,512,512]{2,1,0:T(8,128)S(1)} %convert_convert_fusion.1, f32[4,512,512]{2,1,0:T(8,128)S(1)} %convert_convert_fusion.2, pred[]{:T(512)S(6)} %eq.253, pred[]{:T(512)S(6)} %eq.251, pred[]{:T(512)S(6)} %eq.225, pred[]{:T(512)S(6)} %eq.254, ...), kind=kLoop, calls=%fused_computation.44 | loop fusion | flops 13893632 | bytes 13631506 | tf_op jit(solution)/shard_map/add | solution.py:101
  211.8 10.7 %collective-permute-start.22 = (bf16[128,512]{1,0:T(8,128)(2,1)S(1)}, bf16[128,512]{1,0:T(8,128)(2,1)S(1)}, u32[]{:S(2)}, u32[]{:S(2)}) collective-permute-start(bf16[128,512]{1,0:T(8,128)(2,1)S(1)} %copy-done.5), channel_id=1, source_target_pairs={{0,24},{1,25},{2,26},{3,27},{4,28},{5,29},{6,30},{7,31},{8,0},{9,1... | collective-permute-start | bytes 393224 | tf_op jit(solution)/shard_map/ppermute | solution.py:52
  230.8 4.3 %collective-permute-done.23 = bf16[128,512]{1,0:T(8,128)(2,1)S(1)} collective-permute-done((bf16[128,512]{1,0:T(8,128)(2,1)S(1)}, bf16[128,512]{1,0:T(8,128)(2,1)S(1)}, u32[]{:S(2)}, u32[]{:S(2)}) %collective-permute-start.23) | collective-permute-done | bytes 131104 | tf_op jit(solution)/shard_map/ppermute | solution.py:52
  (113 shorter events, 67.5 us)
Async XLA Ops:
  0.6 81.9 %copy-start = (bf16[512,256]{1,0:T(8,128)(2,1)S(1)}, bf16[512,256]{1,0:T(8,128)(2,1)}, u32[]{:S(2)}) copy-start(bf16[512,256]{1,0:T(8,128)(2,1)} %param.16) | copy-start | bytes 786436
  5.4 19.0 %collective-permute-start.1 = (bf16[128,578]{1,0:T(8,128)(2,1)S(1)}, bf16[128,578]{1,0:T(8,128)(2,1)S(1)}, u32[]{:S(2)}, u32[]{:S(2)}) collective-permute-start(bf16[128,578]{1,0:T(8,128)(2,1)S(1)} %pad_maximum_fusion.5), channel_id=1, source_target_pairs={{0,64},{32,96},{64,128},{96,160},{128,0},{160,32},{192,256},{224,2... | collective-permute-start | bytes 443912 | tf_op jit(solution)/shard_map/ppermute | solution.py:52
  16.3 19.6 %collective-permute-start = (bf16[128,578]{1,0:T(8,128)(2,1)S(1)}, bf16[128,578]{1,0:T(8,128)(2,1)S(1)}, u32[]{:S(2)}, u32[]{:S(2)}) collective-permute-start(bf16[128,578]{1,0:T(8,128)(2,1)S(1)} %pad_maximum_fusion.5), channel_id=1, source_target_pairs={{0,128},{32,160},{64,0},{96,32},{128,64},{160,96},{192,320},{224,3... | collective-permute-start | bytes 443912 | tf_op jit(solution)/shard_map/ppermute | solution.py:52
  36.0 16.3 %collective-permute-start.4 = (bf16[3,128,578]{2,1,0:T(8,128)(2,1)S(1)}, bf16[3,128,578]{2,1,0:T(8,128)(2,1)S(1)}, u32[]{:S(2)}, u32[]{:S(2)}) collective-permute-start(bf16[3,128,578]{2,1,0:T(8,128)(2,1)S(1)} %get-tuple-element.49), channel_id=1, source_target_pairs={{0,192},{32,224},{64,256},{96,288},{128,320},{160,352},{192,384},{... | collective-permute-start | bytes 1331720 | tf_op jit(solution)/shard_map/ppermute | solution.py:52
  39.4 22.6 %collective-permute-start.3 = (bf16[3,128,578]{2,1,0:T(8,128)(2,1)S(1)}, bf16[3,128,578]{2,1,0:T(8,128)(2,1)S(1)}, u32[]{:S(2)}, u32[]{:S(2)}) collective-permute-start(bf16[3,128,578]{2,1,0:T(8,128)(2,1)S(1)} %get-tuple-element.49), channel_id=1, source_target_pairs={{0,384},{32,416},{64,448},{96,480},{128,512},{160,544},{192,576},{... | collective-permute-start | bytes 1331720 | tf_op jit(solution)/shard_map/ppermute | solution.py:52
  44.1 19.5 %collective-permute-start.2 = (bf16[3,128,578]{2,1,0:T(8,128)(2,1)S(1)}, bf16[3,128,578]{2,1,0:T(8,128)(2,1)S(1)}, u32[]{:S(2)}, u32[]{:S(2)}) collective-permute-start(bf16[3,128,578]{2,1,0:T(8,128)(2,1)S(1)} %get-tuple-element.49), channel_id=1, source_target_pairs={{0,576},{32,608},{64,640},{96,672},{128,704},{160,736},{192,0},{22... | collective-permute-start | bytes 1331720 | tf_op jit(solution)/shard_map/ppermute | solution.py:52
  65.3 5.2 %copy-start.12 = (bf16[128,256]{1,0:T(8,128)(2,1)S(1)}, bf16[128,256]{1,0:T(8,128)(2,1)}, u32[]{:S(2)}) copy-start(bf16[128,256]{1,0:T(8,128)(2,1)} %param.11) | copy-start | bytes 196612
  65.3 5.3 %copy-start.14 = (bf16[128,128]{1,0:T(8,128)(2,1)S(1)}, bf16[128,128]{1,0:T(8,128)(2,1)}, u32[]{:S(2)}) copy-start(bf16[128,128]{1,0:T(8,128)(2,1)} %param.10) | copy-start | bytes 98308
  65.3 6.0 %copy-start.13 = (bf16[128,256]{1,0:T(8,128)(2,1)S(1)}, bf16[128,256]{1,0:T(8,128)(2,1)}, u32[]{:S(2)}) copy-start(bf16[128,256]{1,0:T(8,128)(2,1)} %param.9) | copy-start | bytes 196612
  68.4 10.8 %copy-start.2 = (bf16[1,4,3,128,578]{4,3,2,1,0:T(8,128)(2,1)S(1)}, bf16[1,4,3,128,578]{4,3,2,1,0:T(8,128)(2,1)}, u32[]{:S(2)}) copy-start(bf16[1,4,3,128,578]{4,3,2,1,0:T(8,128)(2,1)} %get-tuple-element.41) | copy-start | bytes 5326852
  68.4 6.1 %collective-permute-start.5 = (bf16[4,3,128,578]{2,0,3,1:T(4,128)(2,1)}, bf16[4,3,128,578]{2,0,3,1:T(4,128)(2,1)}, u32[]{:S(2)}, u32[]{:S(2)}) collective-permute-start(bf16[4,3,128,578]{2,0,3,1:T(4,128)(2,1)} %copy.112), channel_id=1, source_target_pairs={{0,32},{32,0},{64,96},{96,64},{128,160},{160,128},{192,224},{224,1... | collective-permute-start | bytes 5326856 | tf_op jit(solution)/shard_map/ppermute | solution.py:52
  93.4 5.3 %collective-permute-start.6 = (bf16[2,2,4,3,128,128]{5,4,3,2,1,0:T(8,128)(2,1)S(1)}, bf16[2,2,4,3,128,128]{5,4,3,2,1,0:T(8,128)(2,1)S(1)}, u32[]{:S(2)}, u32[]{:S(2)}) collective-permute-start(bf16[2,2,4,3,128,128]{5,4,3,2,1,0:T(8,128)(2,1)S(1)} %fusion.17), channel_id=1, source_target_pairs={{0,32},{32,0},{64,96},{96,64},{128,160},{160,128},{192,224},{224,1... | collective-permute-start | bytes 4718600 | tf_op jit(solution)/shard_map/ppermute | solution.py:52
  99.6 21.7 %collective-permute-start.9 = (bf16[2,2,3,128,128]{4,3,2,1,0:T(8,128)(2,1)S(1)}, bf16[2,2,3,128,128]{4,3,2,1,0:T(8,128)(2,1)S(1)}, u32[]{:S(2)}, u32[]{:S(2)}) collective-permute-start(bf16[2,2,3,128,128]{4,3,2,1,0:T(8,128)(2,1)S(1)} %get-tuple-element.44), channel_id=1, source_target_pairs={{0,576},{32,608},{64,640},{96,672},{128,704},{160,736},{192,0},{22... | collective-permute-start | bytes 1179656 | tf_op jit(solution)/shard_map/ppermute | solution.py:52
  104.1 17.1 %collective-permute-start.8 = (bf16[2,2,3,128,128]{4,3,2,1,0:T(8,128)(2,1)S(1)}, bf16[2,2,3,128,128]{4,3,2,1,0:T(8,128)(2,1)S(1)}, u32[]{:S(2)}, u32[]{:S(2)}) collective-permute-start(bf16[2,2,3,128,128]{4,3,2,1,0:T(8,128)(2,1)S(1)} %get-tuple-element.45), channel_id=1, source_target_pairs={{0,384},{32,416},{64,448},{96,480},{128,512},{160,544},{192,576},{... | collective-permute-start | bytes 1179656 | tf_op jit(solution)/shard_map/ppermute | solution.py:52
  107.9 19.0 %collective-permute-start.7 = (bf16[2,2,3,128,128]{4,3,2,1,0:T(8,128)(2,1)S(1)}, bf16[2,2,3,128,128]{4,3,2,1,0:T(8,128)(2,1)S(1)}, u32[]{:S(2)}, u32[]{:S(2)}) collective-permute-start(bf16[2,2,3,128,128]{4,3,2,1,0:T(8,128)(2,1)S(1)} %get-tuple-element.43), channel_id=1, source_target_pairs={{0,192},{32,224},{64,256},{96,288},{128,320},{160,352},{192,384},{... | collective-permute-start | bytes 1179656 | tf_op jit(solution)/shard_map/ppermute | solution.py:52
  127.1 12.2 %collective-permute-start.11 = (bf16[2,2,128,128]{3,2,1,0:T(8,128)(2,1)S(1)}, bf16[2,2,128,128]{3,2,1,0:T(8,128)(2,1)S(1)}, u32[]{:S(2)}, u32[]{:S(2)}) collective-permute-start(bf16[2,2,128,128]{3,2,1,0:T(8,128)(2,1)S(1)} %get-tuple-element.51), channel_id=1, source_target_pairs={{0,128},{32,160},{64,0},{96,32},{128,64},{160,96},{192,320},{224,3... | collective-permute-start | bytes 393224 | tf_op jit(solution)/shard_map/ppermute | solution.py:52
  134.2 13.0 %collective-permute-start.10 = (bf16[2,2,128,128]{3,2,1,0:T(8,128)(2,1)S(1)}, bf16[2,2,128,128]{3,2,1,0:T(8,128)(2,1)S(1)}, u32[]{:S(2)}, u32[]{:S(2)}) collective-permute-start(bf16[2,2,128,128]{3,2,1,0:T(8,128)(2,1)S(1)} %get-tuple-element.50), channel_id=1, source_target_pairs={{0,64},{32,96},{64,128},{96,160},{128,0},{160,32},{192,256},{224,2... | collective-permute-start | bytes 393224 | tf_op jit(solution)/shard_map/ppermute | solution.py:52
  148.1 16.7 %collective-permute-start.13 = (bf16[128,512]{1,0:T(8,128)(2,1)}, bf16[128,512]{1,0:T(8,128)(2,1)}, u32[]{:S(2)}, u32[]{:S(2)}) collective-permute-start(bf16[128,512]{1,0:T(8,128)(2,1)} %convert_element_type.218), channel_id=1, source_target_pairs={{0,64},{32,96},{64,128},{96,160},{128,0},{160,32},{192,256},{224,2... | collective-permute-start | bytes 393224 | tf_op jit(solution)/shard_map/ppermute | solution.py:52
  152.3 13.8 %collective-permute-start.12 = (bf16[128,512]{1,0:T(8,128)(2,1)}, bf16[128,512]{1,0:T(8,128)(2,1)}, u32[]{:S(2)}, u32[]{:S(2)}) collective-permute-start(bf16[128,512]{1,0:T(8,128)(2,1)} %convert_element_type.218), channel_id=1, source_target_pairs={{0,128},{32,160},{64,0},{96,32},{128,64},{160,96},{192,320},{224,3... | collective-permute-start | bytes 393224 | tf_op jit(solution)/shard_map/ppermute | solution.py:52
  160.8 7.2 %collective-permute-start.14 = (bf16[128,512]{1,0:T(8,128)(2,1)}, bf16[128,512]{1,0:T(8,128)(2,1)}, u32[]{:S(2)}, u32[]{:S(2)}) collective-permute-start(bf16[128,512]{1,0:T(8,128)(2,1)} %fusion.21), channel_id=1, source_target_pairs={{0,1},{1,0},{2,3},{3,2},{4,5},{5,4},{6,7},{7,6},{8,9},{9,8},{10,11... | collective-permute-start | bytes 393224 | tf_op jit(solution)/shard_map/ppermute | solution.py:52
  169.0 19.4 %collective-permute-start.18 = (bf16[128,512]{1,0:T(8,128)(2,1)S(1)}, bf16[128,512]{1,0:T(8,128)(2,1)S(1)}, u32[]{:S(2)}, u32[]{:S(2)}) collective-permute-start(bf16[128,512]{1,0:T(8,128)(2,1)S(1)} %convert_add_fusion.2), channel_id=1, source_target_pairs={{0,6},{1,7},{2,0},{3,1},{4,2},{5,3},{6,4},{7,5},{8,14},{9,15},{10,... | collective-permute-start | bytes 393224 | tf_op jit(solution)/shard_map/ppermute | solution.py:52
  173.0 28.8 %collective-permute-start.17 = (bf16[3,128,512]{2,1,0:T(8,128)(2,1)}, bf16[3,128,512]{2,1,0:T(8,128)(2,1)}, u32[]{:S(2)}, u32[]{:S(2)}) collective-permute-start(bf16[3,128,512]{2,1,0:T(8,128)(2,1)} %pad_maximum_fusion.4), channel_id=1, source_target_pairs={{0,192},{32,224},{64,256},{96,288},{128,320},{160,352},{192,384},{... | collective-permute-start | bytes 1179656 | tf_op jit(solution)/shard_map/ppermute | solution.py:52
  178.9 22.9 %collective-permute-start.16 = (bf16[3,128,512]{2,1,0:T(8,128)(2,1)}, bf16[3,128,512]{2,1,0:T(8,128)(2,1)}, u32[]{:S(2)}, u32[]{:S(2)}) collective-permute-start(bf16[3,128,512]{2,1,0:T(8,128)(2,1)} %pad_maximum_fusion.4), channel_id=1, source_target_pairs={{0,384},{32,416},{64,448},{96,480},{128,512},{160,544},{192,576},{... | collective-permute-start | bytes 1179656 | tf_op jit(solution)/shard_map/ppermute | solution.py:52
  182.5 19.3 %collective-permute-start.15 = (bf16[3,128,512]{2,1,0:T(8,128)(2,1)}, bf16[3,128,512]{2,1,0:T(8,128)(2,1)}, u32[]{:S(2)}, u32[]{:S(2)}) collective-permute-start(bf16[3,128,512]{2,1,0:T(8,128)(2,1)} %pad_maximum_fusion.4), channel_id=1, source_target_pairs={{0,576},{32,608},{64,640},{96,672},{128,704},{160,736},{192,0},{22... | collective-permute-start | bytes 1179656 | tf_op jit(solution)/shard_map/ppermute | solution.py:52
  185.4 11.1 %collective-permute-start.19 = (bf16[128,512]{1,0:T(8,128)(2,1)S(1)}, bf16[128,512]{1,0:T(8,128)(2,1)}, u32[]{:S(2)}, u32[]{:S(2)}) collective-permute-start(bf16[128,512]{1,0:T(8,128)(2,1)S(1)} %convert_add_fusion.2), channel_id=1, source_target_pairs={{0,4},{1,5},{2,6},{3,7},{4,0},{5,1},{6,2},{7,3},{8,12},{9,13},{10,... | collective-permute-start | bytes 393224 | tf_op jit(solution)/shard_map/ppermute | solution.py:52
  189.0 11.1 %collective-permute-start.20 = (bf16[128,512]{1,0:T(8,128)(2,1)S(1)}, bf16[128,512]{1,0:T(8,128)(2,1)}, u32[]{:S(2)}, u32[]{:S(2)}) collective-permute-start(bf16[128,512]{1,0:T(8,128)(2,1)S(1)} %convert_add_fusion.2), channel_id=1, source_target_pairs={{0,2},{1,3},{2,4},{3,5},{4,6},{5,7},{6,0},{7,1},{8,10},{9,11},{10,... | collective-permute-start | bytes 393224 | tf_op jit(solution)/shard_map/ppermute | solution.py:52
  194.9 5.1 %copy-start.11 = (bf16[128,512]{1,0:T(8,128)(2,1)S(1)}, bf16[128,512]{1,0:T(8,128)(2,1)}, u32[]{:S(2)}) copy-start(bf16[128,512]{1,0:T(8,128)(2,1)} %copy-done.10) | copy-start | bytes 393220
  208.4 26.8 %collective-permute-start.21 = (f32[512,512]{1,0:T(8,128)}, f32[512,512]{1,0:T(8,128)}, u32[]{:S(2)}, u32[]{:S(2)}) collective-permute-start(f32[512,512]{1,0:T(8,128)} %add_bitcast_fusion), channel_id=1, source_target_pairs={{0,32},{32,0},{64,96},{96,64},{128,160},{160,128},{192,224},{224,1... | collective-permute-start | bytes 3145736 | tf_op jit(solution)/shard_map/ppermute | solution.py:52
  211.8 25.2 %copy-start.4 = (f32[128,4,128]{2,1,0:T(4,128)S(1)}, f32[128,4,128]{2,1,0:T(4,128)}, u32[]{:S(2)}) copy-start(f32[128,4,128]{2,1,0:T(4,128)} %copy-done.3) | copy-start | bytes 786436
  211.8 19.0 %collective-permute-start.22 = (bf16[128,512]{1,0:T(8,128)(2,1)S(1)}, bf16[128,512]{1,0:T(8,128)(2,1)S(1)}, u32[]{:S(2)}, u32[]{:S(2)}) collective-permute-start(bf16[128,512]{1,0:T(8,128)(2,1)S(1)} %copy-done.5), channel_id=1, source_target_pairs={{0,24},{1,25},{2,26},{3,27},{4,28},{5,29},{6,30},{7,31},{8,0},{9,1... | collective-permute-start | bytes 393224 | tf_op jit(solution)/shard_map/ppermute | solution.py:52
  222.5 12.6 %collective-permute-start.23 = (bf16[128,512]{1,0:T(8,128)(2,1)S(1)}, bf16[128,512]{1,0:T(8,128)(2,1)S(1)}, u32[]{:S(2)}, u32[]{:S(2)}) collective-permute-start(bf16[128,512]{1,0:T(8,128)(2,1)S(1)} %copy-done.5), channel_id=1, source_target_pairs={{0,16},{1,17},{2,18},{3,19},{4,20},{5,21},{6,22},{7,23},{8,24},{9,... | collective-permute-start | bytes 393224 | tf_op jit(solution)/shard_map/ppermute | solution.py:52
  224.4 10.6 %collective-permute-start.24 = (bf16[128,512]{1,0:T(8,128)(2,1)S(1)}, bf16[128,512]{1,0:T(8,128)(2,1)S(1)}, u32[]{:S(2)}, u32[]{:S(2)}) collective-permute-start(bf16[128,512]{1,0:T(8,128)(2,1)S(1)} %copy-done.5), channel_id=1, source_target_pairs={{0,8},{1,9},{2,10},{3,11},{4,12},{5,13},{6,14},{7,15},{8,16},{9,17... | collective-permute-start | bytes 393224 | tf_op jit(solution)/shard_map/ppermute | solution.py:52
  (9 other events, 15.7 us)

commit v8 on v7

--- a/solution.py
+++ b/solution.py
@@ -7,6 +7,7 @@
 D_NOPE = 128
 D_V = 128
 POS_SPLIT = 64
+LANE = 128
 
 
 lowest = -1e30
@@ -76,9 +77,13 @@
 
 def gather_relative(block, axis):
     buf = block
-    for radix, stride in gather_order(lax.axis_size(axis)):
+    levels = gather_order(lax.axis_size(axis))
+    for radix, stride in levels[:-1]:
         buf = gather_step(buf, axis, radix, stride)
-    return buf
+    width = buf.shape[-1]
+    lanes = -(-width // LANE) * LANE
+    padded = jnp.pad(buf, [(0, 0)] * (buf.ndim - 1) + [(0, lanes - width)])
+    return gather_step(padded, axis, *levels[-1])[..., :width]
 
 
 def scatter_relative(data, axis, lead, wire):

time: 241 us -> 232 us (0.963)
  local copies, waits for them, and re-layouts: 21.2 us -> 13.1 us
    ppermute x1 -> x0, local copies, waits for them, and re-layouts: 4.78 us -> none  [shift_digit(): return lax.ppermute(x, axis, pairs)]
    another operation x1 -> x0, local copies, waits for them, and re-layouts: 3.09 us -> none  [gather_step(): return jnp.stack(pieces, axis=0)]
    unnamed x39 -> x41, local copies, waits for them, and re-layouts: 5.07 us -> 4.84 us
    another operation x6 -> x7, other arithmetic: 7.43 us -> 7.31 us  [gather_step(): return jnp.stack(pieces, axis=0)]
  transfers between devices with their start and end apart: 25 -> 25, of which waited for: 15 -> 15; matrix products, arithmetic and copies ran while one was open for 7% -> 8% of each run, Pallas kernels for 0% -> 0%
where the time goes in v8:
time: 232 us; the launch traced here: 229 us
  starting transfers between devices  106 us (46%)
  waiting for transfers between devices  71.3 us (31%)
  other arithmetic  23.8 us (10%)
  matrix products  13.5 us (6%)
  local copies, waits for them, and re-layouts  13.1 us (6%)
    ppermute x25, starting transfers between devices, shift_digit(): return lax.ppermute(x, axis, pairs)  106 us
    ppermute x25, waiting for transfers between devices, shift_digit(): return lax.ppermute(x, axis, pairs)  71.3 us
    another operation x7, other arithmetic, gather_step(): return jnp.stack(pieces, axis=0)  7.31 us
    unnamed x41, local copies, waits for them, and re-layouts  4.84 us
  transfers between devices with their start and end apart: 25, of which 15 were waited for; matrix products, arithmetic and copies ran while one was open for 8% of the time, Pallas kernels for 0%

profile of v8, /device:TPU:56, one launch (start us, length us, event | category | flops | bytes accessed | tf_op | source)
XLA Modules:
  0.0 229.3 jit_solution(2892212878346077218)
XLA Ops:
  4.7 11.0 %collective-permute-start.1 = (bf16[128,578]{1,0:T(8,128)(2,1)S(1)}, bf16[128,578]{1,0:T(8,128)(2,1)S(1)}, u32[]{:S(2)}, u32[]{:S(2)}) collective-permute-start(bf16[128,578]{1,0:T(8,128)(2,1)S(1)} %pad_maximum_fusion.4), channel_id=1, source_target_pairs={{0,64},{32,96},{64,128},{96,160},{128,0},{160,32},{192,256},{224,2... | collective-permute-start | bytes 443912 | tf_op jit(solution)/shard_map/ppermute | solution.py:53
  15.8 5.6 %collective-permute-start = (bf16[128,578]{1,0:T(8,128)(2,1)S(1)}, bf16[128,578]{1,0:T(8,128)(2,1)S(1)}, u32[]{:S(2)}, u32[]{:S(2)}) collective-permute-start(bf16[128,578]{1,0:T(8,128)(2,1)S(1)} %pad_maximum_fusion.4), channel_id=1, source_target_pairs={{0,128},{32,160},{64,0},{96,32},{128,64},{160,96},{192,320},{224,3... | collective-permute-start | bytes 443912 | tf_op jit(solution)/shard_map/ppermute | solution.py:53
  21.4 2.5 %collective-permute-done.1 = bf16[128,578]{1,0:T(8,128)(2,1)S(1)} collective-permute-done((bf16[128,578]{1,0:T(8,128)(2,1)S(1)}, bf16[128,578]{1,0:T(8,128)(2,1)S(1)}, u32[]{:S(2)}, u32[]{:S(2)}) %collective-permute-start.1) | collective-permute-done | bytes 148000 | tf_op jit(solution)/shard_map/ppermute | solution.py:53
  23.9 11.5 %collective-permute-done = bf16[128,578]{1,0:T(8,128)(2,1)S(1)} collective-permute-done((bf16[128,578]{1,0:T(8,128)(2,1)S(1)}, bf16[128,578]{1,0:T(8,128)(2,1)S(1)}, u32[]{:S(2)}, u32[]{:S(2)}) %collective-permute-start) | collective-permute-done | bytes 148000 | tf_op jit(solution)/shard_map/ppermute | solution.py:53
  35.5 3.4 %collective-permute-start.4 = (bf16[3,128,578]{2,1,0:T(8,128)(2,1)S(1)}, bf16[3,128,578]{2,1,0:T(8,128)(2,1)S(1)}, u32[]{:S(2)}, u32[]{:S(2)}) collective-permute-start(bf16[3,128,578]{2,1,0:T(8,128)(2,1)S(1)} %get-tuple-element.42), channel_id=1, source_target_pairs={{0,192},{32,224},{64,256},{96,288},{128,320},{160,352},{192,384},{... | collective-permute-start | bytes 1331720 | tf_op jit(solution)/shard_map/ppermute | solution.py:53
  38.9 4.6 %collective-permute-start.3 = (bf16[3,128,578]{2,1,0:T(8,128)(2,1)S(1)}, bf16[3,128,578]{2,1,0:T(8,128)(2,1)S(1)}, u32[]{:S(2)}, u32[]{:S(2)}) collective-permute-start(bf16[3,128,578]{2,1,0:T(8,128)(2,1)S(1)} %get-tuple-element.42), channel_id=1, source_target_pairs={{0,384},{32,416},{64,448},{96,480},{128,512},{160,544},{192,576},{... | collective-permute-start | bytes 1331720 | tf_op jit(solution)/shard_map/ppermute | solution.py:53
  43.6 3.3 %collective-permute-start.2 = (bf16[3,128,578]{2,1,0:T(8,128)(2,1)S(1)}, bf16[3,128,578]{2,1,0:T(8,128)(2,1)S(1)}, u32[]{:S(2)}, u32[]{:S(2)}) collective-permute-start(bf16[3,128,578]{2,1,0:T(8,128)(2,1)S(1)} %get-tuple-element.42), channel_id=1, source_target_pairs={{0,576},{32,608},{64,640},{96,672},{128,704},{160,736},{192,0},{22... | collective-permute-start | bytes 1331720 | tf_op jit(solution)/shard_map/ppermute | solution.py:53
  46.9 4.9 %collective-permute-done.4 = bf16[3,128,578]{2,1,0:T(8,128)(2,1)S(1)} collective-permute-done((bf16[3,128,578]{2,1,0:T(8,128)(2,1)S(1)}, bf16[3,128,578]{2,1,0:T(8,128)(2,1)S(1)}, u32[]{:S(2)}, u32[]{:S(2)}) %collective-permute-start.4) | collective-permute-done | bytes 443936 | tf_op jit(solution)/shard_map/ppermute | solution.py:53
  51.8 9.7 %collective-permute-done.3 = bf16[3,128,578]{2,1,0:T(8,128)(2,1)S(1)} collective-permute-done((bf16[3,128,578]{2,1,0:T(8,128)(2,1)S(1)}, bf16[3,128,578]{2,1,0:T(8,128)(2,1)S(1)}, u32[]{:S(2)}, u32[]{:S(2)}) %collective-permute-start.3) | collective-permute-done | bytes 443936 | tf_op jit(solution)/shard_map/ppermute | solution.py:53
  86.3 2.8 %collective-permute-done.6 = bf16[2,2,4,3,128,128]{5,4,3,2,1,0:T(8,128)(2,1)S(1)} collective-permute-done((bf16[2,2,4,3,128,128]{5,4,3,2,1,0:T(8,128)(2,1)S(1)}, bf16[2,2,4,3,128,128]{5,4,3,2,1,0:T(8,128)(2,1)S(1)}, u32[]{:S(2)}, u32[]{:S(2)}) %collective-permute-start.6) | collective-permute-done | bytes 1572896 | tf_op jit(solution)/shard_map/ppermute | solution.py:53
  90.0 4.5 %collective-permute-start.9 = (bf16[2,2,3,128,128]{4,3,2,1,0:T(8,128)(2,1)S(1)}, bf16[2,2,3,128,128]{4,3,2,1,0:T(8,128)(2,1)S(1)}, u32[]{:S(2)}, u32[]{:S(2)}) collective-permute-start(bf16[2,2,3,128,128]{4,3,2,1,0:T(8,128)(2,1)S(1)} %get-tuple-element.37), channel_id=1, source_target_pairs={{0,576},{32,608},{64,640},{96,672},{128,704},{160,736},{192,0},{22... | collective-permute-start | bytes 1179656 | tf_op jit(solution)/shard_map/ppermute | solution.py:53
  94.6 3.7 %collective-permute-start.8 = (bf16[2,2,3,128,128]{4,3,2,1,0:T(8,128)(2,1)S(1)}, bf16[2,2,3,128,128]{4,3,2,1,0:T(8,128)(2,1)S(1)}, u32[]{:S(2)}, u32[]{:S(2)}) collective-permute-start(bf16[2,2,3,128,128]{4,3,2,1,0:T(8,128)(2,1)S(1)} %get-tuple-element.38), channel_id=1, source_target_pairs={{0,384},{32,416},{64,448},{96,480},{128,512},{160,544},{192,576},{... | collective-permute-start | bytes 1179656 | tf_op jit(solution)/shard_map/ppermute | solution.py:53
  100.2 11.7 %collective-permute-done.9 = bf16[2,2,3,128,128]{4,3,2,1,0:T(8,128)(2,1)S(1)} collective-permute-done((bf16[2,2,3,128,128]{4,3,2,1,0:T(8,128)(2,1)S(1)}, bf16[2,2,3,128,128]{4,3,2,1,0:T(8,128)(2,1)S(1)}, u32[]{:S(2)}, u32[]{:S(2)}) %collective-permute-start.9) | collective-permute-done | bytes 393248 | tf_op jit(solution)/shard_map/ppermute | solution.py:53
  111.9 5.6 %collective-permute-done.7 = bf16[2,2,3,128,128]{4,3,2,1,0:T(8,128)(2,1)S(1)} collective-permute-done((bf16[2,2,3,128,128]{4,3,2,1,0:T(8,128)(2,1)S(1)}, bf16[2,2,3,128,128]{4,3,2,1,0:T(8,128)(2,1)S(1)}, u32[]{:S(2)}, u32[]{:S(2)}) %collective-permute-start.7) | collective-permute-done | bytes 393248 | tf_op jit(solution)/shard_map/ppermute | solution.py:53
  117.7 7.1 %collective-permute-start.11 = (bf16[2,2,128,128]{3,2,1,0:T(8,128)(2,1)S(1)}, bf16[2,2,128,128]{3,2,1,0:T(8,128)(2,1)S(1)}, u32[]{:S(2)}, u32[]{:S(2)}) collective-permute-start(bf16[2,2,128,128]{3,2,1,0:T(8,128)(2,1)S(1)} %get-tuple-element.44), channel_id=1, source_target_pairs={{0,128},{32,160},{64,0},{96,32},{128,64},{160,96},{192,320},{224,3... | collective-permute-start | bytes 393224 | tf_op jit(solution)/shard_map/ppermute | solution.py:53
  124.8 2.7 %collective-permute-start.10 = (bf16[2,2,128,128]{3,2,1,0:T(8,128)(2,1)S(1)}, bf16[2,2,128,128]{3,2,1,0:T(8,128)(2,1)S(1)}, u32[]{:S(2)}, u32[]{:S(2)}) collective-permute-start(bf16[2,2,128,128]{3,2,1,0:T(8,128)(2,1)S(1)} %get-tuple-element.43), channel_id=1, source_target_pairs={{0,64},{32,96},{64,128},{96,160},{128,0},{160,32},{192,256},{224,2... | collective-permute-start | bytes 393224 | tf_op jit(solution)/shard_map/ppermute | solution.py:53
  127.5 2.5 %collective-permute-done.11 = bf16[2,2,128,128]{3,2,1,0:T(8,128)(2,1)S(1)} collective-permute-done((bf16[2,2,128,128]{3,2,1,0:T(8,128)(2,1)S(1)}, bf16[2,2,128,128]{3,2,1,0:T(8,128)(2,1)S(1)}, u32[]{:S(2)}, u32[]{:S(2)}) %collective-permute-start.11) | collective-permute-done | bytes 131104 | tf_op jit(solution)/shard_map/ppermute | solution.py:53
  130.0 7.8 %collective-permute-done.10 = bf16[2,2,128,128]{3,2,1,0:T(8,128)(2,1)S(1)} collective-permute-done((bf16[2,2,128,128]{3,2,1,0:T(8,128)(2,1)S(1)}, bf16[2,2,128,128]{3,2,1,0:T(8,128)(2,1)S(1)}, u32[]{:S(2)}, u32[]{:S(2)}) %collective-permute-start.10) | collective-permute-done | bytes 131104 | tf_op jit(solution)/shard_map/ppermute | solution.py:53
  138.7 4.2 %collective-permute-start.13 = (bf16[128,512]{1,0:T(8,128)(2,1)}, bf16[128,512]{1,0:T(8,128)(2,1)}, u32[]{:S(2)}, u32[]{:S(2)}) collective-permute-start(bf16[128,512]{1,0:T(8,128)(2,1)} %convert_element_type.220), channel_id=1, source_target_pairs={{0,64},{32,96},{64,128},{96,160},{128,0},{160,32},{192,256},{224,2... | collective-permute-start | bytes 393224 | tf_op jit(solution)/shard_map/ppermute | solution.py:53
  142.9 5.5 %collective-permute-start.12 = (bf16[128,512]{1,0:T(8,128)(2,1)}, bf16[128,512]{1,0:T(8,128)(2,1)}, u32[]{:S(2)}, u32[]{:S(2)}) collective-permute-start(bf16[128,512]{1,0:T(8,128)(2,1)} %convert_element_type.220), channel_id=1, source_target_pairs={{0,128},{32,160},{64,0},{96,32},{128,64},{160,96},{192,320},{224,3... | collective-permute-start | bytes 393224 | tf_op jit(solution)/shard_map/ppermute | solution.py:53
  151.4 3.2 %collective-permute-start.14 = (bf16[128,512]{1,0:T(8,128)(2,1)}, bf16[128,512]{1,0:T(8,128)(2,1)}, u32[]{:S(2)}, u32[]{:S(2)}) collective-permute-start(bf16[128,512]{1,0:T(8,128)(2,1)} %fusion.28), channel_id=1, source_target_pairs={{0,1},{1,0},{2,3},{3,2},{4,5},{5,4},{6,7},{7,6},{8,9},{9,8},{10,11... | collective-permute-start | bytes 393224 | tf_op jit(solution)/shard_map/ppermute | solution.py:53
  159.6 4.0 %collective-permute-start.18 = (bf16[128,512]{1,0:T(8,128)(2,1)S(1)}, bf16[128,512]{1,0:T(8,128)(2,1)S(1)}, u32[]{:S(2)}, u32[]{:S(2)}) collective-permute-start(bf16[128,512]{1,0:T(8,128)(2,1)S(1)} %convert_add_fusion.2), channel_id=1, source_target_pairs={{0,6},{1,7},{2,0},{3,1},{4,2},{5,3},{6,4},{7,5},{8,14},{9,15},{10,... | collective-permute-start | bytes 393224 | tf_op jit(solution)/shard_map/ppermute | solution.py:53
  163.6 3.8 %collective-permute-start.17 = (bf16[3,128,512]{2,1,0:T(8,128)(2,1)}, bf16[3,128,512]{2,1,0:T(8,128)(2,1)}, u32[]{:S(2)}, u32[]{:S(2)}) collective-permute-start(bf16[3,128,512]{2,1,0:T(8,128)(2,1)} %pad_maximum_fusion.3), channel_id=1, source_target_pairs={{0,192},{32,224},{64,256},{96,288},{128,320},{160,352},{192,384},{... | collective-permute-start | bytes 1179656 | tf_op jit(solution)/shard_map/ppermute | solution.py:53
  167.5 3.6 %collective-permute-start.16 = (bf16[3,128,512]{2,1,0:T(8,128)(2,1)}, bf16[3,128,512]{2,1,0:T(8,128)(2,1)}, u32[]{:S(2)}, u32[]{:S(2)}) collective-permute-start(bf16[3,128,512]{2,1,0:T(8,128)(2,1)} %pad_maximum_fusion.3), channel_id=1, source_target_pairs={{0,384},{32,416},{64,448},{96,480},{128,512},{160,544},{192,576},{... | collective-permute-start | bytes 1179656 | tf_op jit(solution)/shard_map/ppermute | solution.py:53
  171.1 2.9 %collective-permute-start.15 = (bf16[3,128,512]{2,1,0:T(8,128)(2,1)}, bf16[3,128,512]{2,1,0:T(8,128)(2,1)}, u32[]{:S(2)}, u32[]{:S(2)}) collective-permute-start(bf16[3,128,512]{2,1,0:T(8,128)(2,1)} %pad_maximum_fusion.3), channel_id=1, source_target_pairs={{0,576},{32,608},{64,640},{96,672},{128,704},{160,736},{192,0},{22... | collective-permute-start | bytes 1179656 | tf_op jit(solution)/shard_map/ppermute | solution.py:53
  174.0 2.9 %collective-permute-start.19 = (bf16[128,512]{1,0:T(8,128)(2,1)S(1)}, bf16[128,512]{1,0:T(8,128)(2,1)}, u32[]{:S(2)}, u32[]{:S(2)}) collective-permute-start(bf16[128,512]{1,0:T(8,128)(2,1)S(1)} %convert_add_fusion.2), channel_id=1, source_target_pairs={{0,4},{1,5},{2,6},{3,7},{4,0},{5,1},{6,2},{7,3},{8,12},{9,13},{10,... | collective-permute-start | bytes 393224 | tf_op jit(solution)/shard_map/ppermute | solution.py:53
  177.6 5.7 %collective-permute-start.20 = (bf16[128,512]{1,0:T(8,128)(2,1)S(1)}, bf16[128,512]{1,0:T(8,128)(2,1)}, u32[]{:S(2)}, u32[]{:S(2)}) collective-permute-start(bf16[128,512]{1,0:T(8,128)(2,1)S(1)} %convert_add_fusion.2), channel_id=1, source_target_pairs={{0,2},{1,3},{2,4},{3,5},{4,6},{5,7},{6,0},{7,1},{8,10},{9,11},{10,... | collective-permute-start | bytes 393224 | tf_op jit(solution)/shard_map/ppermute | solution.py:53
  185.2 4.9 %collective-permute-done.20 = bf16[128,512]{1,0:T(8,128)(2,1)} collective-permute-done((bf16[128,512]{1,0:T(8,128)(2,1)S(1)}, bf16[128,512]{1,0:T(8,128)(2,1)}, u32[]{:S(2)}, u32[]{:S(2)}) %collective-permute-start.20) | collective-permute-done | bytes 131104 | tf_op jit(solution)/shard_map/ppermute | solution.py:53
  195.7 2.7 %add_bitcast_fusion = f32[512,512]{1,0:T(8,128)} fusion(f32[4,512,512]{2,1,0:T(8,128)S(1)} %convert_convert_fusion, f32[4,512,512]{2,1,0:T(8,128)S(1)} %convert_convert_fusion.1, f32[4,512,512]{2,1,0:T(8,128)S(1)} %convert_convert_fusion.2, pred[]{:T(512)S(6)} %eq.253, pred[]{:T(512)S(6)} %eq.251, pred[]{:T(512)S(6)} %eq.225, pred[]{:T(512)S(6)} %eq.254, ...), kind=kLoop, calls=%fused_computation.51 | loop fusion | flops 13893632 | bytes 13631506 | tf_op jit(solution)/shard_map/add | solution.py:106
  201.8 11.3 %collective-permute-start.22 = (bf16[128,512]{1,0:T(8,128)(2,1)S(1)}, bf16[128,512]{1,0:T(8,128)(2,1)S(1)}, u32[]{:S(2)}, u32[]{:S(2)}) collective-permute-start(bf16[128,512]{1,0:T(8,128)(2,1)S(1)} %copy-done.6), channel_id=1, source_target_pairs={{0,24},{1,25},{2,26},{3,27},{4,28},{5,29},{6,30},{7,31},{8,0},{9,1... | collective-permute-start | bytes 393224 | tf_op jit(solution)/shard_map/ppermute | solution.py:53
  215.1 2.5 %collective-permute-start.24 = (bf16[128,512]{1,0:T(8,128)(2,1)S(1)}, bf16[128,512]{1,0:T(8,128)(2,1)S(1)}, u32[]{:S(2)}, u32[]{:S(2)}) collective-permute-start(bf16[128,512]{1,0:T(8,128)(2,1)S(1)} %copy-done.6), channel_id=1, source_target_pairs={{0,8},{1,9},{2,10},{3,11},{4,12},{5,13},{6,14},{7,15},{8,16},{9,17... | collective-permute-start | bytes 393224 | tf_op jit(solution)/shard_map/ppermute | solution.py:53
  221.4 4.3 %collective-permute-done.23 = bf16[128,512]{1,0:T(8,128)(2,1)S(1)} collective-permute-done((bf16[128,512]{1,0:T(8,128)(2,1)S(1)}, bf16[128,512]{1,0:T(8,128)(2,1)S(1)}, u32[]{:S(2)}, u32[]{:S(2)}) %collective-permute-start.23) | collective-permute-done | bytes 131104 | tf_op jit(solution)/shard_map/ppermute | solution.py:53
  (114 shorter events, 60.9 us)
Async XLA Ops:
  0.6 72.3 %copy-start = (bf16[512,256]{1,0:T(8,128)(2,1)S(1)}, bf16[512,256]{1,0:T(8,128)(2,1)}, u32[]{:S(2)}) copy-start(bf16[512,256]{1,0:T(8,128)(2,1)} %param.16) | copy-start | bytes 786436
  4.5 30.9 %copy-start.2 = (f32[128,4,128]{2,1,0:T(4,128)}, f32[128,4,128]{2,1,0:T(4,128)S(1)}, u32[]{:S(2)}) copy-start(f32[128,4,128]{2,1,0:T(4,128)S(1)} %broadcast_in_dim.42) | copy-start | bytes 786436
  4.6 61.2 %copy-start.13 = (bf16[128,256]{1,0:T(8,128)(2,1)S(1)}, bf16[128,256]{1,0:T(8,128)(2,1)}, u32[]{:S(2)}) copy-start(bf16[128,256]{1,0:T(8,128)(2,1)} %param.11) | copy-start | bytes 196612
  4.6 61.3 %copy-start.15 = (bf16[128,128]{1,0:T(8,128)(2,1)S(1)}, bf16[128,128]{1,0:T(8,128)(2,1)}, u32[]{:S(2)}) copy-start(bf16[128,128]{1,0:T(8,128)(2,1)} %param.10) | copy-start | bytes 98308
  4.6 62.0 %copy-start.14 = (bf16[128,256]{1,0:T(8,128)(2,1)S(1)}, bf16[128,256]{1,0:T(8,128)(2,1)}, u32[]{:S(2)}) copy-start(bf16[128,256]{1,0:T(8,128)(2,1)} %param.9) | copy-start | bytes 196612
  4.7 19.2 %collective-permute-start.1 = (bf16[128,578]{1,0:T(8,128)(2,1)S(1)}, bf16[128,578]{1,0:T(8,128)(2,1)S(1)}, u32[]{:S(2)}, u32[]{:S(2)}) collective-permute-start(bf16[128,578]{1,0:T(8,128)(2,1)S(1)} %pad_maximum_fusion.4), channel_id=1, source_target_pairs={{0,64},{32,96},{64,128},{96,160},{128,0},{160,32},{192,256},{224,2... | collective-permute-start | bytes 443912 | tf_op jit(solution)/shard_map/ppermute | solution.py:53
  15.8 19.6 %collective-permute-start = (bf16[128,578]{1,0:T(8,128)(2,1)S(1)}, bf16[128,578]{1,0:T(8,128)(2,1)S(1)}, u32[]{:S(2)}, u32[]{:S(2)}) collective-permute-start(bf16[128,578]{1,0:T(8,128)(2,1)S(1)} %pad_maximum_fusion.4), channel_id=1, source_target_pairs={{0,128},{32,160},{64,0},{96,32},{128,64},{160,96},{192,320},{224,3... | collective-permute-start | bytes 443912 | tf_op jit(solution)/shard_map/ppermute | solution.py:53
  35.5 16.3 %collective-permute-start.4 = (bf16[3,128,578]{2,1,0:T(8,128)(2,1)S(1)}, bf16[3,128,578]{2,1,0:T(8,128)(2,1)S(1)}, u32[]{:S(2)}, u32[]{:S(2)}) collective-permute-start(bf16[3,128,578]{2,1,0:T(8,128)(2,1)S(1)} %get-tuple-element.42), channel_id=1, source_target_pairs={{0,192},{32,224},{64,256},{96,288},{128,320},{160,352},{192,384},{... | collective-permute-start | bytes 1331720 | tf_op jit(solution)/shard_map/ppermute | solution.py:53
  38.9 22.6 %collective-permute-start.3 = (bf16[3,128,578]{2,1,0:T(8,128)(2,1)S(1)}, bf16[3,128,578]{2,1,0:T(8,128)(2,1)S(1)}, u32[]{:S(2)}, u32[]{:S(2)}) collective-permute-start(bf16[3,128,578]{2,1,0:T(8,128)(2,1)S(1)} %get-tuple-element.42), channel_id=1, source_target_pairs={{0,384},{32,416},{64,448},{96,480},{128,512},{160,544},{192,576},{... | collective-permute-start | bytes 1331720 | tf_op jit(solution)/shard_map/ppermute | solution.py:53
  43.6 19.5 %collective-permute-start.2 = (bf16[3,128,578]{2,1,0:T(8,128)(2,1)S(1)}, bf16[3,128,578]{2,1,0:T(8,128)(2,1)S(1)}, u32[]{:S(2)}, u32[]{:S(2)}) collective-permute-start(bf16[3,128,578]{2,1,0:T(8,128)(2,1)S(1)} %get-tuple-element.42), channel_id=1, source_target_pairs={{0,576},{32,608},{64,640},{96,672},{128,704},{160,736},{192,0},{22... | collective-permute-start | bytes 1331720 | tf_op jit(solution)/shard_map/ppermute | solution.py:53
  63.9 6.0 %collective-permute-start.5 = (bf16[4,3,128,640]{3,2,1,0:T(8,128)(2,1)S(1)}, bf16[4,3,128,640]{3,2,1,0:T(8,128)(2,1)}, u32[]{:S(2)}, u32[]{:S(2)}) collective-permute-start(bf16[4,3,128,640]{3,2,1,0:T(8,128)(2,1)S(1)} %fusion.22), channel_id=1, source_target_pairs={{0,32},{32,0},{64,96},{96,64},{128,160},{160,128},{192,224},{224,1... | collective-permute-start | bytes 5898248 | tf_op jit(solution)/shard_map/ppermute | solution.py:53
  83.9 5.3 %collective-permute-start.6 = (bf16[2,2,4,3,128,128]{5,4,3,2,1,0:T(8,128)(2,1)S(1)}, bf16[2,2,4,3,128,128]{5,4,3,2,1,0:T(8,128)(2,1)S(1)}, u32[]{:S(2)}, u32[]{:S(2)}) collective-permute-start(bf16[2,2,4,3,128,128]{5,4,3,2,1,0:T(8,128)(2,1)S(1)} %fusion.24), channel_id=1, source_target_pairs={{0,32},{32,0},{64,96},{96,64},{128,160},{160,128},{192,224},{224,1... | collective-permute-start | bytes 4718600 | tf_op jit(solution)/shard_map/ppermute | solution.py:53
  90.0 21.9 %collective-permute-start.9 = (bf16[2,2,3,128,128]{4,3,2,1,0:T(8,128)(2,1)S(1)}, bf16[2,2,3,128,128]{4,3,2,1,0:T(8,128)(2,1)S(1)}, u32[]{:S(2)}, u32[]{:S(2)}) collective-permute-start(bf16[2,2,3,128,128]{4,3,2,1,0:T(8,128)(2,1)S(1)} %get-tuple-element.37), channel_id=1, source_target_pairs={{0,576},{32,608},{64,640},{96,672},{128,704},{160,736},{192,0},{22... | collective-permute-start | bytes 1179656 | tf_op jit(solution)/shard_map/ppermute | solution.py:53
  94.6 17.3 %collective-permute-start.8 = (bf16[2,2,3,128,128]{4,3,2,1,0:T(8,128)(2,1)S(1)}, bf16[2,2,3,128,128]{4,3,2,1,0:T(8,128)(2,1)S(1)}, u32[]{:S(2)}, u32[]{:S(2)}) collective-permute-start(bf16[2,2,3,128,128]{4,3,2,1,0:T(8,128)(2,1)S(1)} %get-tuple-element.38), channel_id=1, source_target_pairs={{0,384},{32,416},{64,448},{96,480},{128,512},{160,544},{192,576},{... | collective-permute-start | bytes 1179656 | tf_op jit(solution)/shard_map/ppermute | solution.py:53
  98.3 19.2 %collective-permute-start.7 = (bf16[2,2,3,128,128]{4,3,2,1,0:T(8,128)(2,1)S(1)}, bf16[2,2,3,128,128]{4,3,2,1,0:T(8,128)(2,1)S(1)}, u32[]{:S(2)}, u32[]{:S(2)}) collective-permute-start(bf16[2,2,3,128,128]{4,3,2,1,0:T(8,128)(2,1)S(1)} %get-tuple-element.36), channel_id=1, source_target_pairs={{0,192},{32,224},{64,256},{96,288},{128,320},{160,352},{192,384},{... | collective-permute-start | bytes 1179656 | tf_op jit(solution)/shard_map/ppermute | solution.py:53
  117.7 12.3 %collective-permute-start.11 = (bf16[2,2,128,128]{3,2,1,0:T(8,128)(2,1)S(1)}, bf16[2,2,128,128]{3,2,1,0:T(8,128)(2,1)S(1)}, u32[]{:S(2)}, u32[]{:S(2)}) collective-permute-start(bf16[2,2,128,128]{3,2,1,0:T(8,128)(2,1)S(1)} %get-tuple-element.44), channel_id=1, source_target_pairs={{0,128},{32,160},{64,0},{96,32},{128,64},{160,96},{192,320},{224,3... | collective-permute-start | bytes 393224 | tf_op jit(solution)/shard_map/ppermute | solution.py:53
  124.8 13.0 %collective-permute-start.10 = (bf16[2,2,128,128]{3,2,1,0:T(8,128)(2,1)S(1)}, bf16[2,2,128,128]{3,2,1,0:T(8,128)(2,1)S(1)}, u32[]{:S(2)}, u32[]{:S(2)}) collective-permute-start(bf16[2,2,128,128]{3,2,1,0:T(8,128)(2,1)S(1)} %get-tuple-element.43), channel_id=1, source_target_pairs={{0,64},{32,96},{64,128},{96,160},{128,0},{160,32},{192,256},{224,2... | collective-permute-start | bytes 393224 | tf_op jit(solution)/shard_map/ppermute | solution.py:53
  138.7 16.7 %collective-permute-start.13 = (bf16[128,512]{1,0:T(8,128)(2,1)}, bf16[128,512]{1,0:T(8,128)(2,1)}, u32[]{:S(2)}, u32[]{:S(2)}) collective-permute-start(bf16[128,512]{1,0:T(8,128)(2,1)} %convert_element_type.220), channel_id=1, source_target_pairs={{0,64},{32,96},{64,128},{96,160},{128,0},{160,32},{192,256},{224,2... | collective-permute-start | bytes 393224 | tf_op jit(solution)/shard_map/ppermute | solution.py:53
  142.9 13.8 %collective-permute-start.12 = (bf16[128,512]{1,0:T(8,128)(2,1)}, bf16[128,512]{1,0:T(8,128)(2,1)}, u32[]{:S(2)}, u32[]{:S(2)}) collective-permute-start(bf16[128,512]{1,0:T(8,128)(2,1)} %convert_element_type.220), channel_id=1, source_target_pairs={{0,128},{32,160},{64,0},{96,32},{128,64},{160,96},{192,320},{224,3... | collective-permute-start | bytes 393224 | tf_op jit(solution)/shard_map/ppermute | solution.py:53
  151.4 7.2 %collective-permute-start.14 = (bf16[128,512]{1,0:T(8,128)(2,1)}, bf16[128,512]{1,0:T(8,128)(2,1)}, u32[]{:S(2)}, u32[]{:S(2)}) collective-permute-start(bf16[128,512]{1,0:T(8,128)(2,1)} %fusion.28), channel_id=1, source_target_pairs={{0,1},{1,0},{2,3},{3,2},{4,5},{5,4},{6,7},{7,6},{8,9},{9,8},{10,11... | collective-permute-start | bytes 393224 | tf_op jit(solution)/shard_map/ppermute | solution.py:53
  159.6 17.3 %collective-permute-start.18 = (bf16[128,512]{1,0:T(8,128)(2,1)S(1)}, bf16[128,512]{1,0:T(8,128)(2,1)S(1)}, u32[]{:S(2)}, u32[]{:S(2)}) collective-permute-start(bf16[128,512]{1,0:T(8,128)(2,1)S(1)} %convert_add_fusion.2), channel_id=1, source_target_pairs={{0,6},{1,7},{2,0},{3,1},{4,2},{5,3},{6,4},{7,5},{8,14},{9,15},{10,... | collective-permute-start | bytes 393224 | tf_op jit(solution)/shard_map/ppermute | solution.py:53
  163.6 28.2 %collective-permute-start.17 = (bf16[3,128,512]{2,1,0:T(8,128)(2,1)}, bf16[3,128,512]{2,1,0:T(8,128)(2,1)}, u32[]{:S(2)}, u32[]{:S(2)}) collective-permute-start(bf16[3,128,512]{2,1,0:T(8,128)(2,1)} %pad_maximum_fusion.3), channel_id=1, source_target_pairs={{0,192},{32,224},{64,256},{96,288},{128,320},{160,352},{192,384},{... | collective-permute-start | bytes 1179656 | tf_op jit(solution)/shard_map/ppermute | solution.py:53
  167.5 24.4 %collective-permute-start.16 = (bf16[3,128,512]{2,1,0:T(8,128)(2,1)}, bf16[3,128,512]{2,1,0:T(8,128)(2,1)}, u32[]{:S(2)}, u32[]{:S(2)}) collective-permute-start(bf16[3,128,512]{2,1,0:T(8,128)(2,1)} %pad_maximum_fusion.3), channel_id=1, source_target_pairs={{0,384},{32,416},{64,448},{96,480},{128,512},{160,544},{192,576},{... | collective-permute-start | bytes 1179656 | tf_op jit(solution)/shard_map/ppermute | solution.py:53
  171.1 20.7 %collective-permute-start.15 = (bf16[3,128,512]{2,1,0:T(8,128)(2,1)}, bf16[3,128,512]{2,1,0:T(8,128)(2,1)}, u32[]{:S(2)}, u32[]{:S(2)}) collective-permute-start(bf16[3,128,512]{2,1,0:T(8,128)(2,1)} %pad_maximum_fusion.3), channel_id=1, source_target_pairs={{0,576},{32,608},{64,640},{96,672},{128,704},{160,736},{192,0},{22... | collective-permute-start | bytes 1179656 | tf_op jit(solution)/shard_map/ppermute | solution.py:53
  174.0 11.2 %collective-permute-start.19 = (bf16[128,512]{1,0:T(8,128)(2,1)S(1)}, bf16[128,512]{1,0:T(8,128)(2,1)}, u32[]{:S(2)}, u32[]{:S(2)}) collective-permute-start(bf16[128,512]{1,0:T(8,128)(2,1)S(1)} %convert_add_fusion.2), channel_id=1, source_target_pairs={{0,4},{1,5},{2,6},{3,7},{4,0},{5,1},{6,2},{7,3},{8,12},{9,13},{10,... | collective-permute-start | bytes 393224 | tf_op jit(solution)/shard_map/ppermute | solution.py:53
  177.6 12.5 %collective-permute-start.20 = (bf16[128,512]{1,0:T(8,128)(2,1)S(1)}, bf16[128,512]{1,0:T(8,128)(2,1)}, u32[]{:S(2)}, u32[]{:S(2)}) collective-permute-start(bf16[128,512]{1,0:T(8,128)(2,1)S(1)} %convert_add_fusion.2), channel_id=1, source_target_pairs={{0,2},{1,3},{2,4},{3,5},{4,6},{5,7},{6,0},{7,1},{8,10},{9,11},{10,... | collective-permute-start | bytes 393224 | tf_op jit(solution)/shard_map/ppermute | solution.py:53
  183.6 6.5 %copy-start.12 = (bf16[128,512]{1,0:T(8,128)(2,1)S(1)}, bf16[128,512]{1,0:T(8,128)(2,1)}, u32[]{:S(2)}) copy-start(bf16[128,512]{1,0:T(8,128)(2,1)} %copy-done.11) | copy-start | bytes 393220
  198.4 27.4 %collective-permute-start.21 = (f32[512,512]{1,0:T(8,128)}, f32[512,512]{1,0:T(8,128)}, u32[]{:S(2)}, u32[]{:S(2)}) collective-permute-start(f32[512,512]{1,0:T(8,128)} %add_bitcast_fusion), channel_id=1, source_target_pairs={{0,32},{32,0},{64,96},{96,64},{128,160},{160,128},{192,224},{224,1... | collective-permute-start | bytes 3145736 | tf_op jit(solution)/shard_map/ppermute | solution.py:53
  201.8 25.8 %copy-start.3 = (f32[128,4,128]{2,1,0:T(4,128)S(1)}, f32[128,4,128]{2,1,0:T(4,128)}, u32[]{:S(2)}) copy-start(f32[128,4,128]{2,1,0:T(4,128)} %copy-done.2) | copy-start | bytes 786436
  201.8 19.6 %collective-permute-start.22 = (bf16[128,512]{1,0:T(8,128)(2,1)S(1)}, bf16[128,512]{1,0:T(8,128)(2,1)S(1)}, u32[]{:S(2)}, u32[]{:S(2)}) collective-permute-start(bf16[128,512]{1,0:T(8,128)(2,1)S(1)} %copy-done.6), channel_id=1, source_target_pairs={{0,24},{1,25},{2,26},{3,27},{4,28},{5,29},{6,30},{7,31},{8,0},{9,1... | collective-permute-start | bytes 393224 | tf_op jit(solution)/shard_map/ppermute | solution.py:53
  213.1 12.6 %collective-permute-start.23 = (bf16[128,512]{1,0:T(8,128)(2,1)S(1)}, bf16[128,512]{1,0:T(8,128)(2,1)S(1)}, u32[]{:S(2)}, u32[]{:S(2)}) collective-permute-start(bf16[128,512]{1,0:T(8,128)(2,1)S(1)} %copy-done.6), channel_id=1, source_target_pairs={{0,16},{1,17},{2,18},{3,19},{4,20},{5,21},{6,22},{7,23},{8,24},{9,... | collective-permute-start | bytes 393224 | tf_op jit(solution)/shard_map/ppermute | solution.py:53
  215.1 10.6 %collective-permute-start.24 = (bf16[128,512]{1,0:T(8,128)(2,1)S(1)}, bf16[128,512]{1,0:T(8,128)(2,1)S(1)}, u32[]{:S(2)}, u32[]{:S(2)}) collective-permute-start(bf16[128,512]{1,0:T(8,128)(2,1)S(1)} %copy-done.6), channel_id=1, source_target_pairs={{0,8},{1,9},{2,10},{3,11},{4,12},{5,13},{6,14},{7,15},{8,16},{9,17... | collective-permute-start | bytes 393224 | tf_op jit(solution)/shard_map/ppermute | solution.py:53
  (10 other events, 17.3 us)

commit v9 on v8

--- a/solution.py
+++ b/solution.py
@@ -131,8 +131,10 @@
     compressed = (latent[:, :col_width].astype(jnp.float32) * factor).astype(jnp.bfloat16)
     pos_hi = (positions // POS_SPLIT).astype(jnp.bfloat16)
     pos_lo = (positions % POS_SPLIT).astype(jnp.bfloat16)
+    used = col_width + D_ROPE + 2
+    spare = jnp.zeros((row_count, -(-used // LANE) * LANE - used), jnp.bfloat16)
     packed = jnp.concatenate(
-        [compressed, latent[:, col_width:], pos_hi[:, None], pos_lo[:, None]], axis=1
+        [compressed, latent[:, col_width:], pos_hi[:, None], pos_lo[:, None], spare], axis=1
     )
     everything = gather_relative(packed, "blk").reshape(key_count, packed.shape[1])
     comp_all = everything[:, :col_width]

time: 232 us -> 233 us (level)
    another operation x7 -> x5, other arithmetic: 7.31 us -> 7.08 us  [gather_step(): return jnp.stack(pieces, axis=0)]
    unnamed x41 -> x37, local copies, waits for them, and re-layouts: 4.84 us -> 5.06 us
  transfers between devices with their start and end apart: 25 -> 25, of which waited for: 15 -> 15; matrix products, arithmetic and copies ran while one was open for 8% -> 7% of each run, Pallas kernels for 0% -> 0%
where the time goes in v9:
time: 233 us; the launch traced here: 231 us
  starting transfers between devices  107 us (46%)
  waiting for transfers between devices  71.6 us (31%)
  other arithmetic  23.5 us (10%)
  local copies, waits for them, and re-layouts  13.5 us (6%)
  matrix products  13.5 us (6%)
    ppermute x25, starting transfers between devices, shift_digit(): return lax.ppermute(x, axis, pairs)  107 us
    ppermute x25, waiting for transfers between devices, shift_digit(): return lax.ppermute(x, axis, pairs)  71.6 us
    another operation x5, other arithmetic, gather_step(): return jnp.stack(pieces, axis=0)  7.08 us
    unnamed x37, local copies, waits for them, and re-layouts  5.06 us
  transfers between devices with their start and end apart: 25, of which 15 were waited for; matrix products, arithmetic and copies ran while one was open for 7% of the time, Pallas kernels for 0%

profile of v9, /device:TPU:56, one launch (start us, length us, event | category | flops | bytes accessed | tf_op | source)
XLA Modules:
  0.0 230.9 jit_solution(5808440390361069096)
XLA Ops:
  5.4 10.9 %collective-permute-start.1 = (bf16[128,640]{1,0:T(8,128)(2,1)S(1)}, bf16[128,640]{1,0:T(8,128)(2,1)S(1)}, u32[]{:S(2)}, u32[]{:S(2)}) collective-permute-start(bf16[128,640]{1,0:T(8,128)(2,1)S(1)} %concatenate.3), channel_id=1, source_target_pairs={{0,64},{32,96},{64,128},{96,160},{128,0},{160,32},{192,256},{224,2... | collective-permute-start | bytes 491528 | tf_op jit(solution)/shard_map/ppermute | solution.py:53
  16.3 5.6 %collective-permute-start = (bf16[128,640]{1,0:T(8,128)(2,1)S(1)}, bf16[128,640]{1,0:T(8,128)(2,1)S(1)}, u32[]{:S(2)}, u32[]{:S(2)}) collective-permute-start(bf16[128,640]{1,0:T(8,128)(2,1)S(1)} %concatenate.3), channel_id=1, source_target_pairs={{0,128},{32,160},{64,0},{96,32},{128,64},{160,96},{192,320},{224,3... | collective-permute-start | bytes 491528 | tf_op jit(solution)/shard_map/ppermute | solution.py:53
  21.9 2.6 %collective-permute-done.1 = bf16[128,640]{1,0:T(8,128)(2,1)S(1)} collective-permute-done((bf16[128,640]{1,0:T(8,128)(2,1)S(1)}, bf16[128,640]{1,0:T(8,128)(2,1)S(1)}, u32[]{:S(2)}, u32[]{:S(2)}) %collective-permute-start.1) | collective-permute-done | bytes 163872 | tf_op jit(solution)/shard_map/ppermute | solution.py:53
  24.5 11.5 %collective-permute-done = bf16[128,640]{1,0:T(8,128)(2,1)S(1)} collective-permute-done((bf16[128,640]{1,0:T(8,128)(2,1)S(1)}, bf16[128,640]{1,0:T(8,128)(2,1)S(1)}, u32[]{:S(2)}, u32[]{:S(2)}) %collective-permute-start) | collective-permute-done | bytes 163872 | tf_op jit(solution)/shard_map/ppermute | solution.py:53
  36.1 3.5 %collective-permute-start.4 = (bf16[3,128,640]{2,1,0:T(8,128)(2,1)S(1)}, bf16[3,128,640]{2,1,0:T(8,128)(2,1)S(1)}, u32[]{:S(2)}, u32[]{:S(2)}) collective-permute-start(bf16[3,128,640]{2,1,0:T(8,128)(2,1)S(1)} %get-tuple-element.44), channel_id=1, source_target_pairs={{0,192},{32,224},{64,256},{96,288},{128,320},{160,352},{192,384},{... | collective-permute-start | bytes 1474568 | tf_op jit(solution)/shard_map/ppermute | solution.py:53
  39.6 4.6 %collective-permute-start.3 = (bf16[3,128,640]{2,1,0:T(8,128)(2,1)S(1)}, bf16[3,128,640]{2,1,0:T(8,128)(2,1)S(1)}, u32[]{:S(2)}, u32[]{:S(2)}) collective-permute-start(bf16[3,128,640]{2,1,0:T(8,128)(2,1)S(1)} %get-tuple-element.44), channel_id=1, source_target_pairs={{0,384},{32,416},{64,448},{96,480},{128,512},{160,544},{192,576},{... | collective-permute-start | bytes 1474568 | tf_op jit(solution)/shard_map/ppermute | solution.py:53
  44.3 3.3 %collective-permute-start.2 = (bf16[3,128,640]{2,1,0:T(8,128)(2,1)S(1)}, bf16[3,128,640]{2,1,0:T(8,128)(2,1)S(1)}, u32[]{:S(2)}, u32[]{:S(2)}) collective-permute-start(bf16[3,128,640]{2,1,0:T(8,128)(2,1)S(1)} %get-tuple-element.44), channel_id=1, source_target_pairs={{0,576},{32,608},{64,640},{96,672},{128,704},{160,736},{192,0},{22... | collective-permute-start | bytes 1474568 | tf_op jit(solution)/shard_map/ppermute | solution.py:53
  47.6 4.9 %collective-permute-done.4 = bf16[3,128,640]{2,1,0:T(8,128)(2,1)S(1)} collective-permute-done((bf16[3,128,640]{2,1,0:T(8,128)(2,1)S(1)}, bf16[3,128,640]{2,1,0:T(8,128)(2,1)S(1)}, u32[]{:S(2)}, u32[]{:S(2)}) %collective-permute-start.4) | collective-permute-done | bytes 491552 | tf_op jit(solution)/shard_map/ppermute | solution.py:53
  52.5 9.7 %collective-permute-done.3 = bf16[3,128,640]{2,1,0:T(8,128)(2,1)S(1)} collective-permute-done((bf16[3,128,640]{2,1,0:T(8,128)(2,1)S(1)}, bf16[3,128,640]{2,1,0:T(8,128)(2,1)S(1)}, u32[]{:S(2)}, u32[]{:S(2)}) %collective-permute-start.3) | collective-permute-done | bytes 491552 | tf_op jit(solution)/shard_map/ppermute | solution.py:53
  87.9 3.1 %collective-permute-done.6 = bf16[2,2,4,3,128,128]{5,4,3,2,1,0:T(8,128)(2,1)S(1)} collective-permute-done((bf16[2,2,4,3,128,128]{5,4,3,2,1,0:T(8,128)(2,1)S(1)}, bf16[2,2,4,3,128,128]{5,4,3,2,1,0:T(8,128)(2,1)S(1)}, u32[]{:S(2)}, u32[]{:S(2)}) %collective-permute-start.6) | collective-permute-done | bytes 1572896 | tf_op jit(solution)/shard_map/ppermute | solution.py:53
  91.8 4.5 %collective-permute-start.9 = (bf16[2,2,3,128,128]{4,3,2,1,0:T(8,128)(2,1)S(1)}, bf16[2,2,3,128,128]{4,3,2,1,0:T(8,128)(2,1)S(1)}, u32[]{:S(2)}, u32[]{:S(2)}) collective-permute-start(bf16[2,2,3,128,128]{4,3,2,1,0:T(8,128)(2,1)S(1)} %get-tuple-element.39), channel_id=1, source_target_pairs={{0,576},{32,608},{64,640},{96,672},{128,704},{160,736},{192,0},{22... | collective-permute-start | bytes 1179656 | tf_op jit(solution)/shard_map/ppermute | solution.py:53
  96.4 3.7 %collective-permute-start.8 = (bf16[2,2,3,128,128]{4,3,2,1,0:T(8,128)(2,1)S(1)}, bf16[2,2,3,128,128]{4,3,2,1,0:T(8,128)(2,1)S(1)}, u32[]{:S(2)}, u32[]{:S(2)}) collective-permute-start(bf16[2,2,3,128,128]{4,3,2,1,0:T(8,128)(2,1)S(1)} %get-tuple-element.40), channel_id=1, source_target_pairs={{0,384},{32,416},{64,448},{96,480},{128,512},{160,544},{192,576},{... | collective-permute-start | bytes 1179656 | tf_op jit(solution)/shard_map/ppermute | solution.py:53
  102.0 11.5 %collective-permute-done.9 = bf16[2,2,3,128,128]{4,3,2,1,0:T(8,128)(2,1)S(1)} collective-permute-done((bf16[2,2,3,128,128]{4,3,2,1,0:T(8,128)(2,1)S(1)}, bf16[2,2,3,128,128]{4,3,2,1,0:T(8,128)(2,1)S(1)}, u32[]{:S(2)}, u32[]{:S(2)}) %collective-permute-start.9) | collective-permute-done | bytes 393248 | tf_op jit(solution)/shard_map/ppermute | solution.py:53
  113.5 5.6 %collective-permute-done.7 = bf16[2,2,3,128,128]{4,3,2,1,0:T(8,128)(2,1)S(1)} collective-permute-done((bf16[2,2,3,128,128]{4,3,2,1,0:T(8,128)(2,1)S(1)}, bf16[2,2,3,128,128]{4,3,2,1,0:T(8,128)(2,1)S(1)}, u32[]{:S(2)}, u32[]{:S(2)}) %collective-permute-start.7) | collective-permute-done | bytes 393248 | tf_op jit(solution)/shard_map/ppermute | solution.py:53
  119.3 7.1 %collective-permute-start.11 = (bf16[2,2,128,128]{3,2,1,0:T(8,128)(2,1)S(1)}, bf16[2,2,128,128]{3,2,1,0:T(8,128)(2,1)S(1)}, u32[]{:S(2)}, u32[]{:S(2)}) collective-permute-start(bf16[2,2,128,128]{3,2,1,0:T(8,128)(2,1)S(1)} %get-tuple-element.46), channel_id=1, source_target_pairs={{0,128},{32,160},{64,0},{96,32},{128,64},{160,96},{192,320},{224,3... | collective-permute-start | bytes 393224 | tf_op jit(solution)/shard_map/ppermute | solution.py:53
  126.4 2.7 %collective-permute-start.10 = (bf16[2,2,128,128]{3,2,1,0:T(8,128)(2,1)S(1)}, bf16[2,2,128,128]{3,2,1,0:T(8,128)(2,1)S(1)}, u32[]{:S(2)}, u32[]{:S(2)}) collective-permute-start(bf16[2,2,128,128]{3,2,1,0:T(8,128)(2,1)S(1)} %get-tuple-element.45), channel_id=1, source_target_pairs={{0,64},{32,96},{64,128},{96,160},{128,0},{160,32},{192,256},{224,2... | collective-permute-start | bytes 393224 | tf_op jit(solution)/shard_map/ppermute | solution.py:53
  129.1 2.5 %collective-permute-done.11 = bf16[2,2,128,128]{3,2,1,0:T(8,128)(2,1)S(1)} collective-permute-done((bf16[2,2,128,128]{3,2,1,0:T(8,128)(2,1)S(1)}, bf16[2,2,128,128]{3,2,1,0:T(8,128)(2,1)S(1)}, u32[]{:S(2)}, u32[]{:S(2)}) %collective-permute-start.11) | collective-permute-done | bytes 131104 | tf_op jit(solution)/shard_map/ppermute | solution.py:53
  131.6 7.8 %collective-permute-done.10 = bf16[2,2,128,128]{3,2,1,0:T(8,128)(2,1)S(1)} collective-permute-done((bf16[2,2,128,128]{3,2,1,0:T(8,128)(2,1)S(1)}, bf16[2,2,128,128]{3,2,1,0:T(8,128)(2,1)S(1)}, u32[]{:S(2)}, u32[]{:S(2)}) %collective-permute-start.10) | collective-permute-done | bytes 131104 | tf_op jit(solution)/shard_map/ppermute | solution.py:53
  140.3 4.2 %collective-permute-start.13 = (bf16[128,512]{1,0:T(8,128)(2,1)}, bf16[128,512]{1,0:T(8,128)(2,1)}, u32[]{:S(2)}, u32[]{:S(2)}) collective-permute-start(bf16[128,512]{1,0:T(8,128)(2,1)} %convert_element_type.218), channel_id=1, source_target_pairs={{0,64},{32,96},{64,128},{96,160},{128,0},{160,32},{192,256},{224,2... | collective-permute-start | bytes 393224 | tf_op jit(solution)/shard_map/ppermute | solution.py:53
  144.5 5.5 %collective-permute-start.12 = (bf16[128,512]{1,0:T(8,128)(2,1)}, bf16[128,512]{1,0:T(8,128)(2,1)}, u32[]{:S(2)}, u32[]{:S(2)}) collective-permute-start(bf16[128,512]{1,0:T(8,128)(2,1)} %convert_element_type.218), channel_id=1, source_target_pairs={{0,128},{32,160},{64,0},{96,32},{128,64},{160,96},{192,320},{224,3... | collective-permute-start | bytes 393224 | tf_op jit(solution)/shard_map/ppermute | solution.py:53
  153.0 3.2 %collective-permute-start.14 = (bf16[128,512]{1,0:T(8,128)(2,1)}, bf16[128,512]{1,0:T(8,128)(2,1)}, u32[]{:S(2)}, u32[]{:S(2)}) collective-permute-start(bf16[128,512]{1,0:T(8,128)(2,1)} %fusion.21), channel_id=1, source_target_pairs={{0,1},{1,0},{2,3},{3,2},{4,5},{5,4},{6,7},{7,6},{8,9},{9,8},{10,11... | collective-permute-start | bytes 393224 | tf_op jit(solution)/shard_map/ppermute | solution.py:53
  161.2 4.0 %collective-permute-start.18 = (bf16[128,512]{1,0:T(8,128)(2,1)S(1)}, bf16[128,512]{1,0:T(8,128)(2,1)S(1)}, u32[]{:S(2)}, u32[]{:S(2)}) collective-permute-start(bf16[128,512]{1,0:T(8,128)(2,1)S(1)} %convert_add_fusion.2), channel_id=1, source_target_pairs={{0,6},{1,7},{2,0},{3,1},{4,2},{5,3},{6,4},{7,5},{8,14},{9,15},{10,... | collective-permute-start | bytes 393224 | tf_op jit(solution)/shard_map/ppermute | solution.py:53
  165.2 5.9 %collective-permute-start.17 = (bf16[3,128,512]{2,1,0:T(8,128)(2,1)}, bf16[3,128,512]{2,1,0:T(8,128)(2,1)}, u32[]{:S(2)}, u32[]{:S(2)}) collective-permute-start(bf16[3,128,512]{2,1,0:T(8,128)(2,1)} %pad_maximum_fusion.4), channel_id=1, source_target_pairs={{0,192},{32,224},{64,256},{96,288},{128,320},{160,352},{192,384},{... | collective-permute-start | bytes 1179656 | tf_op jit(solution)/shard_map/ppermute | solution.py:53
  171.1 3.6 %collective-permute-start.16 = (bf16[3,128,512]{2,1,0:T(8,128)(2,1)}, bf16[3,128,512]{2,1,0:T(8,128)(2,1)}, u32[]{:S(2)}, u32[]{:S(2)}) collective-permute-start(bf16[3,128,512]{2,1,0:T(8,128)(2,1)} %pad_maximum_fusion.4), channel_id=1, source_target_pairs={{0,384},{32,416},{64,448},{96,480},{128,512},{160,544},{192,576},{... | collective-permute-start | bytes 1179656 | tf_op jit(solution)/shard_map/ppermute | solution.py:53
  174.8 2.9 %collective-permute-start.15 = (bf16[3,128,512]{2,1,0:T(8,128)(2,1)}, bf16[3,128,512]{2,1,0:T(8,128)(2,1)}, u32[]{:S(2)}, u32[]{:S(2)}) collective-permute-start(bf16[3,128,512]{2,1,0:T(8,128)(2,1)} %pad_maximum_fusion.4), channel_id=1, source_target_pairs={{0,576},{32,608},{64,640},{96,672},{128,704},{160,736},{192,0},{22... | collective-permute-start | bytes 1179656 | tf_op jit(solution)/shard_map/ppermute | solution.py:53
  177.6 2.9 %collective-permute-start.19 = (bf16[128,512]{1,0:T(8,128)(2,1)S(1)}, bf16[128,512]{1,0:T(8,128)(2,1)}, u32[]{:S(2)}, u32[]{:S(2)}) collective-permute-start(bf16[128,512]{1,0:T(8,128)(2,1)S(1)} %convert_add_fusion.2), channel_id=1, source_target_pairs={{0,4},{1,5},{2,6},{3,7},{4,0},{5,1},{6,2},{7,3},{8,12},{9,13},{10,... | collective-permute-start | bytes 393224 | tf_op jit(solution)/shard_map/ppermute | solution.py:53
  181.2 5.7 %collective-permute-start.20 = (bf16[128,512]{1,0:T(8,128)(2,1)S(1)}, bf16[128,512]{1,0:T(8,128)(2,1)}, u32[]{:S(2)}, u32[]{:S(2)}) collective-permute-start(bf16[128,512]{1,0:T(8,128)(2,1)S(1)} %convert_add_fusion.2), channel_id=1, source_target_pairs={{0,2},{1,3},{2,4},{3,5},{4,6},{5,7},{6,0},{7,1},{8,10},{9,11},{10,... | collective-permute-start | bytes 393224 | tf_op jit(solution)/shard_map/ppermute | solution.py:53
  188.8 3.5 %collective-permute-done.20 = bf16[128,512]{1,0:T(8,128)(2,1)} collective-permute-done((bf16[128,512]{1,0:T(8,128)(2,1)S(1)}, bf16[128,512]{1,0:T(8,128)(2,1)}, u32[]{:S(2)}, u32[]{:S(2)}) %collective-permute-start.20) | collective-permute-done | bytes 131104 | tf_op jit(solution)/shard_map/ppermute | solution.py:53
  197.9 2.7 %add_bitcast_fusion = f32[512,512]{1,0:T(8,128)} fusion(f32[4,512,512]{2,1,0:T(8,128)S(1)} %convert_convert_fusion, f32[4,512,512]{2,1,0:T(8,128)S(1)} %convert_convert_fusion.1, f32[4,512,512]{2,1,0:T(8,128)S(1)} %convert_convert_fusion.2, pred[]{:T(512)S(6)} %eq.253, pred[]{:T(512)S(6)} %eq.251, pred[]{:T(512)S(6)} %eq.225, pred[]{:T(512)S(6)} %eq.254, ...), kind=kLoop, calls=%fused_computation.44 | loop fusion | flops 13893632 | bytes 13631506 | tf_op jit(solution)/shard_map/add | solution.py:106
  204.0 10.7 %collective-permute-start.22 = (bf16[128,512]{1,0:T(8,128)(2,1)S(1)}, bf16[128,512]{1,0:T(8,128)(2,1)S(1)}, u32[]{:S(2)}, u32[]{:S(2)}) collective-permute-start(bf16[128,512]{1,0:T(8,128)(2,1)S(1)} %copy-done.4), channel_id=1, source_target_pairs={{0,24},{1,25},{2,26},{3,27},{4,28},{5,29},{6,30},{7,31},{8,0},{9,1... | collective-permute-start | bytes 393224 | tf_op jit(solution)/shard_map/ppermute | solution.py:53
  216.6 2.5 %collective-permute-start.24 = (bf16[128,512]{1,0:T(8,128)(2,1)S(1)}, bf16[128,512]{1,0:T(8,128)(2,1)S(1)}, u32[]{:S(2)}, u32[]{:S(2)}) collective-permute-start(bf16[128,512]{1,0:T(8,128)(2,1)S(1)} %copy-done.4), channel_id=1, source_target_pairs={{0,8},{1,9},{2,10},{3,11},{4,12},{5,13},{6,14},{7,15},{8,16},{9,17... | collective-permute-start | bytes 393224 | tf_op jit(solution)/shard_map/ppermute | solution.py:53
  223.0 4.3 %collective-permute-done.23 = bf16[128,512]{1,0:T(8,128)(2,1)S(1)} collective-permute-done((bf16[128,512]{1,0:T(8,128)(2,1)S(1)}, bf16[128,512]{1,0:T(8,128)(2,1)S(1)}, u32[]{:S(2)}, u32[]{:S(2)}) %collective-permute-start.23) | collective-permute-done | bytes 131104 | tf_op jit(solution)/shard_map/ppermute | solution.py:53
  (109 shorter events, 62.4 us)
Async XLA Ops:
  0.6 74.1 %copy-start = (bf16[512,256]{1,0:T(8,128)(2,1)S(1)}, bf16[512,256]{1,0:T(8,128)(2,1)}, u32[]{:S(2)}) copy-start(bf16[512,256]{1,0:T(8,128)(2,1)} %param.16) | copy-start | bytes 786436
  5.4 19.0 %collective-permute-start.1 = (bf16[128,640]{1,0:T(8,128)(2,1)S(1)}, bf16[128,640]{1,0:T(8,128)(2,1)S(1)}, u32[]{:S(2)}, u32[]{:S(2)}) collective-permute-start(bf16[128,640]{1,0:T(8,128)(2,1)S(1)} %concatenate.3), channel_id=1, source_target_pairs={{0,64},{32,96},{64,128},{96,160},{128,0},{160,32},{192,256},{224,2... | collective-permute-start | bytes 491528 | tf_op jit(solution)/shard_map/ppermute | solution.py:53
  16.3 19.6 %collective-permute-start = (bf16[128,640]{1,0:T(8,128)(2,1)S(1)}, bf16[128,640]{1,0:T(8,128)(2,1)S(1)}, u32[]{:S(2)}, u32[]{:S(2)}) collective-permute-start(bf16[128,640]{1,0:T(8,128)(2,1)S(1)} %concatenate.3), channel_id=1, source_target_pairs={{0,128},{32,160},{64,0},{96,32},{128,64},{160,96},{192,320},{224,3... | collective-permute-start | bytes 491528 | tf_op jit(solution)/shard_map/ppermute | solution.py:53
  36.1 31.3 %copy-start.11 = (bf16[128,256]{1,0:T(8,128)(2,1)S(1)}, bf16[128,256]{1,0:T(8,128)(2,1)}, u32[]{:S(2)}) copy-start(bf16[128,256]{1,0:T(8,128)(2,1)} %param.11) | copy-start | bytes 196612
  36.1 31.4 %copy-start.13 = (bf16[128,128]{1,0:T(8,128)(2,1)S(1)}, bf16[128,128]{1,0:T(8,128)(2,1)}, u32[]{:S(2)}) copy-start(bf16[128,128]{1,0:T(8,128)(2,1)} %param.10) | copy-start | bytes 98308
  36.1 32.2 %copy-start.12 = (bf16[128,256]{1,0:T(8,128)(2,1)S(1)}, bf16[128,256]{1,0:T(8,128)(2,1)}, u32[]{:S(2)}) copy-start(bf16[128,256]{1,0:T(8,128)(2,1)} %param.9) | copy-start | bytes 196612
  36.1 16.4 %collective-permute-start.4 = (bf16[3,128,640]{2,1,0:T(8,128)(2,1)S(1)}, bf16[3,128,640]{2,1,0:T(8,128)(2,1)S(1)}, u32[]{:S(2)}, u32[]{:S(2)}) collective-permute-start(bf16[3,128,640]{2,1,0:T(8,128)(2,1)S(1)} %get-tuple-element.44), channel_id=1, source_target_pairs={{0,192},{32,224},{64,256},{96,288},{128,320},{160,352},{192,384},{... | collective-permute-start | bytes 1474568 | tf_op jit(solution)/shard_map/ppermute | solution.py:53
  39.6 22.6 %collective-permute-start.3 = (bf16[3,128,640]{2,1,0:T(8,128)(2,1)S(1)}, bf16[3,128,640]{2,1,0:T(8,128)(2,1)S(1)}, u32[]{:S(2)}, u32[]{:S(2)}) collective-permute-start(bf16[3,128,640]{2,1,0:T(8,128)(2,1)S(1)} %get-tuple-element.44), channel_id=1, source_target_pairs={{0,384},{32,416},{64,448},{96,480},{128,512},{160,544},{192,576},{... | collective-permute-start | bytes 1474568 | tf_op jit(solution)/shard_map/ppermute | solution.py:53
  44.3 19.5 %collective-permute-start.2 = (bf16[3,128,640]{2,1,0:T(8,128)(2,1)S(1)}, bf16[3,128,640]{2,1,0:T(8,128)(2,1)S(1)}, u32[]{:S(2)}, u32[]{:S(2)}) collective-permute-start(bf16[3,128,640]{2,1,0:T(8,128)(2,1)S(1)} %get-tuple-element.44), channel_id=1, source_target_pairs={{0,576},{32,608},{64,640},{96,672},{128,704},{160,736},{192,0},{22... | collective-permute-start | bytes 1474568 | tf_op jit(solution)/shard_map/ppermute | solution.py:53
  65.5 6.2 %collective-permute-start.5 = (bf16[4,3,128,640]{3,2,1,0:T(8,128)(2,1)}, bf16[4,3,128,640]{3,2,1,0:T(8,128)(2,1)}, u32[]{:S(2)}, u32[]{:S(2)}) collective-permute-start(bf16[4,3,128,640]{3,2,1,0:T(8,128)(2,1)} %get-tuple-element.37), channel_id=1, source_target_pairs={{0,32},{32,0},{64,96},{96,64},{128,160},{160,128},{192,224},{224,1... | collective-permute-start | bytes 5898248 | tf_op jit(solution)/shard_map/ppermute | solution.py:53
  73.6 4.1 %copy-start.1 = (bf16[2,4,3,128,640]{4,3,2,1,0:T(8,128)(2,1)}, bf16[2,4,3,128,640]{4,3,2,1,0:T(8,128)(2,1)S(1)}, u32[]{:S(2)}) copy-start(bf16[2,4,3,128,640]{4,3,2,1,0:T(8,128)(2,1)S(1)} %pad_maximum_fusion) | copy-start | bytes 11796484
  85.7 5.3 %collective-permute-start.6 = (bf16[2,2,4,3,128,128]{5,4,3,2,1,0:T(8,128)(2,1)S(1)}, bf16[2,2,4,3,128,128]{5,4,3,2,1,0:T(8,128)(2,1)S(1)}, u32[]{:S(2)}, u32[]{:S(2)}) collective-permute-start(bf16[2,2,4,3,128,128]{5,4,3,2,1,0:T(8,128)(2,1)S(1)} %fusion.17), channel_id=1, source_target_pairs={{0,32},{32,0},{64,96},{96,64},{128,160},{160,128},{192,224},{224,1... | collective-permute-start | bytes 4718600 | tf_op jit(solution)/shard_map/ppermute | solution.py:53
  91.8 21.7 %collective-permute-start.9 = (bf16[2,2,3,128,128]{4,3,2,1,0:T(8,128)(2,1)S(1)}, bf16[2,2,3,128,128]{4,3,2,1,0:T(8,128)(2,1)S(1)}, u32[]{:S(2)}, u32[]{:S(2)}) collective-permute-start(bf16[2,2,3,128,128]{4,3,2,1,0:T(8,128)(2,1)S(1)} %get-tuple-element.39), channel_id=1, source_target_pairs={{0,576},{32,608},{64,640},{96,672},{128,704},{160,736},{192,0},{22... | collective-permute-start | bytes 1179656 | tf_op jit(solution)/shard_map/ppermute | solution.py:53
  96.4 17.1 %collective-permute-start.8 = (bf16[2,2,3,128,128]{4,3,2,1,0:T(8,128)(2,1)S(1)}, bf16[2,2,3,128,128]{4,3,2,1,0:T(8,128)(2,1)S(1)}, u32[]{:S(2)}, u32[]{:S(2)}) collective-permute-start(bf16[2,2,3,128,128]{4,3,2,1,0:T(8,128)(2,1)S(1)} %get-tuple-element.40), channel_id=1, source_target_pairs={{0,384},{32,416},{64,448},{96,480},{128,512},{160,544},{192,576},{... | collective-permute-start | bytes 1179656 | tf_op jit(solution)/shard_map/ppermute | solution.py:53
  100.1 19.0 %collective-permute-start.7 = (bf16[2,2,3,128,128]{4,3,2,1,0:T(8,128)(2,1)S(1)}, bf16[2,2,3,128,128]{4,3,2,1,0:T(8,128)(2,1)S(1)}, u32[]{:S(2)}, u32[]{:S(2)}) collective-permute-start(bf16[2,2,3,128,128]{4,3,2,1,0:T(8,128)(2,1)S(1)} %get-tuple-element.38), channel_id=1, source_target_pairs={{0,192},{32,224},{64,256},{96,288},{128,320},{160,352},{192,384},{... | collective-permute-start | bytes 1179656 | tf_op jit(solution)/shard_map/ppermute | solution.py:53
  119.3 12.2 %collective-permute-start.11 = (bf16[2,2,128,128]{3,2,1,0:T(8,128)(2,1)S(1)}, bf16[2,2,128,128]{3,2,1,0:T(8,128)(2,1)S(1)}, u32[]{:S(2)}, u32[]{:S(2)}) collective-permute-start(bf16[2,2,128,128]{3,2,1,0:T(8,128)(2,1)S(1)} %get-tuple-element.46), channel_id=1, source_target_pairs={{0,128},{32,160},{64,0},{96,32},{128,64},{160,96},{192,320},{224,3... | collective-permute-start | bytes 393224 | tf_op jit(solution)/shard_map/ppermute | solution.py:53
  126.4 13.0 %collective-permute-start.10 = (bf16[2,2,128,128]{3,2,1,0:T(8,128)(2,1)S(1)}, bf16[2,2,128,128]{3,2,1,0:T(8,128)(2,1)S(1)}, u32[]{:S(2)}, u32[]{:S(2)}) collective-permute-start(bf16[2,2,128,128]{3,2,1,0:T(8,128)(2,1)S(1)} %get-tuple-element.45), channel_id=1, source_target_pairs={{0,64},{32,96},{64,128},{96,160},{128,0},{160,32},{192,256},{224,2... | collective-permute-start | bytes 393224 | tf_op jit(solution)/shard_map/ppermute | solution.py:53
  140.3 16.7 %collective-permute-start.13 = (bf16[128,512]{1,0:T(8,128)(2,1)}, bf16[128,512]{1,0:T(8,128)(2,1)}, u32[]{:S(2)}, u32[]{:S(2)}) collective-permute-start(bf16[128,512]{1,0:T(8,128)(2,1)} %convert_element_type.218), channel_id=1, source_target_pairs={{0,64},{32,96},{64,128},{96,160},{128,0},{160,32},{192,256},{224,2... | collective-permute-start | bytes 393224 | tf_op jit(solution)/shard_map/ppermute | solution.py:53
  144.5 13.8 %collective-permute-start.12 = (bf16[128,512]{1,0:T(8,128)(2,1)}, bf16[128,512]{1,0:T(8,128)(2,1)}, u32[]{:S(2)}, u32[]{:S(2)}) collective-permute-start(bf16[128,512]{1,0:T(8,128)(2,1)} %convert_element_type.218), channel_id=1, source_target_pairs={{0,128},{32,160},{64,0},{96,32},{128,64},{160,96},{192,320},{224,3... | collective-permute-start | bytes 393224 | tf_op jit(solution)/shard_map/ppermute | solution.py:53
  153.0 7.2 %collective-permute-start.14 = (bf16[128,512]{1,0:T(8,128)(2,1)}, bf16[128,512]{1,0:T(8,128)(2,1)}, u32[]{:S(2)}, u32[]{:S(2)}) collective-permute-start(bf16[128,512]{1,0:T(8,128)(2,1)} %fusion.21), channel_id=1, source_target_pairs={{0,1},{1,0},{2,3},{3,2},{4,5},{5,4},{6,7},{7,6},{8,9},{9,8},{10,11... | collective-permute-start | bytes 393224 | tf_op jit(solution)/shard_map/ppermute | solution.py:53
  161.2 19.4 %collective-permute-start.18 = (bf16[128,512]{1,0:T(8,128)(2,1)S(1)}, bf16[128,512]{1,0:T(8,128)(2,1)S(1)}, u32[]{:S(2)}, u32[]{:S(2)}) collective-permute-start(bf16[128,512]{1,0:T(8,128)(2,1)S(1)} %convert_add_fusion.2), channel_id=1, source_target_pairs={{0,6},{1,7},{2,0},{3,1},{4,2},{5,3},{6,4},{7,5},{8,14},{9,15},{10,... | collective-permute-start | bytes 393224 | tf_op jit(solution)/shard_map/ppermute | solution.py:53
  165.2 28.9 %collective-permute-start.17 = (bf16[3,128,512]{2,1,0:T(8,128)(2,1)}, bf16[3,128,512]{2,1,0:T(8,128)(2,1)}, u32[]{:S(2)}, u32[]{:S(2)}) collective-permute-start(bf16[3,128,512]{2,1,0:T(8,128)(2,1)} %pad_maximum_fusion.4), channel_id=1, source_target_pairs={{0,192},{32,224},{64,256},{96,288},{128,320},{160,352},{192,384},{... | collective-permute-start | bytes 1179656 | tf_op jit(solution)/shard_map/ppermute | solution.py:53
  171.1 22.9 %collective-permute-start.16 = (bf16[3,128,512]{2,1,0:T(8,128)(2,1)}, bf16[3,128,512]{2,1,0:T(8,128)(2,1)}, u32[]{:S(2)}, u32[]{:S(2)}) collective-permute-start(bf16[3,128,512]{2,1,0:T(8,128)(2,1)} %pad_maximum_fusion.4), channel_id=1, source_target_pairs={{0,384},{32,416},{64,448},{96,480},{128,512},{160,544},{192,576},{... | collective-permute-start | bytes 1179656 | tf_op jit(solution)/shard_map/ppermute | solution.py:53
  174.8 19.3 %collective-permute-start.15 = (bf16[3,128,512]{2,1,0:T(8,128)(2,1)}, bf16[3,128,512]{2,1,0:T(8,128)(2,1)}, u32[]{:S(2)}, u32[]{:S(2)}) collective-permute-start(bf16[3,128,512]{2,1,0:T(8,128)(2,1)} %pad_maximum_fusion.4), channel_id=1, source_target_pairs={{0,576},{32,608},{64,640},{96,672},{128,704},{160,736},{192,0},{22... | collective-permute-start | bytes 1179656 | tf_op jit(solution)/shard_map/ppermute | solution.py:53
  177.6 11.2 %collective-permute-start.19 = (bf16[128,512]{1,0:T(8,128)(2,1)S(1)}, bf16[128,512]{1,0:T(8,128)(2,1)}, u32[]{:S(2)}, u32[]{:S(2)}) collective-permute-start(bf16[128,512]{1,0:T(8,128)(2,1)S(1)} %convert_add_fusion.2), channel_id=1, source_target_pairs={{0,4},{1,5},{2,6},{3,7},{4,0},{5,1},{6,2},{7,3},{8,12},{9,13},{10,... | collective-permute-start | bytes 393224 | tf_op jit(solution)/shard_map/ppermute | solution.py:53
  181.2 11.1 %collective-permute-start.20 = (bf16[128,512]{1,0:T(8,128)(2,1)S(1)}, bf16[128,512]{1,0:T(8,128)(2,1)}, u32[]{:S(2)}, u32[]{:S(2)}) collective-permute-start(bf16[128,512]{1,0:T(8,128)(2,1)S(1)} %convert_add_fusion.2), channel_id=1, source_target_pairs={{0,2},{1,3},{2,4},{3,5},{4,6},{5,7},{6,0},{7,1},{8,10},{9,11},{10,... | collective-permute-start | bytes 393224 | tf_op jit(solution)/shard_map/ppermute | solution.py:53
  187.3 5.1 %copy-start.10 = (bf16[128,512]{1,0:T(8,128)(2,1)S(1)}, bf16[128,512]{1,0:T(8,128)(2,1)}, u32[]{:S(2)}) copy-start(bf16[128,512]{1,0:T(8,128)(2,1)} %copy-done.9) | copy-start | bytes 393220
  200.6 26.8 %collective-permute-start.21 = (f32[512,512]{1,0:T(8,128)}, f32[512,512]{1,0:T(8,128)}, u32[]{:S(2)}, u32[]{:S(2)}) collective-permute-start(f32[512,512]{1,0:T(8,128)} %add_bitcast_fusion), channel_id=1, source_target_pairs={{0,32},{32,0},{64,96},{96,64},{128,160},{160,128},{192,224},{224,1... | collective-permute-start | bytes 3145736 | tf_op jit(solution)/shard_map/ppermute | solution.py:53
  204.0 25.2 %copy-start.3 = (f32[128,4,128]{2,1,0:T(4,128)S(1)}, f32[128,4,128]{2,1,0:T(4,128)}, u32[]{:S(2)}) copy-start(f32[128,4,128]{2,1,0:T(4,128)} %copy-done.2) | copy-start | bytes 786436
  204.0 19.0 %collective-permute-start.22 = (bf16[128,512]{1,0:T(8,128)(2,1)S(1)}, bf16[128,512]{1,0:T(8,128)(2,1)S(1)}, u32[]{:S(2)}, u32[]{:S(2)}) collective-permute-start(bf16[128,512]{1,0:T(8,128)(2,1)S(1)} %copy-done.4), channel_id=1, source_target_pairs={{0,24},{1,25},{2,26},{3,27},{4,28},{5,29},{6,30},{7,31},{8,0},{9,1... | collective-permute-start | bytes 393224 | tf_op jit(solution)/shard_map/ppermute | solution.py:53
  214.7 12.6 %collective-permute-start.23 = (bf16[128,512]{1,0:T(8,128)(2,1)S(1)}, bf16[128,512]{1,0:T(8,128)(2,1)S(1)}, u32[]{:S(2)}, u32[]{:S(2)}) collective-permute-start(bf16[128,512]{1,0:T(8,128)(2,1)S(1)} %copy-done.4), channel_id=1, source_target_pairs={{0,16},{1,17},{2,18},{3,19},{4,20},{5,21},{6,22},{7,23},{8,24},{9,... | collective-permute-start | bytes 393224 | tf_op jit(solution)/shard_map/ppermute | solution.py:53
  216.6 10.6 %collective-permute-start.24 = (bf16[128,512]{1,0:T(8,128)(2,1)S(1)}, bf16[128,512]{1,0:T(8,128)(2,1)S(1)}, u32[]{:S(2)}, u32[]{:S(2)}) collective-permute-start(bf16[128,512]{1,0:T(8,128)(2,1)S(1)} %copy-done.4), channel_id=1, source_target_pairs={{0,8},{1,9},{2,10},{3,11},{4,12},{5,13},{6,14},{7,15},{8,16},{9,17... | collective-permute-start | bytes 393224 | tf_op jit(solution)/shard_map/ppermute | solution.py:53
  (8 other events, 11.6 us)

commit v10 on v8

--- a/solution.py
+++ b/solution.py
@@ -193,6 +193,9 @@
 
     latent_part = back_project(key_flat, w_uk) + back_project(value_flat, w_uv)
     sum_levels = digits_of(lax.axis_size("heads"))
+    if len(sum_levels) > 2 and sum_levels[-1][0] == 4:
+        last_stride = sum_levels[-1][1]
+        sum_levels = sum_levels[:-1] + [(2, last_stride), (2, last_stride * 2)]
     gather_levels = gather_order(block_count)
     comp_own = comp_all.reshape(radices + (row_count, col_width))[0]
 

time: 232 us -> 228 us (0.983)
  starting transfers between devices: 106 us -> 102 us
  waiting for transfers between devices: 71.3 us -> 75.1 us
    ppermute x25 -> x24, starting transfers between devices: 106 us -> 102 us  [shift_digit(): return lax.ppermute(x, axis, pairs)]
    ppermute x25 -> x24, waiting for transfers between devices: 71.3 us -> 75.1 us  [shift_digit(): return lax.ppermute(x, axis, pairs)]
  transfers between devices with their start and end apart: 25 -> 24, of which waited for: 15 -> 16; matrix products, arithmetic and copies ran while one was open for 8% -> 7% of each run, Pallas kernels for 0% -> 0%
where the time goes in v10:
time: 228 us; the launch traced here: 226 us
  starting transfers between devices  102 us (45%)
  waiting for transfers between devices  75.1 us (33%)
  other arithmetic  21.6 us (9%)
  matrix products  13.5 us (6%)
  local copies, waits for them, and re-layouts  12.3 us (5%)
    ppermute x24, starting transfers between devices, shift_digit(): return lax.ppermute(x, axis, pairs)  102 us
    ppermute x24, waiting for transfers between devices, shift_digit(): return lax.ppermute(x, axis, pairs)  75.1 us
    another operation x7, other arithmetic, gather_step(): return jnp.stack(pieces, axis=0)  7.31 us
  transfers between devices with their start and end apart: 24, of which 16 were waited for; matrix products, arithmetic and copies ran while one was open for 7% of the time, Pallas kernels for 0%

profile of v10, /device:TPU:56, one launch (start us, length us, event | category | flops | bytes accessed | tf_op | source)
XLA Modules:
  0.0 226.2 jit_solution(13123254640719896943)
XLA Ops:
  4.7 11.0 %collective-permute-start.1 = (bf16[128,578]{1,0:T(8,128)(2,1)S(1)}, bf16[128,578]{1,0:T(8,128)(2,1)S(1)}, u32[]{:S(2)}, u32[]{:S(2)}) collective-permute-start(bf16[128,578]{1,0:T(8,128)(2,1)S(1)} %pad_maximum_fusion.4), channel_id=1, source_target_pairs={{0,64},{32,96},{64,128},{96,160},{128,0},{160,32},{192,256},{224,2... | collective-permute-start | bytes 443912 | tf_op jit(solution)/shard_map/ppermute | solution.py:53
  15.8 5.6 %collective-permute-start = (bf16[128,578]{1,0:T(8,128)(2,1)S(1)}, bf16[128,578]{1,0:T(8,128)(2,1)S(1)}, u32[]{:S(2)}, u32[]{:S(2)}) collective-permute-start(bf16[128,578]{1,0:T(8,128)(2,1)S(1)} %pad_maximum_fusion.4), channel_id=1, source_target_pairs={{0,128},{32,160},{64,0},{96,32},{128,64},{160,96},{192,320},{224,3... | collective-permute-start | bytes 443912 | tf_op jit(solution)/shard_map/ppermute | solution.py:53
  21.4 2.5 %collective-permute-done.1 = bf16[128,578]{1,0:T(8,128)(2,1)S(1)} collective-permute-done((bf16[128,578]{1,0:T(8,128)(2,1)S(1)}, bf16[128,578]{1,0:T(8,128)(2,1)S(1)}, u32[]{:S(2)}, u32[]{:S(2)}) %collective-permute-start.1) | collective-permute-done | bytes 148000 | tf_op jit(solution)/shard_map/ppermute | solution.py:53
  23.9 11.5 %collective-permute-done = bf16[128,578]{1,0:T(8,128)(2,1)S(1)} collective-permute-done((bf16[128,578]{1,0:T(8,128)(2,1)S(1)}, bf16[128,578]{1,0:T(8,128)(2,1)S(1)}, u32[]{:S(2)}, u32[]{:S(2)}) %collective-permute-start) | collective-permute-done | bytes 148000 | tf_op jit(solution)/shard_map/ppermute | solution.py:53
  35.5 3.4 %collective-permute-start.4 = (bf16[3,128,578]{2,1,0:T(8,128)(2,1)S(1)}, bf16[3,128,578]{2,1,0:T(8,128)(2,1)S(1)}, u32[]{:S(2)}, u32[]{:S(2)}) collective-permute-start(bf16[3,128,578]{2,1,0:T(8,128)(2,1)S(1)} %get-tuple-element.46), channel_id=1, source_target_pairs={{0,192},{32,224},{64,256},{96,288},{128,320},{160,352},{192,384},{... | collective-permute-start | bytes 1331720 | tf_op jit(solution)/shard_map/ppermute | solution.py:53
  38.9 4.6 %collective-permute-start.3 = (bf16[3,128,578]{2,1,0:T(8,128)(2,1)S(1)}, bf16[3,128,578]{2,1,0:T(8,128)(2,1)S(1)}, u32[]{:S(2)}, u32[]{:S(2)}) collective-permute-start(bf16[3,128,578]{2,1,0:T(8,128)(2,1)S(1)} %get-tuple-element.46), channel_id=1, source_target_pairs={{0,384},{32,416},{64,448},{96,480},{128,512},{160,544},{192,576},{... | collective-permute-start | bytes 1331720 | tf_op jit(solution)/shard_map/ppermute | solution.py:53
  43.6 3.3 %collective-permute-start.2 = (bf16[3,128,578]{2,1,0:T(8,128)(2,1)S(1)}, bf16[3,128,578]{2,1,0:T(8,128)(2,1)S(1)}, u32[]{:S(2)}, u32[]{:S(2)}) collective-permute-start(bf16[3,128,578]{2,1,0:T(8,128)(2,1)S(1)} %get-tuple-element.46), channel_id=1, source_target_pairs={{0,576},{32,608},{64,640},{96,672},{128,704},{160,736},{192,0},{22... | collective-permute-start | bytes 1331720 | tf_op jit(solution)/shard_map/ppermute | solution.py:53
  46.9 4.9 %collective-permute-done.4 = bf16[3,128,578]{2,1,0:T(8,128)(2,1)S(1)} collective-permute-done((bf16[3,128,578]{2,1,0:T(8,128)(2,1)S(1)}, bf16[3,128,578]{2,1,0:T(8,128)(2,1)S(1)}, u32[]{:S(2)}, u32[]{:S(2)}) %collective-permute-start.4) | collective-permute-done | bytes 443936 | tf_op jit(solution)/shard_map/ppermute | solution.py:53
  51.8 9.7 %collective-permute-done.3 = bf16[3,128,578]{2,1,0:T(8,128)(2,1)S(1)} collective-permute-done((bf16[3,128,578]{2,1,0:T(8,128)(2,1)S(1)}, bf16[3,128,578]{2,1,0:T(8,128)(2,1)S(1)}, u32[]{:S(2)}, u32[]{:S(2)}) %collective-permute-start.3) | collective-permute-done | bytes 443936 | tf_op jit(solution)/shard_map/ppermute | solution.py:53
  83.9 2.4 %collective-permute-start.6 = (bf16[2,2,4,3,128,128]{5,4,3,2,1,0:T(8,128)(2,1)S(1)}, bf16[2,2,4,3,128,128]{5,4,3,2,1,0:T(8,128)(2,1)S(1)}, u32[]{:S(2)}, u32[]{:S(2)}) collective-permute-start(bf16[2,2,4,3,128,128]{5,4,3,2,1,0:T(8,128)(2,1)S(1)} %fusion.24), channel_id=1, source_target_pairs={{0,32},{32,0},{64,96},{96,64},{128,160},{160,128},{192,224},{224,1... | collective-permute-start | bytes 4718600 | tf_op jit(solution)/shard_map/ppermute | solution.py:53
  86.3 2.8 %collective-permute-done.6 = bf16[2,2,4,3,128,128]{5,4,3,2,1,0:T(8,128)(2,1)S(1)} collective-permute-done((bf16[2,2,4,3,128,128]{5,4,3,2,1,0:T(8,128)(2,1)S(1)}, bf16[2,2,4,3,128,128]{5,4,3,2,1,0:T(8,128)(2,1)S(1)}, u32[]{:S(2)}, u32[]{:S(2)}) %collective-permute-start.6) | collective-permute-done | bytes 1572896 | tf_op jit(solution)/shard_map/ppermute | solution.py:53
  90.0 4.5 %collective-permute-start.9 = (bf16[2,2,3,128,128]{4,3,2,1,0:T(8,128)(2,1)S(1)}, bf16[2,2,3,128,128]{4,3,2,1,0:T(8,128)(2,1)S(1)}, u32[]{:S(2)}, u32[]{:S(2)}) collective-permute-start(bf16[2,2,3,128,128]{4,3,2,1,0:T(8,128)(2,1)S(1)} %get-tuple-element.41), channel_id=1, source_target_pairs={{0,576},{32,608},{64,640},{96,672},{128,704},{160,736},{192,0},{22... | collective-permute-start | bytes 1179656 | tf_op jit(solution)/shard_map/ppermute | solution.py:53
  94.6 3.7 %collective-permute-start.8 = (bf16[2,2,3,128,128]{4,3,2,1,0:T(8,128)(2,1)S(1)}, bf16[2,2,3,128,128]{4,3,2,1,0:T(8,128)(2,1)S(1)}, u32[]{:S(2)}, u32[]{:S(2)}) collective-permute-start(bf16[2,2,3,128,128]{4,3,2,1,0:T(8,128)(2,1)S(1)} %get-tuple-element.42), channel_id=1, source_target_pairs={{0,384},{32,416},{64,448},{96,480},{128,512},{160,544},{192,576},{... | collective-permute-start | bytes 1179656 | tf_op jit(solution)/shard_map/ppermute | solution.py:53
  100.2 11.7 %collective-permute-done.9 = bf16[2,2,3,128,128]{4,3,2,1,0:T(8,128)(2,1)S(1)} collective-permute-done((bf16[2,2,3,128,128]{4,3,2,1,0:T(8,128)(2,1)S(1)}, bf16[2,2,3,128,128]{4,3,2,1,0:T(8,128)(2,1)S(1)}, u32[]{:S(2)}, u32[]{:S(2)}) %collective-permute-start.9) | collective-permute-done | bytes 393248 | tf_op jit(solution)/shard_map/ppermute | solution.py:53
  111.9 5.6 %collective-permute-done.7 = bf16[2,2,3,128,128]{4,3,2,1,0:T(8,128)(2,1)S(1)} collective-permute-done((bf16[2,2,3,128,128]{4,3,2,1,0:T(8,128)(2,1)S(1)}, bf16[2,2,3,128,128]{4,3,2,1,0:T(8,128)(2,1)S(1)}, u32[]{:S(2)}, u32[]{:S(2)}) %collective-permute-start.7) | collective-permute-done | bytes 393248 | tf_op jit(solution)/shard_map/ppermute | solution.py:53
  117.7 7.1 %collective-permute-start.11 = (bf16[2,2,128,128]{3,2,1,0:T(8,128)(2,1)S(1)}, bf16[2,2,128,128]{3,2,1,0:T(8,128)(2,1)S(1)}, u32[]{:S(2)}, u32[]{:S(2)}) collective-permute-start(bf16[2,2,128,128]{3,2,1,0:T(8,128)(2,1)S(1)} %get-tuple-element.48), channel_id=1, source_target_pairs={{0,128},{32,160},{64,0},{96,32},{128,64},{160,96},{192,320},{224,3... | collective-permute-start | bytes 393224 | tf_op jit(solution)/shard_map/ppermute | solution.py:53
  124.8 2.7 %collective-permute-start.10 = (bf16[2,2,128,128]{3,2,1,0:T(8,128)(2,1)S(1)}, bf16[2,2,128,128]{3,2,1,0:T(8,128)(2,1)S(1)}, u32[]{:S(2)}, u32[]{:S(2)}) collective-permute-start(bf16[2,2,128,128]{3,2,1,0:T(8,128)(2,1)S(1)} %get-tuple-element.47), channel_id=1, source_target_pairs={{0,64},{32,96},{64,128},{96,160},{128,0},{160,32},{192,256},{224,2... | collective-permute-start | bytes 393224 | tf_op jit(solution)/shard_map/ppermute | solution.py:53
  127.5 2.5 %collective-permute-done.11 = bf16[2,2,128,128]{3,2,1,0:T(8,128)(2,1)S(1)} collective-permute-done((bf16[2,2,128,128]{3,2,1,0:T(8,128)(2,1)S(1)}, bf16[2,2,128,128]{3,2,1,0:T(8,128)(2,1)S(1)}, u32[]{:S(2)}, u32[]{:S(2)}) %collective-permute-start.11) | collective-permute-done | bytes 131104 | tf_op jit(solution)/shard_map/ppermute | solution.py:53
  130.0 7.8 %collective-permute-done.10 = bf16[2,2,128,128]{3,2,1,0:T(8,128)(2,1)S(1)} collective-permute-done((bf16[2,2,128,128]{3,2,1,0:T(8,128)(2,1)S(1)}, bf16[2,2,128,128]{3,2,1,0:T(8,128)(2,1)S(1)}, u32[]{:S(2)}, u32[]{:S(2)}) %collective-permute-start.10) | collective-permute-done | bytes 131104 | tf_op jit(solution)/shard_map/ppermute | solution.py:53
  138.7 4.2 %collective-permute-start.13 = (bf16[128,512]{1,0:T(8,128)(2,1)}, bf16[128,512]{1,0:T(8,128)(2,1)}, u32[]{:S(2)}, u32[]{:S(2)}) collective-permute-start(bf16[128,512]{1,0:T(8,128)(2,1)} %convert_element_type.223), channel_id=1, source_target_pairs={{0,64},{32,96},{64,128},{96,160},{128,0},{160,32},{192,256},{224,2... | collective-permute-start | bytes 393224 | tf_op jit(solution)/shard_map/ppermute | solution.py:53
  142.9 5.5 %collective-permute-start.12 = (bf16[128,512]{1,0:T(8,128)(2,1)}, bf16[128,512]{1,0:T(8,128)(2,1)}, u32[]{:S(2)}, u32[]{:S(2)}) collective-permute-start(bf16[128,512]{1,0:T(8,128)(2,1)} %convert_element_type.223), channel_id=1, source_target_pairs={{0,128},{32,160},{64,0},{96,32},{128,64},{160,96},{192,320},{224,3... | collective-permute-start | bytes 393224 | tf_op jit(solution)/shard_map/ppermute | solution.py:53
  151.4 3.2 %collective-permute-start.14 = (bf16[128,512]{1,0:T(8,128)(2,1)}, bf16[128,512]{1,0:T(8,128)(2,1)}, u32[]{:S(2)}, u32[]{:S(2)}) collective-permute-start(bf16[128,512]{1,0:T(8,128)(2,1)} %fusion.28), channel_id=1, source_target_pairs={{0,1},{1,0},{2,3},{3,2},{4,5},{5,4},{6,7},{7,6},{8,9},{9,8},{10,11... | collective-permute-start | bytes 393224 | tf_op jit(solution)/shard_map/ppermute | solution.py:53
  159.6 4.0 %collective-permute-start.18 = (bf16[128,512]{1,0:T(8,128)(2,1)S(1)}, bf16[128,512]{1,0:T(8,128)(2,1)S(1)}, u32[]{:S(2)}, u32[]{:S(2)}) collective-permute-start(bf16[128,512]{1,0:T(8,128)(2,1)S(1)} %convert_add_fusion.3), channel_id=1, source_target_pairs={{0,6},{1,7},{2,0},{3,1},{4,2},{5,3},{6,4},{7,5},{8,14},{9,15},{10,... | collective-permute-start | bytes 393224 | tf_op jit(solution)/shard_map/ppermute | solution.py:53
  163.6 3.8 %collective-permute-start.17 = (bf16[3,128,512]{2,1,0:T(8,128)(2,1)}, bf16[3,128,512]{2,1,0:T(8,128)(2,1)}, u32[]{:S(2)}, u32[]{:S(2)}) collective-permute-start(bf16[3,128,512]{2,1,0:T(8,128)(2,1)} %pad_maximum_fusion.3), channel_id=1, source_target_pairs={{0,192},{32,224},{64,256},{96,288},{128,320},{160,352},{192,384},{... | collective-permute-start | bytes 1179656 | tf_op jit(solution)/shard_map/ppermute | solution.py:53
  167.5 3.6 %collective-permute-start.16 = (bf16[3,128,512]{2,1,0:T(8,128)(2,1)}, bf16[3,128,512]{2,1,0:T(8,128)(2,1)}, u32[]{:S(2)}, u32[]{:S(2)}) collective-permute-start(bf16[3,128,512]{2,1,0:T(8,128)(2,1)} %pad_maximum_fusion.3), channel_id=1, source_target_pairs={{0,384},{32,416},{64,448},{96,480},{128,512},{160,544},{192,576},{... | collective-permute-start | bytes 1179656 | tf_op jit(solution)/shard_map/ppermute | solution.py:53
  171.1 2.9 %collective-permute-start.15 = (bf16[3,128,512]{2,1,0:T(8,128)(2,1)}, bf16[3,128,512]{2,1,0:T(8,128)(2,1)}, u32[]{:S(2)}, u32[]{:S(2)}) collective-permute-start(bf16[3,128,512]{2,1,0:T(8,128)(2,1)} %pad_maximum_fusion.3), channel_id=1, source_target_pairs={{0,576},{32,608},{64,640},{96,672},{128,704},{160,736},{192,0},{22... | collective-permute-start | bytes 1179656 | tf_op jit(solution)/shard_map/ppermute | solution.py:53
  174.0 2.9 %collective-permute-start.19 = (bf16[128,512]{1,0:T(8,128)(2,1)S(1)}, bf16[128,512]{1,0:T(8,128)(2,1)}, u32[]{:S(2)}, u32[]{:S(2)}) collective-permute-start(bf16[128,512]{1,0:T(8,128)(2,1)S(1)} %convert_add_fusion.3), channel_id=1, source_target_pairs={{0,4},{1,5},{2,6},{3,7},{4,0},{5,1},{6,2},{7,3},{8,12},{9,13},{10,... | collective-permute-start | bytes 393224 | tf_op jit(solution)/shard_map/ppermute | solution.py:53
  177.6 5.7 %collective-permute-start.20 = (bf16[128,512]{1,0:T(8,128)(2,1)S(1)}, bf16[128,512]{1,0:T(8,128)(2,1)}, u32[]{:S(2)}, u32[]{:S(2)}) collective-permute-start(bf16[128,512]{1,0:T(8,128)(2,1)S(1)} %convert_add_fusion.3), channel_id=1, source_target_pairs={{0,2},{1,3},{2,4},{3,5},{4,6},{5,7},{6,0},{7,1},{8,10},{9,11},{10,... | collective-permute-start | bytes 393224 | tf_op jit(solution)/shard_map/ppermute | solution.py:53
  185.2 4.9 %collective-permute-done.20 = bf16[128,512]{1,0:T(8,128)(2,1)} collective-permute-done((bf16[128,512]{1,0:T(8,128)(2,1)S(1)}, bf16[128,512]{1,0:T(8,128)(2,1)}, u32[]{:S(2)}, u32[]{:S(2)}) %collective-permute-start.20) | collective-permute-done | bytes 131104 | tf_op jit(solution)/shard_map/ppermute | solution.py:53
  202.1 4.7 %collective-permute-done.22 = bf16[128,512]{1,0:T(8,128)(2,1)S(1)} collective-permute-done((bf16[128,512]{1,0:T(8,128)(2,1)S(1)}, bf16[128,512]{1,0:T(8,128)(2,1)S(1)}, u32[]{:S(2)}, u32[]{:S(2)}) %collective-permute-start.22) | collective-permute-done | bytes 131104 | tf_op jit(solution)/shard_map/ppermute | solution.py:53
  207.0 10.1 %collective-permute-start.23 = (bf16[128,512]{1,0:T(8,128)(2,1)S(1)}, bf16[128,512]{1,0:T(8,128)(2,1)}, u32[]{:S(2)}, u32[]{:S(2)}) collective-permute-start(bf16[128,512]{1,0:T(8,128)(2,1)S(1)} %convert_add_fusion.1), channel_id=1, source_target_pairs={{0,16},{1,17},{2,18},{3,19},{4,20},{5,21},{6,22},{7,23},{8,24},{9,... | collective-permute-start | bytes 393224 | tf_op jit(solution)/shard_map/ppermute | solution.py:53
  220.1 3.4 %collective-permute-done.23 = bf16[128,512]{1,0:T(8,128)(2,1)} collective-permute-done((bf16[128,512]{1,0:T(8,128)(2,1)S(1)}, bf16[128,512]{1,0:T(8,128)(2,1)}, u32[]{:S(2)}, u32[]{:S(2)}) %collective-permute-start.23) | collective-permute-done | bytes 131104 | tf_op jit(solution)/shard_map/ppermute | solution.py:53
  (113 shorter events, 58.1 us)
Async XLA Ops:
  0.6 72.3 %copy-start = (bf16[512,256]{1,0:T(8,128)(2,1)S(1)}, bf16[512,256]{1,0:T(8,128)(2,1)}, u32[]{:S(2)}) copy-start(bf16[512,256]{1,0:T(8,128)(2,1)} %param.16) | copy-start | bytes 786436
  4.5 30.9 %copy-start.2 = (f32[128,4,128]{2,1,0:T(4,128)}, f32[128,4,128]{2,1,0:T(4,128)S(1)}, u32[]{:S(2)}) copy-start(f32[128,4,128]{2,1,0:T(4,128)S(1)} %broadcast_in_dim.42) | copy-start | bytes 786436
  4.6 61.2 %copy-start.13 = (bf16[128,256]{1,0:T(8,128)(2,1)S(1)}, bf16[128,256]{1,0:T(8,128)(2,1)}, u32[]{:S(2)}) copy-start(bf16[128,256]{1,0:T(8,128)(2,1)} %param.11) | copy-start | bytes 196612
  4.6 61.3 %copy-start.15 = (bf16[128,128]{1,0:T(8,128)(2,1)S(1)}, bf16[128,128]{1,0:T(8,128)(2,1)}, u32[]{:S(2)}) copy-start(bf16[128,128]{1,0:T(8,128)(2,1)} %param.10) | copy-start | bytes 98308
  4.6 62.0 %copy-start.14 = (bf16[128,256]{1,0:T(8,128)(2,1)S(1)}, bf16[128,256]{1,0:T(8,128)(2,1)}, u32[]{:S(2)}) copy-start(bf16[128,256]{1,0:T(8,128)(2,1)} %param.9) | copy-start | bytes 196612
  4.7 19.2 %collective-permute-start.1 = (bf16[128,578]{1,0:T(8,128)(2,1)S(1)}, bf16[128,578]{1,0:T(8,128)(2,1)S(1)}, u32[]{:S(2)}, u32[]{:S(2)}) collective-permute-start(bf16[128,578]{1,0:T(8,128)(2,1)S(1)} %pad_maximum_fusion.4), channel_id=1, source_target_pairs={{0,64},{32,96},{64,128},{96,160},{128,0},{160,32},{192,256},{224,2... | collective-permute-start | bytes 443912 | tf_op jit(solution)/shard_map/ppermute | solution.py:53
  15.8 19.6 %collective-permute-start = (bf16[128,578]{1,0:T(8,128)(2,1)S(1)}, bf16[128,578]{1,0:T(8,128)(2,1)S(1)}, u32[]{:S(2)}, u32[]{:S(2)}) collective-permute-start(bf16[128,578]{1,0:T(8,128)(2,1)S(1)} %pad_maximum_fusion.4), channel_id=1, source_target_pairs={{0,128},{32,160},{64,0},{96,32},{128,64},{160,96},{192,320},{224,3... | collective-permute-start | bytes 443912 | tf_op jit(solution)/shard_map/ppermute | solution.py:53
  35.5 16.3 %collective-permute-start.4 = (bf16[3,128,578]{2,1,0:T(8,128)(2,1)S(1)}, bf16[3,128,578]{2,1,0:T(8,128)(2,1)S(1)}, u32[]{:S(2)}, u32[]{:S(2)}) collective-permute-start(bf16[3,128,578]{2,1,0:T(8,128)(2,1)S(1)} %get-tuple-element.46), channel_id=1, source_target_pairs={{0,192},{32,224},{64,256},{96,288},{128,320},{160,352},{192,384},{... | collective-permute-start | bytes 1331720 | tf_op jit(solution)/shard_map/ppermute | solution.py:53
  38.9 22.6 %collective-permute-start.3 = (bf16[3,128,578]{2,1,0:T(8,128)(2,1)S(1)}, bf16[3,128,578]{2,1,0:T(8,128)(2,1)S(1)}, u32[]{:S(2)}, u32[]{:S(2)}) collective-permute-start(bf16[3,128,578]{2,1,0:T(8,128)(2,1)S(1)} %get-tuple-element.46), channel_id=1, source_target_pairs={{0,384},{32,416},{64,448},{96,480},{128,512},{160,544},{192,576},{... | collective-permute-start | bytes 1331720 | tf_op jit(solution)/shard_map/ppermute | solution.py:53
  43.6 19.5 %collective-permute-start.2 = (bf16[3,128,578]{2,1,0:T(8,128)(2,1)S(1)}, bf16[3,128,578]{2,1,0:T(8,128)(2,1)S(1)}, u32[]{:S(2)}, u32[]{:S(2)}) collective-permute-start(bf16[3,128,578]{2,1,0:T(8,128)(2,1)S(1)} %get-tuple-element.46), channel_id=1, source_target_pairs={{0,576},{32,608},{64,640},{96,672},{128,704},{160,736},{192,0},{22... | collective-permute-start | bytes 1331720 | tf_op jit(solution)/shard_map/ppermute | solution.py:53
  63.9 6.0 %collective-permute-start.5 = (bf16[4,3,128,640]{3,2,1,0:T(8,128)(2,1)S(1)}, bf16[4,3,128,640]{3,2,1,0:T(8,128)(2,1)}, u32[]{:S(2)}, u32[]{:S(2)}) collective-permute-start(bf16[4,3,128,640]{3,2,1,0:T(8,128)(2,1)S(1)} %fusion.22), channel_id=1, source_target_pairs={{0,32},{32,0},{64,96},{96,64},{128,160},{160,128},{192,224},{224,1... | collective-permute-start | bytes 5898248 | tf_op jit(solution)/shard_map/ppermute | solution.py:53
  83.9 5.3 %collective-permute-start.6 = (bf16[2,2,4,3,128,128]{5,4,3,2,1,0:T(8,128)(2,1)S(1)}, bf16[2,2,4,3,128,128]{5,4,3,2,1,0:T(8,128)(2,1)S(1)}, u32[]{:S(2)}, u32[]{:S(2)}) collective-permute-start(bf16[2,2,4,3,128,128]{5,4,3,2,1,0:T(8,128)(2,1)S(1)} %fusion.24), channel_id=1, source_target_pairs={{0,32},{32,0},{64,96},{96,64},{128,160},{160,128},{192,224},{224,1... | collective-permute-start | bytes 4718600 | tf_op jit(solution)/shard_map/ppermute | solution.py:53
  90.0 21.9 %collective-permute-start.9 = (bf16[2,2,3,128,128]{4,3,2,1,0:T(8,128)(2,1)S(1)}, bf16[2,2,3,128,128]{4,3,2,1,0:T(8,128)(2,1)S(1)}, u32[]{:S(2)}, u32[]{:S(2)}) collective-permute-start(bf16[2,2,3,128,128]{4,3,2,1,0:T(8,128)(2,1)S(1)} %get-tuple-element.41), channel_id=1, source_target_pairs={{0,576},{32,608},{64,640},{96,672},{128,704},{160,736},{192,0},{22... | collective-permute-start | bytes 1179656 | tf_op jit(solution)/shard_map/ppermute | solution.py:53
  94.6 17.3 %collective-permute-start.8 = (bf16[2,2,3,128,128]{4,3,2,1,0:T(8,128)(2,1)S(1)}, bf16[2,2,3,128,128]{4,3,2,1,0:T(8,128)(2,1)S(1)}, u32[]{:S(2)}, u32[]{:S(2)}) collective-permute-start(bf16[2,2,3,128,128]{4,3,2,1,0:T(8,128)(2,1)S(1)} %get-tuple-element.42), channel_id=1, source_target_pairs={{0,384},{32,416},{64,448},{96,480},{128,512},{160,544},{192,576},{... | collective-permute-start | bytes 1179656 | tf_op jit(solution)/shard_map/ppermute | solution.py:53
  98.3 19.2 %collective-permute-start.7 = (bf16[2,2,3,128,128]{4,3,2,1,0:T(8,128)(2,1)S(1)}, bf16[2,2,3,128,128]{4,3,2,1,0:T(8,128)(2,1)S(1)}, u32[]{:S(2)}, u32[]{:S(2)}) collective-permute-start(bf16[2,2,3,128,128]{4,3,2,1,0:T(8,128)(2,1)S(1)} %get-tuple-element.40), channel_id=1, source_target_pairs={{0,192},{32,224},{64,256},{96,288},{128,320},{160,352},{192,384},{... | collective-permute-start | bytes 1179656 | tf_op jit(solution)/shard_map/ppermute | solution.py:53
  117.7 12.3 %collective-permute-start.11 = (bf16[2,2,128,128]{3,2,1,0:T(8,128)(2,1)S(1)}, bf16[2,2,128,128]{3,2,1,0:T(8,128)(2,1)S(1)}, u32[]{:S(2)}, u32[]{:S(2)}) collective-permute-start(bf16[2,2,128,128]{3,2,1,0:T(8,128)(2,1)S(1)} %get-tuple-element.48), channel_id=1, source_target_pairs={{0,128},{32,160},{64,0},{96,32},{128,64},{160,96},{192,320},{224,3... | collective-permute-start | bytes 393224 | tf_op jit(solution)/shard_map/ppermute | solution.py:53
  124.8 13.0 %collective-permute-start.10 = (bf16[2,2,128,128]{3,2,1,0:T(8,128)(2,1)S(1)}, bf16[2,2,128,128]{3,2,1,0:T(8,128)(2,1)S(1)}, u32[]{:S(2)}, u32[]{:S(2)}) collective-permute-start(bf16[2,2,128,128]{3,2,1,0:T(8,128)(2,1)S(1)} %get-tuple-element.47), channel_id=1, source_target_pairs={{0,64},{32,96},{64,128},{96,160},{128,0},{160,32},{192,256},{224,2... | collective-permute-start | bytes 393224 | tf_op jit(solution)/shard_map/ppermute | solution.py:53
  138.7 16.7 %collective-permute-start.13 = (bf16[128,512]{1,0:T(8,128)(2,1)}, bf16[128,512]{1,0:T(8,128)(2,1)}, u32[]{:S(2)}, u32[]{:S(2)}) collective-permute-start(bf16[128,512]{1,0:T(8,128)(2,1)} %convert_element_type.223), channel_id=1, source_target_pairs={{0,64},{32,96},{64,128},{96,160},{128,0},{160,32},{192,256},{224,2... | collective-permute-start | bytes 393224 | tf_op jit(solution)/shard_map/ppermute | solution.py:53
  142.9 13.8 %collective-permute-start.12 = (bf16[128,512]{1,0:T(8,128)(2,1)}, bf16[128,512]{1,0:T(8,128)(2,1)}, u32[]{:S(2)}, u32[]{:S(2)}) collective-permute-start(bf16[128,512]{1,0:T(8,128)(2,1)} %convert_element_type.223), channel_id=1, source_target_pairs={{0,128},{32,160},{64,0},{96,32},{128,64},{160,96},{192,320},{224,3... | collective-permute-start | bytes 393224 | tf_op jit(solution)/shard_map/ppermute | solution.py:53
  151.4 7.2 %collective-permute-start.14 = (bf16[128,512]{1,0:T(8,128)(2,1)}, bf16[128,512]{1,0:T(8,128)(2,1)}, u32[]{:S(2)}, u32[]{:S(2)}) collective-permute-start(bf16[128,512]{1,0:T(8,128)(2,1)} %fusion.28), channel_id=1, source_target_pairs={{0,1},{1,0},{2,3},{3,2},{4,5},{5,4},{6,7},{7,6},{8,9},{9,8},{10,11... | collective-permute-start | bytes 393224 | tf_op jit(solution)/shard_map/ppermute | solution.py:53
  159.6 17.3 %collective-permute-start.18 = (bf16[128,512]{1,0:T(8,128)(2,1)S(1)}, bf16[128,512]{1,0:T(8,128)(2,1)S(1)}, u32[]{:S(2)}, u32[]{:S(2)}) collective-permute-start(bf16[128,512]{1,0:T(8,128)(2,1)S(1)} %convert_add_fusion.3), channel_id=1, source_target_pairs={{0,6},{1,7},{2,0},{3,1},{4,2},{5,3},{6,4},{7,5},{8,14},{9,15},{10,... | collective-permute-start | bytes 393224 | tf_op jit(solution)/shard_map/ppermute | solution.py:53
  163.6 27.6 %collective-permute-start.17 = (bf16[3,128,512]{2,1,0:T(8,128)(2,1)}, bf16[3,128,512]{2,1,0:T(8,128)(2,1)}, u32[]{:S(2)}, u32[]{:S(2)}) collective-permute-start(bf16[3,128,512]{2,1,0:T(8,128)(2,1)} %pad_maximum_fusion.3), channel_id=1, source_target_pairs={{0,192},{32,224},{64,256},{96,288},{128,320},{160,352},{192,384},{... | collective-permute-start | bytes 1179656 | tf_op jit(solution)/shard_map/ppermute | solution.py:53
  167.5 23.7 %collective-permute-start.16 = (bf16[3,128,512]{2,1,0:T(8,128)(2,1)}, bf16[3,128,512]{2,1,0:T(8,128)(2,1)}, u32[]{:S(2)}, u32[]{:S(2)}) collective-permute-start(bf16[3,128,512]{2,1,0:T(8,128)(2,1)} %pad_maximum_fusion.3), channel_id=1, source_target_pairs={{0,384},{32,416},{64,448},{96,480},{128,512},{160,544},{192,576},{... | collective-permute-start | bytes 1179656 | tf_op jit(solution)/shard_map/ppermute | solution.py:53
  171.1 20.1 %collective-permute-start.15 = (bf16[3,128,512]{2,1,0:T(8,128)(2,1)}, bf16[3,128,512]{2,1,0:T(8,128)(2,1)}, u32[]{:S(2)}, u32[]{:S(2)}) collective-permute-start(bf16[3,128,512]{2,1,0:T(8,128)(2,1)} %pad_maximum_fusion.3), channel_id=1, source_target_pairs={{0,576},{32,608},{64,640},{96,672},{128,704},{160,736},{192,0},{22... | collective-permute-start | bytes 1179656 | tf_op jit(solution)/shard_map/ppermute | solution.py:53
  174.0 11.2 %collective-permute-start.19 = (bf16[128,512]{1,0:T(8,128)(2,1)S(1)}, bf16[128,512]{1,0:T(8,128)(2,1)}, u32[]{:S(2)}, u32[]{:S(2)}) collective-permute-start(bf16[128,512]{1,0:T(8,128)(2,1)S(1)} %convert_add_fusion.3), channel_id=1, source_target_pairs={{0,4},{1,5},{2,6},{3,7},{4,0},{5,1},{6,2},{7,3},{8,12},{9,13},{10,... | collective-permute-start | bytes 393224 | tf_op jit(solution)/shard_map/ppermute | solution.py:53
  177.6 12.5 %collective-permute-start.20 = (bf16[128,512]{1,0:T(8,128)(2,1)S(1)}, bf16[128,512]{1,0:T(8,128)(2,1)}, u32[]{:S(2)}, u32[]{:S(2)}) collective-permute-start(bf16[128,512]{1,0:T(8,128)(2,1)S(1)} %convert_add_fusion.3), channel_id=1, source_target_pairs={{0,2},{1,3},{2,4},{3,5},{4,6},{5,7},{6,0},{7,1},{8,10},{9,11},{10,... | collective-permute-start | bytes 393224 | tf_op jit(solution)/shard_map/ppermute | solution.py:53
  183.6 6.5 %copy-start.12 = (bf16[128,512]{1,0:T(8,128)(2,1)S(1)}, bf16[128,512]{1,0:T(8,128)(2,1)}, u32[]{:S(2)}) copy-start(bf16[128,512]{1,0:T(8,128)(2,1)} %copy-done.11) | copy-start | bytes 393220
  197.0 9.8 %collective-permute-start.21 = (f32[512,512]{1,0:T(8,128)S(1)}, f32[512,512]{1,0:T(8,128)S(1)}, u32[]{:S(2)}, u32[]{:S(2)}) collective-permute-start(f32[512,512]{1,0:T(8,128)S(1)} %add_bitcast_fusion), channel_id=1, source_target_pairs={{0,32},{32,0},{64,96},{96,64},{128,160},{160,128},{192,224},{224,1... | collective-permute-start | bytes 3145736 | tf_op jit(solution)/shard_map/ppermute | solution.py:53
  198.9 7.8 %collective-permute-start.22 = (bf16[128,512]{1,0:T(8,128)(2,1)S(1)}, bf16[128,512]{1,0:T(8,128)(2,1)S(1)}, u32[]{:S(2)}, u32[]{:S(2)}) collective-permute-start(bf16[128,512]{1,0:T(8,128)(2,1)S(1)} %convert_add_fusion.2), channel_id=1, source_target_pairs={{0,8},{1,9},{2,10},{3,11},{4,12},{5,13},{6,14},{7,15},{8,0},{9,1},... | collective-permute-start | bytes 393224 | tf_op jit(solution)/shard_map/ppermute | solution.py:53
  202.1 16.6 %copy-start.8 = (bf16[2,128,128]{2,1,0:T(8,128)(2,1)S(1)}, bf16[2,128,128]{2,1,0:T(8,128)(2,1)}, u32[]{:S(2)}) copy-start(bf16[2,128,128]{2,1,0:T(8,128)(2,1)} %convolution_convert_fusion.2) | copy-start | bytes 196612
  206.8 17.7 %copy-start.3 = (f32[128,4,128]{2,1,0:T(4,128)S(1)}, f32[128,4,128]{2,1,0:T(4,128)}, u32[]{:S(2)}) copy-start(f32[128,4,128]{2,1,0:T(4,128)} %copy-done.2) | copy-start | bytes 786436
  207.0 16.5 %collective-permute-start.23 = (bf16[128,512]{1,0:T(8,128)(2,1)S(1)}, bf16[128,512]{1,0:T(8,128)(2,1)}, u32[]{:S(2)}, u32[]{:S(2)}) collective-permute-start(bf16[128,512]{1,0:T(8,128)(2,1)S(1)} %convert_add_fusion.1), channel_id=1, source_target_pairs={{0,16},{1,17},{2,18},{3,19},{4,20},{5,21},{6,22},{7,23},{8,24},{9,... | collective-permute-start | bytes 393224 | tf_op jit(solution)/shard_map/ppermute | solution.py:53
  (9 other events, 13.9 us)

commit v11 on v8

--- a/solution.py
+++ b/solution.py
@@ -192,7 +192,12 @@
         )
 
     latent_part = back_project(key_flat, w_uk) + back_project(value_flat, w_uv)
-    sum_levels = digits_of(lax.axis_size("heads"))
+    sum_levels = []
+    for radix, stride in digits_of(lax.axis_size("heads")):
+        if radix == 4:
+            sum_levels += [(2, stride), (2, stride * 2)]
+        else:
+            sum_levels.append((radix, stride))
     gather_levels = gather_order(block_count)
     comp_own = comp_all.reshape(radices + (row_count, col_width))[0]
 

time: 232 us -> 236 us (1.017)
  waiting for transfers between devices: 71.3 us -> 84.4 us
  starting transfers between devices: 106 us -> 98.5 us
    ppermute x25 -> x23, waiting for transfers between devices: 71.3 us -> 84.4 us  [shift_digit(): return lax.ppermute(x, axis, pairs)]
    ppermute x25 -> x23, starting transfers between devices: 106 us -> 98.5 us  [shift_digit(): return lax.ppermute(x, axis, pairs)]
    unnamed x41 -> x35, local copies, waits for them, and re-layouts: 4.84 us -> 2.9 us
  transfers between devices with their start and end apart: 25 -> 23, of which waited for: 15 -> 18; matrix products, arithmetic and copies ran while one was open for 8% -> 7% of each run, Pallas kernels for 0% -> 0%
where the time goes in v11:
time: 236 us; the launch traced here: 233 us
  starting transfers between devices  98.5 us (42%)
  waiting for transfers between devices  84.4 us (36%)
  other arithmetic  24.8 us (11%)
  matrix products  12.8 us (5%)
  local copies, waits for them, and re-layouts  11.1 us (5%)
    ppermute x23, starting transfers between devices, shift_digit(): return lax.ppermute(x, axis, pairs)  98.5 us
    ppermute x23, waiting for transfers between devices, shift_digit(): return lax.ppermute(x, axis, pairs)  84.4 us
    another operation x7, other arithmetic, gather_step(): return jnp.stack(pieces, axis=0)  8.64 us
  transfers between devices with their start and end apart: 23, of which 18 were waited for; matrix products, arithmetic and copies ran while one was open for 7% of the time, Pallas kernels for 0%

profile of v11, /device:TPU:56, one launch (start us, length us, event | category | flops | bytes accessed | tf_op | source)
XLA Modules:
  0.0 233.1 jit_solution(1490602137083880563)
XLA Ops:
  4.7 11.0 %collective-permute-start.1 = (bf16[128,578]{1,0:T(8,128)(2,1)S(1)}, bf16[128,578]{1,0:T(8,128)(2,1)S(1)}, u32[]{:S(2)}, u32[]{:S(2)}) collective-permute-start(bf16[128,578]{1,0:T(8,128)(2,1)S(1)} %pad_maximum_fusion.4), channel_id=1, source_target_pairs={{0,64},{32,96},{64,128},{96,160},{128,0},{160,32},{192,256},{224,2... | collective-permute-start | bytes 443912 | tf_op jit(solution)/shard_map/ppermute | solution.py:53
  15.8 5.6 %collective-permute-start = (bf16[128,578]{1,0:T(8,128)(2,1)S(1)}, bf16[128,578]{1,0:T(8,128)(2,1)S(1)}, u32[]{:S(2)}, u32[]{:S(2)}) collective-permute-start(bf16[128,578]{1,0:T(8,128)(2,1)S(1)} %pad_maximum_fusion.4), channel_id=1, source_target_pairs={{0,128},{32,160},{64,0},{96,32},{128,64},{160,96},{192,320},{224,3... | collective-permute-start | bytes 443912 | tf_op jit(solution)/shard_map/ppermute | solution.py:53
  21.4 2.5 %collective-permute-done.1 = bf16[128,578]{1,0:T(8,128)(2,1)S(1)} collective-permute-done((bf16[128,578]{1,0:T(8,128)(2,1)S(1)}, bf16[128,578]{1,0:T(8,128)(2,1)S(1)}, u32[]{:S(2)}, u32[]{:S(2)}) %collective-permute-start.1) | collective-permute-done | bytes 148000 | tf_op jit(solution)/shard_map/ppermute | solution.py:53
  23.9 11.5 %collective-permute-done = bf16[128,578]{1,0:T(8,128)(2,1)S(1)} collective-permute-done((bf16[128,578]{1,0:T(8,128)(2,1)S(1)}, bf16[128,578]{1,0:T(8,128)(2,1)S(1)}, u32[]{:S(2)}, u32[]{:S(2)}) %collective-permute-start) | collective-permute-done | bytes 148000 | tf_op jit(solution)/shard_map/ppermute | solution.py:53
  35.5 3.4 %collective-permute-start.4 = (bf16[3,128,578]{2,1,0:T(8,128)(2,1)S(1)}, bf16[3,128,578]{2,1,0:T(8,128)(2,1)S(1)}, u32[]{:S(2)}, u32[]{:S(2)}) collective-permute-start(bf16[3,128,578]{2,1,0:T(8,128)(2,1)S(1)} %get-tuple-element.50), channel_id=1, source_target_pairs={{0,192},{32,224},{64,256},{96,288},{128,320},{160,352},{192,384},{... | collective-permute-start | bytes 1331720 | tf_op jit(solution)/shard_map/ppermute | solution.py:53
  38.9 4.6 %collective-permute-start.3 = (bf16[3,128,578]{2,1,0:T(8,128)(2,1)S(1)}, bf16[3,128,578]{2,1,0:T(8,128)(2,1)S(1)}, u32[]{:S(2)}, u32[]{:S(2)}) collective-permute-start(bf16[3,128,578]{2,1,0:T(8,128)(2,1)S(1)} %get-tuple-element.50), channel_id=1, source_target_pairs={{0,384},{32,416},{64,448},{96,480},{128,512},{160,544},{192,576},{... | collective-permute-start | bytes 1331720 | tf_op jit(solution)/shard_map/ppermute | solution.py:53
  43.6 3.3 %collective-permute-start.2 = (bf16[3,128,578]{2,1,0:T(8,128)(2,1)S(1)}, bf16[3,128,578]{2,1,0:T(8,128)(2,1)S(1)}, u32[]{:S(2)}, u32[]{:S(2)}) collective-permute-start(bf16[3,128,578]{2,1,0:T(8,128)(2,1)S(1)} %get-tuple-element.50), channel_id=1, source_target_pairs={{0,576},{32,608},{64,640},{96,672},{128,704},{160,736},{192,0},{22... | collective-permute-start | bytes 1331720 | tf_op jit(solution)/shard_map/ppermute | solution.py:53
  46.9 4.9 %collective-permute-done.4 = bf16[3,128,578]{2,1,0:T(8,128)(2,1)S(1)} collective-permute-done((bf16[3,128,578]{2,1,0:T(8,128)(2,1)S(1)}, bf16[3,128,578]{2,1,0:T(8,128)(2,1)S(1)}, u32[]{:S(2)}, u32[]{:S(2)}) %collective-permute-start.4) | collective-permute-done | bytes 443936 | tf_op jit(solution)/shard_map/ppermute | solution.py:53
  51.8 9.7 %collective-permute-done.3 = bf16[3,128,578]{2,1,0:T(8,128)(2,1)S(1)} collective-permute-done((bf16[3,128,578]{2,1,0:T(8,128)(2,1)S(1)}, bf16[3,128,578]{2,1,0:T(8,128)(2,1)S(1)}, u32[]{:S(2)}, u32[]{:S(2)}) %collective-permute-start.3) | collective-permute-done | bytes 443936 | tf_op jit(solution)/shard_map/ppermute | solution.py:53
  87.2 3.0 %collective-permute-done.6 = bf16[2,2,4,3,128,128]{5,4,3,2,1,0:T(8,128)(2,1)S(1)} collective-permute-done((bf16[2,2,4,3,128,128]{5,4,3,2,1,0:T(8,128)(2,1)S(1)}, bf16[2,2,4,3,128,128]{5,4,3,2,1,0:T(8,128)(2,1)S(1)}, u32[]{:S(2)}, u32[]{:S(2)}) %collective-permute-start.6) | collective-permute-done | bytes 1572896 | tf_op jit(solution)/shard_map/ppermute | solution.py:53
  91.1 4.5 %collective-permute-start.9 = (bf16[2,2,3,128,128]{4,3,2,1,0:T(8,128)(2,1)S(1)}, bf16[2,2,3,128,128]{4,3,2,1,0:T(8,128)(2,1)S(1)}, u32[]{:S(2)}, u32[]{:S(2)}) collective-permute-start(bf16[2,2,3,128,128]{4,3,2,1,0:T(8,128)(2,1)S(1)} %get-tuple-element.45), channel_id=1, source_target_pairs={{0,576},{32,608},{64,640},{96,672},{128,704},{160,736},{192,0},{22... | collective-permute-start | bytes 1179656 | tf_op jit(solution)/shard_map/ppermute | solution.py:53
  95.6 3.7 %collective-permute-start.8 = (bf16[2,2,3,128,128]{4,3,2,1,0:T(8,128)(2,1)S(1)}, bf16[2,2,3,128,128]{4,3,2,1,0:T(8,128)(2,1)S(1)}, u32[]{:S(2)}, u32[]{:S(2)}) collective-permute-start(bf16[2,2,3,128,128]{4,3,2,1,0:T(8,128)(2,1)S(1)} %get-tuple-element.46), channel_id=1, source_target_pairs={{0,384},{32,416},{64,448},{96,480},{128,512},{160,544},{192,576},{... | collective-permute-start | bytes 1179656 | tf_op jit(solution)/shard_map/ppermute | solution.py:53
  101.3 11.5 %collective-permute-done.9 = bf16[2,2,3,128,128]{4,3,2,1,0:T(8,128)(2,1)S(1)} collective-permute-done((bf16[2,2,3,128,128]{4,3,2,1,0:T(8,128)(2,1)S(1)}, bf16[2,2,3,128,128]{4,3,2,1,0:T(8,128)(2,1)S(1)}, u32[]{:S(2)}, u32[]{:S(2)}) %collective-permute-start.9) | collective-permute-done | bytes 393248 | tf_op jit(solution)/shard_map/ppermute | solution.py:53
  112.8 5.6 %collective-permute-done.7 = bf16[2,2,3,128,128]{4,3,2,1,0:T(8,128)(2,1)S(1)} collective-permute-done((bf16[2,2,3,128,128]{4,3,2,1,0:T(8,128)(2,1)S(1)}, bf16[2,2,3,128,128]{4,3,2,1,0:T(8,128)(2,1)S(1)}, u32[]{:S(2)}, u32[]{:S(2)}) %collective-permute-start.7) | collective-permute-done | bytes 393248 | tf_op jit(solution)/shard_map/ppermute | solution.py:53
  118.6 7.1 %collective-permute-start.11 = (bf16[2,2,128,128]{3,2,1,0:T(8,128)(2,1)S(1)}, bf16[2,2,128,128]{3,2,1,0:T(8,128)(2,1)S(1)}, u32[]{:S(2)}, u32[]{:S(2)}) collective-permute-start(bf16[2,2,128,128]{3,2,1,0:T(8,128)(2,1)S(1)} %get-tuple-element.52), channel_id=1, source_target_pairs={{0,128},{32,160},{64,0},{96,32},{128,64},{160,96},{192,320},{224,3... | collective-permute-start | bytes 393224 | tf_op jit(solution)/shard_map/ppermute | solution.py:53
  125.7 2.7 %collective-permute-start.10 = (bf16[2,2,128,128]{3,2,1,0:T(8,128)(2,1)S(1)}, bf16[2,2,128,128]{3,2,1,0:T(8,128)(2,1)S(1)}, u32[]{:S(2)}, u32[]{:S(2)}) collective-permute-start(bf16[2,2,128,128]{3,2,1,0:T(8,128)(2,1)S(1)} %get-tuple-element.51), channel_id=1, source_target_pairs={{0,64},{32,96},{64,128},{96,160},{128,0},{160,32},{192,256},{224,2... | collective-permute-start | bytes 393224 | tf_op jit(solution)/shard_map/ppermute | solution.py:53
  128.4 2.5 %collective-permute-done.11 = bf16[2,2,128,128]{3,2,1,0:T(8,128)(2,1)S(1)} collective-permute-done((bf16[2,2,128,128]{3,2,1,0:T(8,128)(2,1)S(1)}, bf16[2,2,128,128]{3,2,1,0:T(8,128)(2,1)S(1)}, u32[]{:S(2)}, u32[]{:S(2)}) %collective-permute-start.11) | collective-permute-done | bytes 131104 | tf_op jit(solution)/shard_map/ppermute | solution.py:53
  130.9 7.8 %collective-permute-done.10 = bf16[2,2,128,128]{3,2,1,0:T(8,128)(2,1)S(1)} collective-permute-done((bf16[2,2,128,128]{3,2,1,0:T(8,128)(2,1)S(1)}, bf16[2,2,128,128]{3,2,1,0:T(8,128)(2,1)S(1)}, u32[]{:S(2)}, u32[]{:S(2)}) %collective-permute-start.10) | collective-permute-done | bytes 131104 | tf_op jit(solution)/shard_map/ppermute | solution.py:53
  139.6 4.2 %collective-permute-start.13 = (bf16[128,512]{1,0:T(8,128)(2,1)}, bf16[128,512]{1,0:T(8,128)(2,1)}, u32[]{:S(2)}, u32[]{:S(2)}) collective-permute-start(bf16[128,512]{1,0:T(8,128)(2,1)} %convert_element_type.226), channel_id=1, source_target_pairs={{0,64},{32,96},{64,128},{96,160},{128,0},{160,32},{192,256},{224,2... | collective-permute-start | bytes 393224 | tf_op jit(solution)/shard_map/ppermute | solution.py:53
  143.8 5.5 %collective-permute-start.12 = (bf16[128,512]{1,0:T(8,128)(2,1)}, bf16[128,512]{1,0:T(8,128)(2,1)}, u32[]{:S(2)}, u32[]{:S(2)}) collective-permute-start(bf16[128,512]{1,0:T(8,128)(2,1)} %convert_element_type.226), channel_id=1, source_target_pairs={{0,128},{32,160},{64,0},{96,32},{128,64},{160,96},{192,320},{224,3... | collective-permute-start | bytes 393224 | tf_op jit(solution)/shard_map/ppermute | solution.py:53
  152.3 3.3 %collective-permute-start.14 = (bf16[128,512]{1,0:T(8,128)(2,1)}, bf16[128,512]{1,0:T(8,128)(2,1)}, u32[]{:S(2)}, u32[]{:S(2)}) collective-permute-start(bf16[128,512]{1,0:T(8,128)(2,1)} %fusion.28), channel_id=1, source_target_pairs={{0,1},{1,0},{2,3},{3,2},{4,5},{5,4},{6,7},{7,6},{8,9},{9,8},{10,11... | collective-permute-start | bytes 393224 | tf_op jit(solution)/shard_map/ppermute | solution.py:53
  160.5 4.3 %collective-permute-start.17 = (bf16[3,128,512]{2,1,0:T(8,128)(2,1)}, bf16[3,128,512]{2,1,0:T(8,128)(2,1)}, u32[]{:S(2)}, u32[]{:S(2)}) collective-permute-start(bf16[3,128,512]{2,1,0:T(8,128)(2,1)} %pad_maximum_fusion.3), channel_id=1, source_target_pairs={{0,192},{32,224},{64,256},{96,288},{128,320},{160,352},{192,384},{... | collective-permute-start | bytes 1179656 | tf_op jit(solution)/shard_map/ppermute | solution.py:53
  164.8 3.6 %collective-permute-start.16 = (bf16[3,128,512]{2,1,0:T(8,128)(2,1)}, bf16[3,128,512]{2,1,0:T(8,128)(2,1)}, u32[]{:S(2)}, u32[]{:S(2)}) collective-permute-start(bf16[3,128,512]{2,1,0:T(8,128)(2,1)} %pad_maximum_fusion.3), channel_id=1, source_target_pairs={{0,384},{32,416},{64,448},{96,480},{128,512},{160,544},{192,576},{... | collective-permute-start | bytes 1179656 | tf_op jit(solution)/shard_map/ppermute | solution.py:53
  168.4 2.9 %collective-permute-start.15 = (bf16[3,128,512]{2,1,0:T(8,128)(2,1)}, bf16[3,128,512]{2,1,0:T(8,128)(2,1)}, u32[]{:S(2)}, u32[]{:S(2)}) collective-permute-start(bf16[3,128,512]{2,1,0:T(8,128)(2,1)} %pad_maximum_fusion.3), channel_id=1, source_target_pairs={{0,576},{32,608},{64,640},{96,672},{128,704},{160,736},{192,0},{22... | collective-permute-start | bytes 1179656 | tf_op jit(solution)/shard_map/ppermute | solution.py:53
  171.3 4.1 %collective-permute-start.18 = (bf16[128,512]{1,0:T(8,128)(2,1)S(1)}, bf16[128,512]{1,0:T(8,128)(2,1)}, u32[]{:S(2)}, u32[]{:S(2)}) collective-permute-start(bf16[128,512]{1,0:T(8,128)(2,1)S(1)} %convert_add_fusion.4), channel_id=1, source_target_pairs={{0,2},{1,3},{2,0},{3,1},{4,6},{5,7},{6,4},{7,5},{8,10},{9,11},{10,... | collective-permute-start | bytes 393224 | tf_op jit(solution)/shard_map/ppermute | solution.py:53
  177.1 3.5 %collective-permute-done.18 = bf16[128,512]{1,0:T(8,128)(2,1)} collective-permute-done((bf16[128,512]{1,0:T(8,128)(2,1)S(1)}, bf16[128,512]{1,0:T(8,128)(2,1)}, u32[]{:S(2)}, u32[]{:S(2)}) %collective-permute-start.18) | collective-permute-done | bytes 131104 | tf_op jit(solution)/shard_map/ppermute | solution.py:53
  181.6 2.5 %collective-permute-done.15 = bf16[3,128,512]{2,1,0:T(8,128)(2,1)} collective-permute-done((bf16[3,128,512]{2,1,0:T(8,128)(2,1)}, bf16[3,128,512]{2,1,0:T(8,128)(2,1)}, u32[]{:S(2)}, u32[]{:S(2)}) %collective-permute-start.15) | collective-permute-done | bytes 393248 | tf_op jit(solution)/shard_map/ppermute | solution.py:53
  191.8 4.7 %collective-permute-start.20 = (bf16[128,512]{1,0:T(8,128)(2,1)S(1)}, bf16[128,512]{1,0:T(8,128)(2,1)S(1)}, u32[]{:S(2)}, u32[]{:S(2)}) collective-permute-start(bf16[128,512]{1,0:T(8,128)(2,1)S(1)} %convert_add_fusion.3), channel_id=1, source_target_pairs={{0,4},{1,5},{2,6},{3,7},{4,0},{5,1},{6,2},{7,3},{8,12},{9,13},{10,... | collective-permute-start | bytes 393224 | tf_op jit(solution)/shard_map/ppermute | solution.py:53
  196.5 9.4 %collective-permute-done.20 = bf16[128,512]{1,0:T(8,128)(2,1)S(1)} collective-permute-done((bf16[128,512]{1,0:T(8,128)(2,1)S(1)}, bf16[128,512]{1,0:T(8,128)(2,1)S(1)}, u32[]{:S(2)}, u32[]{:S(2)}) %collective-permute-start.20) | collective-permute-done | bytes 131104 | tf_op jit(solution)/shard_map/ppermute | solution.py:53
  209.7 4.4 %collective-permute-done.21 = bf16[128,512]{1,0:T(8,128)(2,1)S(1)} collective-permute-done((bf16[128,512]{1,0:T(8,128)(2,1)S(1)}, bf16[128,512]{1,0:T(8,128)(2,1)S(1)}, u32[]{:S(2)}, u32[]{:S(2)}) %collective-permute-start.21) | collective-permute-done | bytes 131104 | tf_op jit(solution)/shard_map/ppermute | solution.py:53
  214.1 10.0 %collective-permute-start.22 = (bf16[128,512]{1,0:T(8,128)(2,1)S(1)}, bf16[128,512]{1,0:T(8,128)(2,1)}, u32[]{:S(2)}, u32[]{:S(2)}) collective-permute-start(bf16[128,512]{1,0:T(8,128)(2,1)S(1)} %convert_add_fusion.1), channel_id=1, source_target_pairs={{0,16},{1,17},{2,18},{3,19},{4,20},{5,21},{6,22},{7,23},{8,24},{9,... | collective-permute-start | bytes 393224 | tf_op jit(solution)/shard_map/ppermute | solution.py:53
  227.1 2.4 %collective-permute-done.22 = bf16[128,512]{1,0:T(8,128)(2,1)} collective-permute-done((bf16[128,512]{1,0:T(8,128)(2,1)S(1)}, bf16[128,512]{1,0:T(8,128)(2,1)}, u32[]{:S(2)}, u32[]{:S(2)}) %collective-permute-start.22) | collective-permute-done | bytes 131104 | tf_op jit(solution)/shard_map/ppermute | solution.py:53
  (106 shorter events, 61.9 us)
Async XLA Ops:
  0.6 73.3 %copy-start = (bf16[512,256]{1,0:T(8,128)(2,1)S(1)}, bf16[512,256]{1,0:T(8,128)(2,1)}, u32[]{:S(2)}) copy-start(bf16[512,256]{1,0:T(8,128)(2,1)} %param.16) | copy-start | bytes 786436
  4.5 30.9 %copy-start.3 = (f32[128,4,128]{2,1,0:T(4,128)}, f32[128,4,128]{2,1,0:T(4,128)S(1)}, u32[]{:S(2)}) copy-start(f32[128,4,128]{2,1,0:T(4,128)S(1)} %broadcast_in_dim.42) | copy-start | bytes 786436
  4.6 62.0 %copy-start.10 = (bf16[128,256]{1,0:T(8,128)(2,1)S(1)}, bf16[128,256]{1,0:T(8,128)(2,1)}, u32[]{:S(2)}) copy-start(bf16[128,256]{1,0:T(8,128)(2,1)} %param.11) | copy-start | bytes 196612
  4.6 62.1 %copy-start.12 = (bf16[128,128]{1,0:T(8,128)(2,1)S(1)}, bf16[128,128]{1,0:T(8,128)(2,1)}, u32[]{:S(2)}) copy-start(bf16[128,128]{1,0:T(8,128)(2,1)} %param.10) | copy-start | bytes 98308
  4.6 62.9 %copy-start.11 = (bf16[128,256]{1,0:T(8,128)(2,1)S(1)}, bf16[128,256]{1,0:T(8,128)(2,1)}, u32[]{:S(2)}) copy-start(bf16[128,256]{1,0:T(8,128)(2,1)} %param.9) | copy-start | bytes 196612
  4.7 19.2 %collective-permute-start.1 = (bf16[128,578]{1,0:T(8,128)(2,1)S(1)}, bf16[128,578]{1,0:T(8,128)(2,1)S(1)}, u32[]{:S(2)}, u32[]{:S(2)}) collective-permute-start(bf16[128,578]{1,0:T(8,128)(2,1)S(1)} %pad_maximum_fusion.4), channel_id=1, source_target_pairs={{0,64},{32,96},{64,128},{96,160},{128,0},{160,32},{192,256},{224,2... | collective-permute-start | bytes 443912 | tf_op jit(solution)/shard_map/ppermute | solution.py:53
  15.8 19.6 %collective-permute-start = (bf16[128,578]{1,0:T(8,128)(2,1)S(1)}, bf16[128,578]{1,0:T(8,128)(2,1)S(1)}, u32[]{:S(2)}, u32[]{:S(2)}) collective-permute-start(bf16[128,578]{1,0:T(8,128)(2,1)S(1)} %pad_maximum_fusion.4), channel_id=1, source_target_pairs={{0,128},{32,160},{64,0},{96,32},{128,64},{160,96},{192,320},{224,3... | collective-permute-start | bytes 443912 | tf_op jit(solution)/shard_map/ppermute | solution.py:53
  35.5 16.3 %collective-permute-start.4 = (bf16[3,128,578]{2,1,0:T(8,128)(2,1)S(1)}, bf16[3,128,578]{2,1,0:T(8,128)(2,1)S(1)}, u32[]{:S(2)}, u32[]{:S(2)}) collective-permute-start(bf16[3,128,578]{2,1,0:T(8,128)(2,1)S(1)} %get-tuple-element.50), channel_id=1, source_target_pairs={{0,192},{32,224},{64,256},{96,288},{128,320},{160,352},{192,384},{... | collective-permute-start | bytes 1331720 | tf_op jit(solution)/shard_map/ppermute | solution.py:53
  38.9 22.6 %collective-permute-start.3 = (bf16[3,128,578]{2,1,0:T(8,128)(2,1)S(1)}, bf16[3,128,578]{2,1,0:T(8,128)(2,1)S(1)}, u32[]{:S(2)}, u32[]{:S(2)}) collective-permute-start(bf16[3,128,578]{2,1,0:T(8,128)(2,1)S(1)} %get-tuple-element.50), channel_id=1, source_target_pairs={{0,384},{32,416},{64,448},{96,480},{128,512},{160,544},{192,576},{... | collective-permute-start | bytes 1331720 | tf_op jit(solution)/shard_map/ppermute | solution.py:53
  43.6 19.5 %collective-permute-start.2 = (bf16[3,128,578]{2,1,0:T(8,128)(2,1)S(1)}, bf16[3,128,578]{2,1,0:T(8,128)(2,1)S(1)}, u32[]{:S(2)}, u32[]{:S(2)}) collective-permute-start(bf16[3,128,578]{2,1,0:T(8,128)(2,1)S(1)} %get-tuple-element.50), channel_id=1, source_target_pairs={{0,576},{32,608},{64,640},{96,672},{128,704},{160,736},{192,0},{22... | collective-permute-start | bytes 1331720 | tf_op jit(solution)/shard_map/ppermute | solution.py:53
  61.5 6.8 %copy-start.4 = (bf16[3,128,578]{2,1,0:T(8,128)(2,1)}, bf16[3,128,578]{2,1,0:T(8,128)(2,1)S(1)}, u32[]{:S(2)}) copy-start(bf16[3,128,578]{2,1,0:T(8,128)(2,1)S(1)} %collective-permute-done.3) | copy-start | bytes 1331716
  63.1 5.3 %copy-start.5 = (bf16[3,128,578]{2,1,0:T(8,128)(2,1)}, bf16[3,128,578]{2,1,0:T(8,128)(2,1)S(1)}, u32[]{:S(2)}) copy-start(bf16[3,128,578]{2,1,0:T(8,128)(2,1)S(1)} %collective-permute-done.2) | copy-start | bytes 1331716
  64.7 6.2 %collective-permute-start.5 = (bf16[4,3,128,640]{3,2,1,0:T(8,128)(2,1)}, bf16[4,3,128,640]{3,2,1,0:T(8,128)(2,1)}, u32[]{:S(2)}, u32[]{:S(2)}) collective-permute-start(bf16[4,3,128,640]{3,2,1,0:T(8,128)(2,1)} %fusion.22), channel_id=1, source_target_pairs={{0,32},{32,0},{64,96},{96,64},{128,160},{160,128},{192,224},{224,1... | collective-permute-start | bytes 5898248 | tf_op jit(solution)/shard_map/ppermute | solution.py:53
  72.9 4.1 %copy-start.1 = (bf16[2,4,3,128,578]{4,3,2,1,0:T(8,128)(2,1)}, bf16[2,4,3,128,578]{4,3,2,1,0:T(8,128)(2,1)S(1)}, u32[]{:S(2)}) copy-start(bf16[2,4,3,128,578]{4,3,2,1,0:T(8,128)(2,1)S(1)} %pad_maximum_fusion) | copy-start | bytes 10653700
  84.9 5.3 %collective-permute-start.6 = (bf16[2,2,4,3,128,128]{5,4,3,2,1,0:T(8,128)(2,1)S(1)}, bf16[2,2,4,3,128,128]{5,4,3,2,1,0:T(8,128)(2,1)S(1)}, u32[]{:S(2)}, u32[]{:S(2)}) collective-permute-start(bf16[2,2,4,3,128,128]{5,4,3,2,1,0:T(8,128)(2,1)S(1)} %fusion.24), channel_id=1, source_target_pairs={{0,32},{32,0},{64,96},{96,64},{128,160},{160,128},{192,224},{224,1... | collective-permute-start | bytes 4718600 | tf_op jit(solution)/shard_map/ppermute | solution.py:53
  91.1 21.7 %collective-permute-start.9 = (bf16[2,2,3,128,128]{4,3,2,1,0:T(8,128)(2,1)S(1)}, bf16[2,2,3,128,128]{4,3,2,1,0:T(8,128)(2,1)S(1)}, u32[]{:S(2)}, u32[]{:S(2)}) collective-permute-start(bf16[2,2,3,128,128]{4,3,2,1,0:T(8,128)(2,1)S(1)} %get-tuple-element.45), channel_id=1, source_target_pairs={{0,576},{32,608},{64,640},{96,672},{128,704},{160,736},{192,0},{22... | collective-permute-start | bytes 1179656 | tf_op jit(solution)/shard_map/ppermute | solution.py:53
  95.6 17.2 %collective-permute-start.8 = (bf16[2,2,3,128,128]{4,3,2,1,0:T(8,128)(2,1)S(1)}, bf16[2,2,3,128,128]{4,3,2,1,0:T(8,128)(2,1)S(1)}, u32[]{:S(2)}, u32[]{:S(2)}) collective-permute-start(bf16[2,2,3,128,128]{4,3,2,1,0:T(8,128)(2,1)S(1)} %get-tuple-element.46), channel_id=1, source_target_pairs={{0,384},{32,416},{64,448},{96,480},{128,512},{160,544},{192,576},{... | collective-permute-start | bytes 1179656 | tf_op jit(solution)/shard_map/ppermute | solution.py:53
  99.3 19.0 %collective-permute-start.7 = (bf16[2,2,3,128,128]{4,3,2,1,0:T(8,128)(2,1)S(1)}, bf16[2,2,3,128,128]{4,3,2,1,0:T(8,128)(2,1)S(1)}, u32[]{:S(2)}, u32[]{:S(2)}) collective-permute-start(bf16[2,2,3,128,128]{4,3,2,1,0:T(8,128)(2,1)S(1)} %get-tuple-element.44), channel_id=1, source_target_pairs={{0,192},{32,224},{64,256},{96,288},{128,320},{160,352},{192,384},{... | collective-permute-start | bytes 1179656 | tf_op jit(solution)/shard_map/ppermute | solution.py:53
  118.6 12.3 %collective-permute-start.11 = (bf16[2,2,128,128]{3,2,1,0:T(8,128)(2,1)S(1)}, bf16[2,2,128,128]{3,2,1,0:T(8,128)(2,1)S(1)}, u32[]{:S(2)}, u32[]{:S(2)}) collective-permute-start(bf16[2,2,128,128]{3,2,1,0:T(8,128)(2,1)S(1)} %get-tuple-element.52), channel_id=1, source_target_pairs={{0,128},{32,160},{64,0},{96,32},{128,64},{160,96},{192,320},{224,3... | collective-permute-start | bytes 393224 | tf_op jit(solution)/shard_map/ppermute | solution.py:53
  125.7 13.0 %collective-permute-start.10 = (bf16[2,2,128,128]{3,2,1,0:T(8,128)(2,1)S(1)}, bf16[2,2,128,128]{3,2,1,0:T(8,128)(2,1)S(1)}, u32[]{:S(2)}, u32[]{:S(2)}) collective-permute-start(bf16[2,2,128,128]{3,2,1,0:T(8,128)(2,1)S(1)} %get-tuple-element.51), channel_id=1, source_target_pairs={{0,64},{32,96},{64,128},{96,160},{128,0},{160,32},{192,256},{224,2... | collective-permute-start | bytes 393224 | tf_op jit(solution)/shard_map/ppermute | solution.py:53
  139.6 16.7 %collective-permute-start.13 = (bf16[128,512]{1,0:T(8,128)(2,1)}, bf16[128,512]{1,0:T(8,128)(2,1)}, u32[]{:S(2)}, u32[]{:S(2)}) collective-permute-start(bf16[128,512]{1,0:T(8,128)(2,1)} %convert_element_type.226), channel_id=1, source_target_pairs={{0,64},{32,96},{64,128},{96,160},{128,0},{160,32},{192,256},{224,2... | collective-permute-start | bytes 393224 | tf_op jit(solution)/shard_map/ppermute | solution.py:53
  143.8 13.8 %collective-permute-start.12 = (bf16[128,512]{1,0:T(8,128)(2,1)}, bf16[128,512]{1,0:T(8,128)(2,1)}, u32[]{:S(2)}, u32[]{:S(2)}) collective-permute-start(bf16[128,512]{1,0:T(8,128)(2,1)} %convert_element_type.226), channel_id=1, source_target_pairs={{0,128},{32,160},{64,0},{96,32},{128,64},{160,96},{192,320},{224,3... | collective-permute-start | bytes 393224 | tf_op jit(solution)/shard_map/ppermute | solution.py:53
  152.3 7.2 %collective-permute-start.14 = (bf16[128,512]{1,0:T(8,128)(2,1)}, bf16[128,512]{1,0:T(8,128)(2,1)}, u32[]{:S(2)}, u32[]{:S(2)}) collective-permute-start(bf16[128,512]{1,0:T(8,128)(2,1)} %fusion.28), channel_id=1, source_target_pairs={{0,1},{1,0},{2,3},{3,2},{4,5},{5,4},{6,7},{7,6},{8,9},{9,8},{10,11... | collective-permute-start | bytes 393224 | tf_op jit(solution)/shard_map/ppermute | solution.py:53
  160.5 21.1 %collective-permute-start.17 = (bf16[3,128,512]{2,1,0:T(8,128)(2,1)}, bf16[3,128,512]{2,1,0:T(8,128)(2,1)}, u32[]{:S(2)}, u32[]{:S(2)}) collective-permute-start(bf16[3,128,512]{2,1,0:T(8,128)(2,1)} %pad_maximum_fusion.3), channel_id=1, source_target_pairs={{0,192},{32,224},{64,256},{96,288},{128,320},{160,352},{192,384},{... | collective-permute-start | bytes 1179656 | tf_op jit(solution)/shard_map/ppermute | solution.py:53
  164.8 16.8 %collective-permute-start.16 = (bf16[3,128,512]{2,1,0:T(8,128)(2,1)}, bf16[3,128,512]{2,1,0:T(8,128)(2,1)}, u32[]{:S(2)}, u32[]{:S(2)}) collective-permute-start(bf16[3,128,512]{2,1,0:T(8,128)(2,1)} %pad_maximum_fusion.3), channel_id=1, source_target_pairs={{0,384},{32,416},{64,448},{96,480},{128,512},{160,544},{192,576},{... | collective-permute-start | bytes 1179656 | tf_op jit(solution)/shard_map/ppermute | solution.py:53
  168.4 15.6 %collective-permute-start.15 = (bf16[3,128,512]{2,1,0:T(8,128)(2,1)}, bf16[3,128,512]{2,1,0:T(8,128)(2,1)}, u32[]{:S(2)}, u32[]{:S(2)}) collective-permute-start(bf16[3,128,512]{2,1,0:T(8,128)(2,1)} %pad_maximum_fusion.3), channel_id=1, source_target_pairs={{0,576},{32,608},{64,640},{96,672},{128,704},{160,736},{192,0},{22... | collective-permute-start | bytes 1179656 | tf_op jit(solution)/shard_map/ppermute | solution.py:53
  171.3 9.3 %collective-permute-start.18 = (bf16[128,512]{1,0:T(8,128)(2,1)S(1)}, bf16[128,512]{1,0:T(8,128)(2,1)}, u32[]{:S(2)}, u32[]{:S(2)}) collective-permute-start(bf16[128,512]{1,0:T(8,128)(2,1)S(1)} %convert_add_fusion.4), channel_id=1, source_target_pairs={{0,2},{1,3},{2,0},{3,1},{4,6},{5,7},{6,4},{7,5},{8,10},{9,11},{10,... | collective-permute-start | bytes 393224 | tf_op jit(solution)/shard_map/ppermute | solution.py:53
  189.9 16.1 %collective-permute-start.19 = (f32[512,512]{1,0:T(8,128)S(1)}, f32[512,512]{1,0:T(8,128)S(1)}, u32[]{:S(2)}, u32[]{:S(2)}) collective-permute-start(f32[512,512]{1,0:T(8,128)S(1)} %add_bitcast_fusion), channel_id=1, source_target_pairs={{0,32},{32,0},{64,96},{96,64},{128,160},{160,128},{192,224},{224,1... | collective-permute-start | bytes 3145736 | tf_op jit(solution)/shard_map/ppermute | solution.py:53
  191.8 14.2 %collective-permute-start.20 = (bf16[128,512]{1,0:T(8,128)(2,1)S(1)}, bf16[128,512]{1,0:T(8,128)(2,1)S(1)}, u32[]{:S(2)}, u32[]{:S(2)}) collective-permute-start(bf16[128,512]{1,0:T(8,128)(2,1)S(1)} %convert_add_fusion.3), channel_id=1, source_target_pairs={{0,4},{1,5},{2,6},{3,7},{4,0},{5,1},{6,2},{7,3},{8,12},{9,13},{10,... | collective-permute-start | bytes 393224 | tf_op jit(solution)/shard_map/ppermute | solution.py:53
  207.2 6.8 %collective-permute-start.21 = (bf16[128,512]{1,0:T(8,128)(2,1)S(1)}, bf16[128,512]{1,0:T(8,128)(2,1)S(1)}, u32[]{:S(2)}, u32[]{:S(2)}) collective-permute-start(bf16[128,512]{1,0:T(8,128)(2,1)S(1)} %convert_add_fusion.2), channel_id=1, source_target_pairs={{0,8},{1,9},{2,10},{3,11},{4,12},{5,13},{6,14},{7,15},{8,0},{9,1},... | collective-permute-start | bytes 393224 | tf_op jit(solution)/shard_map/ppermute | solution.py:53
  209.7 22.4 %copy-start.2 = (f32[512,512]{1,0:T(8,128)S(1)}, f32[512,512]{1,0:T(8,128)}, u32[]{:S(2)}) copy-start(f32[512,512]{1,0:T(8,128)} %add.220) | copy-start | bytes 3145732
  214.1 15.4 %collective-permute-start.22 = (bf16[128,512]{1,0:T(8,128)(2,1)S(1)}, bf16[128,512]{1,0:T(8,128)(2,1)}, u32[]{:S(2)}, u32[]{:S(2)}) collective-permute-start(bf16[128,512]{1,0:T(8,128)(2,1)S(1)} %convert_add_fusion.1), channel_id=1, source_target_pairs={{0,16},{1,17},{2,18},{3,19},{4,20},{5,21},{6,22},{7,23},{8,24},{9,... | collective-permute-start | bytes 393224 | tf_op jit(solution)/shard_map/ppermute | solution.py:53
  (5 other events, 6.9 us)

commit v12 on v10

--- a/solution.py
+++ b/solution.py
@@ -196,6 +196,7 @@
     if len(sum_levels) > 2 and sum_levels[-1][0] == 4:
         last_stride = sum_levels[-1][1]
         sum_levels = sum_levels[:-1] + [(2, last_stride), (2, last_stride * 2)]
+    sum_levels = sorted(sum_levels, key=lambda d: -d[0])
     gather_levels = gather_order(block_count)
     comp_own = comp_all.reshape(radices + (row_count, col_width))[0]
 

time: 228 us -> 232 us (1.018)
  waiting for transfers between devices: 75.1 us -> 86.2 us
  starting transfers between devices: 102 us -> 96.4 us
    ppermute x24, waiting for transfers between devices: 75.1 us -> 86.2 us  [shift_digit(): return lax.ppermute(x, axis, pairs)]
    ppermute x24, starting transfers between devices: 102 us -> 96.4 us  [shift_digit(): return lax.ppermute(x, axis, pairs)]
  transfers between devices with their start and end apart: 24 -> 24, of which waited for: 16 -> 18; matrix products, arithmetic and copies ran while one was open for 7% -> 7% of each run, Pallas kernels for 0% -> 0%
where the time goes in v12:
time: 232 us; the launch traced here: 231 us
  starting transfers between devices  96.4 us (42%)
  waiting for transfers between devices  86.2 us (37%)
  other arithmetic  21.7 us (9%)
  matrix products  13.5 us (6%)
  local copies, waits for them, and re-layouts  11.6 us (5%)
    ppermute x24, starting transfers between devices, shift_digit(): return lax.ppermute(x, axis, pairs)  96.4 us
    ppermute x24, waiting for transfers between devices, shift_digit(): return lax.ppermute(x, axis, pairs)  86.2 us
    another operation x7, other arithmetic, gather_step(): return jnp.stack(pieces, axis=0)  7.3 us
  transfers between devices with their start and end apart: 24, of which 18 were waited for; matrix products, arithmetic and copies ran while one was open for 7% of the time, Pallas kernels for 0%

profile of v12, /device:TPU:56, one launch (start us, length us, event | category | flops | bytes accessed | tf_op | source)
XLA Modules:
  0.0 230.9 jit_solution(12410709280199735844)
XLA Ops:
  4.7 11.0 %collective-permute-start.1 = (bf16[128,578]{1,0:T(8,128)(2,1)S(1)}, bf16[128,578]{1,0:T(8,128)(2,1)S(1)}, u32[]{:S(2)}, u32[]{:S(2)}) collective-permute-start(bf16[128,578]{1,0:T(8,128)(2,1)S(1)} %pad_maximum_fusion.4), channel_id=1, source_target_pairs={{0,64},{32,96},{64,128},{96,160},{128,0},{160,32},{192,256},{224,2... | collective-permute-start | bytes 443912 | tf_op jit(solution)/shard_map/ppermute | solution.py:53
  15.8 5.6 %collective-permute-start = (bf16[128,578]{1,0:T(8,128)(2,1)S(1)}, bf16[128,578]{1,0:T(8,128)(2,1)S(1)}, u32[]{:S(2)}, u32[]{:S(2)}) collective-permute-start(bf16[128,578]{1,0:T(8,128)(2,1)S(1)} %pad_maximum_fusion.4), channel_id=1, source_target_pairs={{0,128},{32,160},{64,0},{96,32},{128,64},{160,96},{192,320},{224,3... | collective-permute-start | bytes 443912 | tf_op jit(solution)/shard_map/ppermute | solution.py:53
  23.9 11.5 %collective-permute-done = bf16[128,578]{1,0:T(8,128)(2,1)S(1)} collective-permute-done((bf16[128,578]{1,0:T(8,128)(2,1)S(1)}, bf16[128,578]{1,0:T(8,128)(2,1)S(1)}, u32[]{:S(2)}, u32[]{:S(2)}) %collective-permute-start) | collective-permute-done | bytes 148000 | tf_op jit(solution)/shard_map/ppermute | solution.py:53
  35.5 3.4 %collective-permute-start.4 = (bf16[3,128,578]{2,1,0:T(8,128)(2,1)S(1)}, bf16[3,128,578]{2,1,0:T(8,128)(2,1)S(1)}, u32[]{:S(2)}, u32[]{:S(2)}) collective-permute-start(bf16[3,128,578]{2,1,0:T(8,128)(2,1)S(1)} %get-tuple-element.46), channel_id=1, source_target_pairs={{0,192},{32,224},{64,256},{96,288},{128,320},{160,352},{192,384},{... | collective-permute-start | bytes 1331720 | tf_op jit(solution)/shard_map/ppermute | solution.py:53
  38.9 4.6 %collective-permute-start.3 = (bf16[3,128,578]{2,1,0:T(8,128)(2,1)S(1)}, bf16[3,128,578]{2,1,0:T(8,128)(2,1)S(1)}, u32[]{:S(2)}, u32[]{:S(2)}) collective-permute-start(bf16[3,128,578]{2,1,0:T(8,128)(2,1)S(1)} %get-tuple-element.46), channel_id=1, source_target_pairs={{0,384},{32,416},{64,448},{96,480},{128,512},{160,544},{192,576},{... | collective-permute-start | bytes 1331720 | tf_op jit(solution)/shard_map/ppermute | solution.py:53
  43.6 3.3 %collective-permute-start.2 = (bf16[3,128,578]{2,1,0:T(8,128)(2,1)S(1)}, bf16[3,128,578]{2,1,0:T(8,128)(2,1)S(1)}, u32[]{:S(2)}, u32[]{:S(2)}) collective-permute-start(bf16[3,128,578]{2,1,0:T(8,128)(2,1)S(1)} %get-tuple-element.46), channel_id=1, source_target_pairs={{0,576},{32,608},{64,640},{96,672},{128,704},{160,736},{192,0},{22... | collective-permute-start | bytes 1331720 | tf_op jit(solution)/shard_map/ppermute | solution.py:53
  46.9 4.9 %collective-permute-done.4 = bf16[3,128,578]{2,1,0:T(8,128)(2,1)S(1)} collective-permute-done((bf16[3,128,578]{2,1,0:T(8,128)(2,1)S(1)}, bf16[3,128,578]{2,1,0:T(8,128)(2,1)S(1)}, u32[]{:S(2)}, u32[]{:S(2)}) %collective-permute-start.4) | collective-permute-done | bytes 443936 | tf_op jit(solution)/shard_map/ppermute | solution.py:53
  51.8 9.7 %collective-permute-done.3 = bf16[3,128,578]{2,1,0:T(8,128)(2,1)S(1)} collective-permute-done((bf16[3,128,578]{2,1,0:T(8,128)(2,1)S(1)}, bf16[3,128,578]{2,1,0:T(8,128)(2,1)S(1)}, u32[]{:S(2)}, u32[]{:S(2)}) %collective-permute-start.3) | collective-permute-done | bytes 443936 | tf_op jit(solution)/shard_map/ppermute | solution.py:53
  86.3 2.8 %collective-permute-done.6 = bf16[2,2,4,3,128,128]{5,4,3,2,1,0:T(8,128)(2,1)S(1)} collective-permute-done((bf16[2,2,4,3,128,128]{5,4,3,2,1,0:T(8,128)(2,1)S(1)}, bf16[2,2,4,3,128,128]{5,4,3,2,1,0:T(8,128)(2,1)S(1)}, u32[]{:S(2)}, u32[]{:S(2)}) %collective-permute-start.6) | collective-permute-done | bytes 1572896 | tf_op jit(solution)/shard_map/ppermute | solution.py:53
  90.0 4.5 %collective-permute-start.9 = (bf16[2,2,3,128,128]{4,3,2,1,0:T(8,128)(2,1)S(1)}, bf16[2,2,3,128,128]{4,3,2,1,0:T(8,128)(2,1)S(1)}, u32[]{:S(2)}, u32[]{:S(2)}) collective-permute-start(bf16[2,2,3,128,128]{4,3,2,1,0:T(8,128)(2,1)S(1)} %get-tuple-element.41), channel_id=1, source_target_pairs={{0,576},{32,608},{64,640},{96,672},{128,704},{160,736},{192,0},{22... | collective-permute-start | bytes 1179656 | tf_op jit(solution)/shard_map/ppermute | solution.py:53
  94.6 3.7 %collective-permute-start.8 = (bf16[2,2,3,128,128]{4,3,2,1,0:T(8,128)(2,1)S(1)}, bf16[2,2,3,128,128]{4,3,2,1,0:T(8,128)(2,1)S(1)}, u32[]{:S(2)}, u32[]{:S(2)}) collective-permute-start(bf16[2,2,3,128,128]{4,3,2,1,0:T(8,128)(2,1)S(1)} %get-tuple-element.42), channel_id=1, source_target_pairs={{0,384},{32,416},{64,448},{96,480},{128,512},{160,544},{192,576},{... | collective-permute-start | bytes 1179656 | tf_op jit(solution)/shard_map/ppermute | solution.py:53
  100.2 11.7 %collective-permute-done.9 = bf16[2,2,3,128,128]{4,3,2,1,0:T(8,128)(2,1)S(1)} collective-permute-done((bf16[2,2,3,128,128]{4,3,2,1,0:T(8,128)(2,1)S(1)}, bf16[2,2,3,128,128]{4,3,2,1,0:T(8,128)(2,1)S(1)}, u32[]{:S(2)}, u32[]{:S(2)}) %collective-permute-start.9) | collective-permute-done | bytes 393248 | tf_op jit(solution)/shard_map/ppermute | solution.py:53
  111.9 5.6 %collective-permute-done.7 = bf16[2,2,3,128,128]{4,3,2,1,0:T(8,128)(2,1)S(1)} collective-permute-done((bf16[2,2,3,128,128]{4,3,2,1,0:T(8,128)(2,1)S(1)}, bf16[2,2,3,128,128]{4,3,2,1,0:T(8,128)(2,1)S(1)}, u32[]{:S(2)}, u32[]{:S(2)}) %collective-permute-start.7) | collective-permute-done | bytes 393248 | tf_op jit(solution)/shard_map/ppermute | solution.py:53
  117.7 7.1 %collective-permute-start.11 = (bf16[2,2,128,128]{3,2,1,0:T(8,128)(2,1)S(1)}, bf16[2,2,128,128]{3,2,1,0:T(8,128)(2,1)S(1)}, u32[]{:S(2)}, u32[]{:S(2)}) collective-permute-start(bf16[2,2,128,128]{3,2,1,0:T(8,128)(2,1)S(1)} %get-tuple-element.48), channel_id=1, source_target_pairs={{0,128},{32,160},{64,0},{96,32},{128,64},{160,96},{192,320},{224,3... | collective-permute-start | bytes 393224 | tf_op jit(solution)/shard_map/ppermute | solution.py:53
  124.8 2.7 %collective-permute-start.10 = (bf16[2,2,128,128]{3,2,1,0:T(8,128)(2,1)S(1)}, bf16[2,2,128,128]{3,2,1,0:T(8,128)(2,1)S(1)}, u32[]{:S(2)}, u32[]{:S(2)}) collective-permute-start(bf16[2,2,128,128]{3,2,1,0:T(8,128)(2,1)S(1)} %get-tuple-element.47), channel_id=1, source_target_pairs={{0,64},{32,96},{64,128},{96,160},{128,0},{160,32},{192,256},{224,2... | collective-permute-start | bytes 393224 | tf_op jit(solution)/shard_map/ppermute | solution.py:53
  127.5 2.5 %collective-permute-done.11 = bf16[2,2,128,128]{3,2,1,0:T(8,128)(2,1)S(1)} collective-permute-done((bf16[2,2,128,128]{3,2,1,0:T(8,128)(2,1)S(1)}, bf16[2,2,128,128]{3,2,1,0:T(8,128)(2,1)S(1)}, u32[]{:S(2)}, u32[]{:S(2)}) %collective-permute-start.11) | collective-permute-done | bytes 131104 | tf_op jit(solution)/shard_map/ppermute | solution.py:53
  130.0 7.8 %collective-permute-done.10 = bf16[2,2,128,128]{3,2,1,0:T(8,128)(2,1)S(1)} collective-permute-done((bf16[2,2,128,128]{3,2,1,0:T(8,128)(2,1)S(1)}, bf16[2,2,128,128]{3,2,1,0:T(8,128)(2,1)S(1)}, u32[]{:S(2)}, u32[]{:S(2)}) %collective-permute-start.10) | collective-permute-done | bytes 131104 | tf_op jit(solution)/shard_map/ppermute | solution.py:53
  138.7 4.2 %collective-permute-start.13 = (bf16[128,512]{1,0:T(8,128)(2,1)}, bf16[128,512]{1,0:T(8,128)(2,1)}, u32[]{:S(2)}, u32[]{:S(2)}) collective-permute-start(bf16[128,512]{1,0:T(8,128)(2,1)} %convert_element_type.223), channel_id=1, source_target_pairs={{0,64},{32,96},{64,128},{96,160},{128,0},{160,32},{192,256},{224,2... | collective-permute-start | bytes 393224 | tf_op jit(solution)/shard_map/ppermute | solution.py:53
  142.9 5.5 %collective-permute-start.12 = (bf16[128,512]{1,0:T(8,128)(2,1)}, bf16[128,512]{1,0:T(8,128)(2,1)}, u32[]{:S(2)}, u32[]{:S(2)}) collective-permute-start(bf16[128,512]{1,0:T(8,128)(2,1)} %convert_element_type.223), channel_id=1, source_target_pairs={{0,128},{32,160},{64,0},{96,32},{128,64},{160,96},{192,320},{224,3... | collective-permute-start | bytes 393224 | tf_op jit(solution)/shard_map/ppermute | solution.py:53
  151.4 4.0 %collective-permute-start.14 = (bf16[128,512]{1,0:T(8,128)(2,1)}, bf16[128,512]{1,0:T(8,128)(2,1)}, u32[]{:S(2)}, u32[]{:S(2)}) collective-permute-start(bf16[128,512]{1,0:T(8,128)(2,1)} %fusion.28), channel_id=1, source_target_pairs={{0,6},{1,7},{2,0},{3,1},{4,2},{5,3},{6,4},{7,5},{8,14},{9,15},{10,... | collective-permute-start | bytes 393224 | tf_op jit(solution)/shard_map/ppermute | solution.py:53
  155.5 2.9 %collective-permute-start.15 = (bf16[128,512]{1,0:T(8,128)(2,1)}, bf16[128,512]{1,0:T(8,128)(2,1)}, u32[]{:S(2)}, u32[]{:S(2)}) collective-permute-start(bf16[128,512]{1,0:T(8,128)(2,1)} %fusion.28), channel_id=1, source_target_pairs={{0,4},{1,5},{2,6},{3,7},{4,0},{5,1},{6,2},{7,3},{8,12},{9,13},{10,... | collective-permute-start | bytes 393224 | tf_op jit(solution)/shard_map/ppermute | solution.py:53
  158.4 5.7 %collective-permute-start.16 = (bf16[128,512]{1,0:T(8,128)(2,1)}, bf16[128,512]{1,0:T(8,128)(2,1)}, u32[]{:S(2)}, u32[]{:S(2)}) collective-permute-start(bf16[128,512]{1,0:T(8,128)(2,1)} %fusion.28), channel_id=1, source_target_pairs={{0,2},{1,3},{2,4},{3,5},{4,6},{5,7},{6,0},{7,1},{8,10},{9,11},{10,... | collective-permute-start | bytes 393224 | tf_op jit(solution)/shard_map/ppermute | solution.py:53
  166.8 3.0 %collective-permute-done.15 = bf16[128,512]{1,0:T(8,128)(2,1)} collective-permute-done((bf16[128,512]{1,0:T(8,128)(2,1)}, bf16[128,512]{1,0:T(8,128)(2,1)}, u32[]{:S(2)}, u32[]{:S(2)}) %collective-permute-start.15) | collective-permute-done | bytes 131104 | tf_op jit(solution)/shard_map/ppermute | solution.py:53
  169.8 3.9 %collective-permute-done.16 = bf16[128,512]{1,0:T(8,128)(2,1)} collective-permute-done((bf16[128,512]{1,0:T(8,128)(2,1)}, bf16[128,512]{1,0:T(8,128)(2,1)}, u32[]{:S(2)}, u32[]{:S(2)}) %collective-permute-start.16) | collective-permute-done | bytes 131104 | tf_op jit(solution)/shard_map/ppermute | solution.py:53
  176.8 3.7 %collective-permute-start.18 = (bf16[3,128,512]{2,1,0:T(8,128)(2,1)}, bf16[3,128,512]{2,1,0:T(8,128)(2,1)}, u32[]{:S(2)}, u32[]{:S(2)}) collective-permute-start(bf16[3,128,512]{2,1,0:T(8,128)(2,1)} %pad_maximum_fusion.3), channel_id=1, source_target_pairs={{0,384},{32,416},{64,448},{96,480},{128,512},{160,544},{192,576},{... | collective-permute-start | bytes 1179656 | tf_op jit(solution)/shard_map/ppermute | solution.py:53
  180.5 4.5 %collective-permute-start.17 = (bf16[3,128,512]{2,1,0:T(8,128)(2,1)}, bf16[3,128,512]{2,1,0:T(8,128)(2,1)}, u32[]{:S(2)}, u32[]{:S(2)}) collective-permute-start(bf16[3,128,512]{2,1,0:T(8,128)(2,1)} %pad_maximum_fusion.3), channel_id=1, source_target_pairs={{0,576},{32,608},{64,640},{96,672},{128,704},{160,736},{192,0},{22... | collective-permute-start | bytes 1179656 | tf_op jit(solution)/shard_map/ppermute | solution.py:53
  188.7 3.3 %collective-permute-done.20 = bf16[128,512]{1,0:T(8,128)(2,1)} collective-permute-done((bf16[128,512]{1,0:T(8,128)(2,1)S(1)}, bf16[128,512]{1,0:T(8,128)(2,1)}, u32[]{:S(2)}, u32[]{:S(2)}) %collective-permute-start.20) | collective-permute-done | bytes 131104 | tf_op jit(solution)/shard_map/ppermute | solution.py:53
  193.0 4.7 %collective-permute-done.19 = bf16[3,128,512]{2,1,0:T(8,128)(2,1)} collective-permute-done((bf16[3,128,512]{2,1,0:T(8,128)(2,1)}, bf16[3,128,512]{2,1,0:T(8,128)(2,1)}, u32[]{:S(2)}, u32[]{:S(2)}) %collective-permute-start.19) | collective-permute-done | bytes 393248 | tf_op jit(solution)/shard_map/ppermute | solution.py:53
  197.6 2.5 %collective-permute-done.17 = bf16[3,128,512]{2,1,0:T(8,128)(2,1)} collective-permute-done((bf16[3,128,512]{2,1,0:T(8,128)(2,1)}, bf16[3,128,512]{2,1,0:T(8,128)(2,1)}, u32[]{:S(2)}, u32[]{:S(2)}) %collective-permute-start.17) | collective-permute-done | bytes 393248 | tf_op jit(solution)/shard_map/ppermute | solution.py:53
  211.0 4.7 %collective-permute-done.22 = bf16[128,512]{1,0:T(8,128)(2,1)S(1)} collective-permute-done((bf16[128,512]{1,0:T(8,128)(2,1)S(1)}, bf16[128,512]{1,0:T(8,128)(2,1)S(1)}, u32[]{:S(2)}, u32[]{:S(2)}) %collective-permute-start.22) | collective-permute-done | bytes 131104 | tf_op jit(solution)/shard_map/ppermute | solution.py:53
  216.0 5.7 %collective-permute-start.23 = (bf16[128,512]{1,0:T(8,128)(2,1)S(1)}, bf16[128,512]{1,0:T(8,128)(2,1)}, u32[]{:S(2)}, u32[]{:S(2)}) collective-permute-start(bf16[128,512]{1,0:T(8,128)(2,1)S(1)} %convert_add_fusion.1), channel_id=1, source_target_pairs={{0,16},{1,17},{2,18},{3,19},{4,20},{5,21},{6,22},{7,23},{8,24},{9,... | collective-permute-start | bytes 393224 | tf_op jit(solution)/shard_map/ppermute | solution.py:53
  224.8 3.4 %collective-permute-done.23 = bf16[128,512]{1,0:T(8,128)(2,1)} collective-permute-done((bf16[128,512]{1,0:T(8,128)(2,1)S(1)}, bf16[128,512]{1,0:T(8,128)(2,1)}, u32[]{:S(2)}, u32[]{:S(2)}) %collective-permute-start.23) | collective-permute-done | bytes 131104 | tf_op jit(solution)/shard_map/ppermute | solution.py:53
  (109 shorter events, 64.9 us)
Async XLA Ops:
  0.6 72.3 %copy-start = (bf16[512,256]{1,0:T(8,128)(2,1)S(1)}, bf16[512,256]{1,0:T(8,128)(2,1)}, u32[]{:S(2)}) copy-start(bf16[512,256]{1,0:T(8,128)(2,1)} %param.16) | copy-start | bytes 786436
  4.5 30.9 %copy-start.2 = (f32[128,4,128]{2,1,0:T(4,128)}, f32[128,4,128]{2,1,0:T(4,128)S(1)}, u32[]{:S(2)}) copy-start(f32[128,4,128]{2,1,0:T(4,128)S(1)} %broadcast_in_dim.42) | copy-start | bytes 786436
  4.6 61.2 %copy-start.11 = (bf16[128,256]{1,0:T(8,128)(2,1)S(1)}, bf16[128,256]{1,0:T(8,128)(2,1)}, u32[]{:S(2)}) copy-start(bf16[128,256]{1,0:T(8,128)(2,1)} %param.11) | copy-start | bytes 196612
  4.6 61.3 %copy-start.13 = (bf16[128,128]{1,0:T(8,128)(2,1)S(1)}, bf16[128,128]{1,0:T(8,128)(2,1)}, u32[]{:S(2)}) copy-start(bf16[128,128]{1,0:T(8,128)(2,1)} %param.10) | copy-start | bytes 98308
  4.6 62.0 %copy-start.12 = (bf16[128,256]{1,0:T(8,128)(2,1)S(1)}, bf16[128,256]{1,0:T(8,128)(2,1)}, u32[]{:S(2)}) copy-start(bf16[128,256]{1,0:T(8,128)(2,1)} %param.9) | copy-start | bytes 196612
  4.7 19.2 %collective-permute-start.1 = (bf16[128,578]{1,0:T(8,128)(2,1)S(1)}, bf16[128,578]{1,0:T(8,128)(2,1)S(1)}, u32[]{:S(2)}, u32[]{:S(2)}) collective-permute-start(bf16[128,578]{1,0:T(8,128)(2,1)S(1)} %pad_maximum_fusion.4), channel_id=1, source_target_pairs={{0,64},{32,96},{64,128},{96,160},{128,0},{160,32},{192,256},{224,2... | collective-permute-start | bytes 443912 | tf_op jit(solution)/shard_map/ppermute | solution.py:53
  15.8 19.6 %collective-permute-start = (bf16[128,578]{1,0:T(8,128)(2,1)S(1)}, bf16[128,578]{1,0:T(8,128)(2,1)S(1)}, u32[]{:S(2)}, u32[]{:S(2)}) collective-permute-start(bf16[128,578]{1,0:T(8,128)(2,1)S(1)} %pad_maximum_fusion.4), channel_id=1, source_target_pairs={{0,128},{32,160},{64,0},{96,32},{128,64},{160,96},{192,320},{224,3... | collective-permute-start | bytes 443912 | tf_op jit(solution)/shard_map/ppermute | solution.py:53
  35.5 16.3 %collective-permute-start.4 = (bf16[3,128,578]{2,1,0:T(8,128)(2,1)S(1)}, bf16[3,128,578]{2,1,0:T(8,128)(2,1)S(1)}, u32[]{:S(2)}, u32[]{:S(2)}) collective-permute-start(bf16[3,128,578]{2,1,0:T(8,128)(2,1)S(1)} %get-tuple-element.46), channel_id=1, source_target_pairs={{0,192},{32,224},{64,256},{96,288},{128,320},{160,352},{192,384},{... | collective-permute-start | bytes 1331720 | tf_op jit(solution)/shard_map/ppermute | solution.py:53
  38.9 22.6 %collective-permute-start.3 = (bf16[3,128,578]{2,1,0:T(8,128)(2,1)S(1)}, bf16[3,128,578]{2,1,0:T(8,128)(2,1)S(1)}, u32[]{:S(2)}, u32[]{:S(2)}) collective-permute-start(bf16[3,128,578]{2,1,0:T(8,128)(2,1)S(1)} %get-tuple-element.46), channel_id=1, source_target_pairs={{0,384},{32,416},{64,448},{96,480},{128,512},{160,544},{192,576},{... | collective-permute-start | bytes 1331720 | tf_op jit(solution)/shard_map/ppermute | solution.py:53
  43.6 19.5 %collective-permute-start.2 = (bf16[3,128,578]{2,1,0:T(8,128)(2,1)S(1)}, bf16[3,128,578]{2,1,0:T(8,128)(2,1)S(1)}, u32[]{:S(2)}, u32[]{:S(2)}) collective-permute-start(bf16[3,128,578]{2,1,0:T(8,128)(2,1)S(1)} %get-tuple-element.46), channel_id=1, source_target_pairs={{0,576},{32,608},{64,640},{96,672},{128,704},{160,736},{192,0},{22... | collective-permute-start | bytes 1331720 | tf_op jit(solution)/shard_map/ppermute | solution.py:53
  63.9 6.0 %collective-permute-start.5 = (bf16[4,3,128,640]{3,2,1,0:T(8,128)(2,1)S(1)}, bf16[4,3,128,640]{3,2,1,0:T(8,128)(2,1)}, u32[]{:S(2)}, u32[]{:S(2)}) collective-permute-start(bf16[4,3,128,640]{3,2,1,0:T(8,128)(2,1)S(1)} %fusion.22), channel_id=1, source_target_pairs={{0,32},{32,0},{64,96},{96,64},{128,160},{160,128},{192,224},{224,1... | collective-permute-start | bytes 5898248 | tf_op jit(solution)/shard_map/ppermute | solution.py:53
  71.8 4.1 %copy-start.1 = (bf16[2,4,3,128,578]{4,3,2,1,0:T(8,128)(2,1)}, bf16[2,4,3,128,578]{4,3,2,1,0:T(8,128)(2,1)S(1)}, u32[]{:S(2)}) copy-start(bf16[2,4,3,128,578]{4,3,2,1,0:T(8,128)(2,1)S(1)} %pad_maximum_fusion) | copy-start | bytes 10653700
  83.9 5.3 %collective-permute-start.6 = (bf16[2,2,4,3,128,128]{5,4,3,2,1,0:T(8,128)(2,1)S(1)}, bf16[2,2,4,3,128,128]{5,4,3,2,1,0:T(8,128)(2,1)S(1)}, u32[]{:S(2)}, u32[]{:S(2)}) collective-permute-start(bf16[2,2,4,3,128,128]{5,4,3,2,1,0:T(8,128)(2,1)S(1)} %fusion.24), channel_id=1, source_target_pairs={{0,32},{32,0},{64,96},{96,64},{128,160},{160,128},{192,224},{224,1... | collective-permute-start | bytes 4718600 | tf_op jit(solution)/shard_map/ppermute | solution.py:53
  90.0 21.9 %collective-permute-start.9 = (bf16[2,2,3,128,128]{4,3,2,1,0:T(8,128)(2,1)S(1)}, bf16[2,2,3,128,128]{4,3,2,1,0:T(8,128)(2,1)S(1)}, u32[]{:S(2)}, u32[]{:S(2)}) collective-permute-start(bf16[2,2,3,128,128]{4,3,2,1,0:T(8,128)(2,1)S(1)} %get-tuple-element.41), channel_id=1, source_target_pairs={{0,576},{32,608},{64,640},{96,672},{128,704},{160,736},{192,0},{22... | collective-permute-start | bytes 1179656 | tf_op jit(solution)/shard_map/ppermute | solution.py:53
  94.6 17.3 %collective-permute-start.8 = (bf16[2,2,3,128,128]{4,3,2,1,0:T(8,128)(2,1)S(1)}, bf16[2,2,3,128,128]{4,3,2,1,0:T(8,128)(2,1)S(1)}, u32[]{:S(2)}, u32[]{:S(2)}) collective-permute-start(bf16[2,2,3,128,128]{4,3,2,1,0:T(8,128)(2,1)S(1)} %get-tuple-element.42), channel_id=1, source_target_pairs={{0,384},{32,416},{64,448},{96,480},{128,512},{160,544},{192,576},{... | collective-permute-start | bytes 1179656 | tf_op jit(solution)/shard_map/ppermute | solution.py:53
  98.3 19.2 %collective-permute-start.7 = (bf16[2,2,3,128,128]{4,3,2,1,0:T(8,128)(2,1)S(1)}, bf16[2,2,3,128,128]{4,3,2,1,0:T(8,128)(2,1)S(1)}, u32[]{:S(2)}, u32[]{:S(2)}) collective-permute-start(bf16[2,2,3,128,128]{4,3,2,1,0:T(8,128)(2,1)S(1)} %get-tuple-element.40), channel_id=1, source_target_pairs={{0,192},{32,224},{64,256},{96,288},{128,320},{160,352},{192,384},{... | collective-permute-start | bytes 1179656 | tf_op jit(solution)/shard_map/ppermute | solution.py:53
  117.7 12.3 %collective-permute-start.11 = (bf16[2,2,128,128]{3,2,1,0:T(8,128)(2,1)S(1)}, bf16[2,2,128,128]{3,2,1,0:T(8,128)(2,1)S(1)}, u32[]{:S(2)}, u32[]{:S(2)}) collective-permute-start(bf16[2,2,128,128]{3,2,1,0:T(8,128)(2,1)S(1)} %get-tuple-element.48), channel_id=1, source_target_pairs={{0,128},{32,160},{64,0},{96,32},{128,64},{160,96},{192,320},{224,3... | collective-permute-start | bytes 393224 | tf_op jit(solution)/shard_map/ppermute | solution.py:53
  124.8 13.0 %collective-permute-start.10 = (bf16[2,2,128,128]{3,2,1,0:T(8,128)(2,1)S(1)}, bf16[2,2,128,128]{3,2,1,0:T(8,128)(2,1)S(1)}, u32[]{:S(2)}, u32[]{:S(2)}) collective-permute-start(bf16[2,2,128,128]{3,2,1,0:T(8,128)(2,1)S(1)} %get-tuple-element.47), channel_id=1, source_target_pairs={{0,64},{32,96},{64,128},{96,160},{128,0},{160,32},{192,256},{224,2... | collective-permute-start | bytes 393224 | tf_op jit(solution)/shard_map/ppermute | solution.py:53
  138.7 26.2 %collective-permute-start.13 = (bf16[128,512]{1,0:T(8,128)(2,1)}, bf16[128,512]{1,0:T(8,128)(2,1)}, u32[]{:S(2)}, u32[]{:S(2)}) collective-permute-start(bf16[128,512]{1,0:T(8,128)(2,1)} %convert_element_type.223), channel_id=1, source_target_pairs={{0,64},{32,96},{64,128},{96,160},{128,0},{160,32},{192,256},{224,2... | collective-permute-start | bytes 393224 | tf_op jit(solution)/shard_map/ppermute | solution.py:53
  142.9 22.0 %collective-permute-start.12 = (bf16[128,512]{1,0:T(8,128)(2,1)}, bf16[128,512]{1,0:T(8,128)(2,1)}, u32[]{:S(2)}, u32[]{:S(2)}) collective-permute-start(bf16[128,512]{1,0:T(8,128)(2,1)} %convert_element_type.223), channel_id=1, source_target_pairs={{0,128},{32,160},{64,0},{96,32},{128,64},{160,96},{192,320},{224,3... | collective-permute-start | bytes 393224 | tf_op jit(solution)/shard_map/ppermute | solution.py:53
  151.4 15.3 %collective-permute-start.14 = (bf16[128,512]{1,0:T(8,128)(2,1)}, bf16[128,512]{1,0:T(8,128)(2,1)}, u32[]{:S(2)}, u32[]{:S(2)}) collective-permute-start(bf16[128,512]{1,0:T(8,128)(2,1)} %fusion.28), channel_id=1, source_target_pairs={{0,6},{1,7},{2,0},{3,1},{4,2},{5,3},{6,4},{7,5},{8,14},{9,15},{10,... | collective-permute-start | bytes 393224 | tf_op jit(solution)/shard_map/ppermute | solution.py:53
  155.5 14.3 %collective-permute-start.15 = (bf16[128,512]{1,0:T(8,128)(2,1)}, bf16[128,512]{1,0:T(8,128)(2,1)}, u32[]{:S(2)}, u32[]{:S(2)}) collective-permute-start(bf16[128,512]{1,0:T(8,128)(2,1)} %fusion.28), channel_id=1, source_target_pairs={{0,4},{1,5},{2,6},{3,7},{4,0},{5,1},{6,2},{7,3},{8,12},{9,13},{10,... | collective-permute-start | bytes 393224 | tf_op jit(solution)/shard_map/ppermute | solution.py:53
  158.4 15.2 %collective-permute-start.16 = (bf16[128,512]{1,0:T(8,128)(2,1)}, bf16[128,512]{1,0:T(8,128)(2,1)}, u32[]{:S(2)}, u32[]{:S(2)}) collective-permute-start(bf16[128,512]{1,0:T(8,128)(2,1)} %fusion.28), channel_id=1, source_target_pairs={{0,2},{1,3},{2,4},{3,5},{4,6},{5,7},{6,0},{7,1},{8,10},{9,11},{10,... | collective-permute-start | bytes 393224 | tf_op jit(solution)/shard_map/ppermute | solution.py:53
  174.9 22.8 %collective-permute-start.19 = (bf16[3,128,512]{2,1,0:T(8,128)(2,1)}, bf16[3,128,512]{2,1,0:T(8,128)(2,1)}, u32[]{:S(2)}, u32[]{:S(2)}) collective-permute-start(bf16[3,128,512]{2,1,0:T(8,128)(2,1)} %pad_maximum_fusion.3), channel_id=1, source_target_pairs={{0,192},{32,224},{64,256},{96,288},{128,320},{160,352},{192,384},{... | collective-permute-start | bytes 1179656 | tf_op jit(solution)/shard_map/ppermute | solution.py:53
  176.8 20.9 %collective-permute-start.18 = (bf16[3,128,512]{2,1,0:T(8,128)(2,1)}, bf16[3,128,512]{2,1,0:T(8,128)(2,1)}, u32[]{:S(2)}, u32[]{:S(2)}) collective-permute-start(bf16[3,128,512]{2,1,0:T(8,128)(2,1)} %pad_maximum_fusion.3), channel_id=1, source_target_pairs={{0,384},{32,416},{64,448},{96,480},{128,512},{160,544},{192,576},{... | collective-permute-start | bytes 1179656 | tf_op jit(solution)/shard_map/ppermute | solution.py:53
  180.5 19.7 %collective-permute-start.17 = (bf16[3,128,512]{2,1,0:T(8,128)(2,1)}, bf16[3,128,512]{2,1,0:T(8,128)(2,1)}, u32[]{:S(2)}, u32[]{:S(2)}) collective-permute-start(bf16[3,128,512]{2,1,0:T(8,128)(2,1)} %pad_maximum_fusion.3), channel_id=1, source_target_pairs={{0,576},{32,608},{64,640},{96,672},{128,704},{160,736},{192,0},{22... | collective-permute-start | bytes 1179656 | tf_op jit(solution)/shard_map/ppermute | solution.py:53
  185.1 7.0 %collective-permute-start.20 = (bf16[128,512]{1,0:T(8,128)(2,1)S(1)}, bf16[128,512]{1,0:T(8,128)(2,1)}, u32[]{:S(2)}, u32[]{:S(2)}) collective-permute-start(bf16[128,512]{1,0:T(8,128)(2,1)S(1)} %convert_add_fusion.3), channel_id=1, source_target_pairs={{0,1},{1,0},{2,3},{3,2},{4,5},{5,4},{6,7},{7,6},{8,9},{9,8},{10,11... | collective-permute-start | bytes 393224 | tf_op jit(solution)/shard_map/ppermute | solution.py:53
  206.0 9.8 %collective-permute-start.21 = (f32[512,512]{1,0:T(8,128)S(1)}, f32[512,512]{1,0:T(8,128)S(1)}, u32[]{:S(2)}, u32[]{:S(2)}) collective-permute-start(f32[512,512]{1,0:T(8,128)S(1)} %add_bitcast_fusion), channel_id=1, source_target_pairs={{0,32},{32,0},{64,96},{96,64},{128,160},{160,128},{192,224},{224,1... | collective-permute-start | bytes 3145736 | tf_op jit(solution)/shard_map/ppermute | solution.py:53
  207.9 7.8 %collective-permute-start.22 = (bf16[128,512]{1,0:T(8,128)(2,1)S(1)}, bf16[128,512]{1,0:T(8,128)(2,1)S(1)}, u32[]{:S(2)}, u32[]{:S(2)}) collective-permute-start(bf16[128,512]{1,0:T(8,128)(2,1)S(1)} %convert_add_fusion.2), channel_id=1, source_target_pairs={{0,8},{1,9},{2,10},{3,11},{4,12},{5,13},{6,14},{7,15},{8,0},{9,1},... | collective-permute-start | bytes 393224 | tf_op jit(solution)/shard_map/ppermute | solution.py:53
  211.0 12.3 %copy-start.8 = (bf16[2,128,128]{2,1,0:T(8,128)(2,1)S(1)}, bf16[2,128,128]{2,1,0:T(8,128)(2,1)}, u32[]{:S(2)}) copy-start(bf16[2,128,128]{2,1,0:T(8,128)(2,1)} %convolution_convert_fusion.2) | copy-start | bytes 196612
  215.7 13.4 %copy-start.3 = (f32[128,4,128]{2,1,0:T(4,128)S(1)}, f32[128,4,128]{2,1,0:T(4,128)}, u32[]{:S(2)}) copy-start(f32[128,4,128]{2,1,0:T(4,128)} %copy-done.2) | copy-start | bytes 786436
  216.0 12.2 %collective-permute-start.23 = (bf16[128,512]{1,0:T(8,128)(2,1)S(1)}, bf16[128,512]{1,0:T(8,128)(2,1)}, u32[]{:S(2)}, u32[]{:S(2)}) collective-permute-start(bf16[128,512]{1,0:T(8,128)(2,1)S(1)} %convert_add_fusion.1), channel_id=1, source_target_pairs={{0,16},{1,17},{2,18},{3,19},{4,20},{5,21},{6,22},{7,23},{8,24},{9,... | collective-permute-start | bytes 393224 | tf_op jit(solution)/shard_map/ppermute | solution.py:53
  (7 other events, 9.2 us)

commit v13 on v10

--- a/solution.py
+++ b/solution.py
@@ -216,11 +216,13 @@
 
     latent_sum = latent_part
     flats = flat
-    for level in range(max(len(sum_levels), len(gather_levels))):
+    for level in range(max(len(sum_levels), len(gather_levels) + 1)):
         if level < len(gather_levels) - 1:
             flats = gather_step(flats, "blk", *gather_levels[level])
         elif level == len(gather_levels) - 1:
-            flats = reduce_step(own_products(flats), "blk", *gather_levels[level], jnp.float32)
+            flats = own_products(flats)
+        elif level == len(gather_levels):
+            flats = reduce_step(flats, "blk", *gather_levels[-1], jnp.float32)
         if level < len(sum_levels):
             latent_sum = reduce_step(latent_sum, "heads", *sum_levels[level], jnp.bfloat16)
         flats, latent_sum = lax.optimization_barrier((flats, latent_sum))

time: 228 us -> 228 us (level)
  waiting for transfers between devices: 75.1 us -> 72.3 us
    ppermute x24, waiting for transfers between devices: 75.1 us -> 72.3 us  [shift_digit(): return lax.ppermute(x, axis, pairs)]
    unnamed x41 -> x39, local copies, waits for them, and re-layouts: 4.01 us -> 4.84 us
  transfers between devices with their start and end apart: 24 -> 24, of which waited for: 16 -> 16; matrix products, arithmetic and copies ran while one was open for 7% -> 9% of each run, Pallas kernels for 0% -> 0%
where the time goes in v13:
time: 228 us; the launch traced here: 226 us
  starting transfers between devices  103 us (45%)
  waiting for transfers between devices  72.3 us (32%)
  other arithmetic  23.1 us (10%)
  matrix products  13.5 us (6%)
  local copies, waits for them, and re-layouts  13.1 us (6%)
    ppermute x24, starting transfers between devices, shift_digit(): return lax.ppermute(x, axis, pairs)  103 us
    ppermute x24, waiting for transfers between devices, shift_digit(): return lax.ppermute(x, axis, pairs)  72.3 us
    another operation x7, other arithmetic, gather_step(): return jnp.stack(pieces, axis=0)  7.31 us
    unnamed x39, local copies, waits for them, and re-layouts  4.84 us
  transfers between devices with their start and end apart: 24, of which 16 were waited for; matrix products, arithmetic and copies ran while one was open for 9% of the time, Pallas kernels for 0%

profile of v13, /device:TPU:56, one launch (start us, length us, event | category | flops | bytes accessed | tf_op | source)
XLA Modules:
  0.0 226.2 jit_solution(14757942455649368319)
XLA Ops:
  4.7 11.0 %collective-permute-start.1 = (bf16[128,578]{1,0:T(8,128)(2,1)S(1)}, bf16[128,578]{1,0:T(8,128)(2,1)S(1)}, u32[]{:S(2)}, u32[]{:S(2)}) collective-permute-start(bf16[128,578]{1,0:T(8,128)(2,1)S(1)} %pad_maximum_fusion.4), channel_id=1, source_target_pairs={{0,64},{32,96},{64,128},{96,160},{128,0},{160,32},{192,256},{224,2... | collective-permute-start | bytes 443912 | tf_op jit(solution)/shard_map/ppermute | solution.py:53
  15.8 5.6 %collective-permute-start = (bf16[128,578]{1,0:T(8,128)(2,1)S(1)}, bf16[128,578]{1,0:T(8,128)(2,1)S(1)}, u32[]{:S(2)}, u32[]{:S(2)}) collective-permute-start(bf16[128,578]{1,0:T(8,128)(2,1)S(1)} %pad_maximum_fusion.4), channel_id=1, source_target_pairs={{0,128},{32,160},{64,0},{96,32},{128,64},{160,96},{192,320},{224,3... | collective-permute-start | bytes 443912 | tf_op jit(solution)/shard_map/ppermute | solution.py:53
  21.4 2.5 %collective-permute-done.1 = bf16[128,578]{1,0:T(8,128)(2,1)S(1)} collective-permute-done((bf16[128,578]{1,0:T(8,128)(2,1)S(1)}, bf16[128,578]{1,0:T(8,128)(2,1)S(1)}, u32[]{:S(2)}, u32[]{:S(2)}) %collective-permute-start.1) | collective-permute-done | bytes 148000 | tf_op jit(solution)/shard_map/ppermute | solution.py:53
  23.9 11.5 %collective-permute-done = bf16[128,578]{1,0:T(8,128)(2,1)S(1)} collective-permute-done((bf16[128,578]{1,0:T(8,128)(2,1)S(1)}, bf16[128,578]{1,0:T(8,128)(2,1)S(1)}, u32[]{:S(2)}, u32[]{:S(2)}) %collective-permute-start) | collective-permute-done | bytes 148000 | tf_op jit(solution)/shard_map/ppermute | solution.py:53
  35.5 3.4 %collective-permute-start.4 = (bf16[3,128,578]{2,1,0:T(8,128)(2,1)S(1)}, bf16[3,128,578]{2,1,0:T(8,128)(2,1)S(1)}, u32[]{:S(2)}, u32[]{:S(2)}) collective-permute-start(bf16[3,128,578]{2,1,0:T(8,128)(2,1)S(1)} %get-tuple-element.46), channel_id=1, source_target_pairs={{0,192},{32,224},{64,256},{96,288},{128,320},{160,352},{192,384},{... | collective-permute-start | bytes 1331720 | tf_op jit(solution)/shard_map/ppermute | solution.py:53
  38.9 4.6 %collective-permute-start.3 = (bf16[3,128,578]{2,1,0:T(8,128)(2,1)S(1)}, bf16[3,128,578]{2,1,0:T(8,128)(2,1)S(1)}, u32[]{:S(2)}, u32[]{:S(2)}) collective-permute-start(bf16[3,128,578]{2,1,0:T(8,128)(2,1)S(1)} %get-tuple-element.46), channel_id=1, source_target_pairs={{0,384},{32,416},{64,448},{96,480},{128,512},{160,544},{192,576},{... | collective-permute-start | bytes 1331720 | tf_op jit(solution)/shard_map/ppermute | solution.py:53
  43.6 3.3 %collective-permute-start.2 = (bf16[3,128,578]{2,1,0:T(8,128)(2,1)S(1)}, bf16[3,128,578]{2,1,0:T(8,128)(2,1)S(1)}, u32[]{:S(2)}, u32[]{:S(2)}) collective-permute-start(bf16[3,128,578]{2,1,0:T(8,128)(2,1)S(1)} %get-tuple-element.46), channel_id=1, source_target_pairs={{0,576},{32,608},{64,640},{96,672},{128,704},{160,736},{192,0},{22... | collective-permute-start | bytes 1331720 | tf_op jit(solution)/shard_map/ppermute | solution.py:53
  46.9 4.9 %collective-permute-done.4 = bf16[3,128,578]{2,1,0:T(8,128)(2,1)S(1)} collective-permute-done((bf16[3,128,578]{2,1,0:T(8,128)(2,1)S(1)}, bf16[3,128,578]{2,1,0:T(8,128)(2,1)S(1)}, u32[]{:S(2)}, u32[]{:S(2)}) %collective-permute-start.4) | collective-permute-done | bytes 443936 | tf_op jit(solution)/shard_map/ppermute | solution.py:53
  51.8 9.7 %collective-permute-done.3 = bf16[3,128,578]{2,1,0:T(8,128)(2,1)S(1)} collective-permute-done((bf16[3,128,578]{2,1,0:T(8,128)(2,1)S(1)}, bf16[3,128,578]{2,1,0:T(8,128)(2,1)S(1)}, u32[]{:S(2)}, u32[]{:S(2)}) %collective-permute-start.3) | collective-permute-done | bytes 443936 | tf_op jit(solution)/shard_map/ppermute | solution.py:53
  83.9 2.4 %collective-permute-start.6 = (bf16[2,2,4,3,128,128]{5,4,3,2,1,0:T(8,128)(2,1)S(1)}, bf16[2,2,4,3,128,128]{5,4,3,2,1,0:T(8,128)(2,1)S(1)}, u32[]{:S(2)}, u32[]{:S(2)}) collective-permute-start(bf16[2,2,4,3,128,128]{5,4,3,2,1,0:T(8,128)(2,1)S(1)} %fusion.24), channel_id=1, source_target_pairs={{0,32},{32,0},{64,96},{96,64},{128,160},{160,128},{192,224},{224,1... | collective-permute-start | bytes 4718600 | tf_op jit(solution)/shard_map/ppermute | solution.py:53
  86.3 2.8 %collective-permute-done.6 = bf16[2,2,4,3,128,128]{5,4,3,2,1,0:T(8,128)(2,1)S(1)} collective-permute-done((bf16[2,2,4,3,128,128]{5,4,3,2,1,0:T(8,128)(2,1)S(1)}, bf16[2,2,4,3,128,128]{5,4,3,2,1,0:T(8,128)(2,1)S(1)}, u32[]{:S(2)}, u32[]{:S(2)}) %collective-permute-start.6) | collective-permute-done | bytes 1572896 | tf_op jit(solution)/shard_map/ppermute | solution.py:53
  90.0 4.5 %collective-permute-start.9 = (bf16[2,2,3,128,128]{4,3,2,1,0:T(8,128)(2,1)S(1)}, bf16[2,2,3,128,128]{4,3,2,1,0:T(8,128)(2,1)S(1)}, u32[]{:S(2)}, u32[]{:S(2)}) collective-permute-start(bf16[2,2,3,128,128]{4,3,2,1,0:T(8,128)(2,1)S(1)} %get-tuple-element.41), channel_id=1, source_target_pairs={{0,576},{32,608},{64,640},{96,672},{128,704},{160,736},{192,0},{22... | collective-permute-start | bytes 1179656 | tf_op jit(solution)/shard_map/ppermute | solution.py:53
  94.6 3.7 %collective-permute-start.8 = (bf16[2,2,3,128,128]{4,3,2,1,0:T(8,128)(2,1)S(1)}, bf16[2,2,3,128,128]{4,3,2,1,0:T(8,128)(2,1)S(1)}, u32[]{:S(2)}, u32[]{:S(2)}) collective-permute-start(bf16[2,2,3,128,128]{4,3,2,1,0:T(8,128)(2,1)S(1)} %get-tuple-element.42), channel_id=1, source_target_pairs={{0,384},{32,416},{64,448},{96,480},{128,512},{160,544},{192,576},{... | collective-permute-start | bytes 1179656 | tf_op jit(solution)/shard_map/ppermute | solution.py:53
  100.2 11.7 %collective-permute-done.9 = bf16[2,2,3,128,128]{4,3,2,1,0:T(8,128)(2,1)S(1)} collective-permute-done((bf16[2,2,3,128,128]{4,3,2,1,0:T(8,128)(2,1)S(1)}, bf16[2,2,3,128,128]{4,3,2,1,0:T(8,128)(2,1)S(1)}, u32[]{:S(2)}, u32[]{:S(2)}) %collective-permute-start.9) | collective-permute-done | bytes 393248 | tf_op jit(solution)/shard_map/ppermute | solution.py:53
  111.9 5.6 %collective-permute-done.7 = bf16[2,2,3,128,128]{4,3,2,1,0:T(8,128)(2,1)S(1)} collective-permute-done((bf16[2,2,3,128,128]{4,3,2,1,0:T(8,128)(2,1)S(1)}, bf16[2,2,3,128,128]{4,3,2,1,0:T(8,128)(2,1)S(1)}, u32[]{:S(2)}, u32[]{:S(2)}) %collective-permute-start.7) | collective-permute-done | bytes 393248 | tf_op jit(solution)/shard_map/ppermute | solution.py:53
  117.7 7.1 %collective-permute-start.11 = (bf16[2,2,128,128]{3,2,1,0:T(8,128)(2,1)S(1)}, bf16[2,2,128,128]{3,2,1,0:T(8,128)(2,1)S(1)}, u32[]{:S(2)}, u32[]{:S(2)}) collective-permute-start(bf16[2,2,128,128]{3,2,1,0:T(8,128)(2,1)S(1)} %get-tuple-element.48), channel_id=1, source_target_pairs={{0,128},{32,160},{64,0},{96,32},{128,64},{160,96},{192,320},{224,3... | collective-permute-start | bytes 393224 | tf_op jit(solution)/shard_map/ppermute | solution.py:53
  124.8 2.7 %collective-permute-start.10 = (bf16[2,2,128,128]{3,2,1,0:T(8,128)(2,1)S(1)}, bf16[2,2,128,128]{3,2,1,0:T(8,128)(2,1)S(1)}, u32[]{:S(2)}, u32[]{:S(2)}) collective-permute-start(bf16[2,2,128,128]{3,2,1,0:T(8,128)(2,1)S(1)} %get-tuple-element.47), channel_id=1, source_target_pairs={{0,64},{32,96},{64,128},{96,160},{128,0},{160,32},{192,256},{224,2... | collective-permute-start | bytes 393224 | tf_op jit(solution)/shard_map/ppermute | solution.py:53
  127.5 2.5 %collective-permute-done.11 = bf16[2,2,128,128]{3,2,1,0:T(8,128)(2,1)S(1)} collective-permute-done((bf16[2,2,128,128]{3,2,1,0:T(8,128)(2,1)S(1)}, bf16[2,2,128,128]{3,2,1,0:T(8,128)(2,1)S(1)}, u32[]{:S(2)}, u32[]{:S(2)}) %collective-permute-start.11) | collective-permute-done | bytes 131104 | tf_op jit(solution)/shard_map/ppermute | solution.py:53
  130.0 7.8 %collective-permute-done.10 = bf16[2,2,128,128]{3,2,1,0:T(8,128)(2,1)S(1)} collective-permute-done((bf16[2,2,128,128]{3,2,1,0:T(8,128)(2,1)S(1)}, bf16[2,2,128,128]{3,2,1,0:T(8,128)(2,1)S(1)}, u32[]{:S(2)}, u32[]{:S(2)}) %collective-permute-start.10) | collective-permute-done | bytes 131104 | tf_op jit(solution)/shard_map/ppermute | solution.py:53
  138.7 4.2 %collective-permute-start.13 = (bf16[128,512]{1,0:T(8,128)(2,1)}, bf16[128,512]{1,0:T(8,128)(2,1)}, u32[]{:S(2)}, u32[]{:S(2)}) collective-permute-start(bf16[128,512]{1,0:T(8,128)(2,1)} %convert_element_type.223), channel_id=1, source_target_pairs={{0,64},{32,96},{64,128},{96,160},{128,0},{160,32},{192,256},{224,2... | collective-permute-start | bytes 393224 | tf_op jit(solution)/shard_map/ppermute | solution.py:53
  142.9 5.5 %collective-permute-start.12 = (bf16[128,512]{1,0:T(8,128)(2,1)}, bf16[128,512]{1,0:T(8,128)(2,1)}, u32[]{:S(2)}, u32[]{:S(2)}) collective-permute-start(bf16[128,512]{1,0:T(8,128)(2,1)} %convert_element_type.223), channel_id=1, source_target_pairs={{0,128},{32,160},{64,0},{96,32},{128,64},{160,96},{192,320},{224,3... | collective-permute-start | bytes 393224 | tf_op jit(solution)/shard_map/ppermute | solution.py:53
  151.4 3.2 %collective-permute-start.14 = (bf16[128,512]{1,0:T(8,128)(2,1)}, bf16[128,512]{1,0:T(8,128)(2,1)}, u32[]{:S(2)}, u32[]{:S(2)}) collective-permute-start(bf16[128,512]{1,0:T(8,128)(2,1)} %fusion.28), channel_id=1, source_target_pairs={{0,1},{1,0},{2,3},{3,2},{4,5},{5,4},{6,7},{7,6},{8,9},{9,8},{10,11... | collective-permute-start | bytes 393224 | tf_op jit(solution)/shard_map/ppermute | solution.py:53
  159.6 4.0 %collective-permute-start.18 = (bf16[128,512]{1,0:T(8,128)(2,1)S(1)}, bf16[128,512]{1,0:T(8,128)(2,1)S(1)}, u32[]{:S(2)}, u32[]{:S(2)}) collective-permute-start(bf16[128,512]{1,0:T(8,128)(2,1)S(1)} %convert_add_fusion.3), channel_id=1, source_target_pairs={{0,6},{1,7},{2,0},{3,1},{4,2},{5,3},{6,4},{7,5},{8,14},{9,15},{10,... | collective-permute-start | bytes 393224 | tf_op jit(solution)/shard_map/ppermute | solution.py:53
  163.6 3.8 %collective-permute-start.17 = (bf16[3,128,512]{2,1,0:T(8,128)(2,1)}, bf16[3,128,512]{2,1,0:T(8,128)(2,1)}, u32[]{:S(2)}, u32[]{:S(2)}) collective-permute-start(bf16[3,128,512]{2,1,0:T(8,128)(2,1)} %pad_maximum_fusion.3), channel_id=1, source_target_pairs={{0,192},{32,224},{64,256},{96,288},{128,320},{160,352},{192,384},{... | collective-permute-start | bytes 1179656 | tf_op jit(solution)/shard_map/ppermute | solution.py:53
  167.5 3.6 %collective-permute-start.16 = (bf16[3,128,512]{2,1,0:T(8,128)(2,1)}, bf16[3,128,512]{2,1,0:T(8,128)(2,1)}, u32[]{:S(2)}, u32[]{:S(2)}) collective-permute-start(bf16[3,128,512]{2,1,0:T(8,128)(2,1)} %pad_maximum_fusion.3), channel_id=1, source_target_pairs={{0,384},{32,416},{64,448},{96,480},{128,512},{160,544},{192,576},{... | collective-permute-start | bytes 1179656 | tf_op jit(solution)/shard_map/ppermute | solution.py:53
  171.1 2.9 %collective-permute-start.15 = (bf16[3,128,512]{2,1,0:T(8,128)(2,1)}, bf16[3,128,512]{2,1,0:T(8,128)(2,1)}, u32[]{:S(2)}, u32[]{:S(2)}) collective-permute-start(bf16[3,128,512]{2,1,0:T(8,128)(2,1)} %pad_maximum_fusion.3), channel_id=1, source_target_pairs={{0,576},{32,608},{64,640},{96,672},{128,704},{160,736},{192,0},{22... | collective-permute-start | bytes 1179656 | tf_op jit(solution)/shard_map/ppermute | solution.py:53
  174.0 2.9 %collective-permute-start.19 = (bf16[128,512]{1,0:T(8,128)(2,1)S(1)}, bf16[128,512]{1,0:T(8,128)(2,1)}, u32[]{:S(2)}, u32[]{:S(2)}) collective-permute-start(bf16[128,512]{1,0:T(8,128)(2,1)S(1)} %convert_add_fusion.3), channel_id=1, source_target_pairs={{0,4},{1,5},{2,6},{3,7},{4,0},{5,1},{6,2},{7,3},{8,12},{9,13},{10,... | collective-permute-start | bytes 393224 | tf_op jit(solution)/shard_map/ppermute | solution.py:53
  177.6 5.7 %collective-permute-start.20 = (bf16[128,512]{1,0:T(8,128)(2,1)S(1)}, bf16[128,512]{1,0:T(8,128)(2,1)}, u32[]{:S(2)}, u32[]{:S(2)}) collective-permute-start(bf16[128,512]{1,0:T(8,128)(2,1)S(1)} %convert_add_fusion.3), channel_id=1, source_target_pairs={{0,2},{1,3},{2,4},{3,5},{4,6},{5,7},{6,0},{7,1},{8,10},{9,11},{10,... | collective-permute-start | bytes 393224 | tf_op jit(solution)/shard_map/ppermute | solution.py:53
  185.2 4.9 %collective-permute-done.20 = bf16[128,512]{1,0:T(8,128)(2,1)} collective-permute-done((bf16[128,512]{1,0:T(8,128)(2,1)S(1)}, bf16[128,512]{1,0:T(8,128)(2,1)}, u32[]{:S(2)}, u32[]{:S(2)}) %collective-permute-start.20) | collective-permute-done | bytes 131104 | tf_op jit(solution)/shard_map/ppermute | solution.py:53
  197.0 2.7 %add_bitcast_fusion = f32[512,512]{1,0:T(8,128)} fusion(f32[4,512,512]{2,1,0:T(8,128)S(1)} %convert_convert_fusion, f32[4,512,512]{2,1,0:T(8,128)S(1)} %convert_convert_fusion.1, f32[4,512,512]{2,1,0:T(8,128)S(1)} %convert_convert_fusion.2, pred[]{:T(512)S(6)} %eq.204, pred[]{:T(512)S(6)} %eq.202, pred[]{:T(512)S(6)} %eq.176, pred[]{:T(512)S(6)} %eq.205, ...), kind=kLoop, calls=%fused_computation.51 | loop fusion | flops 13893632 | bytes 13631506 | tf_op jit(solution)/shard_map/add | solution.py:106
  205.1 10.6 %collective-permute-start.23 = (bf16[128,512]{1,0:T(8,128)(2,1)S(1)}, bf16[128,512]{1,0:T(8,128)(2,1)S(1)}, u32[]{:S(2)}, u32[]{:S(2)}) collective-permute-start(bf16[128,512]{1,0:T(8,128)(2,1)S(1)} %convert_add_fusion.1), channel_id=1, source_target_pairs={{0,16},{1,17},{2,18},{3,19},{4,20},{5,21},{6,22},{7,23},{8,24},{9,... | collective-permute-start | bytes 393224 | tf_op jit(solution)/shard_map/ppermute | solution.py:53
  219.6 3.1 %collective-permute-done.23 = bf16[128,512]{1,0:T(8,128)(2,1)S(1)} collective-permute-done((bf16[128,512]{1,0:T(8,128)(2,1)S(1)}, bf16[128,512]{1,0:T(8,128)(2,1)S(1)}, u32[]{:S(2)}, u32[]{:S(2)}) %collective-permute-start.23) | collective-permute-done | bytes 131104 | tf_op jit(solution)/shard_map/ppermute | solution.py:53
  (111 shorter events, 59.9 us)
Async XLA Ops:
  0.6 72.3 %copy-start = (bf16[512,256]{1,0:T(8,128)(2,1)S(1)}, bf16[512,256]{1,0:T(8,128)(2,1)}, u32[]{:S(2)}) copy-start(bf16[512,256]{1,0:T(8,128)(2,1)} %param.16) | copy-start | bytes 786436
  4.5 30.9 %copy-start.2 = (f32[128,4,128]{2,1,0:T(4,128)}, f32[128,4,128]{2,1,0:T(4,128)S(1)}, u32[]{:S(2)}) copy-start(f32[128,4,128]{2,1,0:T(4,128)S(1)} %broadcast_in_dim.42) | copy-start | bytes 786436
  4.6 61.2 %copy-start.12 = (bf16[128,256]{1,0:T(8,128)(2,1)S(1)}, bf16[128,256]{1,0:T(8,128)(2,1)}, u32[]{:S(2)}) copy-start(bf16[128,256]{1,0:T(8,128)(2,1)} %param.11) | copy-start | bytes 196612
  4.6 61.3 %copy-start.14 = (bf16[128,128]{1,0:T(8,128)(2,1)S(1)}, bf16[128,128]{1,0:T(8,128)(2,1)}, u32[]{:S(2)}) copy-start(bf16[128,128]{1,0:T(8,128)(2,1)} %param.10) | copy-start | bytes 98308
  4.6 62.0 %copy-start.13 = (bf16[128,256]{1,0:T(8,128)(2,1)S(1)}, bf16[128,256]{1,0:T(8,128)(2,1)}, u32[]{:S(2)}) copy-start(bf16[128,256]{1,0:T(8,128)(2,1)} %param.9) | copy-start | bytes 196612
  4.7 19.2 %collective-permute-start.1 = (bf16[128,578]{1,0:T(8,128)(2,1)S(1)}, bf16[128,578]{1,0:T(8,128)(2,1)S(1)}, u32[]{:S(2)}, u32[]{:S(2)}) collective-permute-start(bf16[128,578]{1,0:T(8,128)(2,1)S(1)} %pad_maximum_fusion.4), channel_id=1, source_target_pairs={{0,64},{32,96},{64,128},{96,160},{128,0},{160,32},{192,256},{224,2... | collective-permute-start | bytes 443912 | tf_op jit(solution)/shard_map/ppermute | solution.py:53
  15.8 19.6 %collective-permute-start = (bf16[128,578]{1,0:T(8,128)(2,1)S(1)}, bf16[128,578]{1,0:T(8,128)(2,1)S(1)}, u32[]{:S(2)}, u32[]{:S(2)}) collective-permute-start(bf16[128,578]{1,0:T(8,128)(2,1)S(1)} %pad_maximum_fusion.4), channel_id=1, source_target_pairs={{0,128},{32,160},{64,0},{96,32},{128,64},{160,96},{192,320},{224,3... | collective-permute-start | bytes 443912 | tf_op jit(solution)/shard_map/ppermute | solution.py:53
  35.5 16.3 %collective-permute-start.4 = (bf16[3,128,578]{2,1,0:T(8,128)(2,1)S(1)}, bf16[3,128,578]{2,1,0:T(8,128)(2,1)S(1)}, u32[]{:S(2)}, u32[]{:S(2)}) collective-permute-start(bf16[3,128,578]{2,1,0:T(8,128)(2,1)S(1)} %get-tuple-element.46), channel_id=1, source_target_pairs={{0,192},{32,224},{64,256},{96,288},{128,320},{160,352},{192,384},{... | collective-permute-start | bytes 1331720 | tf_op jit(solution)/shard_map/ppermute | solution.py:53
  38.9 22.6 %collective-permute-start.3 = (bf16[3,128,578]{2,1,0:T(8,128)(2,1)S(1)}, bf16[3,128,578]{2,1,0:T(8,128)(2,1)S(1)}, u32[]{:S(2)}, u32[]{:S(2)}) collective-permute-start(bf16[3,128,578]{2,1,0:T(8,128)(2,1)S(1)} %get-tuple-element.46), channel_id=1, source_target_pairs={{0,384},{32,416},{64,448},{96,480},{128,512},{160,544},{192,576},{... | collective-permute-start | bytes 1331720 | tf_op jit(solution)/shard_map/ppermute | solution.py:53
  43.6 19.5 %collective-permute-start.2 = (bf16[3,128,578]{2,1,0:T(8,128)(2,1)S(1)}, bf16[3,128,578]{2,1,0:T(8,128)(2,1)S(1)}, u32[]{:S(2)}, u32[]{:S(2)}) collective-permute-start(bf16[3,128,578]{2,1,0:T(8,128)(2,1)S(1)} %get-tuple-element.46), channel_id=1, source_target_pairs={{0,576},{32,608},{64,640},{96,672},{128,704},{160,736},{192,0},{22... | collective-permute-start | bytes 1331720 | tf_op jit(solution)/shard_map/ppermute | solution.py:53
  63.9 6.0 %collective-permute-start.5 = (bf16[4,3,128,640]{3,2,1,0:T(8,128)(2,1)S(1)}, bf16[4,3,128,640]{3,2,1,0:T(8,128)(2,1)}, u32[]{:S(2)}, u32[]{:S(2)}) collective-permute-start(bf16[4,3,128,640]{3,2,1,0:T(8,128)(2,1)S(1)} %fusion.22), channel_id=1, source_target_pairs={{0,32},{32,0},{64,96},{96,64},{128,160},{160,128},{192,224},{224,1... | collective-permute-start | bytes 5898248 | tf_op jit(solution)/shard_map/ppermute | solution.py:53
  71.8 4.1 %copy-start.1 = (bf16[2,4,3,128,578]{4,3,2,1,0:T(8,128)(2,1)}, bf16[2,4,3,128,578]{4,3,2,1,0:T(8,128)(2,1)S(1)}, u32[]{:S(2)}) copy-start(bf16[2,4,3,128,578]{4,3,2,1,0:T(8,128)(2,1)S(1)} %pad_maximum_fusion) | copy-start | bytes 10653700
  83.9 5.3 %collective-permute-start.6 = (bf16[2,2,4,3,128,128]{5,4,3,2,1,0:T(8,128)(2,1)S(1)}, bf16[2,2,4,3,128,128]{5,4,3,2,1,0:T(8,128)(2,1)S(1)}, u32[]{:S(2)}, u32[]{:S(2)}) collective-permute-start(bf16[2,2,4,3,128,128]{5,4,3,2,1,0:T(8,128)(2,1)S(1)} %fusion.24), channel_id=1, source_target_pairs={{0,32},{32,0},{64,96},{96,64},{128,160},{160,128},{192,224},{224,1... | collective-permute-start | bytes 4718600 | tf_op jit(solution)/shard_map/ppermute | solution.py:53
  90.0 21.9 %collective-permute-start.9 = (bf16[2,2,3,128,128]{4,3,2,1,0:T(8,128)(2,1)S(1)}, bf16[2,2,3,128,128]{4,3,2,1,0:T(8,128)(2,1)S(1)}, u32[]{:S(2)}, u32[]{:S(2)}) collective-permute-start(bf16[2,2,3,128,128]{4,3,2,1,0:T(8,128)(2,1)S(1)} %get-tuple-element.41), channel_id=1, source_target_pairs={{0,576},{32,608},{64,640},{96,672},{128,704},{160,736},{192,0},{22... | collective-permute-start | bytes 1179656 | tf_op jit(solution)/shard_map/ppermute | solution.py:53
  94.6 17.3 %collective-permute-start.8 = (bf16[2,2,3,128,128]{4,3,2,1,0:T(8,128)(2,1)S(1)}, bf16[2,2,3,128,128]{4,3,2,1,0:T(8,128)(2,1)S(1)}, u32[]{:S(2)}, u32[]{:S(2)}) collective-permute-start(bf16[2,2,3,128,128]{4,3,2,1,0:T(8,128)(2,1)S(1)} %get-tuple-element.42), channel_id=1, source_target_pairs={{0,384},{32,416},{64,448},{96,480},{128,512},{160,544},{192,576},{... | collective-permute-start | bytes 1179656 | tf_op jit(solution)/shard_map/ppermute | solution.py:53
  98.3 19.2 %collective-permute-start.7 = (bf16[2,2,3,128,128]{4,3,2,1,0:T(8,128)(2,1)S(1)}, bf16[2,2,3,128,128]{4,3,2,1,0:T(8,128)(2,1)S(1)}, u32[]{:S(2)}, u32[]{:S(2)}) collective-permute-start(bf16[2,2,3,128,128]{4,3,2,1,0:T(8,128)(2,1)S(1)} %get-tuple-element.40), channel_id=1, source_target_pairs={{0,192},{32,224},{64,256},{96,288},{128,320},{160,352},{192,384},{... | collective-permute-start | bytes 1179656 | tf_op jit(solution)/shard_map/ppermute | solution.py:53
  117.7 12.3 %collective-permute-start.11 = (bf16[2,2,128,128]{3,2,1,0:T(8,128)(2,1)S(1)}, bf16[2,2,128,128]{3,2,1,0:T(8,128)(2,1)S(1)}, u32[]{:S(2)}, u32[]{:S(2)}) collective-permute-start(bf16[2,2,128,128]{3,2,1,0:T(8,128)(2,1)S(1)} %get-tuple-element.48), channel_id=1, source_target_pairs={{0,128},{32,160},{64,0},{96,32},{128,64},{160,96},{192,320},{224,3... | collective-permute-start | bytes 393224 | tf_op jit(solution)/shard_map/ppermute | solution.py:53
  124.8 13.0 %collective-permute-start.10 = (bf16[2,2,128,128]{3,2,1,0:T(8,128)(2,1)S(1)}, bf16[2,2,128,128]{3,2,1,0:T(8,128)(2,1)S(1)}, u32[]{:S(2)}, u32[]{:S(2)}) collective-permute-start(bf16[2,2,128,128]{3,2,1,0:T(8,128)(2,1)S(1)} %get-tuple-element.47), channel_id=1, source_target_pairs={{0,64},{32,96},{64,128},{96,160},{128,0},{160,32},{192,256},{224,2... | collective-permute-start | bytes 393224 | tf_op jit(solution)/shard_map/ppermute | solution.py:53
  138.7 16.7 %collective-permute-start.13 = (bf16[128,512]{1,0:T(8,128)(2,1)}, bf16[128,512]{1,0:T(8,128)(2,1)}, u32[]{:S(2)}, u32[]{:S(2)}) collective-permute-start(bf16[128,512]{1,0:T(8,128)(2,1)} %convert_element_type.223), channel_id=1, source_target_pairs={{0,64},{32,96},{64,128},{96,160},{128,0},{160,32},{192,256},{224,2... | collective-permute-start | bytes 393224 | tf_op jit(solution)/shard_map/ppermute | solution.py:53
  142.9 13.8 %collective-permute-start.12 = (bf16[128,512]{1,0:T(8,128)(2,1)}, bf16[128,512]{1,0:T(8,128)(2,1)}, u32[]{:S(2)}, u32[]{:S(2)}) collective-permute-start(bf16[128,512]{1,0:T(8,128)(2,1)} %convert_element_type.223), channel_id=1, source_target_pairs={{0,128},{32,160},{64,0},{96,32},{128,64},{160,96},{192,320},{224,3... | collective-permute-start | bytes 393224 | tf_op jit(solution)/shard_map/ppermute | solution.py:53
  151.4 7.2 %collective-permute-start.14 = (bf16[128,512]{1,0:T(8,128)(2,1)}, bf16[128,512]{1,0:T(8,128)(2,1)}, u32[]{:S(2)}, u32[]{:S(2)}) collective-permute-start(bf16[128,512]{1,0:T(8,128)(2,1)} %fusion.28), channel_id=1, source_target_pairs={{0,1},{1,0},{2,3},{3,2},{4,5},{5,4},{6,7},{7,6},{8,9},{9,8},{10,11... | collective-permute-start | bytes 393224 | tf_op jit(solution)/shard_map/ppermute | solution.py:53
  159.6 17.3 %collective-permute-start.18 = (bf16[128,512]{1,0:T(8,128)(2,1)S(1)}, bf16[128,512]{1,0:T(8,128)(2,1)S(1)}, u32[]{:S(2)}, u32[]{:S(2)}) collective-permute-start(bf16[128,512]{1,0:T(8,128)(2,1)S(1)} %convert_add_fusion.3), channel_id=1, source_target_pairs={{0,6},{1,7},{2,0},{3,1},{4,2},{5,3},{6,4},{7,5},{8,14},{9,15},{10,... | collective-permute-start | bytes 393224 | tf_op jit(solution)/shard_map/ppermute | solution.py:53
  163.6 27.6 %collective-permute-start.17 = (bf16[3,128,512]{2,1,0:T(8,128)(2,1)}, bf16[3,128,512]{2,1,0:T(8,128)(2,1)}, u32[]{:S(2)}, u32[]{:S(2)}) collective-permute-start(bf16[3,128,512]{2,1,0:T(8,128)(2,1)} %pad_maximum_fusion.3), channel_id=1, source_target_pairs={{0,192},{32,224},{64,256},{96,288},{128,320},{160,352},{192,384},{... | collective-permute-start | bytes 1179656 | tf_op jit(solution)/shard_map/ppermute | solution.py:53
  167.5 23.7 %collective-permute-start.16 = (bf16[3,128,512]{2,1,0:T(8,128)(2,1)}, bf16[3,128,512]{2,1,0:T(8,128)(2,1)}, u32[]{:S(2)}, u32[]{:S(2)}) collective-permute-start(bf16[3,128,512]{2,1,0:T(8,128)(2,1)} %pad_maximum_fusion.3), channel_id=1, source_target_pairs={{0,384},{32,416},{64,448},{96,480},{128,512},{160,544},{192,576},{... | collective-permute-start | bytes 1179656 | tf_op jit(solution)/shard_map/ppermute | solution.py:53
  171.1 20.1 %collective-permute-start.15 = (bf16[3,128,512]{2,1,0:T(8,128)(2,1)}, bf16[3,128,512]{2,1,0:T(8,128)(2,1)}, u32[]{:S(2)}, u32[]{:S(2)}) collective-permute-start(bf16[3,128,512]{2,1,0:T(8,128)(2,1)} %pad_maximum_fusion.3), channel_id=1, source_target_pairs={{0,576},{32,608},{64,640},{96,672},{128,704},{160,736},{192,0},{22... | collective-permute-start | bytes 1179656 | tf_op jit(solution)/shard_map/ppermute | solution.py:53
  174.0 11.2 %collective-permute-start.19 = (bf16[128,512]{1,0:T(8,128)(2,1)S(1)}, bf16[128,512]{1,0:T(8,128)(2,1)}, u32[]{:S(2)}, u32[]{:S(2)}) collective-permute-start(bf16[128,512]{1,0:T(8,128)(2,1)S(1)} %convert_add_fusion.3), channel_id=1, source_target_pairs={{0,4},{1,5},{2,6},{3,7},{4,0},{5,1},{6,2},{7,3},{8,12},{9,13},{10,... | collective-permute-start | bytes 393224 | tf_op jit(solution)/shard_map/ppermute | solution.py:53
  177.6 12.5 %collective-permute-start.20 = (bf16[128,512]{1,0:T(8,128)(2,1)S(1)}, bf16[128,512]{1,0:T(8,128)(2,1)}, u32[]{:S(2)}, u32[]{:S(2)}) collective-permute-start(bf16[128,512]{1,0:T(8,128)(2,1)S(1)} %convert_add_fusion.3), channel_id=1, source_target_pairs={{0,2},{1,3},{2,4},{3,5},{4,6},{5,7},{6,0},{7,1},{8,10},{9,11},{10,... | collective-permute-start | bytes 393224 | tf_op jit(solution)/shard_map/ppermute | solution.py:53
  183.6 6.5 %copy-start.11 = (bf16[128,512]{1,0:T(8,128)(2,1)S(1)}, bf16[128,512]{1,0:T(8,128)(2,1)}, u32[]{:S(2)}) copy-start(bf16[128,512]{1,0:T(8,128)(2,1)} %copy-done.10) | copy-start | bytes 393220
  195.0 6.9 %collective-permute-start.21 = (bf16[128,512]{1,0:T(8,128)(2,1)S(1)}, bf16[128,512]{1,0:T(8,128)(2,1)S(1)}, u32[]{:S(2)}, u32[]{:S(2)}) collective-permute-start(bf16[128,512]{1,0:T(8,128)(2,1)S(1)} %convert_add_fusion.2), channel_id=1, source_target_pairs={{0,8},{1,9},{2,10},{3,11},{4,12},{5,13},{6,14},{7,15},{8,0},{9,1},... | collective-permute-start | bytes 393224 | tf_op jit(solution)/shard_map/ppermute | solution.py:53
  202.0 20.7 %collective-permute-start.22 = (f32[512,512]{1,0:T(8,128)}, f32[512,512]{1,0:T(8,128)}, u32[]{:S(2)}, u32[]{:S(2)}) collective-permute-start(f32[512,512]{1,0:T(8,128)} %add_bitcast_fusion), channel_id=1, source_target_pairs={{0,32},{32,0},{64,96},{96,64},{128,160},{160,128},{192,224},{224,1... | collective-permute-start | bytes 3145736 | tf_op jit(solution)/shard_map/ppermute | solution.py:53
  205.1 19.4 %copy-start.3 = (f32[128,4,128]{2,1,0:T(4,128)S(1)}, f32[128,4,128]{2,1,0:T(4,128)}, u32[]{:S(2)}) copy-start(f32[128,4,128]{2,1,0:T(4,128)} %copy-done.2) | copy-start | bytes 786436
  205.1 17.6 %collective-permute-start.23 = (bf16[128,512]{1,0:T(8,128)(2,1)S(1)}, bf16[128,512]{1,0:T(8,128)(2,1)S(1)}, u32[]{:S(2)}, u32[]{:S(2)}) collective-permute-start(bf16[128,512]{1,0:T(8,128)(2,1)S(1)} %convert_add_fusion.1), channel_id=1, source_target_pairs={{0,16},{1,17},{2,18},{3,19},{4,20},{5,21},{6,22},{7,23},{8,24},{9,... | collective-permute-start | bytes 393224 | tf_op jit(solution)/shard_map/ppermute | solution.py:53
  (8 other events, 9.8 us)
